TPU v7x, 256 devices: a whole 4x4x8 slice. The times are simulated.
256 devices in a mesh: gy: 4 (over y), gx: 64 (over x, z, core).
Axes of the slice: x: 4, y: 4, z: 8, core: 2. Of those that a mesh axis runs over, the one named last changes fastest.
Arguments:
- fields: bfloat16 [4, 16, 131072], P('gy', None, 'gx'), may hold values from -6 to 6
- leaf_inverse: bfloat16 [4, 512, 256, 256], P('gy', 'gx'), may hold values from -0.375 to 0.375
- coupling: bfloat16 [4, 512, 64, 256], P('gy', 'gx'), may hold values from -0.375 to 0.375
- skeleton_index: int32 [4, 512, 64], P('gy', 'gx'), may hold values from 0 to 255, as said below
- up_coef: float32 [4, 192, 4, 512], P('gy', 'gx'), may hold values from -0.5 to 0.5
- down_coef: float32 [4, 192, 4, 512], P('gy', 'gx'), may hold values from -0.5 to 0.5
- merge_own: bfloat16 [4, 192, 512, 512], P('gy', 'gx'), may hold values from -0.1875 to 0.1875
- merge_other: bfloat16 [4, 192, 512, 512], P('gy', 'gx'), may hold values from -0.1875 to 0.1875
- top_inverse: bfloat16 [4, 32768, 512], P('gy', 'gx'), may hold values from -0.1875 to 0.1875
- compress: bfloat16 [4, 2048, 512], P('gy', 'gx'), may hold values from -0.25 to 0.25
- top_couple: bfloat16 [8192, 8192], P(None, ('gy', 'gx')), may hold values from -0.25 to 0.25
Outputs:
- solution: float32 [4, 16, 131072], P('gy', None, 'gx')
Inputs may be any that keep to these rules, and one draw needn't show every extreme that they name: `skeleton_index`: the 64 positions of one box are distinct.
All inputs are finite; a program needn't handle non-finite values.
Results may differ from a plain program's by a relative error of at most 0.015.
Values may be sent and summed in bfloat16 or wider, within the bound.
No kernel may reach another device: no remote copies, remote signals or barrier semaphores. Data moves between devices by JAX's collectives and lax.ppermute only.
A program may use at most 64 MiB of HBM per device.

v0:
```python
import jax
import jax.numpy as jnp
from jax import lax
from jax.sharding import PartitionSpec as P


def padded_2(shard, sides, width):
    edges = {}
    for axis, dim in sides:
        size, length = (lax.axis_size(axis), shard.shape[dim])
        up = [(i, (i + 1) % size) for i in range(size - 1)]
        last = lax.slice_in_dim(shard, length - width, length, axis=dim)
        leading = lax.slice_in_dim(shard, 0, width, axis=dim)
        edges[dim] = (
            lax.ppermute(last, axis, up),
            lax.ppermute(leading, axis, [(b, a) for a, b in up]),
        )
    done = []
    for _, dim in sides:
        low, high = edges[dim]
        around = [(width, width) if d in done else (0, 0) for d in range(shard.ndim)]
        shard = jnp.concatenate([jnp.pad(low, around), shard, jnp.pad(high, around)], axis=dim)
        done.append(dim)
    return shard


def partner_2(shard, axis, stride):
    return lax.ppermute(shard, axis, [(i, i ^ 1 << stride) for i in range(lax.axis_size(axis))])


def sent_to_all(shard, axis):
    copies = jnp.broadcast_to(shard, (lax.axis_size(axis), *shard.shape))
    return lax.all_to_all(copies, axis, split_axis=0, concat_axis=0, tiled=True)


def joined_along(parts, dim):
    shape = list(parts.shape[1:])
    shape[dim] *= parts.shape[0]
    return jnp.moveaxis(parts, 0, dim).reshape(shape)


def collect(shard, axis, dim):
    parts = sent_to_all(shard, axis)
    return joined_along(parts, dim)


def neighbour_mix(padded, coefs):
    total = coefs[0] * padded[0, 1] + coefs[1] * padded[2, 1]
    return total + coefs[2] * padded[1, 0] + coefs[3] * padded[1, 2]


def right_transpose(values, matrix):
    return lax.dot_general(
        values, matrix, (((1,), (1,)), ((), ())), preferred_element_type=jnp.float32
    )


def body(
    fields,
    leaf_inverse,
    coupling,
    skeleton_index,
    up_coef,
    down_coef,
    merge_own,
    merge_other,
    top_inverse,
    compress,
    top_couple,
):
    field_count = fields.shape[1]
    box_count = leaf_inverse.shape[1]
    box_size = leaf_inverse.shape[2]
    skel_size = coupling.shape[2]
    skel_total = box_count * skel_size
    level_count = merge_own.shape[1]
    blocks = fields[0].reshape(field_count, box_count, box_size)
    inverse = leaf_inverse[0]
    weights = coupling[0]
    index = skeleton_index[0]
    own = merge_own[0]
    other = merge_other[0]
    up_rates = up_coef[0]
    down_rates = down_coef[0]
    positions = lax.broadcasted_iota(jnp.int32, (box_count, skel_size, box_size), 2)
    selector = index[:, :, None] == positions
    select_half = selector.astype(jnp.bfloat16)
    select_full = selector.astype(jnp.float32)
    solved = jnp.einsum("fbq,bqr->fbr", blocks, inverse, preferred_element_type=jnp.float32).astype(
        jnp.bfloat16
    )
    picked = jnp.einsum("fbq,bkq->fbk", blocks, select_half, preferred_element_type=jnp.float32)
    state = picked - jnp.einsum("fbq,bkq->fbk", solved, weights, preferred_element_type=jnp.float32)
    state = state.reshape(field_count, skel_total)
    for level in range(level_count):
        padded = padded_2(state[None, None], (("gy", 0), ("gx", 1)), 1)
        mixed = state - neighbour_mix(padded, up_rates[level])
        rounded = mixed.astype(jnp.bfloat16)
        partner = partner_2(rounded, "gx", level)
        state = jnp.dot(rounded, own[level], preferred_element_type=jnp.float32)
        state = state + jnp.dot(partner, other[level], preferred_element_type=jnp.float32)
    top_state = state.astype(jnp.bfloat16)
    comp = compress[0]
    small = right_transpose(top_state, comp).astype(jnp.bfloat16)
    row_values = collect(small, "gx", 1)
    coarse = jnp.dot(collect(row_values, "gy", 1), top_couple, preferred_element_type=jnp.float32)
    state = jnp.dot(top_state, top_inverse[0], preferred_element_type=jnp.float32)
    state = state + jnp.dot(coarse.astype(jnp.bfloat16), comp, preferred_element_type=jnp.float32)
    for level in reversed(range(level_count)):
        rounded = state.astype(jnp.bfloat16)
        sent = right_transpose(rounded, other[level])
        received = partner_2(sent.astype(jnp.bfloat16), "gx", level).astype(sent.dtype)
        mixed = right_transpose(rounded, own[level]) + received
        padded = padded_2(mixed[None, None].astype(jnp.bfloat16), (("gy", 0), ("gx", 1)), 1).astype(
            jnp.float32
        )
        state = mixed - neighbour_mix(padded, down_rates[level])
    skeleton = state.reshape(field_count, box_count, skel_size)
    back = jnp.einsum(
        "fbk,bkq->fbq", skeleton.astype(jnp.bfloat16), weights, preferred_element_type=jnp.float32
    ).astype(jnp.bfloat16)
    fixed = jnp.einsum("fbq,bqr->fbr", back, inverse, preferred_element_type=jnp.float32)
    placed = jnp.einsum("fbk,bkq->fbq", skeleton, select_full)
    result = solved.astype(jnp.float32) - fixed + placed
    return result.reshape(1, field_count, box_count * box_size)


def solution(mesh):
    placed = (
        P("gy", None, "gx"),
        P("gy", "gx", None, None),
        P("gy", "gx", None, None),
        P("gy", "gx", None),
        P("gy", "gx", None, None),
        P("gy", "gx", None, None),
        P("gy", "gx", None, None),
        P("gy", "gx", None, None),
        P("gy", "gx", None),
        P("gy", "gx", None),
        P(None, ("gy", "gx")),
    )
    return jax.shard_map(
        body, mesh=mesh, in_specs=placed, out_specs=P("gy", None, "gx"), check_vma=False
    )
```

profile of v0, /device:TPU:10, one launch (start us, length us, event | category | flops | bytes accessed | tf_op | source)
XLA Modules:
  0.0 146.5 jit_solution(3164596719614381131)
XLA Ops:
  0.0 0.9 copy.41
  1.0 0.3 copy-done
  1.3 0.2 fusion.3
  1.5 1.2 convolution_bitcast_fusion.2
  2.7 0.3 fusion.4
  3.1 3.5 %collective-permute-start = (f32[1,1,16,512]{3,2,1,0:T(8,128)S(1)}, f32[1,1,16,512]{3,2,1,0:T(8,128)S(1)}, u32[]{:S(2)}, u32[]{:S(2)}) collective-permute-start(f32[1,1,16,512]{3,2,1,0:T(8,128)S(1)} %broadcast_in_dim_reshape.3), channel_id=1, source_target_pairs={{0,64},{64,128},{128,192},{1,65},{65,129},{129,193},{2,66},{66,130... | collective-permute-start | bytes 98312 | tf_op jit(solution)/shard_map/ppermute | solution.py:15
  6.6 2.4 %collective-permute-start.1 = (f32[1,1,16,512]{3,2,1,0:T(8,128)S(1)}, f32[1,1,16,512]{3,2,1,0:T(8,128)S(1)}, u32[]{:S(2)}, u32[]{:S(2)}) collective-permute-start(f32[1,1,16,512]{3,2,1,0:T(8,128)S(1)} %broadcast_in_dim_reshape.3), channel_id=1, source_target_pairs={{64,0},{128,64},{192,128},{65,1},{129,65},{193,129},{66,2},{130,66... | collective-permute-start | bytes 98312 | tf_op jit(solution)/shard_map/ppermute | solution.py:16
  9.0 1.9 %collective-permute-start.2 = (f32[1,1,16,512]{3,2,1,0:T(8,128)S(1)}, f32[1,1,16,512]{3,2,1,0:T(8,128)S(1)}, u32[]{:S(2)}, u32[]{:S(2)}) collective-permute-start(f32[1,1,16,512]{3,2,1,0:T(8,128)S(1)} %broadcast_in_dim_reshape.3), channel_id=1, source_target_pairs={{0,1},{1,2},{2,3},{3,4},{4,5},{5,6},{6,7},{7,8},{8,9},{9,10},{10,1... | collective-permute-start | bytes 98312 | tf_op jit(solution)/shard_map/ppermute | solution.py:15
  10.9 6.6 %collective-permute-start.3 = (f32[1,1,16,512]{3,2,1,0:T(8,128)S(1)}, f32[1,1,16,512]{3,2,1,0:T(8,128)S(1)}, u32[]{:S(2)}, u32[]{:S(2)}) collective-permute-start(f32[1,1,16,512]{3,2,1,0:T(8,128)S(1)} %broadcast_in_dim_reshape.3), channel_id=1, source_target_pairs={{1,0},{2,1},{3,2},{4,3},{5,4},{6,5},{7,6},{8,7},{9,8},{10,9},{11,1... | collective-permute-start | bytes 98312 | tf_op jit(solution)/shard_map/ppermute | solution.py:16
  18.0 1.1 collective-permute-done.3
  19.7 1.2 fusion.25
  21.0 0.2 convolution_add_fusion.5
  21.1 3.5 %collective-permute-start.5 = (f32[1,1,16,512]{3,2,1,0:T(8,128)S(1)}, f32[1,1,16,512]{3,2,1,0:T(8,128)S(1)}, u32[]{:S(2)}, u32[]{:S(2)}) collective-permute-start(f32[1,1,16,512]{3,2,1,0:T(8,128)S(1)} %bitcast.309), channel_id=1, source_target_pairs={{0,64},{64,128},{128,192},{1,65},{65,129},{129,193},{2,66},{66,130... | collective-permute-start | bytes 98312 | tf_op jit(solution)/shard_map/ppermute | solution.py:15
  24.6 2.4 %collective-permute-start.6 = (f32[1,1,16,512]{3,2,1,0:T(8,128)S(1)}, f32[1,1,16,512]{3,2,1,0:T(8,128)S(1)}, u32[]{:S(2)}, u32[]{:S(2)}) collective-permute-start(f32[1,1,16,512]{3,2,1,0:T(8,128)S(1)} %bitcast.310), channel_id=1, source_target_pairs={{64,0},{128,64},{192,128},{65,1},{129,65},{193,129},{66,2},{130,66... | collective-permute-start | bytes 98312 | tf_op jit(solution)/shard_map/ppermute | solution.py:16
  27.0 1.9 %collective-permute-start.7 = (f32[1,1,16,512]{3,2,1,0:T(8,128)S(1)}, f32[1,1,16,512]{3,2,1,0:T(8,128)S(1)}, u32[]{:S(2)}, u32[]{:S(2)}) collective-permute-start(f32[1,1,16,512]{3,2,1,0:T(8,128)S(1)} %bitcast.311), channel_id=1, source_target_pairs={{0,1},{1,2},{2,3},{3,4},{4,5},{5,6},{6,7},{7,8},{8,9},{9,10},{10,1... | collective-permute-start | bytes 98312 | tf_op jit(solution)/shard_map/ppermute | solution.py:15
  28.9 5.8 %collective-permute-start.8 = (f32[1,1,16,512]{3,2,1,0:T(8,128)S(1)}, f32[1,1,16,512]{3,2,1,0:T(8,128)S(1)}, u32[]{:S(2)}, u32[]{:S(2)}) collective-permute-start(f32[1,1,16,512]{3,2,1,0:T(8,128)S(1)} %bitcast.312), channel_id=1, source_target_pairs={{1,0},{2,1},{3,2},{4,3},{5,4},{6,5},{7,6},{8,7},{9,8},{10,9},{11,1... | collective-permute-start | bytes 98312 | tf_op jit(solution)/shard_map/ppermute | solution.py:16
  34.7 1.5 %collective-permute-done.8 = f32[1,1,16,512]{3,2,1,0:T(8,128)S(1)} collective-permute-done((f32[1,1,16,512]{3,2,1,0:T(8,128)S(1)}, f32[1,1,16,512]{3,2,1,0:T(8,128)S(1)}, u32[]{:S(2)}, u32[]{:S(2)}) %collective-permute-start.8) | collective-permute-done | bytes 32800 | tf_op jit(solution)/shard_map/ppermute | solution.py:16
  36.4 1.2 fusion.20
  37.6 2.5 %collective-permute-done.9 = bf16[16,512]{1,0:T(8,128)(2,1)S(1)} collective-permute-done((bf16[16,512]{1,0:T(8,128)(2,1)S(1)}, bf16[16,512]{1,0:T(8,128)(2,1)S(1)}, u32[]{:S(2)}, u32[]{:S(2)}) %collective-permute-start.9) | collective-permute-done | bytes 16416 | tf_op jit(solution)/shard_map/ppermute | solution.py:28
  40.3 3.5 %collective-permute-start.10 = (f32[1,1,16,512]{3,2,1,0:T(8,128)S(1)}, f32[1,1,16,512]{3,2,1,0:T(8,128)S(1)}, u32[]{:S(2)}, u32[]{:S(2)}) collective-permute-start(f32[1,1,16,512]{3,2,1,0:T(8,128)S(1)} %bitcast.305), channel_id=1, source_target_pairs={{0,64},{64,128},{128,192},{1,65},{65,129},{129,193},{2,66},{66,130... | collective-permute-start | bytes 98312 | tf_op jit(solution)/shard_map/ppermute | solution.py:15
  43.8 2.4 %collective-permute-start.11 = (f32[1,1,16,512]{3,2,1,0:T(8,128)S(1)}, f32[1,1,16,512]{3,2,1,0:T(8,128)S(1)}, u32[]{:S(2)}, u32[]{:S(2)}) collective-permute-start(f32[1,1,16,512]{3,2,1,0:T(8,128)S(1)} %bitcast.306), channel_id=1, source_target_pairs={{64,0},{128,64},{192,128},{65,1},{129,65},{193,129},{66,2},{130,66... | collective-permute-start | bytes 98312 | tf_op jit(solution)/shard_map/ppermute | solution.py:16
  46.1 1.9 %collective-permute-start.12 = (f32[1,1,16,512]{3,2,1,0:T(8,128)S(1)}, f32[1,1,16,512]{3,2,1,0:T(8,128)S(1)}, u32[]{:S(2)}, u32[]{:S(2)}) collective-permute-start(f32[1,1,16,512]{3,2,1,0:T(8,128)S(1)} %bitcast.307), channel_id=1, source_target_pairs={{0,1},{1,2},{2,3},{3,4},{4,5},{5,6},{6,7},{7,8},{8,9},{9,10},{10,1... | collective-permute-start | bytes 98312 | tf_op jit(solution)/shard_map/ppermute | solution.py:15
  48.1 5.8 %collective-permute-start.13 = (f32[1,1,16,512]{3,2,1,0:T(8,128)S(1)}, f32[1,1,16,512]{3,2,1,0:T(8,128)S(1)}, u32[]{:S(2)}, u32[]{:S(2)}) collective-permute-start(f32[1,1,16,512]{3,2,1,0:T(8,128)S(1)} %bitcast.308), channel_id=1, source_target_pairs={{1,0},{2,1},{3,2},{4,3},{5,4},{6,5},{7,6},{8,7},{9,8},{10,9},{11,1... | collective-permute-start | bytes 98312 | tf_op jit(solution)/shard_map/ppermute | solution.py:16
  53.9 1.5 %collective-permute-done.13 = f32[1,1,16,512]{3,2,1,0:T(8,128)S(1)} collective-permute-done((f32[1,1,16,512]{3,2,1,0:T(8,128)S(1)}, f32[1,1,16,512]{3,2,1,0:T(8,128)S(1)}, u32[]{:S(2)}, u32[]{:S(2)}) %collective-permute-start.13) | collective-permute-done | bytes 32800 | tf_op jit(solution)/shard_map/ppermute | solution.py:16
  55.4 0.5 collective-permute-start.14
  55.9 1.2 fusion.15
  57.1 3.0 %collective-permute-done.14 = bf16[16,512]{1,0:T(8,128)(2,1)S(1)} collective-permute-done((bf16[16,512]{1,0:T(8,128)(2,1)S(1)}, bf16[16,512]{1,0:T(8,128)(2,1)S(1)}, u32[]{:S(2)}, u32[]{:S(2)}) %collective-permute-start.14) | collective-permute-done | bytes 16416 | tf_op jit(solution)/shard_map/ppermute | solution.py:28
  60.1 0.2 fusion.6
  60.7 17.0 %all_to_all.10 = bf16[64,2,256]{2,1,0:T(2,128)(2,1)S(1)} all-to-all(bf16[64,2,256]{2,1,0:T(2,128)(2,1)S(1)} %reshape.143), channel_id=1, replica_groups=mesh['gy'=4,'gx'=64] {'gx'}, dimensions={0} | all-to-all | bytes 131072 | tf_op jit(solution)/shard_map/all_to_all | solution.py:33
  77.7 0.2 reshape.144
  78.0 0.3 reshape.117
  78.3 0.7 broadcast_in_dim.18
  79.0 4.9 %all-to-all-start.1 = ((bf16[4,16,2048]{2,1,0:T(8,128)(2,1)}), bf16[4,16,2048]{2,1,0:T(8,128)(2,1)S(1)}, u32[]{:S(2)}, u32[]{:S(2)}) async-start(bf16[4,16,2048]{2,1,0:T(8,128)(2,1)} %broadcast_in_dim.18), calls=%async_computation.1 | async-start | bytes 524288 | tf_op jit(solution)/shard_map/all_to_all | solution.py:33
  83.9 1.2 fusion.9
  85.1 4.3 %all-to-all-done.1 = bf16[4,16,2048]{2,1,0:T(8,128)(2,1)S(1)} async-done(((bf16[4,16,2048]{2,1,0:T(8,128)(2,1)}), bf16[4,16,2048]{2,1,0:T(8,128)(2,1)S(1)}, u32[]{:S(2)}, u32[]{:S(2)}) %all-to-all-start.1) | async-done | bytes 262176 | tf_op jit(solution)/shard_map/all_to_all | solution.py:33
  89.4 1.4 fusion.5
  90.9 0.2 convolution_convert_fusion.4
  91.1 1.0 collective-permute-start.15
  92.1 1.3 fusion.13
  93.3 2.4 %collective-permute-done.15 = bf16[16,512]{1,0:T(8,128)(2,1)S(1)} collective-permute-done((bf16[16,512]{1,0:T(8,128)(2,1)S(1)}, bf16[16,512]{1,0:T(8,128)(2,1)S(1)}, u32[]{:S(2)}, u32[]{:S(2)}) %collective-permute-start.15) | collective-permute-done | bytes 16416 | tf_op jit(solution)/shard_map/ppermute | solution.py:28
  95.8 1.9 %collective-permute-start.16 = (bf16[1,1,16,512]{3,2,1,0:T(8,128)(2,1)S(1)}, bf16[1,1,16,512]{3,2,1,0:T(8,128)(2,1)S(1)}, u32[]{:S(2)}, u32[]{:S(2)}) collective-permute-start(bf16[1,1,16,512]{3,2,1,0:T(8,128)(2,1)S(1)} %fusion.111), channel_id=1, source_target_pairs={{0,1},{1,2},{2,3},{3,4},{4,5},{5,6},{6,7},{7,8},{8,9},{9,10},{10,1... | collective-permute-start | bytes 49160 | tf_op jit(solution)/shard_map/ppermute | solution.py:15
  97.7 1.9 %collective-permute-start.17 = (bf16[1,1,16,512]{3,2,1,0:T(8,128)(2,1)S(1)}, bf16[1,1,16,512]{3,2,1,0:T(8,128)(2,1)S(1)}, u32[]{:S(2)}, u32[]{:S(2)}) collective-permute-start(bf16[1,1,16,512]{3,2,1,0:T(8,128)(2,1)S(1)} %fusion.111), channel_id=1, source_target_pairs={{0,64},{64,128},{128,192},{1,65},{65,129},{129,193},{2,66},{66,130... | collective-permute-start | bytes 49160 | tf_op jit(solution)/shard_map/ppermute | solution.py:15
  99.6 3.9 %collective-permute-start.18 = (bf16[1,1,16,512]{3,2,1,0:T(8,128)(2,1)S(1)}, bf16[1,1,16,512]{3,2,1,0:T(8,128)(2,1)S(1)}, u32[]{:S(2)}, u32[]{:S(2)}) collective-permute-start(bf16[1,1,16,512]{3,2,1,0:T(8,128)(2,1)S(1)} %fusion.111), channel_id=1, source_target_pairs={{64,0},{128,64},{192,128},{65,1},{129,65},{193,129},{66,2},{130,66... | collective-permute-start | bytes 49160 | tf_op jit(solution)/shard_map/ppermute | solution.py:16
  103.5 5.2 %collective-permute-start.19 = (bf16[1,1,16,512]{3,2,1,0:T(8,128)(2,1)S(1)}, bf16[1,1,16,512]{3,2,1,0:T(8,128)(2,1)S(1)}, u32[]{:S(2)}, u32[]{:S(2)}) collective-permute-start(bf16[1,1,16,512]{3,2,1,0:T(8,128)(2,1)S(1)} %fusion.111), channel_id=1, source_target_pairs={{1,0},{2,1},{3,2},{4,3},{5,4},{6,5},{7,6},{8,7},{9,8},{10,9},{11,1... | collective-permute-start | bytes 49160 | tf_op jit(solution)/shard_map/ppermute | solution.py:16
  108.8 1.4 collective-permute-done.19
  110.2 0.2 convolution_convert_fusion.3
  110.5 3.7 %collective-permute-done.20 = bf16[16,512]{1,0:T(8,128)(2,1)S(1)} collective-permute-done((bf16[16,512]{1,0:T(8,128)(2,1)S(1)}, bf16[16,512]{1,0:T(8,128)(2,1)S(1)}, u32[]{:S(2)}, u32[]{:S(2)}) %collective-permute-start.20) | collective-permute-done | bytes 16416 | tf_op jit(solution)/shard_map/ppermute | solution.py:28
  114.2 0.2 convolution_add_fusion.2
  114.4 1.9 %collective-permute-start.21 = (bf16[1,1,16,512]{3,2,1,0:T(8,128)(2,1)S(1)}, bf16[1,1,16,512]{3,2,1,0:T(8,128)(2,1)S(1)}, u32[]{:S(2)}, u32[]{:S(2)}) collective-permute-start(bf16[1,1,16,512]{3,2,1,0:T(8,128)(2,1)S(1)} %convert_bitcast_fusion.1), channel_id=1, source_target_pairs={{0,1},{1,2},{2,3},{3,4},{4,5},{5,6},{6,7},{7,8},{8,9},{9,10},{10,1... | collective-permute-start | bytes 49160 | tf_op jit(solution)/shard_map/ppermute | solution.py:15
  116.4 2.2 %collective-permute-start.22 = (bf16[1,1,16,512]{3,2,1,0:T(8,128)(2,1)S(1)}, bf16[1,1,16,512]{3,2,1,0:T(8,128)(2,1)S(1)}, u32[]{:S(2)}, u32[]{:S(2)}) collective-permute-start(bf16[1,1,16,512]{3,2,1,0:T(8,128)(2,1)S(1)} %convert_bitcast_fusion.1), channel_id=1, source_target_pairs={{0,64},{64,128},{128,192},{1,65},{65,129},{129,193},{2,66},{66,130... | collective-permute-start | bytes 49160 | tf_op jit(solution)/shard_map/ppermute | solution.py:15
  118.6 3.6 %collective-permute-start.23 = (bf16[1,1,16,512]{3,2,1,0:T(8,128)(2,1)S(1)}, bf16[1,1,16,512]{3,2,1,0:T(8,128)(2,1)S(1)}, u32[]{:S(2)}, u32[]{:S(2)}) collective-permute-start(bf16[1,1,16,512]{3,2,1,0:T(8,128)(2,1)S(1)} %convert_bitcast_fusion.1), channel_id=1, source_target_pairs={{64,0},{128,64},{192,128},{65,1},{129,65},{193,129},{66,2},{130,66... | collective-permute-start | bytes 49160 | tf_op jit(solution)/shard_map/ppermute | solution.py:16
  122.2 5.2 %collective-permute-start.24 = (bf16[1,1,16,512]{3,2,1,0:T(8,128)(2,1)S(1)}, bf16[1,1,16,512]{3,2,1,0:T(8,128)(2,1)S(1)}, u32[]{:S(2)}, u32[]{:S(2)}) collective-permute-start(bf16[1,1,16,512]{3,2,1,0:T(8,128)(2,1)S(1)} %convert_bitcast_fusion.1), channel_id=1, source_target_pairs={{1,0},{2,1},{3,2},{4,3},{5,4},{6,5},{7,6},{8,7},{9,8},{10,9},{11,1... | collective-permute-start | bytes 49160 | tf_op jit(solution)/shard_map/ppermute | solution.py:16
  127.5 1.4 collective-permute-done.24
  128.9 0.2 convolution_convert_fusion.2
  129.1 1.2 collective-permute-done.25
  130.3 0.2 convolution_add_fusion.1
  130.6 2.1 %collective-permute-start.26 = (bf16[1,1,16,512]{3,2,1,0:T(8,128)(2,1)S(1)}, bf16[1,1,16,512]{3,2,1,0:T(8,128)(2,1)S(1)}, u32[]{:S(2)}, u32[]{:S(2)}) collective-permute-start(bf16[1,1,16,512]{3,2,1,0:T(8,128)(2,1)S(1)} %convert_bitcast_fusion), channel_id=1, source_target_pairs={{0,1},{1,2},{2,3},{3,4},{4,5},{5,6},{6,7},{7,8},{8,9},{9,10},{10,1... | collective-permute-start | bytes 49160 | tf_op jit(solution)/shard_map/ppermute | solution.py:15
  132.7 2.2 %collective-permute-start.27 = (bf16[1,1,16,512]{3,2,1,0:T(8,128)(2,1)S(1)}, bf16[1,1,16,512]{3,2,1,0:T(8,128)(2,1)S(1)}, u32[]{:S(2)}, u32[]{:S(2)}) collective-permute-start(bf16[1,1,16,512]{3,2,1,0:T(8,128)(2,1)S(1)} %convert_bitcast_fusion), channel_id=1, source_target_pairs={{0,64},{64,128},{128,192},{1,65},{65,129},{129,193},{2,66},{66,130... | collective-permute-start | bytes 49160 | tf_op jit(solution)/shard_map/ppermute | solution.py:15
  134.9 3.6 %collective-permute-start.28 = (bf16[1,1,16,512]{3,2,1,0:T(8,128)(2,1)S(1)}, bf16[1,1,16,512]{3,2,1,0:T(8,128)(2,1)S(1)}, u32[]{:S(2)}, u32[]{:S(2)}) collective-permute-start(bf16[1,1,16,512]{3,2,1,0:T(8,128)(2,1)S(1)} %convert_bitcast_fusion), channel_id=1, source_target_pairs={{64,0},{128,64},{192,128},{65,1},{129,65},{193,129},{66,2},{130,66... | collective-permute-start | bytes 49160 | tf_op jit(solution)/shard_map/ppermute | solution.py:16
  138.5 5.0 %collective-permute-start.29 = (bf16[1,1,16,512]{3,2,1,0:T(8,128)(2,1)S(1)}, bf16[1,1,16,512]{3,2,1,0:T(8,128)(2,1)S(1)}, u32[]{:S(2)}, u32[]{:S(2)}) collective-permute-start(bf16[1,1,16,512]{3,2,1,0:T(8,128)(2,1)S(1)} %convert_bitcast_fusion), channel_id=1, source_target_pairs={{1,0},{2,1},{3,2},{4,3},{5,4},{6,5},{7,6},{8,7},{9,8},{10,9},{11,1... | collective-permute-start | bytes 49160 | tf_op jit(solution)/shard_map/ppermute | solution.py:16
  143.6 1.4 collective-permute-done.29
  145.2 0.3 fusion
  145.5 0.3 fusion.1
  145.9 0.7 reshape.120
  (74 shorter events, 2.3 us)
Async XLA Ops:
  0.0 1.3 copy-start
  0.0 2.7 %copy-start.7 = (s32[1,8,64]{2,1,0:T(8,128)S(1)}, s32[1,8,64]{2,1,0:T(8,128)}, u32[]{:S(2)}) copy-start(s32[1,8,64]{2,1,0:T(8,128)} %param.14) | copy-start | bytes 6148
  0.0 17.5 %copy-start.5 = (f32[1,3,4,512]{3,2,1,0:T(4,128)S(1)}, f32[1,3,4,512]{3,2,1,0:T(4,128)}, u32[]{:S(2)}) copy-start(f32[1,3,4,512]{3,2,1,0:T(4,128)} %param.15) | copy-start | bytes 73732
  1.5 19.5 %copy-start.1 = (bf16[1,3,512,512]{3,2,1,0:T(8,128)(2,1)S(1)}, bf16[1,3,512,512]{3,2,1,0:T(8,128)(2,1)}, u32[]{:S(2)}) copy-start(bf16[1,3,512,512]{3,2,1,0:T(8,128)(2,1)} %param.18) | copy-start | bytes 4718596
  3.1 14.8 %collective-permute-start = (f32[1,1,16,512]{3,2,1,0:T(8,128)S(1)}, f32[1,1,16,512]{3,2,1,0:T(8,128)S(1)}, u32[]{:S(2)}, u32[]{:S(2)}) collective-permute-start(f32[1,1,16,512]{3,2,1,0:T(8,128)S(1)} %broadcast_in_dim_reshape.3), channel_id=1, source_target_pairs={{0,64},{64,128},{128,192},{1,65},{65,129},{129,193},{2,66},{66,130... | collective-permute-start | bytes 98312 | tf_op jit(solution)/shard_map/ppermute | solution.py:15
  6.6 11.4 %collective-permute-start.1 = (f32[1,1,16,512]{3,2,1,0:T(8,128)S(1)}, f32[1,1,16,512]{3,2,1,0:T(8,128)S(1)}, u32[]{:S(2)}, u32[]{:S(2)}) collective-permute-start(f32[1,1,16,512]{3,2,1,0:T(8,128)S(1)} %broadcast_in_dim_reshape.3), channel_id=1, source_target_pairs={{64,0},{128,64},{192,128},{65,1},{129,65},{193,129},{66,2},{130,66... | collective-permute-start | bytes 98312 | tf_op jit(solution)/shard_map/ppermute | solution.py:16
  9.0 9.0 %collective-permute-start.2 = (f32[1,1,16,512]{3,2,1,0:T(8,128)S(1)}, f32[1,1,16,512]{3,2,1,0:T(8,128)S(1)}, u32[]{:S(2)}, u32[]{:S(2)}) collective-permute-start(f32[1,1,16,512]{3,2,1,0:T(8,128)S(1)} %broadcast_in_dim_reshape.3), channel_id=1, source_target_pairs={{0,1},{1,2},{2,3},{3,4},{4,5},{5,6},{6,7},{7,8},{8,9},{9,10},{10,1... | collective-permute-start | bytes 98312 | tf_op jit(solution)/shard_map/ppermute | solution.py:15
  10.9 8.2 %collective-permute-start.3 = (f32[1,1,16,512]{3,2,1,0:T(8,128)S(1)}, f32[1,1,16,512]{3,2,1,0:T(8,128)S(1)}, u32[]{:S(2)}, u32[]{:S(2)}) collective-permute-start(f32[1,1,16,512]{3,2,1,0:T(8,128)S(1)} %broadcast_in_dim_reshape.3), channel_id=1, source_target_pairs={{1,0},{2,1},{3,2},{4,3},{5,4},{6,5},{7,6},{8,7},{9,8},{10,9},{11,1... | collective-permute-start | bytes 98312 | tf_op jit(solution)/shard_map/ppermute | solution.py:16
  19.1 1.8 %collective-permute-start.4 = (bf16[16,512]{1,0:T(8,128)(2,1)S(1)}, bf16[16,512]{1,0:T(8,128)(2,1)S(1)}, u32[]{:S(2)}, u32[]{:S(2)}) collective-permute-start(bf16[16,512]{1,0:T(8,128)(2,1)S(1)} %fusion.107), channel_id=1, source_target_pairs={{0,1},{1,0},{2,3},{3,2},{4,5},{5,4},{6,7},{7,6},{8,9},{9,8},{10,11... | collective-permute-start | bytes 49160 | tf_op jit(solution)/shard_map/ppermute | solution.py:28
  20.9 39.4 %copy-start.4 = (bf16[1,32,512]{2,1,0:T(8,128)(2,1)S(1)}, bf16[1,32,512]{2,1,0:T(8,128)(2,1)}, u32[]{:S(2)}) copy-start(bf16[1,32,512]{2,1,0:T(8,128)(2,1)} %param.20) | copy-start | bytes 98308
  21.1 13.5 %collective-permute-start.5 = (f32[1,1,16,512]{3,2,1,0:T(8,128)S(1)}, f32[1,1,16,512]{3,2,1,0:T(8,128)S(1)}, u32[]{:S(2)}, u32[]{:S(2)}) collective-permute-start(f32[1,1,16,512]{3,2,1,0:T(8,128)S(1)} %bitcast.309), channel_id=1, source_target_pairs={{0,64},{64,128},{128,192},{1,65},{65,129},{129,193},{2,66},{66,130... | collective-permute-start | bytes 98312 | tf_op jit(solution)/shard_map/ppermute | solution.py:15
  24.6 10.1 %collective-permute-start.6 = (f32[1,1,16,512]{3,2,1,0:T(8,128)S(1)}, f32[1,1,16,512]{3,2,1,0:T(8,128)S(1)}, u32[]{:S(2)}, u32[]{:S(2)}) collective-permute-start(f32[1,1,16,512]{3,2,1,0:T(8,128)S(1)} %bitcast.310), channel_id=1, source_target_pairs={{64,0},{128,64},{192,128},{65,1},{129,65},{193,129},{66,2},{130,66... | collective-permute-start | bytes 98312 | tf_op jit(solution)/shard_map/ppermute | solution.py:16
  27.0 7.7 %collective-permute-start.7 = (f32[1,1,16,512]{3,2,1,0:T(8,128)S(1)}, f32[1,1,16,512]{3,2,1,0:T(8,128)S(1)}, u32[]{:S(2)}, u32[]{:S(2)}) collective-permute-start(f32[1,1,16,512]{3,2,1,0:T(8,128)S(1)} %bitcast.311), channel_id=1, source_target_pairs={{0,1},{1,2},{2,3},{3,4},{4,5},{5,6},{6,7},{7,8},{8,9},{9,10},{10,1... | collective-permute-start | bytes 98312 | tf_op jit(solution)/shard_map/ppermute | solution.py:15
  28.9 7.3 %collective-permute-start.8 = (f32[1,1,16,512]{3,2,1,0:T(8,128)S(1)}, f32[1,1,16,512]{3,2,1,0:T(8,128)S(1)}, u32[]{:S(2)}, u32[]{:S(2)}) collective-permute-start(f32[1,1,16,512]{3,2,1,0:T(8,128)S(1)} %bitcast.312), channel_id=1, source_target_pairs={{1,0},{2,1},{3,2},{4,3},{5,4},{6,5},{7,6},{8,7},{9,8},{10,9},{11,1... | collective-permute-start | bytes 98312 | tf_op jit(solution)/shard_map/ppermute | solution.py:16
  36.3 3.8 %collective-permute-start.9 = (bf16[16,512]{1,0:T(8,128)(2,1)S(1)}, bf16[16,512]{1,0:T(8,128)(2,1)S(1)}, u32[]{:S(2)}, u32[]{:S(2)}) collective-permute-start(bf16[16,512]{1,0:T(8,128)(2,1)S(1)} %fusion.102), channel_id=1, source_target_pairs={{0,2},{1,3},{2,0},{3,1},{4,6},{5,7},{6,4},{7,5},{8,10},{9,11},{10,... | collective-permute-start | bytes 49160 | tf_op jit(solution)/shard_map/ppermute | solution.py:28
  40.3 13.5 %collective-permute-start.10 = (f32[1,1,16,512]{3,2,1,0:T(8,128)S(1)}, f32[1,1,16,512]{3,2,1,0:T(8,128)S(1)}, u32[]{:S(2)}, u32[]{:S(2)}) collective-permute-start(f32[1,1,16,512]{3,2,1,0:T(8,128)S(1)} %bitcast.305), channel_id=1, source_target_pairs={{0,64},{64,128},{128,192},{1,65},{65,129},{129,193},{2,66},{66,130... | collective-permute-start | bytes 98312 | tf_op jit(solution)/shard_map/ppermute | solution.py:15
  43.8 10.1 %collective-permute-start.11 = (f32[1,1,16,512]{3,2,1,0:T(8,128)S(1)}, f32[1,1,16,512]{3,2,1,0:T(8,128)S(1)}, u32[]{:S(2)}, u32[]{:S(2)}) collective-permute-start(f32[1,1,16,512]{3,2,1,0:T(8,128)S(1)} %bitcast.306), channel_id=1, source_target_pairs={{64,0},{128,64},{192,128},{65,1},{129,65},{193,129},{66,2},{130,66... | collective-permute-start | bytes 98312 | tf_op jit(solution)/shard_map/ppermute | solution.py:16
  46.1 7.7 %collective-permute-start.12 = (f32[1,1,16,512]{3,2,1,0:T(8,128)S(1)}, f32[1,1,16,512]{3,2,1,0:T(8,128)S(1)}, u32[]{:S(2)}, u32[]{:S(2)}) collective-permute-start(f32[1,1,16,512]{3,2,1,0:T(8,128)S(1)} %bitcast.307), channel_id=1, source_target_pairs={{0,1},{1,2},{2,3},{3,4},{4,5},{5,6},{6,7},{7,8},{8,9},{9,10},{10,1... | collective-permute-start | bytes 98312 | tf_op jit(solution)/shard_map/ppermute | solution.py:15
  48.1 7.3 %collective-permute-start.13 = (f32[1,1,16,512]{3,2,1,0:T(8,128)S(1)}, f32[1,1,16,512]{3,2,1,0:T(8,128)S(1)}, u32[]{:S(2)}, u32[]{:S(2)}) collective-permute-start(f32[1,1,16,512]{3,2,1,0:T(8,128)S(1)} %bitcast.308), channel_id=1, source_target_pairs={{1,0},{2,1},{3,2},{4,3},{5,4},{6,5},{7,6},{8,7},{9,8},{10,9},{11,1... | collective-permute-start | bytes 98312 | tf_op jit(solution)/shard_map/ppermute | solution.py:16
  55.4 4.7 %collective-permute-start.14 = (bf16[16,512]{1,0:T(8,128)(2,1)S(1)}, bf16[16,512]{1,0:T(8,128)(2,1)S(1)}, u32[]{:S(2)}, u32[]{:S(2)}) collective-permute-start(bf16[16,512]{1,0:T(8,128)(2,1)S(1)} %fusion.97), channel_id=1, source_target_pairs={{0,4},{1,5},{2,6},{3,7},{4,0},{5,1},{6,2},{7,3},{8,12},{9,13},{10,... | collective-permute-start | bytes 49160 | tf_op jit(solution)/shard_map/ppermute | solution.py:28
  79.0 10.4 %all-to-all-start.1 = ((bf16[4,16,2048]{2,1,0:T(8,128)(2,1)}), bf16[4,16,2048]{2,1,0:T(8,128)(2,1)S(1)}, u32[]{:S(2)}, u32[]{:S(2)}) async-start(bf16[4,16,2048]{2,1,0:T(8,128)(2,1)} %broadcast_in_dim.18), calls=%async_computation.1 | async-start | bytes 524288 | tf_op jit(solution)/shard_map/all_to_all | solution.py:33
  83.9 24.8 %copy-start.6 = (f32[1,3,4,512]{3,2,1,0:T(4,128)S(1)}, f32[1,3,4,512]{3,2,1,0:T(4,128)}, u32[]{:S(2)}) copy-start(f32[1,3,4,512]{3,2,1,0:T(4,128)} %param.16) | copy-start | bytes 73732
  90.8 23.4 %copy-start.2 = (bf16[1,3,512,512]{3,2,1,0:T(8,128)(2,1)S(1)}, bf16[1,3,512,512]{3,2,1,0:T(8,128)(2,1)}, u32[]{:S(2)}) copy-start(bf16[1,3,512,512]{3,2,1,0:T(8,128)(2,1)} %param.17) | copy-start | bytes 4718596
  91.1 4.7 %collective-permute-start.15 = (bf16[16,512]{1,0:T(8,128)(2,1)S(1)}, bf16[16,512]{1,0:T(8,128)(2,1)S(1)}, u32[]{:S(2)}, u32[]{:S(2)}) collective-permute-start(bf16[16,512]{1,0:T(8,128)(2,1)S(1)} %convolution_convert_fusion.4), channel_id=1, source_target_pairs={{0,4},{1,5},{2,6},{3,7},{4,0},{5,1},{6,2},{7,3},{8,12},{9,13},{10,... | collective-permute-start | bytes 49160 | tf_op jit(solution)/shard_map/ppermute | solution.py:28
  95.8 13.0 %collective-permute-start.16 = (bf16[1,1,16,512]{3,2,1,0:T(8,128)(2,1)S(1)}, bf16[1,1,16,512]{3,2,1,0:T(8,128)(2,1)S(1)}, u32[]{:S(2)}, u32[]{:S(2)}) collective-permute-start(bf16[1,1,16,512]{3,2,1,0:T(8,128)(2,1)S(1)} %fusion.111), channel_id=1, source_target_pairs={{0,1},{1,2},{2,3},{3,4},{4,5},{5,6},{6,7},{7,8},{8,9},{9,10},{10,1... | collective-permute-start | bytes 49160 | tf_op jit(solution)/shard_map/ppermute | solution.py:15
  97.7 11.1 %collective-permute-start.17 = (bf16[1,1,16,512]{3,2,1,0:T(8,128)(2,1)S(1)}, bf16[1,1,16,512]{3,2,1,0:T(8,128)(2,1)S(1)}, u32[]{:S(2)}, u32[]{:S(2)}) collective-permute-start(bf16[1,1,16,512]{3,2,1,0:T(8,128)(2,1)S(1)} %fusion.111), channel_id=1, source_target_pairs={{0,64},{64,128},{128,192},{1,65},{65,129},{129,193},{2,66},{66,130... | collective-permute-start | bytes 49160 | tf_op jit(solution)/shard_map/ppermute | solution.py:15
  99.6 9.2 %collective-permute-start.18 = (bf16[1,1,16,512]{3,2,1,0:T(8,128)(2,1)S(1)}, bf16[1,1,16,512]{3,2,1,0:T(8,128)(2,1)S(1)}, u32[]{:S(2)}, u32[]{:S(2)}) collective-permute-start(bf16[1,1,16,512]{3,2,1,0:T(8,128)(2,1)S(1)} %fusion.111), channel_id=1, source_target_pairs={{64,0},{128,64},{192,128},{65,1},{129,65},{193,129},{66,2},{130,66... | collective-permute-start | bytes 49160 | tf_op jit(solution)/shard_map/ppermute | solution.py:16
  103.5 6.6 %collective-permute-start.19 = (bf16[1,1,16,512]{3,2,1,0:T(8,128)(2,1)S(1)}, bf16[1,1,16,512]{3,2,1,0:T(8,128)(2,1)S(1)}, u32[]{:S(2)}, u32[]{:S(2)}) collective-permute-start(bf16[1,1,16,512]{3,2,1,0:T(8,128)(2,1)S(1)} %fusion.111), channel_id=1, source_target_pairs={{1,0},{2,1},{3,2},{4,3},{5,4},{6,5},{7,6},{8,7},{9,8},{10,9},{11,1... | collective-permute-start | bytes 49160 | tf_op jit(solution)/shard_map/ppermute | solution.py:16
  110.4 34.7 %copy-start.3 = (bf16[1,8,64,256]{3,2,1,0:T(8,128)(2,1)S(1)}, bf16[1,8,64,256]{3,2,1,0:T(8,128)(2,1)}, u32[]{:S(2)}) copy-start(bf16[1,8,64,256]{3,2,1,0:T(8,128)(2,1)} %param.13) | copy-start | bytes 786436
  110.4 3.8 %collective-permute-start.20 = (bf16[16,512]{1,0:T(8,128)(2,1)S(1)}, bf16[16,512]{1,0:T(8,128)(2,1)S(1)}, u32[]{:S(2)}, u32[]{:S(2)}) collective-permute-start(bf16[16,512]{1,0:T(8,128)(2,1)S(1)} %convolution_convert_fusion.3), channel_id=1, source_target_pairs={{0,2},{1,3},{2,0},{3,1},{4,6},{5,7},{6,4},{7,5},{8,10},{9,11},{10,... | collective-permute-start | bytes 49160 | tf_op jit(solution)/shard_map/ppermute | solution.py:28
  114.4 13.0 %collective-permute-start.21 = (bf16[1,1,16,512]{3,2,1,0:T(8,128)(2,1)S(1)}, bf16[1,1,16,512]{3,2,1,0:T(8,128)(2,1)S(1)}, u32[]{:S(2)}, u32[]{:S(2)}) collective-permute-start(bf16[1,1,16,512]{3,2,1,0:T(8,128)(2,1)S(1)} %convert_bitcast_fusion.1), channel_id=1, source_target_pairs={{0,1},{1,2},{2,3},{3,4},{4,5},{5,6},{6,7},{7,8},{8,9},{9,10},{10,1... | collective-permute-start | bytes 49160 | tf_op jit(solution)/shard_map/ppermute | solution.py:15
  116.4 11.1 %collective-permute-start.22 = (bf16[1,1,16,512]{3,2,1,0:T(8,128)(2,1)S(1)}, bf16[1,1,16,512]{3,2,1,0:T(8,128)(2,1)S(1)}, u32[]{:S(2)}, u32[]{:S(2)}) collective-permute-start(bf16[1,1,16,512]{3,2,1,0:T(8,128)(2,1)S(1)} %convert_bitcast_fusion.1), channel_id=1, source_target_pairs={{0,64},{64,128},{128,192},{1,65},{65,129},{129,193},{2,66},{66,130... | collective-permute-start | bytes 49160 | tf_op jit(solution)/shard_map/ppermute | solution.py:15
  118.6 8.9 %collective-permute-start.23 = (bf16[1,1,16,512]{3,2,1,0:T(8,128)(2,1)S(1)}, bf16[1,1,16,512]{3,2,1,0:T(8,128)(2,1)S(1)}, u32[]{:S(2)}, u32[]{:S(2)}) collective-permute-start(bf16[1,1,16,512]{3,2,1,0:T(8,128)(2,1)S(1)} %convert_bitcast_fusion.1), channel_id=1, source_target_pairs={{64,0},{128,64},{192,128},{65,1},{129,65},{193,129},{66,2},{130,66... | collective-permute-start | bytes 49160 | tf_op jit(solution)/shard_map/ppermute | solution.py:16
  122.2 6.6 %collective-permute-start.24 = (bf16[1,1,16,512]{3,2,1,0:T(8,128)(2,1)S(1)}, bf16[1,1,16,512]{3,2,1,0:T(8,128)(2,1)S(1)}, u32[]{:S(2)}, u32[]{:S(2)}) collective-permute-start(bf16[1,1,16,512]{3,2,1,0:T(8,128)(2,1)S(1)} %convert_bitcast_fusion.1), channel_id=1, source_target_pairs={{1,0},{2,1},{3,2},{4,3},{5,4},{6,5},{7,6},{8,7},{9,8},{10,9},{11,1... | collective-permute-start | bytes 49160 | tf_op jit(solution)/shard_map/ppermute | solution.py:16
  129.1 1.2 collective-permute-start.25
  130.6 13.0 %collective-permute-start.26 = (bf16[1,1,16,512]{3,2,1,0:T(8,128)(2,1)S(1)}, bf16[1,1,16,512]{3,2,1,0:T(8,128)(2,1)S(1)}, u32[]{:S(2)}, u32[]{:S(2)}) collective-permute-start(bf16[1,1,16,512]{3,2,1,0:T(8,128)(2,1)S(1)} %convert_bitcast_fusion), channel_id=1, source_target_pairs={{0,1},{1,2},{2,3},{3,4},{4,5},{5,6},{6,7},{7,8},{8,9},{9,10},{10,1... | collective-permute-start | bytes 49160 | tf_op jit(solution)/shard_map/ppermute | solution.py:15
  132.7 10.9 %collective-permute-start.27 = (bf16[1,1,16,512]{3,2,1,0:T(8,128)(2,1)S(1)}, bf16[1,1,16,512]{3,2,1,0:T(8,128)(2,1)S(1)}, u32[]{:S(2)}, u32[]{:S(2)}) collective-permute-start(bf16[1,1,16,512]{3,2,1,0:T(8,128)(2,1)S(1)} %convert_bitcast_fusion), channel_id=1, source_target_pairs={{0,64},{64,128},{128,192},{1,65},{65,129},{129,193},{2,66},{66,130... | collective-permute-start | bytes 49160 | tf_op jit(solution)/shard_map/ppermute | solution.py:15
  134.9 8.7 %collective-permute-start.28 = (bf16[1,1,16,512]{3,2,1,0:T(8,128)(2,1)S(1)}, bf16[1,1,16,512]{3,2,1,0:T(8,128)(2,1)S(1)}, u32[]{:S(2)}, u32[]{:S(2)}) collective-permute-start(bf16[1,1,16,512]{3,2,1,0:T(8,128)(2,1)S(1)} %convert_bitcast_fusion), channel_id=1, source_target_pairs={{64,0},{128,64},{192,128},{65,1},{129,65},{193,129},{66,2},{130,66... | collective-permute-start | bytes 49160 | tf_op jit(solution)/shard_map/ppermute | solution.py:16
  138.5 6.5 %collective-permute-start.29 = (bf16[1,1,16,512]{3,2,1,0:T(8,128)(2,1)S(1)}, bf16[1,1,16,512]{3,2,1,0:T(8,128)(2,1)S(1)}, u32[]{:S(2)}, u32[]{:S(2)}) collective-permute-start(bf16[1,1,16,512]{3,2,1,0:T(8,128)(2,1)S(1)} %convert_bitcast_fusion), channel_id=1, source_target_pairs={{1,0},{2,1},{3,2},{4,3},{5,4},{6,5},{7,6},{8,7},{9,8},{10,9},{11,1... | collective-permute-start | bytes 49160 | tf_op jit(solution)/shard_map/ppermute | solution.py:16
where the time goes:
time: 148 us; the launch traced here: 147 us
  starting transfers between devices  86.8 us (59%)
  waiting for transfers between devices  25.6 us (17%)
  blocking collectives  17 us (11%)
  matrix products  11.7 us (8%)
  local copies, waits for them, and re-layouts  4.6 us (3%)
    ppermute x12, starting transfers between devices, padded_2(): lax.ppermute(leading, axis, [(b, a) for a, b in up])  51.8 us
    ppermute x12, starting transfers between devices, padded_2(): lax.ppermute(last, axis, up)  28.5 us
    all_to_all x1, blocking collectives, sent_to_all(): return lax.all_to_all(copies, axis, split_axis=0, concat_axis=0, tiled=True)  17 us
    ppermute x6, waiting for transfers between devices, partner_2(): lax.ppermute(shard, axis, [(i, i ^ 1 << stride) for i in range(lax.axis_s...  12.9 us
    ppermute x12, waiting for transfers between devices, padded_2(): lax.ppermute(leading, axis, [(b, a) for a, b in up])  8.36 us
    all_to_all x1, starting transfers between devices, sent_to_all(): return lax.all_to_all(copies, axis, split_axis=0, concat_axis=0, tiled=True)  4.92 us
    all_to_all x1, waiting for transfers between devices, sent_to_all(): return lax.all_to_all(copies, axis, split_axis=0, concat_axis=0, tiled=True)  4.27 us
    dot_general x3, matrix products, body(): state = jnp.dot(rounded, own[level], preferred_element_type=jnp.float32)  3.63 us
  transfers between devices with their start and end apart: 31, of which 12 were waited for; matrix products, arithmetic and copies ran while one was open for 5% of the time, Pallas kernels for 0%

commit v1 on v0

--- a/solution.py
+++ b/solution.py
@@ -102,8 +102,8 @@
     top_state = state.astype(jnp.bfloat16)
     comp = compress[0]
     small = right_transpose(top_state, comp).astype(jnp.bfloat16)
-    row_values = collect(small, "gx", 1)
-    coarse = jnp.dot(collect(row_values, "gy", 1), top_couple, preferred_element_type=jnp.float32)
+    gathered = lax.all_gather(small, ("gy", "gx"), axis=1, tiled=True)
+    coarse = jnp.dot(gathered, top_couple, preferred_element_type=jnp.float32)
     state = jnp.dot(top_state, top_inverse[0], preferred_element_type=jnp.float32)
     state = state + jnp.dot(coarse.astype(jnp.bfloat16), comp, preferred_element_type=jnp.float32)
     for level in reversed(range(level_count)):

time: 148 us -> 182 us (1.23)
  blocking collectives: 17 us -> 59.2 us
  waiting for transfers between devices: 25.6 us -> 21 us
  starting transfers between devices: 86.8 us -> 82.3 us
  local copies, waits for them, and re-layouts: 4.6 us -> 6.73 us
    all_gather x0 -> x1, blocking collectives: none -> 59.2 us  [body(): gathered = lax.all_gather(small, ('gy', 'gx'), axis=1, tiled=True)]
    all_to_all x1 -> x0, blocking collectives: 17 us -> none  [sent_to_all(): return lax.all_to_all(copies, axis, split_axis=0, concat_axis=0, tiled=True)]
    all_to_all x1 -> x0, starting transfers between devices: 4.92 us -> none  [sent_to_all(): return lax.all_to_all(copies, axis, split_axis=0, concat_axis=0, tiled=True)]
    all_to_all x1 -> x0, waiting for transfers between devices: 4.27 us -> none  [sent_to_all(): return lax.all_to_all(copies, axis, split_axis=0, concat_axis=0, tiled=True)]
    ppermute x12, starting transfers between devices: 28.5 us -> 32 us  [padded_2(): lax.ppermute(last, axis, up)]
    ppermute x12, starting transfers between devices: 51.8 us -> 48.2 us  [padded_2(): lax.ppermute(leading, axis, [(b, a) for a, b in up])]
    unnamed x19 -> x22, local copies, waits for them, and re-layouts: 1.63 us -> 3.65 us
  transfers between devices with their start and end apart: 31 -> 30, of which waited for: 12 -> 11; matrix products, arithmetic and copies ran while one was open for 5% -> 3% of each run, Pallas kernels for 0% -> 0%
where the time goes in v1:
time: 182 us; the launch traced here: 181 us
  starting transfers between devices  82.3 us (45%)
  blocking collectives  59.2 us (33%)
  waiting for transfers between devices  21 us (12%)
  matrix products  10.7 us (6%)
  local copies, waits for them, and re-layouts  6.73 us (4%)
    all_gather x1, blocking collectives, body(): gathered = lax.all_gather(small, ('gy', 'gx'), axis=1, tiled=True)  59.2 us
    ppermute x12, starting transfers between devices, padded_2(): lax.ppermute(leading, axis, [(b, a) for a, b in up])  48.2 us
    ppermute x12, starting transfers between devices, padded_2(): lax.ppermute(last, axis, up)  32 us
    ppermute x6, waiting for transfers between devices, partner_2(): lax.ppermute(shard, axis, [(i, i ^ 1 << stride) for i in range(lax.axis_s...  12.6 us
    ppermute x12, waiting for transfers between devices, padded_2(): lax.ppermute(leading, axis, [(b, a) for a, b in up])  8.36 us
    unnamed x22, local copies, waits for them, and re-layouts  3.65 us
  transfers between devices with their start and end apart: 30, of which 11 were waited for; matrix products, arithmetic and copies ran while one was open for 3% of the time, Pallas kernels for 0%

profile of v1, /device:TPU:10, one launch (start us, length us, event | category | flops | bytes accessed | tf_op | source)
XLA Modules:
  0.0 180.7 jit_solution(5314327930664228072)
XLA Ops:
  0.0 0.9 copy.40
  1.0 0.3 copy-done
  1.3 0.2 fusion.3
  1.5 1.2 convolution_bitcast_fusion.2
  2.7 0.3 fusion.4
  3.1 3.5 %collective-permute-start = (f32[1,1,16,512]{3,2,1,0:T(8,128)S(1)}, f32[1,1,16,512]{3,2,1,0:T(8,128)S(1)}, u32[]{:S(2)}, u32[]{:S(2)}) collective-permute-start(f32[1,1,16,512]{3,2,1,0:T(8,128)S(1)} %broadcast_in_dim_reshape.3), channel_id=1, source_target_pairs={{0,64},{64,128},{128,192},{1,65},{65,129},{129,193},{2,66},{66,130... | collective-permute-start | bytes 98312 | tf_op jit(solution)/shard_map/ppermute | solution.py:15
  6.6 2.4 %collective-permute-start.1 = (f32[1,1,16,512]{3,2,1,0:T(8,128)S(1)}, f32[1,1,16,512]{3,2,1,0:T(8,128)S(1)}, u32[]{:S(2)}, u32[]{:S(2)}) collective-permute-start(f32[1,1,16,512]{3,2,1,0:T(8,128)S(1)} %broadcast_in_dim_reshape.3), channel_id=1, source_target_pairs={{64,0},{128,64},{192,128},{65,1},{129,65},{193,129},{66,2},{130,66... | collective-permute-start | bytes 98312 | tf_op jit(solution)/shard_map/ppermute | solution.py:16
  9.0 1.9 %collective-permute-start.2 = (f32[1,1,16,512]{3,2,1,0:T(8,128)S(1)}, f32[1,1,16,512]{3,2,1,0:T(8,128)S(1)}, u32[]{:S(2)}, u32[]{:S(2)}) collective-permute-start(f32[1,1,16,512]{3,2,1,0:T(8,128)S(1)} %broadcast_in_dim_reshape.3), channel_id=1, source_target_pairs={{0,1},{1,2},{2,3},{3,4},{4,5},{5,6},{6,7},{7,8},{8,9},{9,10},{10,1... | collective-permute-start | bytes 98312 | tf_op jit(solution)/shard_map/ppermute | solution.py:15
  10.9 6.6 %collective-permute-start.3 = (f32[1,1,16,512]{3,2,1,0:T(8,128)S(1)}, f32[1,1,16,512]{3,2,1,0:T(8,128)S(1)}, u32[]{:S(2)}, u32[]{:S(2)}) collective-permute-start(f32[1,1,16,512]{3,2,1,0:T(8,128)S(1)} %broadcast_in_dim_reshape.3), channel_id=1, source_target_pairs={{1,0},{2,1},{3,2},{4,3},{5,4},{6,5},{7,6},{8,7},{9,8},{10,9},{11,1... | collective-permute-start | bytes 98312 | tf_op jit(solution)/shard_map/ppermute | solution.py:16
  18.0 1.1 collective-permute-done.3
  19.6 0.1 convert_element_type.115
  19.7 1.2 fusion.26
  21.0 0.2 convolution_add_fusion.5
  21.1 3.5 %collective-permute-start.5 = (f32[1,1,16,512]{3,2,1,0:T(8,128)S(1)}, f32[1,1,16,512]{3,2,1,0:T(8,128)S(1)}, u32[]{:S(2)}, u32[]{:S(2)}) collective-permute-start(f32[1,1,16,512]{3,2,1,0:T(8,128)S(1)} %bitcast.308), channel_id=1, source_target_pairs={{0,64},{64,128},{128,192},{1,65},{65,129},{129,193},{2,66},{66,130... | collective-permute-start | bytes 98312 | tf_op jit(solution)/shard_map/ppermute | solution.py:15
  24.6 2.4 %collective-permute-start.6 = (f32[1,1,16,512]{3,2,1,0:T(8,128)S(1)}, f32[1,1,16,512]{3,2,1,0:T(8,128)S(1)}, u32[]{:S(2)}, u32[]{:S(2)}) collective-permute-start(f32[1,1,16,512]{3,2,1,0:T(8,128)S(1)} %bitcast.309), channel_id=1, source_target_pairs={{64,0},{128,64},{192,128},{65,1},{129,65},{193,129},{66,2},{130,66... | collective-permute-start | bytes 98312 | tf_op jit(solution)/shard_map/ppermute | solution.py:16
  27.0 1.9 %collective-permute-start.7 = (f32[1,1,16,512]{3,2,1,0:T(8,128)S(1)}, f32[1,1,16,512]{3,2,1,0:T(8,128)S(1)}, u32[]{:S(2)}, u32[]{:S(2)}) collective-permute-start(f32[1,1,16,512]{3,2,1,0:T(8,128)S(1)} %bitcast.310), channel_id=1, source_target_pairs={{0,1},{1,2},{2,3},{3,4},{4,5},{5,6},{6,7},{7,8},{8,9},{9,10},{10,1... | collective-permute-start | bytes 98312 | tf_op jit(solution)/shard_map/ppermute | solution.py:15
  28.9 5.8 %collective-permute-start.8 = (f32[1,1,16,512]{3,2,1,0:T(8,128)S(1)}, f32[1,1,16,512]{3,2,1,0:T(8,128)S(1)}, u32[]{:S(2)}, u32[]{:S(2)}) collective-permute-start(f32[1,1,16,512]{3,2,1,0:T(8,128)S(1)} %bitcast.311), channel_id=1, source_target_pairs={{1,0},{2,1},{3,2},{4,3},{5,4},{6,5},{7,6},{8,7},{9,8},{10,9},{11,1... | collective-permute-start | bytes 98312 | tf_op jit(solution)/shard_map/ppermute | solution.py:16
  34.7 1.5 collective-permute-done.8
  36.4 1.2 fusion.21
  37.6 2.5 %collective-permute-done.9 = bf16[16,512]{1,0:T(8,128)(2,1)S(1)} collective-permute-done((bf16[16,512]{1,0:T(8,128)(2,1)S(1)}, bf16[16,512]{1,0:T(8,128)(2,1)S(1)}, u32[]{:S(2)}, u32[]{:S(2)}) %collective-permute-start.9) | collective-permute-done | bytes 16416 | tf_op jit(solution)/shard_map/ppermute | solution.py:28
  40.1 0.2 convolution_add_fusion.4
  40.3 3.5 %collective-permute-start.10 = (f32[1,1,16,512]{3,2,1,0:T(8,128)S(1)}, f32[1,1,16,512]{3,2,1,0:T(8,128)S(1)}, u32[]{:S(2)}, u32[]{:S(2)}) collective-permute-start(f32[1,1,16,512]{3,2,1,0:T(8,128)S(1)} %bitcast.304), channel_id=1, source_target_pairs={{0,64},{64,128},{128,192},{1,65},{65,129},{129,193},{2,66},{66,130... | collective-permute-start | bytes 98312 | tf_op jit(solution)/shard_map/ppermute | solution.py:15
  43.8 2.4 %collective-permute-start.11 = (f32[1,1,16,512]{3,2,1,0:T(8,128)S(1)}, f32[1,1,16,512]{3,2,1,0:T(8,128)S(1)}, u32[]{:S(2)}, u32[]{:S(2)}) collective-permute-start(f32[1,1,16,512]{3,2,1,0:T(8,128)S(1)} %bitcast.305), channel_id=1, source_target_pairs={{64,0},{128,64},{192,128},{65,1},{129,65},{193,129},{66,2},{130,66... | collective-permute-start | bytes 98312 | tf_op jit(solution)/shard_map/ppermute | solution.py:16
  46.1 1.9 %collective-permute-start.12 = (f32[1,1,16,512]{3,2,1,0:T(8,128)S(1)}, f32[1,1,16,512]{3,2,1,0:T(8,128)S(1)}, u32[]{:S(2)}, u32[]{:S(2)}) collective-permute-start(f32[1,1,16,512]{3,2,1,0:T(8,128)S(1)} %bitcast.306), channel_id=1, source_target_pairs={{0,1},{1,2},{2,3},{3,4},{4,5},{5,6},{6,7},{7,8},{8,9},{9,10},{10,1... | collective-permute-start | bytes 98312 | tf_op jit(solution)/shard_map/ppermute | solution.py:15
  48.1 5.8 %collective-permute-start.13 = (f32[1,1,16,512]{3,2,1,0:T(8,128)S(1)}, f32[1,1,16,512]{3,2,1,0:T(8,128)S(1)}, u32[]{:S(2)}, u32[]{:S(2)}) collective-permute-start(f32[1,1,16,512]{3,2,1,0:T(8,128)S(1)} %bitcast.307), channel_id=1, source_target_pairs={{1,0},{2,1},{3,2},{4,3},{5,4},{6,5},{7,6},{8,7},{9,8},{10,9},{11,1... | collective-permute-start | bytes 98312 | tf_op jit(solution)/shard_map/ppermute | solution.py:16
  53.9 1.5 collective-permute-done.13
  55.4 0.5 collective-permute-start.14
  55.9 1.2 fusion.16
  57.1 3.0 %collective-permute-done.14 = bf16[16,512]{1,0:T(8,128)(2,1)S(1)} collective-permute-done((bf16[16,512]{1,0:T(8,128)(2,1)S(1)}, bf16[16,512]{1,0:T(8,128)(2,1)S(1)}, u32[]{:S(2)}, u32[]{:S(2)}) %collective-permute-start.14) | collective-permute-done | bytes 16416 | tf_op jit(solution)/shard_map/ppermute | solution.py:28
  60.1 0.2 fusion.6
  60.3 0.1 fusion.7
  60.4 59.2 %all-gather = bf16[256,32,16]{1,2,0:T(8,128)(2,1)S(1)} all-gather(bf16[1,32,16]{1,2,0:T(8,128)(2,1)S(1)} %fusion.7), channel_id=1, replica_groups=mesh['gy'=4,'gx'=64] {'gy','gx'}, dimensions={0}, use_global_device_ids=true | all-gather | bytes 263168 | tf_op jit(solution)/shard_map/all_gather | solution.py:105
  119.7 1.3 copy.36
  121.0 2.4 %reshape.114 = bf16[8192,16]{0,1:T(8,128)(2,1)S(1)} reshape(bf16[256,32,16]{1,0,2:T(8,128)(2,1)} %copy.36) | data formatting | bytes 524288
  123.3 0.2 fusion.10
  123.5 1.4 fusion.5
  124.9 0.2 convolution_convert_fusion.4
  125.2 1.3 collective-permute-start.15
  126.5 1.3 fusion.14
  127.8 2.1 %collective-permute-done.15 = bf16[16,512]{1,0:T(8,128)(2,1)S(1)} collective-permute-done((bf16[16,512]{1,0:T(8,128)(2,1)S(1)}, bf16[16,512]{1,0:T(8,128)(2,1)S(1)}, u32[]{:S(2)}, u32[]{:S(2)}) %collective-permute-start.15) | collective-permute-done | bytes 16416 | tf_op jit(solution)/shard_map/ppermute | solution.py:28
  129.9 1.9 %collective-permute-start.16 = (bf16[1,1,16,512]{3,2,1,0:T(8,128)(2,1)S(1)}, bf16[1,1,16,512]{3,2,1,0:T(8,128)(2,1)S(1)}, u32[]{:S(2)}, u32[]{:S(2)}) collective-permute-start(bf16[1,1,16,512]{3,2,1,0:T(8,128)(2,1)S(1)} %fusion.112), channel_id=1, source_target_pairs={{0,1},{1,2},{2,3},{3,4},{4,5},{5,6},{6,7},{7,8},{8,9},{9,10},{10,1... | collective-permute-start | bytes 49160 | tf_op jit(solution)/shard_map/ppermute | solution.py:15
  131.8 3.3 %collective-permute-start.17 = (bf16[1,1,16,512]{3,2,1,0:T(8,128)(2,1)S(1)}, bf16[1,1,16,512]{3,2,1,0:T(8,128)(2,1)S(1)}, u32[]{:S(2)}, u32[]{:S(2)}) collective-permute-start(bf16[1,1,16,512]{3,2,1,0:T(8,128)(2,1)S(1)} %fusion.112), channel_id=1, source_target_pairs={{0,64},{64,128},{128,192},{1,65},{65,129},{129,193},{2,66},{66,130... | collective-permute-start | bytes 49160 | tf_op jit(solution)/shard_map/ppermute | solution.py:15
  135.1 2.5 %collective-permute-start.18 = (bf16[1,1,16,512]{3,2,1,0:T(8,128)(2,1)S(1)}, bf16[1,1,16,512]{3,2,1,0:T(8,128)(2,1)S(1)}, u32[]{:S(2)}, u32[]{:S(2)}) collective-permute-start(bf16[1,1,16,512]{3,2,1,0:T(8,128)(2,1)S(1)} %fusion.112), channel_id=1, source_target_pairs={{64,0},{128,64},{192,128},{65,1},{129,65},{193,129},{66,2},{130,66... | collective-permute-start | bytes 49160 | tf_op jit(solution)/shard_map/ppermute | solution.py:16
  137.7 5.2 %collective-permute-start.19 = (bf16[1,1,16,512]{3,2,1,0:T(8,128)(2,1)S(1)}, bf16[1,1,16,512]{3,2,1,0:T(8,128)(2,1)S(1)}, u32[]{:S(2)}, u32[]{:S(2)}) collective-permute-start(bf16[1,1,16,512]{3,2,1,0:T(8,128)(2,1)S(1)} %fusion.112), channel_id=1, source_target_pairs={{1,0},{2,1},{3,2},{4,3},{5,4},{6,5},{7,6},{8,7},{9,8},{10,9},{11,1... | collective-permute-start | bytes 49160 | tf_op jit(solution)/shard_map/ppermute | solution.py:16
  142.9 1.4 collective-permute-done.19
  144.3 0.2 convolution_convert_fusion.3
  144.6 3.7 %collective-permute-done.20 = bf16[16,512]{1,0:T(8,128)(2,1)S(1)} collective-permute-done((bf16[16,512]{1,0:T(8,128)(2,1)S(1)}, bf16[16,512]{1,0:T(8,128)(2,1)S(1)}, u32[]{:S(2)}, u32[]{:S(2)}) %collective-permute-start.20) | collective-permute-done | bytes 16416 | tf_op jit(solution)/shard_map/ppermute | solution.py:28
  148.3 0.2 convolution_add_fusion.2
  148.6 1.9 %collective-permute-start.21 = (bf16[1,1,16,512]{3,2,1,0:T(8,128)(2,1)S(1)}, bf16[1,1,16,512]{3,2,1,0:T(8,128)(2,1)S(1)}, u32[]{:S(2)}, u32[]{:S(2)}) collective-permute-start(bf16[1,1,16,512]{3,2,1,0:T(8,128)(2,1)S(1)} %convert_bitcast_fusion.1), channel_id=1, source_target_pairs={{0,1},{1,2},{2,3},{3,4},{4,5},{5,6},{6,7},{7,8},{8,9},{9,10},{10,1... | collective-permute-start | bytes 49160 | tf_op jit(solution)/shard_map/ppermute | solution.py:15
  150.5 3.3 %collective-permute-start.22 = (bf16[1,1,16,512]{3,2,1,0:T(8,128)(2,1)S(1)}, bf16[1,1,16,512]{3,2,1,0:T(8,128)(2,1)S(1)}, u32[]{:S(2)}, u32[]{:S(2)}) collective-permute-start(bf16[1,1,16,512]{3,2,1,0:T(8,128)(2,1)S(1)} %convert_bitcast_fusion.1), channel_id=1, source_target_pairs={{0,64},{64,128},{128,192},{1,65},{65,129},{129,193},{2,66},{66,130... | collective-permute-start | bytes 49160 | tf_op jit(solution)/shard_map/ppermute | solution.py:15
  153.8 2.5 %collective-permute-start.23 = (bf16[1,1,16,512]{3,2,1,0:T(8,128)(2,1)S(1)}, bf16[1,1,16,512]{3,2,1,0:T(8,128)(2,1)S(1)}, u32[]{:S(2)}, u32[]{:S(2)}) collective-permute-start(bf16[1,1,16,512]{3,2,1,0:T(8,128)(2,1)S(1)} %convert_bitcast_fusion.1), channel_id=1, source_target_pairs={{64,0},{128,64},{192,128},{65,1},{129,65},{193,129},{66,2},{130,66... | collective-permute-start | bytes 49160 | tf_op jit(solution)/shard_map/ppermute | solution.py:16
  156.4 5.2 %collective-permute-start.24 = (bf16[1,1,16,512]{3,2,1,0:T(8,128)(2,1)S(1)}, bf16[1,1,16,512]{3,2,1,0:T(8,128)(2,1)S(1)}, u32[]{:S(2)}, u32[]{:S(2)}) collective-permute-start(bf16[1,1,16,512]{3,2,1,0:T(8,128)(2,1)S(1)} %convert_bitcast_fusion.1), channel_id=1, source_target_pairs={{1,0},{2,1},{3,2},{4,3},{5,4},{6,5},{7,6},{8,7},{9,8},{10,9},{11,1... | collective-permute-start | bytes 49160 | tf_op jit(solution)/shard_map/ppermute | solution.py:16
  161.6 1.4 collective-permute-done.24
  163.1 0.2 convolution_convert_fusion.2
  163.3 1.2 collective-permute-done.25
  164.5 0.2 convolution_add_fusion.1
  164.7 2.1 %collective-permute-start.26 = (bf16[1,1,16,512]{3,2,1,0:T(8,128)(2,1)S(1)}, bf16[1,1,16,512]{3,2,1,0:T(8,128)(2,1)S(1)}, u32[]{:S(2)}, u32[]{:S(2)}) collective-permute-start(bf16[1,1,16,512]{3,2,1,0:T(8,128)(2,1)S(1)} %convert_bitcast_fusion), channel_id=1, source_target_pairs={{0,1},{1,2},{2,3},{3,4},{4,5},{5,6},{6,7},{7,8},{8,9},{9,10},{10,1... | collective-permute-start | bytes 49160 | tf_op jit(solution)/shard_map/ppermute | solution.py:15
  166.8 3.3 %collective-permute-start.27 = (bf16[1,1,16,512]{3,2,1,0:T(8,128)(2,1)S(1)}, bf16[1,1,16,512]{3,2,1,0:T(8,128)(2,1)S(1)}, u32[]{:S(2)}, u32[]{:S(2)}) collective-permute-start(bf16[1,1,16,512]{3,2,1,0:T(8,128)(2,1)S(1)} %convert_bitcast_fusion), channel_id=1, source_target_pairs={{0,64},{64,128},{128,192},{1,65},{65,129},{129,193},{2,66},{66,130... | collective-permute-start | bytes 49160 | tf_op jit(solution)/shard_map/ppermute | solution.py:15
  170.1 2.5 %collective-permute-start.28 = (bf16[1,1,16,512]{3,2,1,0:T(8,128)(2,1)S(1)}, bf16[1,1,16,512]{3,2,1,0:T(8,128)(2,1)S(1)}, u32[]{:S(2)}, u32[]{:S(2)}) collective-permute-start(bf16[1,1,16,512]{3,2,1,0:T(8,128)(2,1)S(1)} %convert_bitcast_fusion), channel_id=1, source_target_pairs={{64,0},{128,64},{192,128},{65,1},{129,65},{193,129},{66,2},{130,66... | collective-permute-start | bytes 49160 | tf_op jit(solution)/shard_map/ppermute | solution.py:16
  172.7 5.0 %collective-permute-start.29 = (bf16[1,1,16,512]{3,2,1,0:T(8,128)(2,1)S(1)}, bf16[1,1,16,512]{3,2,1,0:T(8,128)(2,1)S(1)}, u32[]{:S(2)}, u32[]{:S(2)}) collective-permute-start(bf16[1,1,16,512]{3,2,1,0:T(8,128)(2,1)S(1)} %convert_bitcast_fusion), channel_id=1, source_target_pairs={{1,0},{2,1},{3,2},{4,3},{5,4},{6,5},{7,6},{8,7},{9,8},{10,9},{11,1... | collective-permute-start | bytes 49160 | tf_op jit(solution)/shard_map/ppermute | solution.py:16
  177.8 1.4 collective-permute-done.29
  179.3 0.3 fusion
  179.7 0.3 fusion.1
  180.0 0.7 reshape.112
  (71 shorter events, 1.6 us)
Async XLA Ops:
  0.0 1.3 copy-start
  0.0 2.7 %copy-start.8 = (s32[1,8,64]{2,1,0:T(8,128)S(1)}, s32[1,8,64]{2,1,0:T(8,128)}, u32[]{:S(2)}) copy-start(s32[1,8,64]{2,1,0:T(8,128)} %param.14) | copy-start | bytes 6148
  0.0 17.5 %copy-start.6 = (f32[1,3,4,512]{3,2,1,0:T(4,128)S(1)}, f32[1,3,4,512]{3,2,1,0:T(4,128)}, u32[]{:S(2)}) copy-start(f32[1,3,4,512]{3,2,1,0:T(4,128)} %param.15) | copy-start | bytes 73732
  1.5 19.5 %copy-start.1 = (bf16[1,3,512,512]{3,2,1,0:T(8,128)(2,1)S(1)}, bf16[1,3,512,512]{3,2,1,0:T(8,128)(2,1)}, u32[]{:S(2)}) copy-start(bf16[1,3,512,512]{3,2,1,0:T(8,128)(2,1)} %param.18) | copy-start | bytes 4718596
  3.1 14.8 %collective-permute-start = (f32[1,1,16,512]{3,2,1,0:T(8,128)S(1)}, f32[1,1,16,512]{3,2,1,0:T(8,128)S(1)}, u32[]{:S(2)}, u32[]{:S(2)}) collective-permute-start(f32[1,1,16,512]{3,2,1,0:T(8,128)S(1)} %broadcast_in_dim_reshape.3), channel_id=1, source_target_pairs={{0,64},{64,128},{128,192},{1,65},{65,129},{129,193},{2,66},{66,130... | collective-permute-start | bytes 98312 | tf_op jit(solution)/shard_map/ppermute | solution.py:15
  6.6 11.4 %collective-permute-start.1 = (f32[1,1,16,512]{3,2,1,0:T(8,128)S(1)}, f32[1,1,16,512]{3,2,1,0:T(8,128)S(1)}, u32[]{:S(2)}, u32[]{:S(2)}) collective-permute-start(f32[1,1,16,512]{3,2,1,0:T(8,128)S(1)} %broadcast_in_dim_reshape.3), channel_id=1, source_target_pairs={{64,0},{128,64},{192,128},{65,1},{129,65},{193,129},{66,2},{130,66... | collective-permute-start | bytes 98312 | tf_op jit(solution)/shard_map/ppermute | solution.py:16
  9.0 9.0 %collective-permute-start.2 = (f32[1,1,16,512]{3,2,1,0:T(8,128)S(1)}, f32[1,1,16,512]{3,2,1,0:T(8,128)S(1)}, u32[]{:S(2)}, u32[]{:S(2)}) collective-permute-start(f32[1,1,16,512]{3,2,1,0:T(8,128)S(1)} %broadcast_in_dim_reshape.3), channel_id=1, source_target_pairs={{0,1},{1,2},{2,3},{3,4},{4,5},{5,6},{6,7},{7,8},{8,9},{9,10},{10,1... | collective-permute-start | bytes 98312 | tf_op jit(solution)/shard_map/ppermute | solution.py:15
  10.9 8.2 %collective-permute-start.3 = (f32[1,1,16,512]{3,2,1,0:T(8,128)S(1)}, f32[1,1,16,512]{3,2,1,0:T(8,128)S(1)}, u32[]{:S(2)}, u32[]{:S(2)}) collective-permute-start(f32[1,1,16,512]{3,2,1,0:T(8,128)S(1)} %broadcast_in_dim_reshape.3), channel_id=1, source_target_pairs={{1,0},{2,1},{3,2},{4,3},{5,4},{6,5},{7,6},{8,7},{9,8},{10,9},{11,1... | collective-permute-start | bytes 98312 | tf_op jit(solution)/shard_map/ppermute | solution.py:16
  19.1 1.8 collective-permute-start.4
  20.9 39.4 %copy-start.5 = (bf16[1,32,512]{2,1,0:T(8,128)(2,1)S(1)}, bf16[1,32,512]{2,1,0:T(8,128)(2,1)}, u32[]{:S(2)}) copy-start(bf16[1,32,512]{2,1,0:T(8,128)(2,1)} %param.20) | copy-start | bytes 98308
  21.1 13.5 %collective-permute-start.5 = (f32[1,1,16,512]{3,2,1,0:T(8,128)S(1)}, f32[1,1,16,512]{3,2,1,0:T(8,128)S(1)}, u32[]{:S(2)}, u32[]{:S(2)}) collective-permute-start(f32[1,1,16,512]{3,2,1,0:T(8,128)S(1)} %bitcast.308), channel_id=1, source_target_pairs={{0,64},{64,128},{128,192},{1,65},{65,129},{129,193},{2,66},{66,130... | collective-permute-start | bytes 98312 | tf_op jit(solution)/shard_map/ppermute | solution.py:15
  24.6 10.1 %collective-permute-start.6 = (f32[1,1,16,512]{3,2,1,0:T(8,128)S(1)}, f32[1,1,16,512]{3,2,1,0:T(8,128)S(1)}, u32[]{:S(2)}, u32[]{:S(2)}) collective-permute-start(f32[1,1,16,512]{3,2,1,0:T(8,128)S(1)} %bitcast.309), channel_id=1, source_target_pairs={{64,0},{128,64},{192,128},{65,1},{129,65},{193,129},{66,2},{130,66... | collective-permute-start | bytes 98312 | tf_op jit(solution)/shard_map/ppermute | solution.py:16
  27.0 7.7 %collective-permute-start.7 = (f32[1,1,16,512]{3,2,1,0:T(8,128)S(1)}, f32[1,1,16,512]{3,2,1,0:T(8,128)S(1)}, u32[]{:S(2)}, u32[]{:S(2)}) collective-permute-start(f32[1,1,16,512]{3,2,1,0:T(8,128)S(1)} %bitcast.310), channel_id=1, source_target_pairs={{0,1},{1,2},{2,3},{3,4},{4,5},{5,6},{6,7},{7,8},{8,9},{9,10},{10,1... | collective-permute-start | bytes 98312 | tf_op jit(solution)/shard_map/ppermute | solution.py:15
  28.9 7.3 %collective-permute-start.8 = (f32[1,1,16,512]{3,2,1,0:T(8,128)S(1)}, f32[1,1,16,512]{3,2,1,0:T(8,128)S(1)}, u32[]{:S(2)}, u32[]{:S(2)}) collective-permute-start(f32[1,1,16,512]{3,2,1,0:T(8,128)S(1)} %bitcast.311), channel_id=1, source_target_pairs={{1,0},{2,1},{3,2},{4,3},{5,4},{6,5},{7,6},{8,7},{9,8},{10,9},{11,1... | collective-permute-start | bytes 98312 | tf_op jit(solution)/shard_map/ppermute | solution.py:16
  36.3 3.8 %collective-permute-start.9 = (bf16[16,512]{1,0:T(8,128)(2,1)S(1)}, bf16[16,512]{1,0:T(8,128)(2,1)S(1)}, u32[]{:S(2)}, u32[]{:S(2)}) collective-permute-start(bf16[16,512]{1,0:T(8,128)(2,1)S(1)} %fusion.103), channel_id=1, source_target_pairs={{0,2},{1,3},{2,0},{3,1},{4,6},{5,7},{6,4},{7,5},{8,10},{9,11},{10,... | collective-permute-start | bytes 49160 | tf_op jit(solution)/shard_map/ppermute | solution.py:28
  40.3 13.5 %collective-permute-start.10 = (f32[1,1,16,512]{3,2,1,0:T(8,128)S(1)}, f32[1,1,16,512]{3,2,1,0:T(8,128)S(1)}, u32[]{:S(2)}, u32[]{:S(2)}) collective-permute-start(f32[1,1,16,512]{3,2,1,0:T(8,128)S(1)} %bitcast.304), channel_id=1, source_target_pairs={{0,64},{64,128},{128,192},{1,65},{65,129},{129,193},{2,66},{66,130... | collective-permute-start | bytes 98312 | tf_op jit(solution)/shard_map/ppermute | solution.py:15
  43.8 10.1 %collective-permute-start.11 = (f32[1,1,16,512]{3,2,1,0:T(8,128)S(1)}, f32[1,1,16,512]{3,2,1,0:T(8,128)S(1)}, u32[]{:S(2)}, u32[]{:S(2)}) collective-permute-start(f32[1,1,16,512]{3,2,1,0:T(8,128)S(1)} %bitcast.305), channel_id=1, source_target_pairs={{64,0},{128,64},{192,128},{65,1},{129,65},{193,129},{66,2},{130,66... | collective-permute-start | bytes 98312 | tf_op jit(solution)/shard_map/ppermute | solution.py:16
  46.1 7.7 %collective-permute-start.12 = (f32[1,1,16,512]{3,2,1,0:T(8,128)S(1)}, f32[1,1,16,512]{3,2,1,0:T(8,128)S(1)}, u32[]{:S(2)}, u32[]{:S(2)}) collective-permute-start(f32[1,1,16,512]{3,2,1,0:T(8,128)S(1)} %bitcast.306), channel_id=1, source_target_pairs={{0,1},{1,2},{2,3},{3,4},{4,5},{5,6},{6,7},{7,8},{8,9},{9,10},{10,1... | collective-permute-start | bytes 98312 | tf_op jit(solution)/shard_map/ppermute | solution.py:15
  48.1 7.3 %collective-permute-start.13 = (f32[1,1,16,512]{3,2,1,0:T(8,128)S(1)}, f32[1,1,16,512]{3,2,1,0:T(8,128)S(1)}, u32[]{:S(2)}, u32[]{:S(2)}) collective-permute-start(f32[1,1,16,512]{3,2,1,0:T(8,128)S(1)} %bitcast.307), channel_id=1, source_target_pairs={{1,0},{2,1},{3,2},{4,3},{5,4},{6,5},{7,6},{8,7},{9,8},{10,9},{11,1... | collective-permute-start | bytes 98312 | tf_op jit(solution)/shard_map/ppermute | solution.py:16
  55.4 4.7 %collective-permute-start.14 = (bf16[16,512]{1,0:T(8,128)(2,1)S(1)}, bf16[16,512]{1,0:T(8,128)(2,1)S(1)}, u32[]{:S(2)}, u32[]{:S(2)}) collective-permute-start(bf16[16,512]{1,0:T(8,128)(2,1)S(1)} %fusion.98), channel_id=1, source_target_pairs={{0,4},{1,5},{2,6},{3,7},{4,0},{5,1},{6,2},{7,3},{8,12},{9,13},{10,... | collective-permute-start | bytes 49160 | tf_op jit(solution)/shard_map/ppermute | solution.py:28
  119.7 3.6 %copy-start.4 = (bf16[1,512,512]{2,1,0:T(8,128)(2,1)S(1)}, bf16[1,512,512]{2,1,0:T(8,128)(2,1)}, u32[]{:S(2)}) copy-start(bf16[1,512,512]{2,1,0:T(8,128)(2,1)} %param.19) | copy-start | bytes 1572868
  123.5 19.4 %copy-start.7 = (f32[1,3,4,512]{3,2,1,0:T(4,128)S(1)}, f32[1,3,4,512]{3,2,1,0:T(4,128)}, u32[]{:S(2)}) copy-start(f32[1,3,4,512]{3,2,1,0:T(4,128)} %param.16) | copy-start | bytes 73732
  124.9 23.4 %copy-start.2 = (bf16[1,3,512,512]{3,2,1,0:T(8,128)(2,1)S(1)}, bf16[1,3,512,512]{3,2,1,0:T(8,128)(2,1)}, u32[]{:S(2)}) copy-start(bf16[1,3,512,512]{3,2,1,0:T(8,128)(2,1)} %param.17) | copy-start | bytes 4718596
  125.2 4.7 %collective-permute-start.15 = (bf16[16,512]{1,0:T(8,128)(2,1)S(1)}, bf16[16,512]{1,0:T(8,128)(2,1)S(1)}, u32[]{:S(2)}, u32[]{:S(2)}) collective-permute-start(bf16[16,512]{1,0:T(8,128)(2,1)S(1)} %convolution_convert_fusion.4), channel_id=1, source_target_pairs={{0,4},{1,5},{2,6},{3,7},{4,0},{5,1},{6,2},{7,3},{8,12},{9,13},{10,... | collective-permute-start | bytes 49160 | tf_op jit(solution)/shard_map/ppermute | solution.py:28
  129.9 13.0 %collective-permute-start.16 = (bf16[1,1,16,512]{3,2,1,0:T(8,128)(2,1)S(1)}, bf16[1,1,16,512]{3,2,1,0:T(8,128)(2,1)S(1)}, u32[]{:S(2)}, u32[]{:S(2)}) collective-permute-start(bf16[1,1,16,512]{3,2,1,0:T(8,128)(2,1)S(1)} %fusion.112), channel_id=1, source_target_pairs={{0,1},{1,2},{2,3},{3,4},{4,5},{5,6},{6,7},{7,8},{8,9},{9,10},{10,1... | collective-permute-start | bytes 49160 | tf_op jit(solution)/shard_map/ppermute | solution.py:15
  131.8 11.1 %collective-permute-start.17 = (bf16[1,1,16,512]{3,2,1,0:T(8,128)(2,1)S(1)}, bf16[1,1,16,512]{3,2,1,0:T(8,128)(2,1)S(1)}, u32[]{:S(2)}, u32[]{:S(2)}) collective-permute-start(bf16[1,1,16,512]{3,2,1,0:T(8,128)(2,1)S(1)} %fusion.112), channel_id=1, source_target_pairs={{0,64},{64,128},{128,192},{1,65},{65,129},{129,193},{2,66},{66,130... | collective-permute-start | bytes 49160 | tf_op jit(solution)/shard_map/ppermute | solution.py:15
  135.1 7.8 %collective-permute-start.18 = (bf16[1,1,16,512]{3,2,1,0:T(8,128)(2,1)S(1)}, bf16[1,1,16,512]{3,2,1,0:T(8,128)(2,1)S(1)}, u32[]{:S(2)}, u32[]{:S(2)}) collective-permute-start(bf16[1,1,16,512]{3,2,1,0:T(8,128)(2,1)S(1)} %fusion.112), channel_id=1, source_target_pairs={{64,0},{128,64},{192,128},{65,1},{129,65},{193,129},{66,2},{130,66... | collective-permute-start | bytes 49160 | tf_op jit(solution)/shard_map/ppermute | solution.py:16
  137.7 6.6 %collective-permute-start.19 = (bf16[1,1,16,512]{3,2,1,0:T(8,128)(2,1)S(1)}, bf16[1,1,16,512]{3,2,1,0:T(8,128)(2,1)S(1)}, u32[]{:S(2)}, u32[]{:S(2)}) collective-permute-start(bf16[1,1,16,512]{3,2,1,0:T(8,128)(2,1)S(1)} %fusion.112), channel_id=1, source_target_pairs={{1,0},{2,1},{3,2},{4,3},{5,4},{6,5},{7,6},{8,7},{9,8},{10,9},{11,1... | collective-permute-start | bytes 49160 | tf_op jit(solution)/shard_map/ppermute | solution.py:16
  144.6 34.7 %copy-start.3 = (bf16[1,8,64,256]{3,2,1,0:T(8,128)(2,1)S(1)}, bf16[1,8,64,256]{3,2,1,0:T(8,128)(2,1)}, u32[]{:S(2)}) copy-start(bf16[1,8,64,256]{3,2,1,0:T(8,128)(2,1)} %param.13) | copy-start | bytes 786436
  144.6 3.8 %collective-permute-start.20 = (bf16[16,512]{1,0:T(8,128)(2,1)S(1)}, bf16[16,512]{1,0:T(8,128)(2,1)S(1)}, u32[]{:S(2)}, u32[]{:S(2)}) collective-permute-start(bf16[16,512]{1,0:T(8,128)(2,1)S(1)} %convolution_convert_fusion.3), channel_id=1, source_target_pairs={{0,2},{1,3},{2,0},{3,1},{4,6},{5,7},{6,4},{7,5},{8,10},{9,11},{10,... | collective-permute-start | bytes 49160 | tf_op jit(solution)/shard_map/ppermute | solution.py:28
  148.6 13.0 %collective-permute-start.21 = (bf16[1,1,16,512]{3,2,1,0:T(8,128)(2,1)S(1)}, bf16[1,1,16,512]{3,2,1,0:T(8,128)(2,1)S(1)}, u32[]{:S(2)}, u32[]{:S(2)}) collective-permute-start(bf16[1,1,16,512]{3,2,1,0:T(8,128)(2,1)S(1)} %convert_bitcast_fusion.1), channel_id=1, source_target_pairs={{0,1},{1,2},{2,3},{3,4},{4,5},{5,6},{6,7},{7,8},{8,9},{9,10},{10,1... | collective-permute-start | bytes 49160 | tf_op jit(solution)/shard_map/ppermute | solution.py:15
  150.5 11.1 %collective-permute-start.22 = (bf16[1,1,16,512]{3,2,1,0:T(8,128)(2,1)S(1)}, bf16[1,1,16,512]{3,2,1,0:T(8,128)(2,1)S(1)}, u32[]{:S(2)}, u32[]{:S(2)}) collective-permute-start(bf16[1,1,16,512]{3,2,1,0:T(8,128)(2,1)S(1)} %convert_bitcast_fusion.1), channel_id=1, source_target_pairs={{0,64},{64,128},{128,192},{1,65},{65,129},{129,193},{2,66},{66,130... | collective-permute-start | bytes 49160 | tf_op jit(solution)/shard_map/ppermute | solution.py:15
  153.8 7.8 %collective-permute-start.23 = (bf16[1,1,16,512]{3,2,1,0:T(8,128)(2,1)S(1)}, bf16[1,1,16,512]{3,2,1,0:T(8,128)(2,1)S(1)}, u32[]{:S(2)}, u32[]{:S(2)}) collective-permute-start(bf16[1,1,16,512]{3,2,1,0:T(8,128)(2,1)S(1)} %convert_bitcast_fusion.1), channel_id=1, source_target_pairs={{64,0},{128,64},{192,128},{65,1},{129,65},{193,129},{66,2},{130,66... | collective-permute-start | bytes 49160 | tf_op jit(solution)/shard_map/ppermute | solution.py:16
  156.4 6.6 %collective-permute-start.24 = (bf16[1,1,16,512]{3,2,1,0:T(8,128)(2,1)S(1)}, bf16[1,1,16,512]{3,2,1,0:T(8,128)(2,1)S(1)}, u32[]{:S(2)}, u32[]{:S(2)}) collective-permute-start(bf16[1,1,16,512]{3,2,1,0:T(8,128)(2,1)S(1)} %convert_bitcast_fusion.1), channel_id=1, source_target_pairs={{1,0},{2,1},{3,2},{4,3},{5,4},{6,5},{7,6},{8,7},{9,8},{10,9},{11,1... | collective-permute-start | bytes 49160 | tf_op jit(solution)/shard_map/ppermute | solution.py:16
  163.1 16.6 %copy-start.9 = (s32[1,8,64]{2,1,0:T(8,128)S(1)}, s32[1,8,64]{2,1,0:T(8,128)}, u32[]{:S(2)}) copy-start(s32[1,8,64]{2,1,0:T(8,128)} %param.14) | copy-start | bytes 6148
  163.3 1.2 collective-permute-start.25
  164.7 13.0 %collective-permute-start.26 = (bf16[1,1,16,512]{3,2,1,0:T(8,128)(2,1)S(1)}, bf16[1,1,16,512]{3,2,1,0:T(8,128)(2,1)S(1)}, u32[]{:S(2)}, u32[]{:S(2)}) collective-permute-start(bf16[1,1,16,512]{3,2,1,0:T(8,128)(2,1)S(1)} %convert_bitcast_fusion), channel_id=1, source_target_pairs={{0,1},{1,2},{2,3},{3,4},{4,5},{5,6},{6,7},{7,8},{8,9},{9,10},{10,1... | collective-permute-start | bytes 49160 | tf_op jit(solution)/shard_map/ppermute | solution.py:15
  166.8 10.9 %collective-permute-start.27 = (bf16[1,1,16,512]{3,2,1,0:T(8,128)(2,1)S(1)}, bf16[1,1,16,512]{3,2,1,0:T(8,128)(2,1)S(1)}, u32[]{:S(2)}, u32[]{:S(2)}) collective-permute-start(bf16[1,1,16,512]{3,2,1,0:T(8,128)(2,1)S(1)} %convert_bitcast_fusion), channel_id=1, source_target_pairs={{0,64},{64,128},{128,192},{1,65},{65,129},{129,193},{2,66},{66,130... | collective-permute-start | bytes 49160 | tf_op jit(solution)/shard_map/ppermute | solution.py:15
  170.1 7.6 %collective-permute-start.28 = (bf16[1,1,16,512]{3,2,1,0:T(8,128)(2,1)S(1)}, bf16[1,1,16,512]{3,2,1,0:T(8,128)(2,1)S(1)}, u32[]{:S(2)}, u32[]{:S(2)}) collective-permute-start(bf16[1,1,16,512]{3,2,1,0:T(8,128)(2,1)S(1)} %convert_bitcast_fusion), channel_id=1, source_target_pairs={{64,0},{128,64},{192,128},{65,1},{129,65},{193,129},{66,2},{130,66... | collective-permute-start | bytes 49160 | tf_op jit(solution)/shard_map/ppermute | solution.py:16
  172.7 6.5 %collective-permute-start.29 = (bf16[1,1,16,512]{3,2,1,0:T(8,128)(2,1)S(1)}, bf16[1,1,16,512]{3,2,1,0:T(8,128)(2,1)S(1)}, u32[]{:S(2)}, u32[]{:S(2)}) collective-permute-start(bf16[1,1,16,512]{3,2,1,0:T(8,128)(2,1)S(1)} %convert_bitcast_fusion), channel_id=1, source_target_pairs={{1,0},{2,1},{3,2},{4,3},{5,4},{6,5},{7,6},{8,7},{9,8},{10,9},{11,1... | collective-permute-start | bytes 49160 | tf_op jit(solution)/shard_map/ppermute | solution.py:16

commit v2 on v1

--- a/solution.py
+++ b/solution.py
@@ -102,7 +102,7 @@
     top_state = state.astype(jnp.bfloat16)
     comp = compress[0]
     small = right_transpose(top_state, comp).astype(jnp.bfloat16)
-    gathered = lax.all_gather(small, ("gy", "gx"), axis=1, tiled=True)
+    gathered = collect(small, ("gy", "gx"), 1)
     coarse = jnp.dot(gathered, top_couple, preferred_element_type=jnp.float32)
     state = jnp.dot(top_state, top_inverse[0], preferred_element_type=jnp.float32)
     state = state + jnp.dot(coarse.astype(jnp.bfloat16), comp, preferred_element_type=jnp.float32)

time: 182 us -> 153 us (0.84)
  blocking collectives: 59.2 us -> 0 us
  waiting for transfers between devices: 21 us -> 34.6 us
  starting transfers between devices: 82.3 us -> 92.6 us
  local copies, waits for them, and re-layouts: 6.73 us -> 14.4 us
    all_gather x1 -> x0, blocking collectives: 59.2 us -> none  [body(): gathered = lax.all_gather(small, ('gy', 'gx'), axis=1, tiled=True)]
    all_to_all x0 -> x1, waiting for transfers between devices: none -> 13.9 us  [sent_to_all(): return lax.all_to_all(copies, axis, split_axis=0, concat_axis=0, tiled=True)]
    all_to_all x0 -> x1, starting transfers between devices: none -> 11 us  [sent_to_all(): return lax.all_to_all(copies, axis, split_axis=0, concat_axis=0, tiled=True)]
    ppermute x12, starting transfers between devices: 32 us -> 28.5 us  [padded_2(): lax.ppermute(last, axis, up)]
    ppermute x12, starting transfers between devices: 48.2 us -> 51.8 us  [padded_2(): lax.ppermute(leading, axis, [(b, a) for a, b in up])]
    transpose x0 -> x1, local copies, waits for them, and re-layouts: none -> 2.53 us  [joined_along(): return jnp.moveaxis(parts, 0, dim).reshape(shape)]
    reshape x0 -> x1, local copies, waits for them, and re-layouts: none -> 2.35 us  [joined_along(): return jnp.moveaxis(parts, 0, dim).reshape(shape)]
    unnamed x22 -> x23, local copies, waits for them, and re-layouts: 3.65 us -> 5.67 us
  transfers between devices with their start and end apart: 30 -> 31, of which waited for: 11 -> 12; matrix products, arithmetic and copies ran while one was open for 3% -> 5% of each run, Pallas kernels for 0% -> 0%
where the time goes in v2:
time: 153 us; the launch traced here: 152 us
  starting transfers between devices  92.6 us (61%)
  waiting for transfers between devices  34.6 us (23%)
  local copies, waits for them, and re-layouts  14.4 us (9%)
  matrix products  9.66 us (6%)
    ppermute x12, starting transfers between devices, padded_2(): lax.ppermute(leading, axis, [(b, a) for a, b in up])  51.8 us
    ppermute x12, starting transfers between devices, padded_2(): lax.ppermute(last, axis, up)  28.5 us
    all_to_all x1, waiting for transfers between devices, sent_to_all(): return lax.all_to_all(copies, axis, split_axis=0, concat_axis=0, tiled=True)  13.9 us
    ppermute x6, waiting for transfers between devices, partner_2(): lax.ppermute(shard, axis, [(i, i ^ 1 << stride) for i in range(lax.axis_s...  13.2 us
    all_to_all x1, starting transfers between devices, sent_to_all(): return lax.all_to_all(copies, axis, split_axis=0, concat_axis=0, tiled=True)  11 us
    ppermute x12, waiting for transfers between devices, padded_2(): lax.ppermute(leading, axis, [(b, a) for a, b in up])  7.47 us
    unnamed x23, local copies, waits for them, and re-layouts  5.67 us
    dot_general x3, matrix products, body(): state = jnp.dot(rounded, own[level], preferred_element_type=jnp.float32)  3.63 us
  transfers between devices with their start and end apart: 31, of which 12 were waited for; matrix products, arithmetic and copies ran while one was open for 5% of the time, Pallas kernels for 0%

profile of v2, /device:TPU:10, one launch (start us, length us, event | category | flops | bytes accessed | tf_op | source)
XLA Modules:
  0.0 152.1 jit_solution(5441189465747685343)
XLA Ops:
  0.0 0.9 copy.39
  1.0 0.3 copy-done
  1.3 0.2 fusion.3
  1.5 1.2 convolution_bitcast_fusion.2
  2.7 0.3 fusion.4
  3.1 3.5 %collective-permute-start = (f32[1,1,16,512]{3,2,1,0:T(8,128)S(1)}, f32[1,1,16,512]{3,2,1,0:T(8,128)S(1)}, u32[]{:S(2)}, u32[]{:S(2)}) collective-permute-start(f32[1,1,16,512]{3,2,1,0:T(8,128)S(1)} %broadcast_in_dim_reshape.3), channel_id=1, source_target_pairs={{0,64},{64,128},{128,192},{1,65},{65,129},{129,193},{2,66},{66,130... | collective-permute-start | bytes 98312 | tf_op jit(solution)/shard_map/ppermute | solution.py:15
  6.6 2.4 %collective-permute-start.1 = (f32[1,1,16,512]{3,2,1,0:T(8,128)S(1)}, f32[1,1,16,512]{3,2,1,0:T(8,128)S(1)}, u32[]{:S(2)}, u32[]{:S(2)}) collective-permute-start(f32[1,1,16,512]{3,2,1,0:T(8,128)S(1)} %broadcast_in_dim_reshape.3), channel_id=1, source_target_pairs={{64,0},{128,64},{192,128},{65,1},{129,65},{193,129},{66,2},{130,66... | collective-permute-start | bytes 98312 | tf_op jit(solution)/shard_map/ppermute | solution.py:16
  9.0 1.9 %collective-permute-start.2 = (f32[1,1,16,512]{3,2,1,0:T(8,128)S(1)}, f32[1,1,16,512]{3,2,1,0:T(8,128)S(1)}, u32[]{:S(2)}, u32[]{:S(2)}) collective-permute-start(f32[1,1,16,512]{3,2,1,0:T(8,128)S(1)} %broadcast_in_dim_reshape.3), channel_id=1, source_target_pairs={{0,1},{1,2},{2,3},{3,4},{4,5},{5,6},{6,7},{7,8},{8,9},{9,10},{10,1... | collective-permute-start | bytes 98312 | tf_op jit(solution)/shard_map/ppermute | solution.py:15
  10.9 6.6 %collective-permute-start.3 = (f32[1,1,16,512]{3,2,1,0:T(8,128)S(1)}, f32[1,1,16,512]{3,2,1,0:T(8,128)S(1)}, u32[]{:S(2)}, u32[]{:S(2)}) collective-permute-start(f32[1,1,16,512]{3,2,1,0:T(8,128)S(1)} %broadcast_in_dim_reshape.3), channel_id=1, source_target_pairs={{1,0},{2,1},{3,2},{4,3},{5,4},{6,5},{7,6},{8,7},{9,8},{10,9},{11,1... | collective-permute-start | bytes 98312 | tf_op jit(solution)/shard_map/ppermute | solution.py:16
  18.0 1.1 collective-permute-done.3
  19.7 1.2 fusion.25
  21.0 0.2 convolution_add_fusion.5
  21.1 3.5 %collective-permute-start.5 = (f32[1,1,16,512]{3,2,1,0:T(8,128)S(1)}, f32[1,1,16,512]{3,2,1,0:T(8,128)S(1)}, u32[]{:S(2)}, u32[]{:S(2)}) collective-permute-start(f32[1,1,16,512]{3,2,1,0:T(8,128)S(1)} %bitcast.304), channel_id=1, source_target_pairs={{0,64},{64,128},{128,192},{1,65},{65,129},{129,193},{2,66},{66,130... | collective-permute-start | bytes 98312 | tf_op jit(solution)/shard_map/ppermute | solution.py:15
  24.6 2.4 %collective-permute-start.6 = (f32[1,1,16,512]{3,2,1,0:T(8,128)S(1)}, f32[1,1,16,512]{3,2,1,0:T(8,128)S(1)}, u32[]{:S(2)}, u32[]{:S(2)}) collective-permute-start(f32[1,1,16,512]{3,2,1,0:T(8,128)S(1)} %bitcast.305), channel_id=1, source_target_pairs={{64,0},{128,64},{192,128},{65,1},{129,65},{193,129},{66,2},{130,66... | collective-permute-start | bytes 98312 | tf_op jit(solution)/shard_map/ppermute | solution.py:16
  27.0 1.9 %collective-permute-start.7 = (f32[1,1,16,512]{3,2,1,0:T(8,128)S(1)}, f32[1,1,16,512]{3,2,1,0:T(8,128)S(1)}, u32[]{:S(2)}, u32[]{:S(2)}) collective-permute-start(f32[1,1,16,512]{3,2,1,0:T(8,128)S(1)} %bitcast.306), channel_id=1, source_target_pairs={{0,1},{1,2},{2,3},{3,4},{4,5},{5,6},{6,7},{7,8},{8,9},{9,10},{10,1... | collective-permute-start | bytes 98312 | tf_op jit(solution)/shard_map/ppermute | solution.py:15
  28.9 5.8 %collective-permute-start.8 = (f32[1,1,16,512]{3,2,1,0:T(8,128)S(1)}, f32[1,1,16,512]{3,2,1,0:T(8,128)S(1)}, u32[]{:S(2)}, u32[]{:S(2)}) collective-permute-start(f32[1,1,16,512]{3,2,1,0:T(8,128)S(1)} %bitcast.307), channel_id=1, source_target_pairs={{1,0},{2,1},{3,2},{4,3},{5,4},{6,5},{7,6},{8,7},{9,8},{10,9},{11,1... | collective-permute-start | bytes 98312 | tf_op jit(solution)/shard_map/ppermute | solution.py:16
  34.7 1.5 %collective-permute-done.8 = f32[1,1,16,512]{3,2,1,0:T(8,128)S(1)} collective-permute-done((f32[1,1,16,512]{3,2,1,0:T(8,128)S(1)}, f32[1,1,16,512]{3,2,1,0:T(8,128)S(1)}, u32[]{:S(2)}, u32[]{:S(2)}) %collective-permute-start.8) | collective-permute-done | bytes 32800 | tf_op jit(solution)/shard_map/ppermute | solution.py:16
  36.4 1.2 fusion.20
  37.6 2.5 %collective-permute-done.9 = bf16[16,512]{1,0:T(8,128)(2,1)S(1)} collective-permute-done((bf16[16,512]{1,0:T(8,128)(2,1)S(1)}, bf16[16,512]{1,0:T(8,128)(2,1)S(1)}, u32[]{:S(2)}, u32[]{:S(2)}) %collective-permute-start.9) | collective-permute-done | bytes 16416 | tf_op jit(solution)/shard_map/ppermute | solution.py:28
  40.3 3.5 %collective-permute-start.10 = (f32[1,1,16,512]{3,2,1,0:T(8,128)S(1)}, f32[1,1,16,512]{3,2,1,0:T(8,128)S(1)}, u32[]{:S(2)}, u32[]{:S(2)}) collective-permute-start(f32[1,1,16,512]{3,2,1,0:T(8,128)S(1)} %bitcast.300), channel_id=1, source_target_pairs={{0,64},{64,128},{128,192},{1,65},{65,129},{129,193},{2,66},{66,130... | collective-permute-start | bytes 98312 | tf_op jit(solution)/shard_map/ppermute | solution.py:15
  43.8 2.4 %collective-permute-start.11 = (f32[1,1,16,512]{3,2,1,0:T(8,128)S(1)}, f32[1,1,16,512]{3,2,1,0:T(8,128)S(1)}, u32[]{:S(2)}, u32[]{:S(2)}) collective-permute-start(f32[1,1,16,512]{3,2,1,0:T(8,128)S(1)} %bitcast.301), channel_id=1, source_target_pairs={{64,0},{128,64},{192,128},{65,1},{129,65},{193,129},{66,2},{130,66... | collective-permute-start | bytes 98312 | tf_op jit(solution)/shard_map/ppermute | solution.py:16
  46.1 1.9 %collective-permute-start.12 = (f32[1,1,16,512]{3,2,1,0:T(8,128)S(1)}, f32[1,1,16,512]{3,2,1,0:T(8,128)S(1)}, u32[]{:S(2)}, u32[]{:S(2)}) collective-permute-start(f32[1,1,16,512]{3,2,1,0:T(8,128)S(1)} %bitcast.302), channel_id=1, source_target_pairs={{0,1},{1,2},{2,3},{3,4},{4,5},{5,6},{6,7},{7,8},{8,9},{9,10},{10,1... | collective-permute-start | bytes 98312 | tf_op jit(solution)/shard_map/ppermute | solution.py:15
  48.1 5.8 %collective-permute-start.13 = (f32[1,1,16,512]{3,2,1,0:T(8,128)S(1)}, f32[1,1,16,512]{3,2,1,0:T(8,128)S(1)}, u32[]{:S(2)}, u32[]{:S(2)}) collective-permute-start(f32[1,1,16,512]{3,2,1,0:T(8,128)S(1)} %bitcast.303), channel_id=1, source_target_pairs={{1,0},{2,1},{3,2},{4,3},{5,4},{6,5},{7,6},{8,7},{9,8},{10,9},{11,1... | collective-permute-start | bytes 98312 | tf_op jit(solution)/shard_map/ppermute | solution.py:16
  53.9 1.5 %collective-permute-done.13 = f32[1,1,16,512]{3,2,1,0:T(8,128)S(1)} collective-permute-done((f32[1,1,16,512]{3,2,1,0:T(8,128)S(1)}, f32[1,1,16,512]{3,2,1,0:T(8,128)S(1)}, u32[]{:S(2)}, u32[]{:S(2)}) %collective-permute-start.13) | collective-permute-done | bytes 32800 | tf_op jit(solution)/shard_map/ppermute | solution.py:16
  55.4 0.5 collective-permute-start.14
  55.9 1.2 fusion.15
  57.1 3.0 %collective-permute-done.14 = bf16[16,512]{1,0:T(8,128)(2,1)S(1)} collective-permute-done((bf16[16,512]{1,0:T(8,128)(2,1)S(1)}, bf16[16,512]{1,0:T(8,128)(2,1)S(1)}, u32[]{:S(2)}, u32[]{:S(2)}) %collective-permute-start.14) | collective-permute-done | bytes 16416 | tf_op jit(solution)/shard_map/ppermute | solution.py:28
  60.5 1.1 broadcast_in_dim.14
  61.6 2.9 %reshape.139 = bf16[256,2,256]{2,1,0:T(2,128)(2,1)} reshape(bf16[256,16,32]{2,1,0:T(8,128)(2,1)} %broadcast_in_dim.14) | data formatting | bytes 524288
  64.5 11.0 %all-to-all-start = ((bf16[256,2,256]{2,1,0:T(2,128)(2,1)}), bf16[256,2,256]{2,1,0:T(2,128)(2,1)S(1)}, u32[]{:S(2)}, u32[]{:S(2)}) async-start(bf16[256,2,256]{2,1,0:T(2,128)(2,1)} %reshape.139), calls=%async_computation | async-start | bytes 524288 | tf_op jit(solution)/shard_map/all_to_all | solution.py:33
  75.7 13.9 %all-to-all-done = bf16[256,2,256]{2,1,0:T(2,128)(2,1)S(1)} async-done(((bf16[256,2,256]{2,1,0:T(2,128)(2,1)}), bf16[256,2,256]{2,1,0:T(2,128)(2,1)S(1)}, u32[]{:S(2)}, u32[]{:S(2)}) %all-to-all-start) | async-done | bytes 262176 | tf_op jit(solution)/shard_map/all_to_all | solution.py:33
  89.6 1.5 reshape.140
  91.1 2.5 %copy.35 = bf16[16,256,32]{2,1,0:T(8,128)(2,1)} copy(bf16[16,256,32]{2,0,1:T(8,128)(2,1)} %bitcast.297) | data formatting | bytes 524288 | tf_op jit(solution)/shard_map/transpose | solution.py:39
  93.6 2.4 %reshape.114 = bf16[16,8192]{1,0:T(8,128)(2,1)S(1)} reshape(bf16[16,256,32]{2,1,0:T(8,128)(2,1)} %copy.35) | data formatting | bytes 524288 | tf_op jit(solution)/shard_map/reshape | solution.py:39
  96.0 0.4 fusion.5
  96.4 0.3 convolution_convert_fusion.4
  96.6 0.7 collective-permute-start.15
  97.3 1.3 fusion.13
  98.6 2.7 %collective-permute-done.15 = bf16[16,512]{1,0:T(8,128)(2,1)S(1)} collective-permute-done((bf16[16,512]{1,0:T(8,128)(2,1)S(1)}, bf16[16,512]{1,0:T(8,128)(2,1)S(1)}, u32[]{:S(2)}, u32[]{:S(2)}) %collective-permute-start.15) | collective-permute-done | bytes 16416 | tf_op jit(solution)/shard_map/ppermute | solution.py:28
  101.3 1.9 %collective-permute-start.16 = (bf16[1,1,16,512]{3,2,1,0:T(8,128)(2,1)S(1)}, bf16[1,1,16,512]{3,2,1,0:T(8,128)(2,1)S(1)}, u32[]{:S(2)}, u32[]{:S(2)}) collective-permute-start(bf16[1,1,16,512]{3,2,1,0:T(8,128)(2,1)S(1)} %fusion.111), channel_id=1, source_target_pairs={{0,1},{1,2},{2,3},{3,4},{4,5},{5,6},{6,7},{7,8},{8,9},{9,10},{10,1... | collective-permute-start | bytes 49160 | tf_op jit(solution)/shard_map/ppermute | solution.py:15
  103.2 1.9 %collective-permute-start.17 = (bf16[1,1,16,512]{3,2,1,0:T(8,128)(2,1)S(1)}, bf16[1,1,16,512]{3,2,1,0:T(8,128)(2,1)S(1)}, u32[]{:S(2)}, u32[]{:S(2)}) collective-permute-start(bf16[1,1,16,512]{3,2,1,0:T(8,128)(2,1)S(1)} %fusion.111), channel_id=1, source_target_pairs={{0,64},{64,128},{128,192},{1,65},{65,129},{129,193},{2,66},{66,130... | collective-permute-start | bytes 49160 | tf_op jit(solution)/shard_map/ppermute | solution.py:15
  105.1 3.9 %collective-permute-start.18 = (bf16[1,1,16,512]{3,2,1,0:T(8,128)(2,1)S(1)}, bf16[1,1,16,512]{3,2,1,0:T(8,128)(2,1)S(1)}, u32[]{:S(2)}, u32[]{:S(2)}) collective-permute-start(bf16[1,1,16,512]{3,2,1,0:T(8,128)(2,1)S(1)} %fusion.111), channel_id=1, source_target_pairs={{64,0},{128,64},{192,128},{65,1},{129,65},{193,129},{66,2},{130,66... | collective-permute-start | bytes 49160 | tf_op jit(solution)/shard_map/ppermute | solution.py:16
  109.1 5.2 %collective-permute-start.19 = (bf16[1,1,16,512]{3,2,1,0:T(8,128)(2,1)S(1)}, bf16[1,1,16,512]{3,2,1,0:T(8,128)(2,1)S(1)}, u32[]{:S(2)}, u32[]{:S(2)}) collective-permute-start(bf16[1,1,16,512]{3,2,1,0:T(8,128)(2,1)S(1)} %fusion.111), channel_id=1, source_target_pairs={{1,0},{2,1},{3,2},{4,3},{5,4},{6,5},{7,6},{8,7},{9,8},{10,9},{11,1... | collective-permute-start | bytes 49160 | tf_op jit(solution)/shard_map/ppermute | solution.py:16
  114.3 0.9 fusion.112
  115.2 0.5 collective-permute-done.19
  115.7 0.2 convolution_convert_fusion.3
  116.0 3.7 %collective-permute-done.20 = bf16[16,512]{1,0:T(8,128)(2,1)S(1)} collective-permute-done((bf16[16,512]{1,0:T(8,128)(2,1)S(1)}, bf16[16,512]{1,0:T(8,128)(2,1)S(1)}, u32[]{:S(2)}, u32[]{:S(2)}) %collective-permute-start.20) | collective-permute-done | bytes 16416 | tf_op jit(solution)/shard_map/ppermute | solution.py:28
  119.7 0.2 convolution_add_fusion.2
  120.0 1.9 %collective-permute-start.21 = (bf16[1,1,16,512]{3,2,1,0:T(8,128)(2,1)S(1)}, bf16[1,1,16,512]{3,2,1,0:T(8,128)(2,1)S(1)}, u32[]{:S(2)}, u32[]{:S(2)}) collective-permute-start(bf16[1,1,16,512]{3,2,1,0:T(8,128)(2,1)S(1)} %convert_bitcast_fusion.1), channel_id=1, source_target_pairs={{0,1},{1,2},{2,3},{3,4},{4,5},{5,6},{6,7},{7,8},{8,9},{9,10},{10,1... | collective-permute-start | bytes 49160 | tf_op jit(solution)/shard_map/ppermute | solution.py:15
  121.9 2.2 %collective-permute-start.22 = (bf16[1,1,16,512]{3,2,1,0:T(8,128)(2,1)S(1)}, bf16[1,1,16,512]{3,2,1,0:T(8,128)(2,1)S(1)}, u32[]{:S(2)}, u32[]{:S(2)}) collective-permute-start(bf16[1,1,16,512]{3,2,1,0:T(8,128)(2,1)S(1)} %convert_bitcast_fusion.1), channel_id=1, source_target_pairs={{0,64},{64,128},{128,192},{1,65},{65,129},{129,193},{2,66},{66,130... | collective-permute-start | bytes 49160 | tf_op jit(solution)/shard_map/ppermute | solution.py:15
  124.1 3.6 %collective-permute-start.23 = (bf16[1,1,16,512]{3,2,1,0:T(8,128)(2,1)S(1)}, bf16[1,1,16,512]{3,2,1,0:T(8,128)(2,1)S(1)}, u32[]{:S(2)}, u32[]{:S(2)}) collective-permute-start(bf16[1,1,16,512]{3,2,1,0:T(8,128)(2,1)S(1)} %convert_bitcast_fusion.1), channel_id=1, source_target_pairs={{64,0},{128,64},{192,128},{65,1},{129,65},{193,129},{66,2},{130,66... | collective-permute-start | bytes 49160 | tf_op jit(solution)/shard_map/ppermute | solution.py:16
  127.8 5.2 %collective-permute-start.24 = (bf16[1,1,16,512]{3,2,1,0:T(8,128)(2,1)S(1)}, bf16[1,1,16,512]{3,2,1,0:T(8,128)(2,1)S(1)}, u32[]{:S(2)}, u32[]{:S(2)}) collective-permute-start(bf16[1,1,16,512]{3,2,1,0:T(8,128)(2,1)S(1)} %convert_bitcast_fusion.1), channel_id=1, source_target_pairs={{1,0},{2,1},{3,2},{4,3},{5,4},{6,5},{7,6},{8,7},{9,8},{10,9},{11,1... | collective-permute-start | bytes 49160 | tf_op jit(solution)/shard_map/ppermute | solution.py:16
  133.0 1.4 collective-permute-done.24
  134.5 0.2 convolution_convert_fusion.2
  134.7 1.2 collective-permute-done.25
  135.9 0.2 convolution_add_fusion.1
  136.1 2.1 %collective-permute-start.26 = (bf16[1,1,16,512]{3,2,1,0:T(8,128)(2,1)S(1)}, bf16[1,1,16,512]{3,2,1,0:T(8,128)(2,1)S(1)}, u32[]{:S(2)}, u32[]{:S(2)}) collective-permute-start(bf16[1,1,16,512]{3,2,1,0:T(8,128)(2,1)S(1)} %convert_bitcast_fusion), channel_id=1, source_target_pairs={{0,1},{1,2},{2,3},{3,4},{4,5},{5,6},{6,7},{7,8},{8,9},{9,10},{10,1... | collective-permute-start | bytes 49160 | tf_op jit(solution)/shard_map/ppermute | solution.py:15
  138.2 2.2 %collective-permute-start.27 = (bf16[1,1,16,512]{3,2,1,0:T(8,128)(2,1)S(1)}, bf16[1,1,16,512]{3,2,1,0:T(8,128)(2,1)S(1)}, u32[]{:S(2)}, u32[]{:S(2)}) collective-permute-start(bf16[1,1,16,512]{3,2,1,0:T(8,128)(2,1)S(1)} %convert_bitcast_fusion), channel_id=1, source_target_pairs={{0,64},{64,128},{128,192},{1,65},{65,129},{129,193},{2,66},{66,130... | collective-permute-start | bytes 49160 | tf_op jit(solution)/shard_map/ppermute | solution.py:15
  140.4 3.6 %collective-permute-start.28 = (bf16[1,1,16,512]{3,2,1,0:T(8,128)(2,1)S(1)}, bf16[1,1,16,512]{3,2,1,0:T(8,128)(2,1)S(1)}, u32[]{:S(2)}, u32[]{:S(2)}) collective-permute-start(bf16[1,1,16,512]{3,2,1,0:T(8,128)(2,1)S(1)} %convert_bitcast_fusion), channel_id=1, source_target_pairs={{64,0},{128,64},{192,128},{65,1},{129,65},{193,129},{66,2},{130,66... | collective-permute-start | bytes 49160 | tf_op jit(solution)/shard_map/ppermute | solution.py:16
  144.1 5.0 %collective-permute-start.29 = (bf16[1,1,16,512]{3,2,1,0:T(8,128)(2,1)S(1)}, bf16[1,1,16,512]{3,2,1,0:T(8,128)(2,1)S(1)}, u32[]{:S(2)}, u32[]{:S(2)}) collective-permute-start(bf16[1,1,16,512]{3,2,1,0:T(8,128)(2,1)S(1)} %convert_bitcast_fusion), channel_id=1, source_target_pairs={{1,0},{2,1},{3,2},{4,3},{5,4},{6,5},{7,6},{8,7},{9,8},{10,9},{11,1... | collective-permute-start | bytes 49160 | tf_op jit(solution)/shard_map/ppermute | solution.py:16
  149.2 1.4 collective-permute-done.29
  150.7 0.3 fusion
  151.1 0.3 fusion.1
  151.4 0.7 reshape.116
  (75 shorter events, 2.3 us)
Async XLA Ops:
  0.0 1.3 copy-start
  0.0 2.7 %copy-start.8 = (s32[1,8,64]{2,1,0:T(8,128)S(1)}, s32[1,8,64]{2,1,0:T(8,128)}, u32[]{:S(2)}) copy-start(s32[1,8,64]{2,1,0:T(8,128)} %param.14) | copy-start | bytes 6148
  0.0 17.5 %copy-start.7 = (f32[1,3,4,512]{3,2,1,0:T(4,128)S(1)}, f32[1,3,4,512]{3,2,1,0:T(4,128)}, u32[]{:S(2)}) copy-start(f32[1,3,4,512]{3,2,1,0:T(4,128)} %param.15) | copy-start | bytes 73732
  1.5 19.5 %copy-start.1 = (bf16[1,3,512,512]{3,2,1,0:T(8,128)(2,1)S(1)}, bf16[1,3,512,512]{3,2,1,0:T(8,128)(2,1)}, u32[]{:S(2)}) copy-start(bf16[1,3,512,512]{3,2,1,0:T(8,128)(2,1)} %param.18) | copy-start | bytes 4718596
  3.1 14.8 %collective-permute-start = (f32[1,1,16,512]{3,2,1,0:T(8,128)S(1)}, f32[1,1,16,512]{3,2,1,0:T(8,128)S(1)}, u32[]{:S(2)}, u32[]{:S(2)}) collective-permute-start(f32[1,1,16,512]{3,2,1,0:T(8,128)S(1)} %broadcast_in_dim_reshape.3), channel_id=1, source_target_pairs={{0,64},{64,128},{128,192},{1,65},{65,129},{129,193},{2,66},{66,130... | collective-permute-start | bytes 98312 | tf_op jit(solution)/shard_map/ppermute | solution.py:15
  6.6 11.4 %collective-permute-start.1 = (f32[1,1,16,512]{3,2,1,0:T(8,128)S(1)}, f32[1,1,16,512]{3,2,1,0:T(8,128)S(1)}, u32[]{:S(2)}, u32[]{:S(2)}) collective-permute-start(f32[1,1,16,512]{3,2,1,0:T(8,128)S(1)} %broadcast_in_dim_reshape.3), channel_id=1, source_target_pairs={{64,0},{128,64},{192,128},{65,1},{129,65},{193,129},{66,2},{130,66... | collective-permute-start | bytes 98312 | tf_op jit(solution)/shard_map/ppermute | solution.py:16
  9.0 9.0 %collective-permute-start.2 = (f32[1,1,16,512]{3,2,1,0:T(8,128)S(1)}, f32[1,1,16,512]{3,2,1,0:T(8,128)S(1)}, u32[]{:S(2)}, u32[]{:S(2)}) collective-permute-start(f32[1,1,16,512]{3,2,1,0:T(8,128)S(1)} %broadcast_in_dim_reshape.3), channel_id=1, source_target_pairs={{0,1},{1,2},{2,3},{3,4},{4,5},{5,6},{6,7},{7,8},{8,9},{9,10},{10,1... | collective-permute-start | bytes 98312 | tf_op jit(solution)/shard_map/ppermute | solution.py:15
  10.9 8.2 %collective-permute-start.3 = (f32[1,1,16,512]{3,2,1,0:T(8,128)S(1)}, f32[1,1,16,512]{3,2,1,0:T(8,128)S(1)}, u32[]{:S(2)}, u32[]{:S(2)}) collective-permute-start(f32[1,1,16,512]{3,2,1,0:T(8,128)S(1)} %broadcast_in_dim_reshape.3), channel_id=1, source_target_pairs={{1,0},{2,1},{3,2},{4,3},{5,4},{6,5},{7,6},{8,7},{9,8},{10,9},{11,1... | collective-permute-start | bytes 98312 | tf_op jit(solution)/shard_map/ppermute | solution.py:16
  19.1 1.8 %collective-permute-start.4 = (bf16[16,512]{1,0:T(8,128)(2,1)S(1)}, bf16[16,512]{1,0:T(8,128)(2,1)S(1)}, u32[]{:S(2)}, u32[]{:S(2)}) collective-permute-start(bf16[16,512]{1,0:T(8,128)(2,1)S(1)} %fusion.107), channel_id=1, source_target_pairs={{0,1},{1,0},{2,3},{3,2},{4,5},{5,4},{6,7},{7,6},{8,9},{9,8},{10,11... | collective-permute-start | bytes 49160 | tf_op jit(solution)/shard_map/ppermute | solution.py:28
  20.9 39.4 %copy-start.6 = (bf16[1,32,512]{2,1,0:T(8,128)(2,1)S(1)}, bf16[1,32,512]{2,1,0:T(8,128)(2,1)}, u32[]{:S(2)}) copy-start(bf16[1,32,512]{2,1,0:T(8,128)(2,1)} %param.20) | copy-start | bytes 98308
  21.1 13.5 %collective-permute-start.5 = (f32[1,1,16,512]{3,2,1,0:T(8,128)S(1)}, f32[1,1,16,512]{3,2,1,0:T(8,128)S(1)}, u32[]{:S(2)}, u32[]{:S(2)}) collective-permute-start(f32[1,1,16,512]{3,2,1,0:T(8,128)S(1)} %bitcast.304), channel_id=1, source_target_pairs={{0,64},{64,128},{128,192},{1,65},{65,129},{129,193},{2,66},{66,130... | collective-permute-start | bytes 98312 | tf_op jit(solution)/shard_map/ppermute | solution.py:15
  24.6 10.1 %collective-permute-start.6 = (f32[1,1,16,512]{3,2,1,0:T(8,128)S(1)}, f32[1,1,16,512]{3,2,1,0:T(8,128)S(1)}, u32[]{:S(2)}, u32[]{:S(2)}) collective-permute-start(f32[1,1,16,512]{3,2,1,0:T(8,128)S(1)} %bitcast.305), channel_id=1, source_target_pairs={{64,0},{128,64},{192,128},{65,1},{129,65},{193,129},{66,2},{130,66... | collective-permute-start | bytes 98312 | tf_op jit(solution)/shard_map/ppermute | solution.py:16
  27.0 7.7 %collective-permute-start.7 = (f32[1,1,16,512]{3,2,1,0:T(8,128)S(1)}, f32[1,1,16,512]{3,2,1,0:T(8,128)S(1)}, u32[]{:S(2)}, u32[]{:S(2)}) collective-permute-start(f32[1,1,16,512]{3,2,1,0:T(8,128)S(1)} %bitcast.306), channel_id=1, source_target_pairs={{0,1},{1,2},{2,3},{3,4},{4,5},{5,6},{6,7},{7,8},{8,9},{9,10},{10,1... | collective-permute-start | bytes 98312 | tf_op jit(solution)/shard_map/ppermute | solution.py:15
  28.9 7.3 %collective-permute-start.8 = (f32[1,1,16,512]{3,2,1,0:T(8,128)S(1)}, f32[1,1,16,512]{3,2,1,0:T(8,128)S(1)}, u32[]{:S(2)}, u32[]{:S(2)}) collective-permute-start(f32[1,1,16,512]{3,2,1,0:T(8,128)S(1)} %bitcast.307), channel_id=1, source_target_pairs={{1,0},{2,1},{3,2},{4,3},{5,4},{6,5},{7,6},{8,7},{9,8},{10,9},{11,1... | collective-permute-start | bytes 98312 | tf_op jit(solution)/shard_map/ppermute | solution.py:16
  36.3 3.8 %collective-permute-start.9 = (bf16[16,512]{1,0:T(8,128)(2,1)S(1)}, bf16[16,512]{1,0:T(8,128)(2,1)S(1)}, u32[]{:S(2)}, u32[]{:S(2)}) collective-permute-start(bf16[16,512]{1,0:T(8,128)(2,1)S(1)} %fusion.102), channel_id=1, source_target_pairs={{0,2},{1,3},{2,0},{3,1},{4,6},{5,7},{6,4},{7,5},{8,10},{9,11},{10,... | collective-permute-start | bytes 49160 | tf_op jit(solution)/shard_map/ppermute | solution.py:28
  40.3 13.5 %collective-permute-start.10 = (f32[1,1,16,512]{3,2,1,0:T(8,128)S(1)}, f32[1,1,16,512]{3,2,1,0:T(8,128)S(1)}, u32[]{:S(2)}, u32[]{:S(2)}) collective-permute-start(f32[1,1,16,512]{3,2,1,0:T(8,128)S(1)} %bitcast.300), channel_id=1, source_target_pairs={{0,64},{64,128},{128,192},{1,65},{65,129},{129,193},{2,66},{66,130... | collective-permute-start | bytes 98312 | tf_op jit(solution)/shard_map/ppermute | solution.py:15
  43.8 10.1 %collective-permute-start.11 = (f32[1,1,16,512]{3,2,1,0:T(8,128)S(1)}, f32[1,1,16,512]{3,2,1,0:T(8,128)S(1)}, u32[]{:S(2)}, u32[]{:S(2)}) collective-permute-start(f32[1,1,16,512]{3,2,1,0:T(8,128)S(1)} %bitcast.301), channel_id=1, source_target_pairs={{64,0},{128,64},{192,128},{65,1},{129,65},{193,129},{66,2},{130,66... | collective-permute-start | bytes 98312 | tf_op jit(solution)/shard_map/ppermute | solution.py:16
  46.1 7.7 %collective-permute-start.12 = (f32[1,1,16,512]{3,2,1,0:T(8,128)S(1)}, f32[1,1,16,512]{3,2,1,0:T(8,128)S(1)}, u32[]{:S(2)}, u32[]{:S(2)}) collective-permute-start(f32[1,1,16,512]{3,2,1,0:T(8,128)S(1)} %bitcast.302), channel_id=1, source_target_pairs={{0,1},{1,2},{2,3},{3,4},{4,5},{5,6},{6,7},{7,8},{8,9},{9,10},{10,1... | collective-permute-start | bytes 98312 | tf_op jit(solution)/shard_map/ppermute | solution.py:15
  48.1 7.3 %collective-permute-start.13 = (f32[1,1,16,512]{3,2,1,0:T(8,128)S(1)}, f32[1,1,16,512]{3,2,1,0:T(8,128)S(1)}, u32[]{:S(2)}, u32[]{:S(2)}) collective-permute-start(f32[1,1,16,512]{3,2,1,0:T(8,128)S(1)} %bitcast.303), channel_id=1, source_target_pairs={{1,0},{2,1},{3,2},{4,3},{5,4},{6,5},{7,6},{8,7},{9,8},{10,9},{11,1... | collective-permute-start | bytes 98312 | tf_op jit(solution)/shard_map/ppermute | solution.py:16
  55.4 4.7 %collective-permute-start.14 = (bf16[16,512]{1,0:T(8,128)(2,1)S(1)}, bf16[16,512]{1,0:T(8,128)(2,1)S(1)}, u32[]{:S(2)}, u32[]{:S(2)}) collective-permute-start(bf16[16,512]{1,0:T(8,128)(2,1)S(1)} %fusion.97), channel_id=1, source_target_pairs={{0,4},{1,5},{2,6},{3,7},{4,0},{5,1},{6,2},{7,3},{8,12},{9,13},{10,... | collective-permute-start | bytes 49160 | tf_op jit(solution)/shard_map/ppermute | solution.py:28
  60.3 15.2 %copy-start.4 = (bf16[1,512,512]{2,1,0:T(8,128)(2,1)S(1)}, bf16[1,512,512]{2,1,0:T(8,128)(2,1)}, u32[]{:S(2)}) copy-start(bf16[1,512,512]{2,1,0:T(8,128)(2,1)} %param.19) | copy-start | bytes 1572868
  64.5 25.2 %all-to-all-start = ((bf16[256,2,256]{2,1,0:T(2,128)(2,1)}), bf16[256,2,256]{2,1,0:T(2,128)(2,1)S(1)}, u32[]{:S(2)}, u32[]{:S(2)}) async-start(bf16[256,2,256]{2,1,0:T(2,128)(2,1)} %reshape.139), calls=%async_computation | async-start | bytes 524288 | tf_op jit(solution)/shard_map/all_to_all | solution.py:33
  91.1 4.9 %copy-start.5 = (bf16[8192,32]{0,1:T(8,128)(2,1)S(1)}, bf16[8192,32]{0,1:T(8,128)(2,1)}, u32[]{:S(2)}) copy-start(bf16[8192,32]{0,1:T(8,128)(2,1)} %param.21) | copy-start | bytes 1572868
  96.4 23.4 %copy-start.2 = (bf16[1,3,512,512]{3,2,1,0:T(8,128)(2,1)S(1)}, bf16[1,3,512,512]{3,2,1,0:T(8,128)(2,1)}, u32[]{:S(2)}) copy-start(bf16[1,3,512,512]{3,2,1,0:T(8,128)(2,1)} %param.17) | copy-start | bytes 4718596
  96.6 4.7 %collective-permute-start.15 = (bf16[16,512]{1,0:T(8,128)(2,1)S(1)}, bf16[16,512]{1,0:T(8,128)(2,1)S(1)}, u32[]{:S(2)}, u32[]{:S(2)}) collective-permute-start(bf16[16,512]{1,0:T(8,128)(2,1)S(1)} %convolution_convert_fusion.4), channel_id=1, source_target_pairs={{0,4},{1,5},{2,6},{3,7},{4,0},{5,1},{6,2},{7,3},{8,12},{9,13},{10,... | collective-permute-start | bytes 49160 | tf_op jit(solution)/shard_map/ppermute | solution.py:28
  101.3 13.9 %collective-permute-start.16 = (bf16[1,1,16,512]{3,2,1,0:T(8,128)(2,1)S(1)}, bf16[1,1,16,512]{3,2,1,0:T(8,128)(2,1)S(1)}, u32[]{:S(2)}, u32[]{:S(2)}) collective-permute-start(bf16[1,1,16,512]{3,2,1,0:T(8,128)(2,1)S(1)} %fusion.111), channel_id=1, source_target_pairs={{0,1},{1,2},{2,3},{3,4},{4,5},{5,6},{6,7},{7,8},{8,9},{9,10},{10,1... | collective-permute-start | bytes 49160 | tf_op jit(solution)/shard_map/ppermute | solution.py:15
  103.2 12.0 %collective-permute-start.17 = (bf16[1,1,16,512]{3,2,1,0:T(8,128)(2,1)S(1)}, bf16[1,1,16,512]{3,2,1,0:T(8,128)(2,1)S(1)}, u32[]{:S(2)}, u32[]{:S(2)}) collective-permute-start(bf16[1,1,16,512]{3,2,1,0:T(8,128)(2,1)S(1)} %fusion.111), channel_id=1, source_target_pairs={{0,64},{64,128},{128,192},{1,65},{65,129},{129,193},{2,66},{66,130... | collective-permute-start | bytes 49160 | tf_op jit(solution)/shard_map/ppermute | solution.py:15
  105.1 10.1 %collective-permute-start.18 = (bf16[1,1,16,512]{3,2,1,0:T(8,128)(2,1)S(1)}, bf16[1,1,16,512]{3,2,1,0:T(8,128)(2,1)S(1)}, u32[]{:S(2)}, u32[]{:S(2)}) collective-permute-start(bf16[1,1,16,512]{3,2,1,0:T(8,128)(2,1)S(1)} %fusion.111), channel_id=1, source_target_pairs={{64,0},{128,64},{192,128},{65,1},{129,65},{193,129},{66,2},{130,66... | collective-permute-start | bytes 49160 | tf_op jit(solution)/shard_map/ppermute | solution.py:16
  109.1 6.6 %collective-permute-start.19 = (bf16[1,1,16,512]{3,2,1,0:T(8,128)(2,1)S(1)}, bf16[1,1,16,512]{3,2,1,0:T(8,128)(2,1)S(1)}, u32[]{:S(2)}, u32[]{:S(2)}) collective-permute-start(bf16[1,1,16,512]{3,2,1,0:T(8,128)(2,1)S(1)} %fusion.111), channel_id=1, source_target_pairs={{1,0},{2,1},{3,2},{4,3},{5,4},{6,5},{7,6},{8,7},{9,8},{10,9},{11,1... | collective-permute-start | bytes 49160 | tf_op jit(solution)/shard_map/ppermute | solution.py:16
  116.0 34.7 %copy-start.3 = (bf16[1,8,64,256]{3,2,1,0:T(8,128)(2,1)S(1)}, bf16[1,8,64,256]{3,2,1,0:T(8,128)(2,1)}, u32[]{:S(2)}) copy-start(bf16[1,8,64,256]{3,2,1,0:T(8,128)(2,1)} %param.13) | copy-start | bytes 786436
  116.0 3.8 %collective-permute-start.20 = (bf16[16,512]{1,0:T(8,128)(2,1)S(1)}, bf16[16,512]{1,0:T(8,128)(2,1)S(1)}, u32[]{:S(2)}, u32[]{:S(2)}) collective-permute-start(bf16[16,512]{1,0:T(8,128)(2,1)S(1)} %convolution_convert_fusion.3), channel_id=1, source_target_pairs={{0,2},{1,3},{2,0},{3,1},{4,6},{5,7},{6,4},{7,5},{8,10},{9,11},{10,... | collective-permute-start | bytes 49160 | tf_op jit(solution)/shard_map/ppermute | solution.py:28
  120.0 13.0 %collective-permute-start.21 = (bf16[1,1,16,512]{3,2,1,0:T(8,128)(2,1)S(1)}, bf16[1,1,16,512]{3,2,1,0:T(8,128)(2,1)S(1)}, u32[]{:S(2)}, u32[]{:S(2)}) collective-permute-start(bf16[1,1,16,512]{3,2,1,0:T(8,128)(2,1)S(1)} %convert_bitcast_fusion.1), channel_id=1, source_target_pairs={{0,1},{1,2},{2,3},{3,4},{4,5},{5,6},{6,7},{7,8},{8,9},{9,10},{10,1... | collective-permute-start | bytes 49160 | tf_op jit(solution)/shard_map/ppermute | solution.py:15
  121.9 11.1 %collective-permute-start.22 = (bf16[1,1,16,512]{3,2,1,0:T(8,128)(2,1)S(1)}, bf16[1,1,16,512]{3,2,1,0:T(8,128)(2,1)S(1)}, u32[]{:S(2)}, u32[]{:S(2)}) collective-permute-start(bf16[1,1,16,512]{3,2,1,0:T(8,128)(2,1)S(1)} %convert_bitcast_fusion.1), channel_id=1, source_target_pairs={{0,64},{64,128},{128,192},{1,65},{65,129},{129,193},{2,66},{66,130... | collective-permute-start | bytes 49160 | tf_op jit(solution)/shard_map/ppermute | solution.py:15
  124.1 8.9 %collective-permute-start.23 = (bf16[1,1,16,512]{3,2,1,0:T(8,128)(2,1)S(1)}, bf16[1,1,16,512]{3,2,1,0:T(8,128)(2,1)S(1)}, u32[]{:S(2)}, u32[]{:S(2)}) collective-permute-start(bf16[1,1,16,512]{3,2,1,0:T(8,128)(2,1)S(1)} %convert_bitcast_fusion.1), channel_id=1, source_target_pairs={{64,0},{128,64},{192,128},{65,1},{129,65},{193,129},{66,2},{130,66... | collective-permute-start | bytes 49160 | tf_op jit(solution)/shard_map/ppermute | solution.py:16
  127.8 6.6 %collective-permute-start.24 = (bf16[1,1,16,512]{3,2,1,0:T(8,128)(2,1)S(1)}, bf16[1,1,16,512]{3,2,1,0:T(8,128)(2,1)S(1)}, u32[]{:S(2)}, u32[]{:S(2)}) collective-permute-start(bf16[1,1,16,512]{3,2,1,0:T(8,128)(2,1)S(1)} %convert_bitcast_fusion.1), channel_id=1, source_target_pairs={{1,0},{2,1},{3,2},{4,3},{5,4},{6,5},{7,6},{8,7},{9,8},{10,9},{11,1... | collective-permute-start | bytes 49160 | tf_op jit(solution)/shard_map/ppermute | solution.py:16
  134.4 16.6 %copy-start.9 = (s32[1,8,64]{2,1,0:T(8,128)S(1)}, s32[1,8,64]{2,1,0:T(8,128)}, u32[]{:S(2)}) copy-start(s32[1,8,64]{2,1,0:T(8,128)} %param.14) | copy-start | bytes 6148
  134.7 1.2 collective-permute-start.25
  136.1 13.0 %collective-permute-start.26 = (bf16[1,1,16,512]{3,2,1,0:T(8,128)(2,1)S(1)}, bf16[1,1,16,512]{3,2,1,0:T(8,128)(2,1)S(1)}, u32[]{:S(2)}, u32[]{:S(2)}) collective-permute-start(bf16[1,1,16,512]{3,2,1,0:T(8,128)(2,1)S(1)} %convert_bitcast_fusion), channel_id=1, source_target_pairs={{0,1},{1,2},{2,3},{3,4},{4,5},{5,6},{6,7},{7,8},{8,9},{9,10},{10,1... | collective-permute-start | bytes 49160 | tf_op jit(solution)/shard_map/ppermute | solution.py:15
  138.2 10.9 %collective-permute-start.27 = (bf16[1,1,16,512]{3,2,1,0:T(8,128)(2,1)S(1)}, bf16[1,1,16,512]{3,2,1,0:T(8,128)(2,1)S(1)}, u32[]{:S(2)}, u32[]{:S(2)}) collective-permute-start(bf16[1,1,16,512]{3,2,1,0:T(8,128)(2,1)S(1)} %convert_bitcast_fusion), channel_id=1, source_target_pairs={{0,64},{64,128},{128,192},{1,65},{65,129},{129,193},{2,66},{66,130... | collective-permute-start | bytes 49160 | tf_op jit(solution)/shard_map/ppermute | solution.py:15
  140.4 8.7 %collective-permute-start.28 = (bf16[1,1,16,512]{3,2,1,0:T(8,128)(2,1)S(1)}, bf16[1,1,16,512]{3,2,1,0:T(8,128)(2,1)S(1)}, u32[]{:S(2)}, u32[]{:S(2)}) collective-permute-start(bf16[1,1,16,512]{3,2,1,0:T(8,128)(2,1)S(1)} %convert_bitcast_fusion), channel_id=1, source_target_pairs={{64,0},{128,64},{192,128},{65,1},{129,65},{193,129},{66,2},{130,66... | collective-permute-start | bytes 49160 | tf_op jit(solution)/shard_map/ppermute | solution.py:16
  144.1 6.5 %collective-permute-start.29 = (bf16[1,1,16,512]{3,2,1,0:T(8,128)(2,1)S(1)}, bf16[1,1,16,512]{3,2,1,0:T(8,128)(2,1)S(1)}, u32[]{:S(2)}, u32[]{:S(2)}) collective-permute-start(bf16[1,1,16,512]{3,2,1,0:T(8,128)(2,1)S(1)} %convert_bitcast_fusion), channel_id=1, source_target_pairs={{1,0},{2,1},{3,2},{4,3},{5,4},{6,5},{7,6},{8,7},{9,8},{10,9},{11,1... | collective-permute-start | bytes 49160 | tf_op jit(solution)/shard_map/ppermute | solution.py:16

commit v3 on v2

--- a/solution.py
+++ b/solution.py
@@ -102,7 +102,12 @@
     top_state = state.astype(jnp.bfloat16)
     comp = compress[0]
     small = right_transpose(top_state, comp).astype(jnp.bfloat16)
-    gathered = collect(small, ("gy", "gx"), 1)
+    slot = lax.axis_index("gy") * lax.axis_size("gx") + lax.axis_index("gx")
+    count = lax.axis_size("gy") * lax.axis_size("gx")
+    spread = jnp.zeros((count,) + small.shape, small.dtype)
+    spread = lax.dynamic_update_index_in_dim(spread, small, slot, 0)
+    summed = lax.psum(spread, ("gy", "gx"))
+    gathered = summed.transpose(1, 0, 2).reshape(small.shape[0], -1)
     coarse = jnp.dot(gathered, top_couple, preferred_element_type=jnp.float32)
     state = jnp.dot(top_state, top_inverse[0], preferred_element_type=jnp.float32)
     state = state + jnp.dot(coarse.astype(jnp.bfloat16), comp, preferred_element_type=jnp.float32)

time: 153 us -> 391 us (2.56)
  waiting for transfers between devices: 34.6 us -> 276 us
  between operations: 0.49 us -> 13.9 us
  starting transfers between devices: 92.6 us -> 80.9 us
  local copies, waits for them, and re-layouts: 14.4 us -> 8.83 us
    psum x0 -> x1, waiting for transfers between devices: none -> 253 us  [body(): summed = lax.psum(spread, ('gy', 'gx'))]
    all_to_all x1 -> x0, waiting for transfers between devices: 13.9 us -> none  [sent_to_all(): return lax.all_to_all(copies, axis, split_axis=0, concat_axis=0, tiled=True)]
    all_to_all x1 -> x0, starting transfers between devices: 11 us -> none  [sent_to_all(): return lax.all_to_all(copies, axis, split_axis=0, concat_axis=0, tiled=True)]
    unnamed x23 -> x19, local copies, waits for them, and re-layouts: 5.67 us -> 1.31 us
  transfers between devices with their start and end apart: 31 -> 31, of which waited for: 12 -> 12; matrix products, arithmetic and copies ran while one was open for 5% -> 2% of each run, Pallas kernels for 0% -> 0%
where the time goes in v3:
time: 391 us; the launch traced here: 390 us
  waiting for transfers between devices  276 us (71%)
  starting transfers between devices  80.9 us (21%)
  between operations  13.9 us (4%)
  matrix products  10.9 us (3%)
  local copies, waits for them, and re-layouts  8.83 us (2%)
    psum x1, waiting for transfers between devices, body(): summed = lax.psum(spread, ('gy', 'gx'))  253 us
    ppermute x12, starting transfers between devices, padded_2(): lax.ppermute(leading, axis, [(b, a) for a, b in up])  48 us
    ppermute x12, starting transfers between devices, padded_2(): lax.ppermute(last, axis, up)  32.3 us
    ppermute x6, waiting for transfers between devices, partner_2(): lax.ppermute(shard, axis, [(i, i ^ 1 << stride) for i in range(lax.axis_s...  13.7 us
    ppermute x12, waiting for transfers between devices, padded_2(): lax.ppermute(leading, axis, [(b, a) for a, b in up])  8.35 us
  transfers between devices with their start and end apart: 31, of which 12 were waited for; matrix products, arithmetic and copies ran while one was open for 2% of the time, Pallas kernels for 0%

profile of v3, /device:TPU:10, one launch (start us, length us, event | category | flops | bytes accessed | tf_op | source)
XLA Modules:
  0.0 390.3 jit_solution(14058796609600300458)
XLA Ops:
  6.5 0.9 copy.28
  7.5 0.3 copy-done
  7.8 0.2 fusion.3
  8.0 1.2 convolution_bitcast_fusion.2
  9.3 0.3 fusion.4
  9.7 3.5 collective-permute-start
  13.2 2.4 collective-permute-start.1
  15.5 1.9 collective-permute-start.2
  17.4 6.6 %collective-permute-start.3 = (f32[1,1,16,512]{3,2,1,0:T(8,128)S(1)}, f32[1,1,16,512]{3,2,1,0:T(8,128)S(1)}, u32[]{:S(2)}, u32[]{:S(2)}) collective-permute-start(f32[1,1,16,512]{3,2,1,0:T(8,128)S(1)} %broadcast_in_dim_reshape.3), channel_id=1, source_target_pairs={{1,0},{2,1},{3,2},{4,3},{5,4},{6,5},{7,6},{8,7},{9,8},{10,9},{11,1... | collective-permute-start | bytes 98312 | tf_op jit(solution)/shard_map/ppermute | solution.py:16
  24.5 1.1 collective-permute-done.3
  26.2 0.1 convert_element_type.115
  26.3 1.2 fusion.26
  27.5 0.2 convolution_add_fusion.5
  27.7 3.5 collective-permute-start.5
  31.2 2.4 collective-permute-start.6
  33.5 1.9 collective-permute-start.7
  35.5 5.8 %collective-permute-start.8 = (f32[1,1,16,512]{3,2,1,0:T(8,128)S(1)}, f32[1,1,16,512]{3,2,1,0:T(8,128)S(1)}, u32[]{:S(2)}, u32[]{:S(2)}) collective-permute-start(f32[1,1,16,512]{3,2,1,0:T(8,128)S(1)} %bitcast.309), channel_id=1, source_target_pairs={{1,0},{2,1},{3,2},{4,3},{5,4},{6,5},{7,6},{8,7},{9,8},{10,9},{11,1... | collective-permute-start | bytes 98312 | tf_op jit(solution)/shard_map/ppermute | solution.py:16
  41.2 1.5 collective-permute-done.8
  42.9 1.2 fusion.21
  44.1 2.5 collective-permute-done.9
  46.6 0.2 convolution_add_fusion.4
  46.8 3.5 collective-permute-start.10
  50.3 2.4 collective-permute-start.11
  52.7 1.9 collective-permute-start.12
  54.6 5.8 %collective-permute-start.13 = (f32[1,1,16,512]{3,2,1,0:T(8,128)S(1)}, f32[1,1,16,512]{3,2,1,0:T(8,128)S(1)}, u32[]{:S(2)}, u32[]{:S(2)}) collective-permute-start(f32[1,1,16,512]{3,2,1,0:T(8,128)S(1)} %bitcast.305), channel_id=1, source_target_pairs={{1,0},{2,1},{3,2},{4,3},{5,4},{6,5},{7,6},{8,7},{9,8},{10,9},{11,1... | collective-permute-start | bytes 98312 | tf_op jit(solution)/shard_map/ppermute | solution.py:16
  60.4 1.5 collective-permute-done.13
  61.9 0.5 collective-permute-start.14
  62.4 1.2 fusion.16
  63.7 3.0 collective-permute-done.14
  66.7 0.2 fusion.6
  66.8 0.1 fusion.7
  67.0 1.2 broadcast_in_dim.18
  68.2 1.4 dynamic_update_slice.4
  69.6 3.1 reshape.114
  72.7 0.2 fusion.10
  72.9 253.4 %all-reduce.8.cloned.1.call-done = bf16[16,8192]{1,0:T(8,128)(2,1)} async-done(((bf16[16,8192]{1,0:T(8,128)(2,1)}), bf16[16,8192]{1,0:T(8,128)(2,1)}) %all-reduce.8.cloned.1.call-update) | async-done | bytes 262160 | tf_op jit(solution)/shard_map/psum | solution.py:109
  326.3 1.5 fusion.5
  327.8 0.2 convolution_convert_fusion.4
  328.0 1.4 fusion.14
  329.5 3.2 collective-permute-done.15
  332.7 1.9 collective-permute-start.16
  334.6 3.4 collective-permute-start.17
  338.0 2.5 collective-permute-start.18
  340.5 5.2 %collective-permute-start.19 = (bf16[1,1,16,512]{3,2,1,0:T(8,128)(2,1)S(1)}, bf16[1,1,16,512]{3,2,1,0:T(8,128)(2,1)S(1)}, u32[]{:S(2)}, u32[]{:S(2)}) collective-permute-start(bf16[1,1,16,512]{3,2,1,0:T(8,128)(2,1)S(1)} %fusion.114), channel_id=1, source_target_pairs={{1,0},{2,1},{3,2},{4,3},{5,4},{6,5},{7,6},{8,7},{9,8},{10,9},{11,1... | collective-permute-start | bytes 49160 | tf_op jit(solution)/shard_map/ppermute | solution.py:16
  345.8 1.4 collective-permute-done.19
  347.2 0.2 convolution_convert_fusion.3
  347.4 3.7 collective-permute-done.20
  351.2 0.2 convolution_add_fusion.2
  351.4 1.9 collective-permute-start.21
  353.3 3.4 collective-permute-start.22
  356.7 2.5 collective-permute-start.23
  359.2 5.2 %collective-permute-start.24 = (bf16[1,1,16,512]{3,2,1,0:T(8,128)(2,1)S(1)}, bf16[1,1,16,512]{3,2,1,0:T(8,128)(2,1)S(1)}, u32[]{:S(2)}, u32[]{:S(2)}) collective-permute-start(bf16[1,1,16,512]{3,2,1,0:T(8,128)(2,1)S(1)} %convert_bitcast_fusion.1), channel_id=1, source_target_pairs={{1,0},{2,1},{3,2},{4,3},{5,4},{6,5},{7,6},{8,7},{9,8},{10,9},{11,1... | collective-permute-start | bytes 49160 | tf_op jit(solution)/shard_map/ppermute | solution.py:16
  364.4 1.4 collective-permute-done.24
  365.9 0.2 convolution_convert_fusion.2
  366.1 1.2 collective-permute-done.25
  367.3 0.2 convolution_add_fusion.1
  367.5 2.1 collective-permute-start.26
  369.6 3.4 collective-permute-start.27
  373.0 2.5 collective-permute-start.28
  375.5 5.0 %collective-permute-start.29 = (bf16[1,1,16,512]{3,2,1,0:T(8,128)(2,1)S(1)}, bf16[1,1,16,512]{3,2,1,0:T(8,128)(2,1)S(1)}, u32[]{:S(2)}, u32[]{:S(2)}) collective-permute-start(bf16[1,1,16,512]{3,2,1,0:T(8,128)(2,1)S(1)} %convert_bitcast_fusion), channel_id=1, source_target_pairs={{1,0},{2,1},{3,2},{4,3},{5,4},{6,5},{7,6},{8,7},{9,8},{10,9},{11,1... | collective-permute-start | bytes 49160 | tf_op jit(solution)/shard_map/ppermute | solution.py:16
  380.6 1.4 collective-permute-done.29
  382.1 0.3 fusion
  382.5 0.3 fusion.1
  382.8 0.7 reshape.116
  (73 shorter events, 1.7 us)
Async XLA Ops:
  6.5 1.3 copy-start
  6.5 2.7 copy-start.8
  6.5 17.5 %copy-start.6 = (f32[1,3,4,512]{3,2,1,0:T(4,128)S(1)}, f32[1,3,4,512]{3,2,1,0:T(4,128)}, u32[]{:S(2)}) copy-start(f32[1,3,4,512]{3,2,1,0:T(4,128)} %param.15) | copy-start | bytes 73732
  6.5 319.8 %all-reduce.8.cloned.1.call-start = ((), (), s32[]{:S(2)}) async-start(), calls=%async_computation | async-start | bytes 524288 | tf_op jit(solution)/shard_map/psum | solution.py:109
  8.0 19.5 %copy-start.1 = (bf16[1,3,512,512]{3,2,1,0:T(8,128)(2,1)S(1)}, bf16[1,3,512,512]{3,2,1,0:T(8,128)(2,1)}, u32[]{:S(2)}) copy-start(bf16[1,3,512,512]{3,2,1,0:T(8,128)(2,1)} %param.18) | copy-start | bytes 4718596
  9.7 14.8 %collective-permute-start = (f32[1,1,16,512]{3,2,1,0:T(8,128)S(1)}, f32[1,1,16,512]{3,2,1,0:T(8,128)S(1)}, u32[]{:S(2)}, u32[]{:S(2)}) collective-permute-start(f32[1,1,16,512]{3,2,1,0:T(8,128)S(1)} %broadcast_in_dim_reshape.3), channel_id=1, source_target_pairs={{0,64},{64,128},{128,192},{1,65},{65,129},{129,193},{2,66},{66,130... | collective-permute-start | bytes 98312 | tf_op jit(solution)/shard_map/ppermute | solution.py:15
  13.2 11.4 %collective-permute-start.1 = (f32[1,1,16,512]{3,2,1,0:T(8,128)S(1)}, f32[1,1,16,512]{3,2,1,0:T(8,128)S(1)}, u32[]{:S(2)}, u32[]{:S(2)}) collective-permute-start(f32[1,1,16,512]{3,2,1,0:T(8,128)S(1)} %broadcast_in_dim_reshape.3), channel_id=1, source_target_pairs={{64,0},{128,64},{192,128},{65,1},{129,65},{193,129},{66,2},{130,66... | collective-permute-start | bytes 98312 | tf_op jit(solution)/shard_map/ppermute | solution.py:16
  15.5 9.0 %collective-permute-start.2 = (f32[1,1,16,512]{3,2,1,0:T(8,128)S(1)}, f32[1,1,16,512]{3,2,1,0:T(8,128)S(1)}, u32[]{:S(2)}, u32[]{:S(2)}) collective-permute-start(f32[1,1,16,512]{3,2,1,0:T(8,128)S(1)} %broadcast_in_dim_reshape.3), channel_id=1, source_target_pairs={{0,1},{1,2},{2,3},{3,4},{4,5},{5,6},{6,7},{7,8},{8,9},{9,10},{10,1... | collective-permute-start | bytes 98312 | tf_op jit(solution)/shard_map/ppermute | solution.py:15
  17.4 8.2 %collective-permute-start.3 = (f32[1,1,16,512]{3,2,1,0:T(8,128)S(1)}, f32[1,1,16,512]{3,2,1,0:T(8,128)S(1)}, u32[]{:S(2)}, u32[]{:S(2)}) collective-permute-start(f32[1,1,16,512]{3,2,1,0:T(8,128)S(1)} %broadcast_in_dim_reshape.3), channel_id=1, source_target_pairs={{1,0},{2,1},{3,2},{4,3},{5,4},{6,5},{7,6},{8,7},{9,8},{10,9},{11,1... | collective-permute-start | bytes 98312 | tf_op jit(solution)/shard_map/ppermute | solution.py:16
  25.7 1.8 collective-permute-start.4
  27.5 39.4 %copy-start.5 = (bf16[1,32,512]{2,1,0:T(8,128)(2,1)S(1)}, bf16[1,32,512]{2,1,0:T(8,128)(2,1)}, u32[]{:S(2)}) copy-start(bf16[1,32,512]{2,1,0:T(8,128)(2,1)} %param.20) | copy-start | bytes 98308
  27.7 13.5 %collective-permute-start.5 = (f32[1,1,16,512]{3,2,1,0:T(8,128)S(1)}, f32[1,1,16,512]{3,2,1,0:T(8,128)S(1)}, u32[]{:S(2)}, u32[]{:S(2)}) collective-permute-start(f32[1,1,16,512]{3,2,1,0:T(8,128)S(1)} %bitcast.306), channel_id=1, source_target_pairs={{0,64},{64,128},{128,192},{1,65},{65,129},{129,193},{2,66},{66,130... | collective-permute-start | bytes 98312 | tf_op jit(solution)/shard_map/ppermute | solution.py:15
  31.2 10.1 %collective-permute-start.6 = (f32[1,1,16,512]{3,2,1,0:T(8,128)S(1)}, f32[1,1,16,512]{3,2,1,0:T(8,128)S(1)}, u32[]{:S(2)}, u32[]{:S(2)}) collective-permute-start(f32[1,1,16,512]{3,2,1,0:T(8,128)S(1)} %bitcast.307), channel_id=1, source_target_pairs={{64,0},{128,64},{192,128},{65,1},{129,65},{193,129},{66,2},{130,66... | collective-permute-start | bytes 98312 | tf_op jit(solution)/shard_map/ppermute | solution.py:16
  33.5 7.7 %collective-permute-start.7 = (f32[1,1,16,512]{3,2,1,0:T(8,128)S(1)}, f32[1,1,16,512]{3,2,1,0:T(8,128)S(1)}, u32[]{:S(2)}, u32[]{:S(2)}) collective-permute-start(f32[1,1,16,512]{3,2,1,0:T(8,128)S(1)} %bitcast.308), channel_id=1, source_target_pairs={{0,1},{1,2},{2,3},{3,4},{4,5},{5,6},{6,7},{7,8},{8,9},{9,10},{10,1... | collective-permute-start | bytes 98312 | tf_op jit(solution)/shard_map/ppermute | solution.py:15
  35.5 7.3 %collective-permute-start.8 = (f32[1,1,16,512]{3,2,1,0:T(8,128)S(1)}, f32[1,1,16,512]{3,2,1,0:T(8,128)S(1)}, u32[]{:S(2)}, u32[]{:S(2)}) collective-permute-start(f32[1,1,16,512]{3,2,1,0:T(8,128)S(1)} %bitcast.309), channel_id=1, source_target_pairs={{1,0},{2,1},{3,2},{4,3},{5,4},{6,5},{7,6},{8,7},{9,8},{10,9},{11,1... | collective-permute-start | bytes 98312 | tf_op jit(solution)/shard_map/ppermute | solution.py:16
  42.8 3.8 collective-permute-start.9
  46.8 13.6 %collective-permute-start.10 = (f32[1,1,16,512]{3,2,1,0:T(8,128)S(1)}, f32[1,1,16,512]{3,2,1,0:T(8,128)S(1)}, u32[]{:S(2)}, u32[]{:S(2)}) collective-permute-start(f32[1,1,16,512]{3,2,1,0:T(8,128)S(1)} %bitcast.302), channel_id=1, source_target_pairs={{0,64},{64,128},{128,192},{1,65},{65,129},{129,193},{2,66},{66,130... | collective-permute-start | bytes 98312 | tf_op jit(solution)/shard_map/ppermute | solution.py:15
  50.3 10.1 %collective-permute-start.11 = (f32[1,1,16,512]{3,2,1,0:T(8,128)S(1)}, f32[1,1,16,512]{3,2,1,0:T(8,128)S(1)}, u32[]{:S(2)}, u32[]{:S(2)}) collective-permute-start(f32[1,1,16,512]{3,2,1,0:T(8,128)S(1)} %bitcast.303), channel_id=1, source_target_pairs={{64,0},{128,64},{192,128},{65,1},{129,65},{193,129},{66,2},{130,66... | collective-permute-start | bytes 98312 | tf_op jit(solution)/shard_map/ppermute | solution.py:16
  52.7 7.7 %collective-permute-start.12 = (f32[1,1,16,512]{3,2,1,0:T(8,128)S(1)}, f32[1,1,16,512]{3,2,1,0:T(8,128)S(1)}, u32[]{:S(2)}, u32[]{:S(2)}) collective-permute-start(f32[1,1,16,512]{3,2,1,0:T(8,128)S(1)} %bitcast.304), channel_id=1, source_target_pairs={{0,1},{1,2},{2,3},{3,4},{4,5},{5,6},{6,7},{7,8},{8,9},{9,10},{10,1... | collective-permute-start | bytes 98312 | tf_op jit(solution)/shard_map/ppermute | solution.py:15
  54.6 7.3 %collective-permute-start.13 = (f32[1,1,16,512]{3,2,1,0:T(8,128)S(1)}, f32[1,1,16,512]{3,2,1,0:T(8,128)S(1)}, u32[]{:S(2)}, u32[]{:S(2)}) collective-permute-start(f32[1,1,16,512]{3,2,1,0:T(8,128)S(1)} %bitcast.305), channel_id=1, source_target_pairs={{1,0},{2,1},{3,2},{4,3},{5,4},{6,5},{7,6},{8,7},{9,8},{10,9},{11,1... | collective-permute-start | bytes 98312 | tf_op jit(solution)/shard_map/ppermute | solution.py:16
  61.9 4.7 %collective-permute-start.14 = (bf16[16,512]{1,0:T(8,128)(2,1)S(1)}, bf16[16,512]{1,0:T(8,128)(2,1)S(1)}, u32[]{:S(2)}, u32[]{:S(2)}) collective-permute-start(bf16[16,512]{1,0:T(8,128)(2,1)S(1)} %fusion.98), channel_id=1, source_target_pairs={{0,4},{1,5},{2,6},{3,7},{4,0},{5,1},{6,2},{7,3},{8,12},{9,13},{10,... | collective-permute-start | bytes 49160 | tf_op jit(solution)/shard_map/ppermute | solution.py:28
  63.7 9.0 %copy-start.4 = (bf16[1,512,512]{2,1,0:T(8,128)(2,1)S(1)}, bf16[1,512,512]{2,1,0:T(8,128)(2,1)}, u32[]{:S(2)}) copy-start(bf16[1,512,512]{2,1,0:T(8,128)(2,1)} %param.19) | copy-start | bytes 1572868
  72.7 273.0 %copy-start.7 = (f32[1,3,4,512]{3,2,1,0:T(4,128)S(1)}, f32[1,3,4,512]{3,2,1,0:T(4,128)}, u32[]{:S(2)}) copy-start(f32[1,3,4,512]{3,2,1,0:T(4,128)} %param.16) | copy-start | bytes 73732
  327.8 23.4 %copy-start.2 = (bf16[1,3,512,512]{3,2,1,0:T(8,128)(2,1)S(1)}, bf16[1,3,512,512]{3,2,1,0:T(8,128)(2,1)}, u32[]{:S(2)}) copy-start(bf16[1,3,512,512]{3,2,1,0:T(8,128)(2,1)} %param.17) | copy-start | bytes 4718596
  328.0 4.7 %collective-permute-start.15 = (bf16[16,512]{1,0:T(8,128)(2,1)S(1)}, bf16[16,512]{1,0:T(8,128)(2,1)S(1)}, u32[]{:S(2)}, u32[]{:S(2)}) collective-permute-start(bf16[16,512]{1,0:T(8,128)(2,1)S(1)} %convolution_convert_fusion.4), channel_id=1, source_target_pairs={{0,4},{1,5},{2,6},{3,7},{4,0},{5,1},{6,2},{7,3},{8,12},{9,13},{10,... | collective-permute-start | bytes 49160 | tf_op jit(solution)/shard_map/ppermute | solution.py:28
  332.7 13.0 %collective-permute-start.16 = (bf16[1,1,16,512]{3,2,1,0:T(8,128)(2,1)S(1)}, bf16[1,1,16,512]{3,2,1,0:T(8,128)(2,1)S(1)}, u32[]{:S(2)}, u32[]{:S(2)}) collective-permute-start(bf16[1,1,16,512]{3,2,1,0:T(8,128)(2,1)S(1)} %fusion.114), channel_id=1, source_target_pairs={{0,1},{1,2},{2,3},{3,4},{4,5},{5,6},{6,7},{7,8},{8,9},{9,10},{10,1... | collective-permute-start | bytes 49160 | tf_op jit(solution)/shard_map/ppermute | solution.py:15
  334.6 11.1 %collective-permute-start.17 = (bf16[1,1,16,512]{3,2,1,0:T(8,128)(2,1)S(1)}, bf16[1,1,16,512]{3,2,1,0:T(8,128)(2,1)S(1)}, u32[]{:S(2)}, u32[]{:S(2)}) collective-permute-start(bf16[1,1,16,512]{3,2,1,0:T(8,128)(2,1)S(1)} %fusion.114), channel_id=1, source_target_pairs={{0,64},{64,128},{128,192},{1,65},{65,129},{129,193},{2,66},{66,130... | collective-permute-start | bytes 49160 | tf_op jit(solution)/shard_map/ppermute | solution.py:15
  338.0 7.7 %collective-permute-start.18 = (bf16[1,1,16,512]{3,2,1,0:T(8,128)(2,1)S(1)}, bf16[1,1,16,512]{3,2,1,0:T(8,128)(2,1)S(1)}, u32[]{:S(2)}, u32[]{:S(2)}) collective-permute-start(bf16[1,1,16,512]{3,2,1,0:T(8,128)(2,1)S(1)} %fusion.114), channel_id=1, source_target_pairs={{64,0},{128,64},{192,128},{65,1},{129,65},{193,129},{66,2},{130,66... | collective-permute-start | bytes 49160 | tf_op jit(solution)/shard_map/ppermute | solution.py:16
  340.5 6.6 %collective-permute-start.19 = (bf16[1,1,16,512]{3,2,1,0:T(8,128)(2,1)S(1)}, bf16[1,1,16,512]{3,2,1,0:T(8,128)(2,1)S(1)}, u32[]{:S(2)}, u32[]{:S(2)}) collective-permute-start(bf16[1,1,16,512]{3,2,1,0:T(8,128)(2,1)S(1)} %fusion.114), channel_id=1, source_target_pairs={{1,0},{2,1},{3,2},{4,3},{5,4},{6,5},{7,6},{8,7},{9,8},{10,9},{11,1... | collective-permute-start | bytes 49160 | tf_op jit(solution)/shard_map/ppermute | solution.py:16
  347.4 34.7 %copy-start.3 = (bf16[1,8,64,256]{3,2,1,0:T(8,128)(2,1)S(1)}, bf16[1,8,64,256]{3,2,1,0:T(8,128)(2,1)}, u32[]{:S(2)}) copy-start(bf16[1,8,64,256]{3,2,1,0:T(8,128)(2,1)} %param.13) | copy-start | bytes 786436
  347.4 3.8 collective-permute-start.20
  351.4 13.0 %collective-permute-start.21 = (bf16[1,1,16,512]{3,2,1,0:T(8,128)(2,1)S(1)}, bf16[1,1,16,512]{3,2,1,0:T(8,128)(2,1)S(1)}, u32[]{:S(2)}, u32[]{:S(2)}) collective-permute-start(bf16[1,1,16,512]{3,2,1,0:T(8,128)(2,1)S(1)} %convert_bitcast_fusion.1), channel_id=1, source_target_pairs={{0,1},{1,2},{2,3},{3,4},{4,5},{5,6},{6,7},{7,8},{8,9},{9,10},{10,1... | collective-permute-start | bytes 49160 | tf_op jit(solution)/shard_map/ppermute | solution.py:15
  353.3 11.1 %collective-permute-start.22 = (bf16[1,1,16,512]{3,2,1,0:T(8,128)(2,1)S(1)}, bf16[1,1,16,512]{3,2,1,0:T(8,128)(2,1)S(1)}, u32[]{:S(2)}, u32[]{:S(2)}) collective-permute-start(bf16[1,1,16,512]{3,2,1,0:T(8,128)(2,1)S(1)} %convert_bitcast_fusion.1), channel_id=1, source_target_pairs={{0,64},{64,128},{128,192},{1,65},{65,129},{129,193},{2,66},{66,130... | collective-permute-start | bytes 49160 | tf_op jit(solution)/shard_map/ppermute | solution.py:15
  356.7 7.7 %collective-permute-start.23 = (bf16[1,1,16,512]{3,2,1,0:T(8,128)(2,1)S(1)}, bf16[1,1,16,512]{3,2,1,0:T(8,128)(2,1)S(1)}, u32[]{:S(2)}, u32[]{:S(2)}) collective-permute-start(bf16[1,1,16,512]{3,2,1,0:T(8,128)(2,1)S(1)} %convert_bitcast_fusion.1), channel_id=1, source_target_pairs={{64,0},{128,64},{192,128},{65,1},{129,65},{193,129},{66,2},{130,66... | collective-permute-start | bytes 49160 | tf_op jit(solution)/shard_map/ppermute | solution.py:16
  359.2 6.6 %collective-permute-start.24 = (bf16[1,1,16,512]{3,2,1,0:T(8,128)(2,1)S(1)}, bf16[1,1,16,512]{3,2,1,0:T(8,128)(2,1)S(1)}, u32[]{:S(2)}, u32[]{:S(2)}) collective-permute-start(bf16[1,1,16,512]{3,2,1,0:T(8,128)(2,1)S(1)} %convert_bitcast_fusion.1), channel_id=1, source_target_pairs={{1,0},{2,1},{3,2},{4,3},{5,4},{6,5},{7,6},{8,7},{9,8},{10,9},{11,1... | collective-permute-start | bytes 49160 | tf_op jit(solution)/shard_map/ppermute | solution.py:16
  366.1 1.2 collective-permute-start.25
  367.5 13.0 %collective-permute-start.26 = (bf16[1,1,16,512]{3,2,1,0:T(8,128)(2,1)S(1)}, bf16[1,1,16,512]{3,2,1,0:T(8,128)(2,1)S(1)}, u32[]{:S(2)}, u32[]{:S(2)}) collective-permute-start(bf16[1,1,16,512]{3,2,1,0:T(8,128)(2,1)S(1)} %convert_bitcast_fusion), channel_id=1, source_target_pairs={{0,1},{1,2},{2,3},{3,4},{4,5},{5,6},{6,7},{7,8},{8,9},{9,10},{10,1... | collective-permute-start | bytes 49160 | tf_op jit(solution)/shard_map/ppermute | solution.py:15
  369.6 10.9 %collective-permute-start.27 = (bf16[1,1,16,512]{3,2,1,0:T(8,128)(2,1)S(1)}, bf16[1,1,16,512]{3,2,1,0:T(8,128)(2,1)S(1)}, u32[]{:S(2)}, u32[]{:S(2)}) collective-permute-start(bf16[1,1,16,512]{3,2,1,0:T(8,128)(2,1)S(1)} %convert_bitcast_fusion), channel_id=1, source_target_pairs={{0,64},{64,128},{128,192},{1,65},{65,129},{129,193},{2,66},{66,130... | collective-permute-start | bytes 49160 | tf_op jit(solution)/shard_map/ppermute | solution.py:15
  373.0 7.5 %collective-permute-start.28 = (bf16[1,1,16,512]{3,2,1,0:T(8,128)(2,1)S(1)}, bf16[1,1,16,512]{3,2,1,0:T(8,128)(2,1)S(1)}, u32[]{:S(2)}, u32[]{:S(2)}) collective-permute-start(bf16[1,1,16,512]{3,2,1,0:T(8,128)(2,1)S(1)} %convert_bitcast_fusion), channel_id=1, source_target_pairs={{64,0},{128,64},{192,128},{65,1},{129,65},{193,129},{66,2},{130,66... | collective-permute-start | bytes 49160 | tf_op jit(solution)/shard_map/ppermute | solution.py:16
  375.5 6.5 %collective-permute-start.29 = (bf16[1,1,16,512]{3,2,1,0:T(8,128)(2,1)S(1)}, bf16[1,1,16,512]{3,2,1,0:T(8,128)(2,1)S(1)}, u32[]{:S(2)}, u32[]{:S(2)}) collective-permute-start(bf16[1,1,16,512]{3,2,1,0:T(8,128)(2,1)S(1)} %convert_bitcast_fusion), channel_id=1, source_target_pairs={{1,0},{2,1},{3,2},{4,3},{5,4},{6,5},{7,6},{8,7},{9,8},{10,9},{11,1... | collective-permute-start | bytes 49160 | tf_op jit(solution)/shard_map/ppermute | solution.py:16
Sparse Core Ops, SparseCore 0:
  72.8 253.4 all-reduce.7

commit v4 on v2

--- a/solution.py
+++ b/solution.py
@@ -92,29 +92,34 @@
     picked = jnp.einsum("fbq,bkq->fbk", blocks, select_half, preferred_element_type=jnp.float32)
     state = picked - jnp.einsum("fbq,bkq->fbk", solved, weights, preferred_element_type=jnp.float32)
     state = state.reshape(field_count, skel_total)
-    for level in range(level_count):
-        padded = padded_2(state[None, None], (("gy", 0), ("gx", 1)), 1)
-        mixed = state - neighbour_mix(padded, up_rates[level])
-        rounded = mixed.astype(jnp.bfloat16)
-        partner = partner_2(rounded, "gx", level)
-        state = jnp.dot(rounded, own[level], preferred_element_type=jnp.float32)
-        state = state + jnp.dot(partner, other[level], preferred_element_type=jnp.float32)
-    top_state = state.astype(jnp.bfloat16)
-    comp = compress[0]
-    small = right_transpose(top_state, comp).astype(jnp.bfloat16)
-    gathered = collect(small, ("gy", "gx"), 1)
-    coarse = jnp.dot(gathered, top_couple, preferred_element_type=jnp.float32)
-    state = jnp.dot(top_state, top_inverse[0], preferred_element_type=jnp.float32)
-    state = state + jnp.dot(coarse.astype(jnp.bfloat16), comp, preferred_element_type=jnp.float32)
-    for level in reversed(range(level_count)):
-        rounded = state.astype(jnp.bfloat16)
-        sent = right_transpose(rounded, other[level])
-        received = partner_2(sent.astype(jnp.bfloat16), "gx", level).astype(sent.dtype)
-        mixed = right_transpose(rounded, own[level]) + received
-        padded = padded_2(mixed[None, None].astype(jnp.bfloat16), (("gy", 0), ("gx", 1)), 1).astype(
-            jnp.float32
-        )
-        state = mixed - neighbour_mix(padded, down_rates[level])
+    def chain(state):
+        for level in range(level_count):
+            padded = padded_2(state[None, None], (("gy", 0), ("gx", 1)), 1)
+            mixed = state - neighbour_mix(padded, up_rates[level])
+            rounded = mixed.astype(jnp.bfloat16)
+            partner = partner_2(rounded, "gx", level)
+            state = jnp.dot(rounded, own[level], preferred_element_type=jnp.float32)
+            state = state + jnp.dot(partner, other[level], preferred_element_type=jnp.float32)
+        top_state = state.astype(jnp.bfloat16)
+        comp = compress[0]
+        small = right_transpose(top_state, comp).astype(jnp.bfloat16)
+        row_values = collect(small, "gx", 1)
+        coarse = jnp.dot(collect(row_values, "gy", 1), top_couple, preferred_element_type=jnp.float32)
+        state = jnp.dot(top_state, top_inverse[0], preferred_element_type=jnp.float32)
+        state = state + jnp.dot(coarse.astype(jnp.bfloat16), comp, preferred_element_type=jnp.float32)
+        for level in reversed(range(level_count)):
+            rounded = state.astype(jnp.bfloat16)
+            sent = right_transpose(rounded, other[level])
+            received = partner_2(sent.astype(jnp.bfloat16), "gx", level).astype(sent.dtype)
+            mixed = right_transpose(rounded, own[level]) + received
+            padded = padded_2(mixed[None, None].astype(jnp.bfloat16), (("gy", 0), ("gx", 1)), 1).astype(
+                jnp.float32
+            )
+            state = mixed - neighbour_mix(padded, down_rates[level])
+        return state
+
+    half = field_count // 2
+    state = jnp.concatenate([chain(state[:half]), chain(state[half:])], axis=0)
     skeleton = state.reshape(field_count, box_count, skel_size)
     back = jnp.einsum(
         "fbk,bkq->fbq", skeleton.astype(jnp.bfloat16), weights, preferred_element_type=jnp.float32

time: 153 us -> 250 us (1.63)
  starting transfers between devices: 92.6 us -> 193 us
  local copies, waits for them, and re-layouts: 14.4 us -> 7.81 us
  matrix products: 9.66 us -> 15.1 us
  waiting for transfers between devices: 34.6 us -> 30.6 us
    ppermute x12 -> x24, starting transfers between devices: 51.8 us -> 95.2 us  [padded_2(): lax.ppermute(leading, axis, [(b, a) for a, b in up])]
    ppermute x12 -> x24, starting transfers between devices: 28.5 us -> 64.7 us  [padded_2(): lax.ppermute(last, axis, up)]
    all_to_all x1 -> x4, starting transfers between devices: 11 us -> 22.7 us  [sent_to_all(): return lax.all_to_all(copies, axis, split_axis=0, concat_axis=0, tiled=True)]
    ppermute x6 -> x12, starting transfers between devices: 1.36 us -> 10.6 us  [partner_2(): lax.ppermute(shard, axis, [(i, i ^ 1 << stride) for i in range(lax.axis_s...]
    ppermute x6 -> x12, waiting for transfers between devices: 13.2 us -> 4.35 us  [partner_2(): lax.ppermute(shard, axis, [(i, i ^ 1 << stride) for i in range(lax.axis_s...]
    all_to_all x1 -> x4, waiting for transfers between devices: 13.9 us -> 19.3 us  [sent_to_all(): return lax.all_to_all(copies, axis, split_axis=0, concat_axis=0, tiled=True)]
    dot_general x8 -> x16, matrix products: 4.67 us -> 7.56 us  [the longest x6 3.22 us: chain(): state = jnp.dot(rounded, own[level], preferred_element_type=jnp.float32)]
    dot_general x7 -> x14, matrix products: 2.61 us -> 5.33 us  [right_transpose(): lax.dot_general(values, matrix, (((1,), (1,)), ((), ())), preferred_eleme...]
  transfers between devices with their start and end apart: 31 -> 64, of which waited for: 12 -> 14; matrix products, arithmetic and copies ran while one was open for 5% -> 7% of each run, Pallas kernels for 0% -> 0%
where the time goes in v4:
time: 250 us; the launch traced here: 248 us
  starting transfers between devices  193 us (77%)
  waiting for transfers between devices  30.6 us (12%)
  matrix products  15.1 us (6%)
  local copies, waits for them, and re-layouts  7.81 us (3%)
    ppermute x24, starting transfers between devices, padded_2(): lax.ppermute(leading, axis, [(b, a) for a, b in up])  95.2 us
    ppermute x24, starting transfers between devices, padded_2(): lax.ppermute(last, axis, up)  64.7 us
    all_to_all x4, starting transfers between devices, sent_to_all(): return lax.all_to_all(copies, axis, split_axis=0, concat_axis=0, tiled=True)  22.7 us
    all_to_all x4, waiting for transfers between devices, sent_to_all(): return lax.all_to_all(copies, axis, split_axis=0, concat_axis=0, tiled=True)  19.3 us
    ppermute x12, starting transfers between devices, partner_2(): lax.ppermute(shard, axis, [(i, i ^ 1 << stride) for i in range(lax.axis_s...  10.6 us
    ppermute x24, waiting for transfers between devices, padded_2(): lax.ppermute(leading, axis, [(b, a) for a, b in up])  6.89 us
    dot_general x14, matrix products, right_transpose(): lax.dot_general(values, matrix, (((1,), (1,)), ((), ())), preferred_eleme...  5.33 us
  transfers between devices with their start and end apart: 64, of which 14 were waited for; matrix products, arithmetic and copies ran while one was open for 7% of the time, Pallas kernels for 0%

profile of v4, /device:TPU:10, one launch (start us, length us, event | category | flops | bytes accessed | tf_op | source)
XLA Modules:
  0.0 248.4 jit_solution(17955028791932314779)
XLA Ops:
  3.0 3.6 %collective-permute-start = (f32[1,1,8,512]{3,2,1,0:T(8,128)S(1)}, f32[1,1,8,512]{3,2,1,0:T(8,128)S(1)}, u32[]{:S(2)}, u32[]{:S(2)}) collective-permute-start(f32[1,1,8,512]{3,2,1,0:T(8,128)S(1)} %broadcast_in_dim.36), channel_id=1, source_target_pairs={{0,64},{64,128},{128,192},{1,65},{65,129},{129,193},{2,66},{66,130... | collective-permute-start | bytes 49160 | tf_op jit(solution)/shard_map/ppermute | solution.py:15
  6.6 2.4 collective-permute-start.1
  9.0 1.9 collective-permute-start.2
  10.9 6.6 %collective-permute-start.3 = (f32[1,1,8,512]{3,2,1,0:T(8,128)S(1)}, f32[1,1,8,512]{3,2,1,0:T(8,128)S(1)}, u32[]{:S(2)}, u32[]{:S(2)}) collective-permute-start(f32[1,1,8,512]{3,2,1,0:T(8,128)S(1)} %broadcast_in_dim.36), channel_id=1, source_target_pairs={{1,0},{2,1},{3,2},{4,3},{5,4},{6,5},{7,6},{8,7},{9,8},{10,9},{11,1... | collective-permute-start | bytes 49160 | tf_op jit(solution)/shard_map/ppermute | solution.py:16
  17.6 3.5 %collective-permute-start.30 = (f32[1,1,8,512]{3,2,1,0:T(8,128)S(1)}, f32[1,1,8,512]{3,2,1,0:T(8,128)S(1)}, u32[]{:S(2)}, u32[]{:S(2)}) collective-permute-start(f32[1,1,8,512]{3,2,1,0:T(8,128)S(1)} %broadcast_in_dim.41), channel_id=1, source_target_pairs={{0,64},{64,128},{128,192},{1,65},{65,129},{129,193},{2,66},{66,130... | collective-permute-start | bytes 49160 | tf_op jit(solution)/shard_map/ppermute | solution.py:15
  21.1 2.4 collective-permute-start.31
  23.5 1.9 collective-permute-start.32
  25.4 5.8 %collective-permute-start.33 = (f32[1,1,8,512]{3,2,1,0:T(8,128)S(1)}, f32[1,1,8,512]{3,2,1,0:T(8,128)S(1)}, u32[]{:S(2)}, u32[]{:S(2)}) collective-permute-start(f32[1,1,8,512]{3,2,1,0:T(8,128)S(1)} %broadcast_in_dim.41), channel_id=1, source_target_pairs={{1,0},{2,1},{3,2},{4,3},{5,4},{6,5},{7,6},{8,7},{9,8},{10,9},{11,1... | collective-permute-start | bytes 49160 | tf_op jit(solution)/shard_map/ppermute | solution.py:16
  34.1 1.3 fusion.42
  36.9 3.6 %collective-permute-start.35 = (f32[1,1,8,512]{3,2,1,0:T(8,128)S(1)}, f32[1,1,8,512]{3,2,1,0:T(8,128)S(1)}, u32[]{:S(2)}, u32[]{:S(2)}) collective-permute-start(f32[1,1,8,512]{3,2,1,0:T(8,128)S(1)} %bitcast.541), channel_id=1, source_target_pairs={{0,64},{64,128},{128,192},{1,65},{65,129},{129,193},{2,66},{66,130... | collective-permute-start | bytes 49160 | tf_op jit(solution)/shard_map/ppermute | solution.py:15
  40.5 2.3 collective-permute-start.36
  42.9 1.9 collective-permute-start.37
  44.8 5.8 %collective-permute-start.38 = (f32[1,1,8,512]{3,2,1,0:T(8,128)S(1)}, f32[1,1,8,512]{3,2,1,0:T(8,128)S(1)}, u32[]{:S(2)}, u32[]{:S(2)}) collective-permute-start(f32[1,1,8,512]{3,2,1,0:T(8,128)S(1)} %bitcast.544), channel_id=1, source_target_pairs={{1,0},{2,1},{3,2},{4,3},{5,4},{6,5},{7,6},{8,7},{9,8},{10,9},{11,1... | collective-permute-start | bytes 49160 | tf_op jit(solution)/shard_map/ppermute | solution.py:16
  50.7 3.5 %collective-permute-start.5 = (f32[1,1,8,512]{3,2,1,0:T(8,128)S(1)}, f32[1,1,8,512]{3,2,1,0:T(8,128)S(1)}, u32[]{:S(2)}, u32[]{:S(2)}) collective-permute-start(f32[1,1,8,512]{3,2,1,0:T(8,128)S(1)} %bitcast.549), channel_id=1, source_target_pairs={{0,64},{64,128},{128,192},{1,65},{65,129},{129,193},{2,66},{66,130... | collective-permute-start | bytes 49160 | tf_op jit(solution)/shard_map/ppermute | solution.py:15
  54.2 2.3 collective-permute-start.6
  56.6 1.9 collective-permute-start.7
  58.5 5.8 %collective-permute-start.8 = (f32[1,1,8,512]{3,2,1,0:T(8,128)S(1)}, f32[1,1,8,512]{3,2,1,0:T(8,128)S(1)}, u32[]{:S(2)}, u32[]{:S(2)}) collective-permute-start(f32[1,1,8,512]{3,2,1,0:T(8,128)S(1)} %bitcast.552), channel_id=1, source_target_pairs={{1,0},{2,1},{3,2},{4,3},{5,4},{6,5},{7,6},{8,7},{9,8},{10,9},{11,1... | collective-permute-start | bytes 49160 | tf_op jit(solution)/shard_map/ppermute | solution.py:16
  64.3 1.4 collective-permute-done.8
  66.0 2.0 collective-permute-start.9
  69.6 3.5 %collective-permute-start.40 = (f32[1,1,8,512]{3,2,1,0:T(8,128)S(1)}, f32[1,1,8,512]{3,2,1,0:T(8,128)S(1)}, u32[]{:S(2)}, u32[]{:S(2)}) collective-permute-start(f32[1,1,8,512]{3,2,1,0:T(8,128)S(1)} %bitcast.537), channel_id=1, source_target_pairs={{0,64},{64,128},{128,192},{1,65},{65,129},{129,193},{2,66},{66,130... | collective-permute-start | bytes 49160 | tf_op jit(solution)/shard_map/ppermute | solution.py:15
  73.2 2.3 collective-permute-start.41
  75.5 1.9 collective-permute-start.42
  77.4 5.8 %collective-permute-start.43 = (f32[1,1,8,512]{3,2,1,0:T(8,128)S(1)}, f32[1,1,8,512]{3,2,1,0:T(8,128)S(1)}, u32[]{:S(2)}, u32[]{:S(2)}) collective-permute-start(f32[1,1,8,512]{3,2,1,0:T(8,128)S(1)} %bitcast.540), channel_id=1, source_target_pairs={{1,0},{2,1},{3,2},{4,3},{5,4},{6,5},{7,6},{8,7},{9,8},{10,9},{11,1... | collective-permute-start | bytes 49160 | tf_op jit(solution)/shard_map/ppermute | solution.py:16
  83.4 3.5 %collective-permute-start.10 = (f32[1,1,8,512]{3,2,1,0:T(8,128)S(1)}, f32[1,1,8,512]{3,2,1,0:T(8,128)S(1)}, u32[]{:S(2)}, u32[]{:S(2)}) collective-permute-start(f32[1,1,8,512]{3,2,1,0:T(8,128)S(1)} %bitcast.545), channel_id=1, source_target_pairs={{0,64},{64,128},{128,192},{1,65},{65,129},{129,193},{2,66},{66,130... | collective-permute-start | bytes 49160 | tf_op jit(solution)/shard_map/ppermute | solution.py:15
  86.9 2.3 collective-permute-start.11
  89.3 1.9 collective-permute-start.12
  91.2 5.8 %collective-permute-start.13 = (f32[1,1,8,512]{3,2,1,0:T(8,128)S(1)}, f32[1,1,8,512]{3,2,1,0:T(8,128)S(1)}, u32[]{:S(2)}, u32[]{:S(2)}) collective-permute-start(f32[1,1,8,512]{3,2,1,0:T(8,128)S(1)} %bitcast.548), channel_id=1, source_target_pairs={{1,0},{2,1},{3,2},{4,3},{5,4},{6,5},{7,6},{8,7},{9,8},{10,9},{11,1... | collective-permute-start | bytes 49160 | tf_op jit(solution)/shard_map/ppermute | solution.py:16
  98.7 2.9 %collective-permute-start.14 = (bf16[8,512]{1,0:T(8,128)(2,1)S(1)}, bf16[8,512]{1,0:T(8,128)(2,1)S(1)}, u32[]{:S(2)}, u32[]{:S(2)}) collective-permute-start(bf16[8,512]{1,0:T(8,128)(2,1)S(1)} %get-tuple-element.43), channel_id=1, source_target_pairs={{0,4},{1,5},{2,6},{3,7},{4,0},{5,1},{6,2},{7,3},{8,12},{9,13},{10,... | collective-permute-start | bytes 24584 | tf_op jit(solution)/shard_map/ppermute | solution.py:28
  104.1 7.5 %all-to-all-start.2 = ((bf16[64,2,128]{2,1,0:T(2,128)(2,1)}), bf16[64,2,128]{2,1,0:T(2,128)(2,1)S(1)}, u32[]{:S(2)}, u32[]{:S(2)}) async-start(bf16[64,2,128]{2,1,0:T(2,128)(2,1)} %reshape.180), calls=%async_computation.2 | async-start | bytes 65536 | tf_op jit(solution)/shard_map/all_to_all | solution.py:33
  112.7 7.5 %all-to-all-done.2 = bf16[64,2,128]{2,1,0:T(2,128)(2,1)S(1)} async-done(((bf16[64,2,128]{2,1,0:T(2,128)(2,1)}), bf16[64,2,128]{2,1,0:T(2,128)(2,1)S(1)}, u32[]{:S(2)}, u32[]{:S(2)}) %all-to-all-start.2) | async-done | bytes 32800 | tf_op jit(solution)/shard_map/all_to_all | solution.py:33
  120.2 5.5 %all-to-all-start = ((bf16[64,2,128]{2,1,0:T(2,128)(2,1)}), bf16[64,2,128]{2,1,0:T(2,128)(2,1)S(1)}, u32[]{:S(2)}, u32[]{:S(2)}) async-start(bf16[64,2,128]{2,1,0:T(2,128)(2,1)} %reshape.182), calls=%async_computation | async-start | bytes 65536 | tf_op jit(solution)/shard_map/all_to_all | solution.py:33
  126.9 7.5 %all-to-all-done = bf16[64,2,128]{2,1,0:T(2,128)(2,1)S(1)} async-done(((bf16[64,2,128]{2,1,0:T(2,128)(2,1)}), bf16[64,2,128]{2,1,0:T(2,128)(2,1)S(1)}, u32[]{:S(2)}, u32[]{:S(2)}) %all-to-all-start) | async-done | bytes 32800 | tf_op jit(solution)/shard_map/all_to_all | solution.py:33
  135.0 4.9 %all-to-all-start.3 = ((bf16[4,8,2048]{2,1,0:T(8,128)(2,1)}), bf16[4,8,2048]{2,1,0:T(8,128)(2,1)}, u32[]{:S(2)}, u32[]{:S(2)}) async-start(bf16[4,8,2048]{2,1,0:T(8,128)(2,1)} %broadcast_in_dim.45), calls=%async_computation.3 | async-start | bytes 262144 | tf_op jit(solution)/shard_map/all_to_all | solution.py:33
  141.0 3.5 %all-to-all-done.3 = bf16[4,8,2048]{2,1,0:T(8,128)(2,1)} async-done(((bf16[4,8,2048]{2,1,0:T(8,128)(2,1)}), bf16[4,8,2048]{2,1,0:T(8,128)(2,1)}, u32[]{:S(2)}, u32[]{:S(2)}) %all-to-all-start.3) | async-done | bytes 131104 | tf_op jit(solution)/shard_map/all_to_all | solution.py:33
  145.2 4.8 %all-to-all-start.1 = ((bf16[4,8,2048]{2,1,0:T(8,128)(2,1)}), bf16[4,8,2048]{2,1,0:T(8,128)(2,1)S(1)}, u32[]{:S(2)}, u32[]{:S(2)}) async-start(bf16[4,8,2048]{2,1,0:T(8,128)(2,1)} %broadcast_in_dim.40), calls=%async_computation.1 | async-start | bytes 262144 | tf_op jit(solution)/shard_map/all_to_all | solution.py:33
  150.0 1.4 fusion.6
  154.8 1.4 fusion.23
  156.5 1.4 collective-permute-start.15
  158.0 1.9 collective-permute-start.46
  159.9 3.4 %collective-permute-start.47 = (bf16[1,1,8,512]{3,2,1,0:T(8,128)(2,1)S(1)}, bf16[1,1,8,512]{3,2,1,0:T(8,128)(2,1)S(1)}, u32[]{:S(2)}, u32[]{:S(2)}) collective-permute-start(bf16[1,1,8,512]{3,2,1,0:T(8,128)(2,1)S(1)} %fusion.207), channel_id=1, source_target_pairs={{0,64},{64,128},{128,192},{1,65},{65,129},{129,193},{2,66},{66,130... | collective-permute-start | bytes 24584 | tf_op jit(solution)/shard_map/ppermute | solution.py:15
  163.3 2.5 collective-permute-start.48
  165.8 5.2 %collective-permute-start.49 = (bf16[1,1,8,512]{3,2,1,0:T(8,128)(2,1)S(1)}, bf16[1,1,8,512]{3,2,1,0:T(8,128)(2,1)S(1)}, u32[]{:S(2)}, u32[]{:S(2)}) collective-permute-start(bf16[1,1,8,512]{3,2,1,0:T(8,128)(2,1)S(1)} %fusion.207), channel_id=1, source_target_pairs={{1,0},{2,1},{3,2},{4,3},{5,4},{6,5},{7,6},{8,7},{9,8},{10,9},{11,1... | collective-permute-start | bytes 24584 | tf_op jit(solution)/shard_map/ppermute | solution.py:16
  171.0 1.9 collective-permute-start.16
  173.0 3.4 %collective-permute-start.17 = (bf16[1,1,8,512]{3,2,1,0:T(8,128)(2,1)S(1)}, bf16[1,1,8,512]{3,2,1,0:T(8,128)(2,1)S(1)}, u32[]{:S(2)}, u32[]{:S(2)}) collective-permute-start(bf16[1,1,8,512]{3,2,1,0:T(8,128)(2,1)S(1)} %fusion.208), channel_id=1, source_target_pairs={{0,64},{64,128},{128,192},{1,65},{65,129},{129,193},{2,66},{66,130... | collective-permute-start | bytes 24584 | tf_op jit(solution)/shard_map/ppermute | solution.py:15
  176.4 2.5 collective-permute-start.18
  178.8 5.2 %collective-permute-start.19 = (bf16[1,1,8,512]{3,2,1,0:T(8,128)(2,1)S(1)}, bf16[1,1,8,512]{3,2,1,0:T(8,128)(2,1)S(1)}, u32[]{:S(2)}, u32[]{:S(2)}) collective-permute-start(bf16[1,1,8,512]{3,2,1,0:T(8,128)(2,1)S(1)} %fusion.208), channel_id=1, source_target_pairs={{1,0},{2,1},{3,2},{4,3},{5,4},{6,5},{7,6},{8,7},{9,8},{10,9},{11,1... | collective-permute-start | bytes 24584 | tf_op jit(solution)/shard_map/ppermute | solution.py:16
  186.1 2.0 collective-permute-start.20
  188.1 1.4 collective-permute-done.50
  189.8 1.9 collective-permute-start.51
  191.7 3.4 %collective-permute-start.52 = (bf16[1,1,8,512]{3,2,1,0:T(8,128)(2,1)S(1)}, bf16[1,1,8,512]{3,2,1,0:T(8,128)(2,1)S(1)}, u32[]{:S(2)}, u32[]{:S(2)}) collective-permute-start(bf16[1,1,8,512]{3,2,1,0:T(8,128)(2,1)S(1)} %convert_bitcast_fusion.1), channel_id=1, source_target_pairs={{0,64},{64,128},{128,192},{1,65},{65,129},{129,193},{2,66},{66,130... | collective-permute-start | bytes 24584 | tf_op jit(solution)/shard_map/ppermute | solution.py:15
  195.1 2.5 collective-permute-start.53
  197.5 5.2 %collective-permute-start.54 = (bf16[1,1,8,512]{3,2,1,0:T(8,128)(2,1)S(1)}, bf16[1,1,8,512]{3,2,1,0:T(8,128)(2,1)S(1)}, u32[]{:S(2)}, u32[]{:S(2)}) collective-permute-start(bf16[1,1,8,512]{3,2,1,0:T(8,128)(2,1)S(1)} %convert_bitcast_fusion.1), channel_id=1, source_target_pairs={{1,0},{2,1},{3,2},{4,3},{5,4},{6,5},{7,6},{8,7},{9,8},{10,9},{11,1... | collective-permute-start | bytes 24584 | tf_op jit(solution)/shard_map/ppermute | solution.py:16
  203.0 1.9 collective-permute-start.21
  205.0 3.4 %collective-permute-start.22 = (bf16[1,1,8,512]{3,2,1,0:T(8,128)(2,1)S(1)}, bf16[1,1,8,512]{3,2,1,0:T(8,128)(2,1)S(1)}, u32[]{:S(2)}, u32[]{:S(2)}) collective-permute-start(bf16[1,1,8,512]{3,2,1,0:T(8,128)(2,1)S(1)} %convert_bitcast_fusion.3), channel_id=1, source_target_pairs={{0,64},{64,128},{128,192},{1,65},{65,129},{129,193},{2,66},{66,130... | collective-permute-start | bytes 24584 | tf_op jit(solution)/shard_map/ppermute | solution.py:15
  208.4 2.5 collective-permute-start.23
  210.9 5.2 %collective-permute-start.24 = (bf16[1,1,8,512]{3,2,1,0:T(8,128)(2,1)S(1)}, bf16[1,1,8,512]{3,2,1,0:T(8,128)(2,1)S(1)}, u32[]{:S(2)}, u32[]{:S(2)}) collective-permute-start(bf16[1,1,8,512]{3,2,1,0:T(8,128)(2,1)S(1)} %convert_bitcast_fusion.3), channel_id=1, source_target_pairs={{1,0},{2,1},{3,2},{4,3},{5,4},{6,5},{7,6},{8,7},{9,8},{10,9},{11,1... | collective-permute-start | bytes 24584 | tf_op jit(solution)/shard_map/ppermute | solution.py:16
  219.2 2.1 collective-permute-start.56
  221.2 3.4 %collective-permute-start.57 = (bf16[1,1,8,512]{3,2,1,0:T(8,128)(2,1)S(1)}, bf16[1,1,8,512]{3,2,1,0:T(8,128)(2,1)S(1)}, u32[]{:S(2)}, u32[]{:S(2)}) collective-permute-start(bf16[1,1,8,512]{3,2,1,0:T(8,128)(2,1)S(1)} %convert_bitcast_fusion), channel_id=1, source_target_pairs={{0,64},{64,128},{128,192},{1,65},{65,129},{129,193},{2,66},{66,130... | collective-permute-start | bytes 24584 | tf_op jit(solution)/shard_map/ppermute | solution.py:15
  224.6 2.4 collective-permute-start.58
  227.1 5.0 %collective-permute-start.59 = (bf16[1,1,8,512]{3,2,1,0:T(8,128)(2,1)S(1)}, bf16[1,1,8,512]{3,2,1,0:T(8,128)(2,1)S(1)}, u32[]{:S(2)}, u32[]{:S(2)}) collective-permute-start(bf16[1,1,8,512]{3,2,1,0:T(8,128)(2,1)S(1)} %convert_bitcast_fusion), channel_id=1, source_target_pairs={{1,0},{2,1},{3,2},{4,3},{5,4},{6,5},{7,6},{8,7},{9,8},{10,9},{11,1... | collective-permute-start | bytes 24584 | tf_op jit(solution)/shard_map/ppermute | solution.py:16
  232.4 1.9 collective-permute-start.26
  234.3 3.4 %collective-permute-start.27 = (bf16[1,1,8,512]{3,2,1,0:T(8,128)(2,1)S(1)}, bf16[1,1,8,512]{3,2,1,0:T(8,128)(2,1)S(1)}, u32[]{:S(2)}, u32[]{:S(2)}) collective-permute-start(bf16[1,1,8,512]{3,2,1,0:T(8,128)(2,1)S(1)} %convert_bitcast_fusion.2), channel_id=1, source_target_pairs={{0,64},{64,128},{128,192},{1,65},{65,129},{129,193},{2,66},{66,130... | collective-permute-start | bytes 24584 | tf_op jit(solution)/shard_map/ppermute | solution.py:15
  237.8 2.4 collective-permute-start.28
  240.2 5.2 %collective-permute-start.29 = (bf16[1,1,8,512]{3,2,1,0:T(8,128)(2,1)S(1)}, bf16[1,1,8,512]{3,2,1,0:T(8,128)(2,1)S(1)}, u32[]{:S(2)}, u32[]{:S(2)}) collective-permute-start(bf16[1,1,8,512]{3,2,1,0:T(8,128)(2,1)S(1)} %convert_bitcast_fusion.2), channel_id=1, source_target_pairs={{1,0},{2,1},{3,2},{4,3},{5,4},{6,5},{7,6},{8,7},{9,8},{10,9},{11,1... | collective-permute-start | bytes 24584 | tf_op jit(solution)/shard_map/ppermute | solution.py:16
  (210 shorter events, 30.7 us)
Async XLA Ops:
  3.0 18.1 %collective-permute-start = (f32[1,1,8,512]{3,2,1,0:T(8,128)S(1)}, f32[1,1,8,512]{3,2,1,0:T(8,128)S(1)}, u32[]{:S(2)}, u32[]{:S(2)}) collective-permute-start(f32[1,1,8,512]{3,2,1,0:T(8,128)S(1)} %broadcast_in_dim.36), channel_id=1, source_target_pairs={{0,64},{64,128},{128,192},{1,65},{65,129},{129,193},{2,66},{66,130... | collective-permute-start | bytes 49160 | tf_op jit(solution)/shard_map/ppermute | solution.py:15
  6.6 16.9 %collective-permute-start.1 = (f32[1,1,8,512]{3,2,1,0:T(8,128)S(1)}, f32[1,1,8,512]{3,2,1,0:T(8,128)S(1)}, u32[]{:S(2)}, u32[]{:S(2)}) collective-permute-start(f32[1,1,8,512]{3,2,1,0:T(8,128)S(1)} %broadcast_in_dim.36), channel_id=1, source_target_pairs={{64,0},{128,64},{192,128},{65,1},{129,65},{193,129},{66,2},{130,66... | collective-permute-start | bytes 49160 | tf_op jit(solution)/shard_map/ppermute | solution.py:16
  9.0 16.4 %collective-permute-start.2 = (f32[1,1,8,512]{3,2,1,0:T(8,128)S(1)}, f32[1,1,8,512]{3,2,1,0:T(8,128)S(1)}, u32[]{:S(2)}, u32[]{:S(2)}) collective-permute-start(f32[1,1,8,512]{3,2,1,0:T(8,128)S(1)} %broadcast_in_dim.36), channel_id=1, source_target_pairs={{0,1},{1,2},{2,3},{3,4},{4,5},{5,6},{6,7},{7,8},{8,9},{9,10},{10,1... | collective-permute-start | bytes 49160 | tf_op jit(solution)/shard_map/ppermute | solution.py:15
  10.9 20.8 %collective-permute-start.3 = (f32[1,1,8,512]{3,2,1,0:T(8,128)S(1)}, f32[1,1,8,512]{3,2,1,0:T(8,128)S(1)}, u32[]{:S(2)}, u32[]{:S(2)}) collective-permute-start(f32[1,1,8,512]{3,2,1,0:T(8,128)S(1)} %broadcast_in_dim.36), channel_id=1, source_target_pairs={{1,0},{2,1},{3,2},{4,3},{5,4},{6,5},{7,6},{8,7},{9,8},{10,9},{11,1... | collective-permute-start | bytes 49160 | tf_op jit(solution)/shard_map/ppermute | solution.py:16
  17.6 14.1 %collective-permute-start.30 = (f32[1,1,8,512]{3,2,1,0:T(8,128)S(1)}, f32[1,1,8,512]{3,2,1,0:T(8,128)S(1)}, u32[]{:S(2)}, u32[]{:S(2)}) collective-permute-start(f32[1,1,8,512]{3,2,1,0:T(8,128)S(1)} %broadcast_in_dim.41), channel_id=1, source_target_pairs={{0,64},{64,128},{128,192},{1,65},{65,129},{129,193},{2,66},{66,130... | collective-permute-start | bytes 49160 | tf_op jit(solution)/shard_map/ppermute | solution.py:15
  21.1 10.6 %collective-permute-start.31 = (f32[1,1,8,512]{3,2,1,0:T(8,128)S(1)}, f32[1,1,8,512]{3,2,1,0:T(8,128)S(1)}, u32[]{:S(2)}, u32[]{:S(2)}) collective-permute-start(f32[1,1,8,512]{3,2,1,0:T(8,128)S(1)} %broadcast_in_dim.41), channel_id=1, source_target_pairs={{64,0},{128,64},{192,128},{65,1},{129,65},{193,129},{66,2},{130,66... | collective-permute-start | bytes 49160 | tf_op jit(solution)/shard_map/ppermute | solution.py:16
  23.5 8.2 %collective-permute-start.32 = (f32[1,1,8,512]{3,2,1,0:T(8,128)S(1)}, f32[1,1,8,512]{3,2,1,0:T(8,128)S(1)}, u32[]{:S(2)}, u32[]{:S(2)}) collective-permute-start(f32[1,1,8,512]{3,2,1,0:T(8,128)S(1)} %broadcast_in_dim.41), channel_id=1, source_target_pairs={{0,1},{1,2},{2,3},{3,4},{4,5},{5,6},{6,7},{7,8},{8,9},{9,10},{10,1... | collective-permute-start | bytes 49160 | tf_op jit(solution)/shard_map/ppermute | solution.py:15
  25.4 7.2 %collective-permute-start.33 = (f32[1,1,8,512]{3,2,1,0:T(8,128)S(1)}, f32[1,1,8,512]{3,2,1,0:T(8,128)S(1)}, u32[]{:S(2)}, u32[]{:S(2)}) collective-permute-start(f32[1,1,8,512]{3,2,1,0:T(8,128)S(1)} %broadcast_in_dim.41), channel_id=1, source_target_pairs={{1,0},{2,1},{3,2},{4,3},{5,4},{6,5},{7,6},{8,7},{9,8},{10,9},{11,1... | collective-permute-start | bytes 49160 | tf_op jit(solution)/shard_map/ppermute | solution.py:16
  32.6 4.0 %collective-permute-start.34 = (bf16[8,512]{1,0:T(8,128)(2,1)S(1)}, bf16[8,512]{1,0:T(8,128)(2,1)S(1)}, u32[]{:S(2)}, u32[]{:S(2)}) collective-permute-start(bf16[8,512]{1,0:T(8,128)(2,1)S(1)} %get-tuple-element.48), channel_id=1, source_target_pairs={{0,1},{1,0},{2,3},{3,2},{4,5},{5,4},{6,7},{7,6},{8,9},{9,8},{10,11... | collective-permute-start | bytes 24584 | tf_op jit(solution)/shard_map/ppermute | solution.py:28
  33.5 17.0 %collective-permute-start.4 = (bf16[8,512]{1,0:T(8,128)(2,1)S(1)}, bf16[8,512]{1,0:T(8,128)(2,1)S(1)}, u32[]{:S(2)}, u32[]{:S(2)}) collective-permute-start(bf16[8,512]{1,0:T(8,128)(2,1)S(1)} %get-tuple-element.47), channel_id=1, source_target_pairs={{0,1},{1,0},{2,3},{3,2},{4,5},{5,4},{6,7},{7,6},{8,9},{9,8},{10,11... | collective-permute-start | bytes 24584 | tf_op jit(solution)/shard_map/ppermute | solution.py:28
  36.9 17.4 %collective-permute-start.35 = (f32[1,1,8,512]{3,2,1,0:T(8,128)S(1)}, f32[1,1,8,512]{3,2,1,0:T(8,128)S(1)}, u32[]{:S(2)}, u32[]{:S(2)}) collective-permute-start(f32[1,1,8,512]{3,2,1,0:T(8,128)S(1)} %bitcast.541), channel_id=1, source_target_pairs={{0,64},{64,128},{128,192},{1,65},{65,129},{129,193},{2,66},{66,130... | collective-permute-start | bytes 49160 | tf_op jit(solution)/shard_map/ppermute | solution.py:15
  40.5 16.1 %collective-permute-start.36 = (f32[1,1,8,512]{3,2,1,0:T(8,128)S(1)}, f32[1,1,8,512]{3,2,1,0:T(8,128)S(1)}, u32[]{:S(2)}, u32[]{:S(2)}) collective-permute-start(f32[1,1,8,512]{3,2,1,0:T(8,128)S(1)} %bitcast.542), channel_id=1, source_target_pairs={{64,0},{128,64},{192,128},{65,1},{129,65},{193,129},{66,2},{130,66... | collective-permute-start | bytes 49160 | tf_op jit(solution)/shard_map/ppermute | solution.py:16
  42.9 15.7 %collective-permute-start.37 = (f32[1,1,8,512]{3,2,1,0:T(8,128)S(1)}, f32[1,1,8,512]{3,2,1,0:T(8,128)S(1)}, u32[]{:S(2)}, u32[]{:S(2)}) collective-permute-start(f32[1,1,8,512]{3,2,1,0:T(8,128)S(1)} %bitcast.543), channel_id=1, source_target_pairs={{0,1},{1,2},{2,3},{3,4},{4,5},{5,6},{6,7},{7,8},{8,9},{9,10},{10,1... | collective-permute-start | bytes 49160 | tf_op jit(solution)/shard_map/ppermute | solution.py:15
  44.8 19.5 %collective-permute-start.38 = (f32[1,1,8,512]{3,2,1,0:T(8,128)S(1)}, f32[1,1,8,512]{3,2,1,0:T(8,128)S(1)}, u32[]{:S(2)}, u32[]{:S(2)}) collective-permute-start(f32[1,1,8,512]{3,2,1,0:T(8,128)S(1)} %bitcast.544), channel_id=1, source_target_pairs={{1,0},{2,1},{3,2},{4,3},{5,4},{6,5},{7,6},{8,7},{9,8},{10,9},{11,1... | collective-permute-start | bytes 49160 | tf_op jit(solution)/shard_map/ppermute | solution.py:16
  50.7 13.6 %collective-permute-start.5 = (f32[1,1,8,512]{3,2,1,0:T(8,128)S(1)}, f32[1,1,8,512]{3,2,1,0:T(8,128)S(1)}, u32[]{:S(2)}, u32[]{:S(2)}) collective-permute-start(f32[1,1,8,512]{3,2,1,0:T(8,128)S(1)} %bitcast.549), channel_id=1, source_target_pairs={{0,64},{64,128},{128,192},{1,65},{65,129},{129,193},{2,66},{66,130... | collective-permute-start | bytes 49160 | tf_op jit(solution)/shard_map/ppermute | solution.py:15
  54.2 10.1 %collective-permute-start.6 = (f32[1,1,8,512]{3,2,1,0:T(8,128)S(1)}, f32[1,1,8,512]{3,2,1,0:T(8,128)S(1)}, u32[]{:S(2)}, u32[]{:S(2)}) collective-permute-start(f32[1,1,8,512]{3,2,1,0:T(8,128)S(1)} %bitcast.550), channel_id=1, source_target_pairs={{64,0},{128,64},{192,128},{65,1},{129,65},{193,129},{66,2},{130,66... | collective-permute-start | bytes 49160 | tf_op jit(solution)/shard_map/ppermute | solution.py:16
  56.6 7.7 %collective-permute-start.7 = (f32[1,1,8,512]{3,2,1,0:T(8,128)S(1)}, f32[1,1,8,512]{3,2,1,0:T(8,128)S(1)}, u32[]{:S(2)}, u32[]{:S(2)}) collective-permute-start(f32[1,1,8,512]{3,2,1,0:T(8,128)S(1)} %bitcast.551), channel_id=1, source_target_pairs={{0,1},{1,2},{2,3},{3,4},{4,5},{5,6},{6,7},{7,8},{8,9},{9,10},{10,1... | collective-permute-start | bytes 49160 | tf_op jit(solution)/shard_map/ppermute | solution.py:15
  58.5 7.2 %collective-permute-start.8 = (f32[1,1,8,512]{3,2,1,0:T(8,128)S(1)}, f32[1,1,8,512]{3,2,1,0:T(8,128)S(1)}, u32[]{:S(2)}, u32[]{:S(2)}) collective-permute-start(f32[1,1,8,512]{3,2,1,0:T(8,128)S(1)} %bitcast.552), channel_id=1, source_target_pairs={{1,0},{2,1},{3,2},{4,3},{5,4},{6,5},{7,6},{8,7},{9,8},{10,9},{11,1... | collective-permute-start | bytes 49160 | tf_op jit(solution)/shard_map/ppermute | solution.py:16
  65.7 3.7 %collective-permute-start.39 = (bf16[8,512]{1,0:T(8,128)(2,1)S(1)}, bf16[8,512]{1,0:T(8,128)(2,1)S(1)}, u32[]{:S(2)}, u32[]{:S(2)}) collective-permute-start(bf16[8,512]{1,0:T(8,128)(2,1)S(1)} %get-tuple-element.46), channel_id=1, source_target_pairs={{0,2},{1,3},{2,0},{3,1},{4,6},{5,7},{6,4},{7,5},{8,10},{9,11},{10,... | collective-permute-start | bytes 24584 | tf_op jit(solution)/shard_map/ppermute | solution.py:28
  66.0 17.2 %collective-permute-start.9 = (bf16[8,512]{1,0:T(8,128)(2,1)S(1)}, bf16[8,512]{1,0:T(8,128)(2,1)S(1)}, u32[]{:S(2)}, u32[]{:S(2)}) collective-permute-start(bf16[8,512]{1,0:T(8,128)(2,1)S(1)} %get-tuple-element.45), channel_id=1, source_target_pairs={{0,2},{1,3},{2,0},{3,1},{4,6},{5,7},{6,4},{7,5},{8,10},{9,11},{10,... | collective-permute-start | bytes 24584 | tf_op jit(solution)/shard_map/ppermute | solution.py:28
  69.6 17.2 %collective-permute-start.40 = (f32[1,1,8,512]{3,2,1,0:T(8,128)S(1)}, f32[1,1,8,512]{3,2,1,0:T(8,128)S(1)}, u32[]{:S(2)}, u32[]{:S(2)}) collective-permute-start(f32[1,1,8,512]{3,2,1,0:T(8,128)S(1)} %bitcast.537), channel_id=1, source_target_pairs={{0,64},{64,128},{128,192},{1,65},{65,129},{129,193},{2,66},{66,130... | collective-permute-start | bytes 49160 | tf_op jit(solution)/shard_map/ppermute | solution.py:15
  73.2 16.1 %collective-permute-start.41 = (f32[1,1,8,512]{3,2,1,0:T(8,128)S(1)}, f32[1,1,8,512]{3,2,1,0:T(8,128)S(1)}, u32[]{:S(2)}, u32[]{:S(2)}) collective-permute-start(f32[1,1,8,512]{3,2,1,0:T(8,128)S(1)} %bitcast.538), channel_id=1, source_target_pairs={{64,0},{128,64},{192,128},{65,1},{129,65},{193,129},{66,2},{130,66... | collective-permute-start | bytes 49160 | tf_op jit(solution)/shard_map/ppermute | solution.py:16
  75.5 15.7 %collective-permute-start.42 = (f32[1,1,8,512]{3,2,1,0:T(8,128)S(1)}, f32[1,1,8,512]{3,2,1,0:T(8,128)S(1)}, u32[]{:S(2)}, u32[]{:S(2)}) collective-permute-start(f32[1,1,8,512]{3,2,1,0:T(8,128)S(1)} %bitcast.539), channel_id=1, source_target_pairs={{0,1},{1,2},{2,3},{3,4},{4,5},{5,6},{6,7},{7,8},{8,9},{9,10},{10,1... | collective-permute-start | bytes 49160 | tf_op jit(solution)/shard_map/ppermute | solution.py:15
  77.4 20.2 %collective-permute-start.43 = (f32[1,1,8,512]{3,2,1,0:T(8,128)S(1)}, f32[1,1,8,512]{3,2,1,0:T(8,128)S(1)}, u32[]{:S(2)}, u32[]{:S(2)}) collective-permute-start(f32[1,1,8,512]{3,2,1,0:T(8,128)S(1)} %bitcast.540), channel_id=1, source_target_pairs={{1,0},{2,1},{3,2},{4,3},{5,4},{6,5},{7,6},{8,7},{9,8},{10,9},{11,1... | collective-permute-start | bytes 49160 | tf_op jit(solution)/shard_map/ppermute | solution.py:16
  83.4 14.2 %collective-permute-start.10 = (f32[1,1,8,512]{3,2,1,0:T(8,128)S(1)}, f32[1,1,8,512]{3,2,1,0:T(8,128)S(1)}, u32[]{:S(2)}, u32[]{:S(2)}) collective-permute-start(f32[1,1,8,512]{3,2,1,0:T(8,128)S(1)} %bitcast.545), channel_id=1, source_target_pairs={{0,64},{64,128},{128,192},{1,65},{65,129},{129,193},{2,66},{66,130... | collective-permute-start | bytes 49160 | tf_op jit(solution)/shard_map/ppermute | solution.py:15
  86.9 10.7 %collective-permute-start.11 = (f32[1,1,8,512]{3,2,1,0:T(8,128)S(1)}, f32[1,1,8,512]{3,2,1,0:T(8,128)S(1)}, u32[]{:S(2)}, u32[]{:S(2)}) collective-permute-start(f32[1,1,8,512]{3,2,1,0:T(8,128)S(1)} %bitcast.546), channel_id=1, source_target_pairs={{64,0},{128,64},{192,128},{65,1},{129,65},{193,129},{66,2},{130,66... | collective-permute-start | bytes 49160 | tf_op jit(solution)/shard_map/ppermute | solution.py:16
  89.3 8.4 %collective-permute-start.12 = (f32[1,1,8,512]{3,2,1,0:T(8,128)S(1)}, f32[1,1,8,512]{3,2,1,0:T(8,128)S(1)}, u32[]{:S(2)}, u32[]{:S(2)}) collective-permute-start(f32[1,1,8,512]{3,2,1,0:T(8,128)S(1)} %bitcast.547), channel_id=1, source_target_pairs={{0,1},{1,2},{2,3},{3,4},{4,5},{5,6},{6,7},{7,8},{8,9},{9,10},{10,1... | collective-permute-start | bytes 49160 | tf_op jit(solution)/shard_map/ppermute | solution.py:15
  91.2 7.2 %collective-permute-start.13 = (f32[1,1,8,512]{3,2,1,0:T(8,128)S(1)}, f32[1,1,8,512]{3,2,1,0:T(8,128)S(1)}, u32[]{:S(2)}, u32[]{:S(2)}) collective-permute-start(f32[1,1,8,512]{3,2,1,0:T(8,128)S(1)} %bitcast.548), channel_id=1, source_target_pairs={{1,0},{2,1},{3,2},{4,3},{5,4},{6,5},{7,6},{8,7},{9,8},{10,9},{11,1... | collective-permute-start | bytes 49160 | tf_op jit(solution)/shard_map/ppermute | solution.py:16
  98.4 4.6 %collective-permute-start.44 = (bf16[8,512]{1,0:T(8,128)(2,1)S(1)}, bf16[8,512]{1,0:T(8,128)(2,1)S(1)}, u32[]{:S(2)}, u32[]{:S(2)}) collective-permute-start(bf16[8,512]{1,0:T(8,128)(2,1)S(1)} %get-tuple-element.44), channel_id=1, source_target_pairs={{0,4},{1,5},{2,6},{3,7},{4,0},{5,1},{6,2},{7,3},{8,12},{9,13},{10,... | collective-permute-start | bytes 24584 | tf_op jit(solution)/shard_map/ppermute | solution.py:28
  98.7 13.0 %collective-permute-start.14 = (bf16[8,512]{1,0:T(8,128)(2,1)S(1)}, bf16[8,512]{1,0:T(8,128)(2,1)S(1)}, u32[]{:S(2)}, u32[]{:S(2)}) collective-permute-start(bf16[8,512]{1,0:T(8,128)(2,1)S(1)} %get-tuple-element.43), channel_id=1, source_target_pairs={{0,4},{1,5},{2,6},{3,7},{4,0},{5,1},{6,2},{7,3},{8,12},{9,13},{10,... | collective-permute-start | bytes 24584 | tf_op jit(solution)/shard_map/ppermute | solution.py:28
  104.1 16.1 %all-to-all-start.2 = ((bf16[64,2,128]{2,1,0:T(2,128)(2,1)}), bf16[64,2,128]{2,1,0:T(2,128)(2,1)S(1)}, u32[]{:S(2)}, u32[]{:S(2)}) async-start(bf16[64,2,128]{2,1,0:T(2,128)(2,1)} %reshape.180), calls=%async_computation.2 | async-start | bytes 65536 | tf_op jit(solution)/shard_map/all_to_all | solution.py:33
  120.2 14.1 %all-to-all-start = ((bf16[64,2,128]{2,1,0:T(2,128)(2,1)}), bf16[64,2,128]{2,1,0:T(2,128)(2,1)S(1)}, u32[]{:S(2)}, u32[]{:S(2)}) async-start(bf16[64,2,128]{2,1,0:T(2,128)(2,1)} %reshape.182), calls=%async_computation | async-start | bytes 65536 | tf_op jit(solution)/shard_map/all_to_all | solution.py:33
  135.0 9.6 %all-to-all-start.3 = ((bf16[4,8,2048]{2,1,0:T(8,128)(2,1)}), bf16[4,8,2048]{2,1,0:T(8,128)(2,1)}, u32[]{:S(2)}, u32[]{:S(2)}) async-start(bf16[4,8,2048]{2,1,0:T(8,128)(2,1)} %broadcast_in_dim.45), calls=%async_computation.3 | async-start | bytes 262144 | tf_op jit(solution)/shard_map/all_to_all | solution.py:33
  145.2 9.3 %all-to-all-start.1 = ((bf16[4,8,2048]{2,1,0:T(8,128)(2,1)}), bf16[4,8,2048]{2,1,0:T(8,128)(2,1)S(1)}, u32[]{:S(2)}, u32[]{:S(2)}) async-start(bf16[4,8,2048]{2,1,0:T(8,128)(2,1)} %broadcast_in_dim.40), calls=%async_computation.1 | async-start | bytes 262144 | tf_op jit(solution)/shard_map/all_to_all | solution.py:33
  153.0 5.0 %collective-permute-start.45 = (bf16[8,512]{1,0:T(8,128)(2,1)S(1)}, bf16[8,512]{1,0:T(8,128)(2,1)S(1)}, u32[]{:S(2)}, u32[]{:S(2)}) collective-permute-start(bf16[8,512]{1,0:T(8,128)(2,1)S(1)} %convolution_convert_fusion.4), channel_id=1, source_target_pairs={{0,4},{1,5},{2,6},{3,7},{4,0},{5,1},{6,2},{7,3},{8,12},{9,13},{10,... | collective-permute-start | bytes 24584 | tf_op jit(solution)/shard_map/ppermute | solution.py:28
  156.5 14.4 %collective-permute-start.15 = (bf16[8,512]{1,0:T(8,128)(2,1)S(1)}, bf16[8,512]{1,0:T(8,128)(2,1)S(1)}, u32[]{:S(2)}, u32[]{:S(2)}) collective-permute-start(bf16[8,512]{1,0:T(8,128)(2,1)S(1)} %convolution_convert_fusion.7), channel_id=1, source_target_pairs={{0,4},{1,5},{2,6},{3,7},{4,0},{5,1},{6,2},{7,3},{8,12},{9,13},{10,... | collective-permute-start | bytes 24584 | tf_op jit(solution)/shard_map/ppermute | solution.py:28
  158.0 15.0 %collective-permute-start.46 = (bf16[1,1,8,512]{3,2,1,0:T(8,128)(2,1)S(1)}, bf16[1,1,8,512]{3,2,1,0:T(8,128)(2,1)S(1)}, u32[]{:S(2)}, u32[]{:S(2)}) collective-permute-start(bf16[1,1,8,512]{3,2,1,0:T(8,128)(2,1)S(1)} %fusion.207), channel_id=1, source_target_pairs={{0,1},{1,2},{2,3},{3,4},{4,5},{5,6},{6,7},{7,8},{8,9},{9,10},{10,1... | collective-permute-start | bytes 24584 | tf_op jit(solution)/shard_map/ppermute | solution.py:15
  159.9 16.4 %collective-permute-start.47 = (bf16[1,1,8,512]{3,2,1,0:T(8,128)(2,1)S(1)}, bf16[1,1,8,512]{3,2,1,0:T(8,128)(2,1)S(1)}, u32[]{:S(2)}, u32[]{:S(2)}) collective-permute-start(bf16[1,1,8,512]{3,2,1,0:T(8,128)(2,1)S(1)} %fusion.207), channel_id=1, source_target_pairs={{0,64},{64,128},{128,192},{1,65},{65,129},{129,193},{2,66},{66,130... | collective-permute-start | bytes 24584 | tf_op jit(solution)/shard_map/ppermute | solution.py:15
  163.3 15.5 %collective-permute-start.48 = (bf16[1,1,8,512]{3,2,1,0:T(8,128)(2,1)S(1)}, bf16[1,1,8,512]{3,2,1,0:T(8,128)(2,1)S(1)}, u32[]{:S(2)}, u32[]{:S(2)}) collective-permute-start(bf16[1,1,8,512]{3,2,1,0:T(8,128)(2,1)S(1)} %fusion.207), channel_id=1, source_target_pairs={{64,0},{128,64},{192,128},{65,1},{129,65},{193,129},{66,2},{130,66... | collective-permute-start | bytes 24584 | tf_op jit(solution)/shard_map/ppermute | solution.py:16
  165.8 18.3 %collective-permute-start.49 = (bf16[1,1,8,512]{3,2,1,0:T(8,128)(2,1)S(1)}, bf16[1,1,8,512]{3,2,1,0:T(8,128)(2,1)S(1)}, u32[]{:S(2)}, u32[]{:S(2)}) collective-permute-start(bf16[1,1,8,512]{3,2,1,0:T(8,128)(2,1)S(1)} %fusion.207), channel_id=1, source_target_pairs={{1,0},{2,1},{3,2},{4,3},{5,4},{6,5},{7,6},{8,7},{9,8},{10,9},{11,1... | collective-permute-start | bytes 24584 | tf_op jit(solution)/shard_map/ppermute | solution.py:16
  171.0 13.0 %collective-permute-start.16 = (bf16[1,1,8,512]{3,2,1,0:T(8,128)(2,1)S(1)}, bf16[1,1,8,512]{3,2,1,0:T(8,128)(2,1)S(1)}, u32[]{:S(2)}, u32[]{:S(2)}) collective-permute-start(bf16[1,1,8,512]{3,2,1,0:T(8,128)(2,1)S(1)} %fusion.208), channel_id=1, source_target_pairs={{0,1},{1,2},{2,3},{3,4},{4,5},{5,6},{6,7},{7,8},{8,9},{9,10},{10,1... | collective-permute-start | bytes 24584 | tf_op jit(solution)/shard_map/ppermute | solution.py:15
  173.0 11.1 %collective-permute-start.17 = (bf16[1,1,8,512]{3,2,1,0:T(8,128)(2,1)S(1)}, bf16[1,1,8,512]{3,2,1,0:T(8,128)(2,1)S(1)}, u32[]{:S(2)}, u32[]{:S(2)}) collective-permute-start(bf16[1,1,8,512]{3,2,1,0:T(8,128)(2,1)S(1)} %fusion.208), channel_id=1, source_target_pairs={{0,64},{64,128},{128,192},{1,65},{65,129},{129,193},{2,66},{66,130... | collective-permute-start | bytes 24584 | tf_op jit(solution)/shard_map/ppermute | solution.py:15
  176.4 7.7 %collective-permute-start.18 = (bf16[1,1,8,512]{3,2,1,0:T(8,128)(2,1)S(1)}, bf16[1,1,8,512]{3,2,1,0:T(8,128)(2,1)S(1)}, u32[]{:S(2)}, u32[]{:S(2)}) collective-permute-start(bf16[1,1,8,512]{3,2,1,0:T(8,128)(2,1)S(1)} %fusion.208), channel_id=1, source_target_pairs={{64,0},{128,64},{192,128},{65,1},{129,65},{193,129},{66,2},{130,66... | collective-permute-start | bytes 24584 | tf_op jit(solution)/shard_map/ppermute | solution.py:16
  178.8 6.5 %collective-permute-start.19 = (bf16[1,1,8,512]{3,2,1,0:T(8,128)(2,1)S(1)}, bf16[1,1,8,512]{3,2,1,0:T(8,128)(2,1)S(1)}, u32[]{:S(2)}, u32[]{:S(2)}) collective-permute-start(bf16[1,1,8,512]{3,2,1,0:T(8,128)(2,1)S(1)} %fusion.208), channel_id=1, source_target_pairs={{1,0},{2,1},{3,2},{4,3},{5,4},{6,5},{7,6},{8,7},{9,8},{10,9},{11,1... | collective-permute-start | bytes 24584 | tf_op jit(solution)/shard_map/ppermute | solution.py:16
  185.7 3.8 %collective-permute-start.50 = (bf16[8,512]{1,0:T(8,128)(2,1)S(1)}, bf16[8,512]{1,0:T(8,128)(2,1)S(1)}, u32[]{:S(2)}, u32[]{:S(2)}) collective-permute-start(bf16[8,512]{1,0:T(8,128)(2,1)S(1)} %convolution_convert_fusion.3), channel_id=1, source_target_pairs={{0,2},{1,3},{2,0},{3,1},{4,6},{5,7},{6,4},{7,5},{8,10},{9,11},{10,... | collective-permute-start | bytes 24584 | tf_op jit(solution)/shard_map/ppermute | solution.py:28
  186.1 16.6 %collective-permute-start.20 = (bf16[8,512]{1,0:T(8,128)(2,1)S(1)}, bf16[8,512]{1,0:T(8,128)(2,1)S(1)}, u32[]{:S(2)}, u32[]{:S(2)}) collective-permute-start(bf16[8,512]{1,0:T(8,128)(2,1)S(1)} %convolution_convert_fusion.6), channel_id=1, source_target_pairs={{0,2},{1,3},{2,0},{3,1},{4,6},{5,7},{6,4},{7,5},{8,10},{9,11},{10,... | collective-permute-start | bytes 24584 | tf_op jit(solution)/shard_map/ppermute | solution.py:28
  189.8 15.2 %collective-permute-start.51 = (bf16[1,1,8,512]{3,2,1,0:T(8,128)(2,1)S(1)}, bf16[1,1,8,512]{3,2,1,0:T(8,128)(2,1)S(1)}, u32[]{:S(2)}, u32[]{:S(2)}) collective-permute-start(bf16[1,1,8,512]{3,2,1,0:T(8,128)(2,1)S(1)} %convert_bitcast_fusion.1), channel_id=1, source_target_pairs={{0,1},{1,2},{2,3},{3,4},{4,5},{5,6},{6,7},{7,8},{8,9},{9,10},{10,1... | collective-permute-start | bytes 24584 | tf_op jit(solution)/shard_map/ppermute | solution.py:15
  191.7 16.7 %collective-permute-start.52 = (bf16[1,1,8,512]{3,2,1,0:T(8,128)(2,1)S(1)}, bf16[1,1,8,512]{3,2,1,0:T(8,128)(2,1)S(1)}, u32[]{:S(2)}, u32[]{:S(2)}) collective-permute-start(bf16[1,1,8,512]{3,2,1,0:T(8,128)(2,1)S(1)} %convert_bitcast_fusion.1), channel_id=1, source_target_pairs={{0,64},{64,128},{128,192},{1,65},{65,129},{129,193},{2,66},{66,130... | collective-permute-start | bytes 24584 | tf_op jit(solution)/shard_map/ppermute | solution.py:15
  195.1 15.8 %collective-permute-start.53 = (bf16[1,1,8,512]{3,2,1,0:T(8,128)(2,1)S(1)}, bf16[1,1,8,512]{3,2,1,0:T(8,128)(2,1)S(1)}, u32[]{:S(2)}, u32[]{:S(2)}) collective-permute-start(bf16[1,1,8,512]{3,2,1,0:T(8,128)(2,1)S(1)} %convert_bitcast_fusion.1), channel_id=1, source_target_pairs={{64,0},{128,64},{192,128},{65,1},{129,65},{193,129},{66,2},{130,66... | collective-permute-start | bytes 24584 | tf_op jit(solution)/shard_map/ppermute | solution.py:16
  197.5 18.5 %collective-permute-start.54 = (bf16[1,1,8,512]{3,2,1,0:T(8,128)(2,1)S(1)}, bf16[1,1,8,512]{3,2,1,0:T(8,128)(2,1)S(1)}, u32[]{:S(2)}, u32[]{:S(2)}) collective-permute-start(bf16[1,1,8,512]{3,2,1,0:T(8,128)(2,1)S(1)} %convert_bitcast_fusion.1), channel_id=1, source_target_pairs={{1,0},{2,1},{3,2},{4,3},{5,4},{6,5},{7,6},{8,7},{9,8},{10,9},{11,1... | collective-permute-start | bytes 24584 | tf_op jit(solution)/shard_map/ppermute | solution.py:16
  203.0 13.0 %collective-permute-start.21 = (bf16[1,1,8,512]{3,2,1,0:T(8,128)(2,1)S(1)}, bf16[1,1,8,512]{3,2,1,0:T(8,128)(2,1)S(1)}, u32[]{:S(2)}, u32[]{:S(2)}) collective-permute-start(bf16[1,1,8,512]{3,2,1,0:T(8,128)(2,1)S(1)} %convert_bitcast_fusion.3), channel_id=1, source_target_pairs={{0,1},{1,2},{2,3},{3,4},{4,5},{5,6},{6,7},{7,8},{8,9},{9,10},{10,1... | collective-permute-start | bytes 24584 | tf_op jit(solution)/shard_map/ppermute | solution.py:15
  205.0 11.1 %collective-permute-start.22 = (bf16[1,1,8,512]{3,2,1,0:T(8,128)(2,1)S(1)}, bf16[1,1,8,512]{3,2,1,0:T(8,128)(2,1)S(1)}, u32[]{:S(2)}, u32[]{:S(2)}) collective-permute-start(bf16[1,1,8,512]{3,2,1,0:T(8,128)(2,1)S(1)} %convert_bitcast_fusion.3), channel_id=1, source_target_pairs={{0,64},{64,128},{128,192},{1,65},{65,129},{129,193},{2,66},{66,130... | collective-permute-start | bytes 24584 | tf_op jit(solution)/shard_map/ppermute | solution.py:15
  208.4 7.7 %collective-permute-start.23 = (bf16[1,1,8,512]{3,2,1,0:T(8,128)(2,1)S(1)}, bf16[1,1,8,512]{3,2,1,0:T(8,128)(2,1)S(1)}, u32[]{:S(2)}, u32[]{:S(2)}) collective-permute-start(bf16[1,1,8,512]{3,2,1,0:T(8,128)(2,1)S(1)} %convert_bitcast_fusion.3), channel_id=1, source_target_pairs={{64,0},{128,64},{192,128},{65,1},{129,65},{193,129},{66,2},{130,66... | collective-permute-start | bytes 24584 | tf_op jit(solution)/shard_map/ppermute | solution.py:16
  210.9 6.5 %collective-permute-start.24 = (bf16[1,1,8,512]{3,2,1,0:T(8,128)(2,1)S(1)}, bf16[1,1,8,512]{3,2,1,0:T(8,128)(2,1)S(1)}, u32[]{:S(2)}, u32[]{:S(2)}) collective-permute-start(bf16[1,1,8,512]{3,2,1,0:T(8,128)(2,1)S(1)} %convert_bitcast_fusion.3), channel_id=1, source_target_pairs={{1,0},{2,1},{3,2},{4,3},{5,4},{6,5},{7,6},{8,7},{9,8},{10,9},{11,1... | collective-permute-start | bytes 24584 | tf_op jit(solution)/shard_map/ppermute | solution.py:16
  217.7 1.2 collective-permute-start.55
  218.0 14.2 %collective-permute-start.25 = (bf16[8,512]{1,0:T(8,128)(2,1)S(1)}, bf16[8,512]{1,0:T(8,128)(2,1)S(1)}, u32[]{:S(2)}, u32[]{:S(2)}) collective-permute-start(bf16[8,512]{1,0:T(8,128)(2,1)S(1)} %convolution_convert_fusion.5), channel_id=1, source_target_pairs={{0,1},{1,0},{2,3},{3,2},{4,5},{5,4},{6,7},{7,6},{8,9},{9,8},{10,11... | collective-permute-start | bytes 24584 | tf_op jit(solution)/shard_map/ppermute | solution.py:28
  219.2 15.2 %collective-permute-start.56 = (bf16[1,1,8,512]{3,2,1,0:T(8,128)(2,1)S(1)}, bf16[1,1,8,512]{3,2,1,0:T(8,128)(2,1)S(1)}, u32[]{:S(2)}, u32[]{:S(2)}) collective-permute-start(bf16[1,1,8,512]{3,2,1,0:T(8,128)(2,1)S(1)} %convert_bitcast_fusion), channel_id=1, source_target_pairs={{0,1},{1,2},{2,3},{3,4},{4,5},{5,6},{6,7},{7,8},{8,9},{9,10},{10,1... | collective-permute-start | bytes 24584 | tf_op jit(solution)/shard_map/ppermute | solution.py:15
  221.2 16.5 %collective-permute-start.57 = (bf16[1,1,8,512]{3,2,1,0:T(8,128)(2,1)S(1)}, bf16[1,1,8,512]{3,2,1,0:T(8,128)(2,1)S(1)}, u32[]{:S(2)}, u32[]{:S(2)}) collective-permute-start(bf16[1,1,8,512]{3,2,1,0:T(8,128)(2,1)S(1)} %convert_bitcast_fusion), channel_id=1, source_target_pairs={{0,64},{64,128},{128,192},{1,65},{65,129},{129,193},{2,66},{66,130... | collective-permute-start | bytes 24584 | tf_op jit(solution)/shard_map/ppermute | solution.py:15
  224.6 15.6 %collective-permute-start.58 = (bf16[1,1,8,512]{3,2,1,0:T(8,128)(2,1)S(1)}, bf16[1,1,8,512]{3,2,1,0:T(8,128)(2,1)S(1)}, u32[]{:S(2)}, u32[]{:S(2)}) collective-permute-start(bf16[1,1,8,512]{3,2,1,0:T(8,128)(2,1)S(1)} %convert_bitcast_fusion), channel_id=1, source_target_pairs={{64,0},{128,64},{192,128},{65,1},{129,65},{193,129},{66,2},{130,66... | collective-permute-start | bytes 24584 | tf_op jit(solution)/shard_map/ppermute | solution.py:16
  227.1 18.3 %collective-permute-start.59 = (bf16[1,1,8,512]{3,2,1,0:T(8,128)(2,1)S(1)}, bf16[1,1,8,512]{3,2,1,0:T(8,128)(2,1)S(1)}, u32[]{:S(2)}, u32[]{:S(2)}) collective-permute-start(bf16[1,1,8,512]{3,2,1,0:T(8,128)(2,1)S(1)} %convert_bitcast_fusion), channel_id=1, source_target_pairs={{1,0},{2,1},{3,2},{4,3},{5,4},{6,5},{7,6},{8,7},{9,8},{10,9},{11,1... | collective-permute-start | bytes 24584 | tf_op jit(solution)/shard_map/ppermute | solution.py:16
  232.4 13.1 %collective-permute-start.26 = (bf16[1,1,8,512]{3,2,1,0:T(8,128)(2,1)S(1)}, bf16[1,1,8,512]{3,2,1,0:T(8,128)(2,1)S(1)}, u32[]{:S(2)}, u32[]{:S(2)}) collective-permute-start(bf16[1,1,8,512]{3,2,1,0:T(8,128)(2,1)S(1)} %convert_bitcast_fusion.2), channel_id=1, source_target_pairs={{0,1},{1,2},{2,3},{3,4},{4,5},{5,6},{6,7},{7,8},{8,9},{9,10},{10,1... | collective-permute-start | bytes 24584 | tf_op jit(solution)/shard_map/ppermute | solution.py:15
  234.3 11.1 %collective-permute-start.27 = (bf16[1,1,8,512]{3,2,1,0:T(8,128)(2,1)S(1)}, bf16[1,1,8,512]{3,2,1,0:T(8,128)(2,1)S(1)}, u32[]{:S(2)}, u32[]{:S(2)}) collective-permute-start(bf16[1,1,8,512]{3,2,1,0:T(8,128)(2,1)S(1)} %convert_bitcast_fusion.2), channel_id=1, source_target_pairs={{0,64},{64,128},{128,192},{1,65},{65,129},{129,193},{2,66},{66,130... | collective-permute-start | bytes 24584 | tf_op jit(solution)/shard_map/ppermute | solution.py:15
  237.8 7.7 %collective-permute-start.28 = (bf16[1,1,8,512]{3,2,1,0:T(8,128)(2,1)S(1)}, bf16[1,1,8,512]{3,2,1,0:T(8,128)(2,1)S(1)}, u32[]{:S(2)}, u32[]{:S(2)}) collective-permute-start(bf16[1,1,8,512]{3,2,1,0:T(8,128)(2,1)S(1)} %convert_bitcast_fusion.2), channel_id=1, source_target_pairs={{64,0},{128,64},{192,128},{65,1},{129,65},{193,129},{66,2},{130,66... | collective-permute-start | bytes 24584 | tf_op jit(solution)/shard_map/ppermute | solution.py:16
  240.2 6.5 %collective-permute-start.29 = (bf16[1,1,8,512]{3,2,1,0:T(8,128)(2,1)S(1)}, bf16[1,1,8,512]{3,2,1,0:T(8,128)(2,1)S(1)}, u32[]{:S(2)}, u32[]{:S(2)}) collective-permute-start(bf16[1,1,8,512]{3,2,1,0:T(8,128)(2,1)S(1)} %convert_bitcast_fusion.2), channel_id=1, source_target_pairs={{1,0},{2,1},{3,2},{4,3},{5,4},{6,5},{7,6},{8,7},{9,8},{10,9},{11,1... | collective-permute-start | bytes 24584 | tf_op jit(solution)/shard_map/ppermute | solution.py:16
  (25 other events, 841.5 us)

commit v5 on v0

--- a/solution.py
+++ b/solution.py
@@ -22,6 +22,25 @@
         shard = jnp.concatenate([jnp.pad(low, around), shard, jnp.pad(high, around)], axis=dim)
         done.append(dim)
     return shard
+
+
+def neighbours_of(shard):
+    rows, cols = (lax.axis_size("gy"), lax.axis_size("gx"))
+    from_below = lax.ppermute(shard, "gy", [(i, i + 1) for i in range(rows - 1)])
+    from_above = lax.ppermute(shard, "gy", [(i + 1, i) for i in range(rows - 1)])
+    pairs = [(i, i + 1) if i % 2 else (i, i - 1) for i in range(cols)]
+    across = lax.ppermute(shard, "gx", [(a, b) for a, b in pairs if 0 <= b < cols])
+    beside = lax.ppermute(shard, "gx", [(i, i ^ 1) for i in range(cols)])
+    odd = lax.axis_index("gx") % 2 == 1
+    left = jnp.where(odd, beside, across)
+    right = jnp.where(odd, across, beside)
+    return from_below, from_above, left, right
+
+
+def neighbour_sum(shard, coefs):
+    below, above, left, right = neighbours_of(shard)
+    total = coefs[0] * below + coefs[1] * above
+    return total + coefs[2] * left + coefs[3] * right
 
 
 def partner_2(shard, axis, stride):
@@ -93,8 +112,7 @@
     state = picked - jnp.einsum("fbq,bkq->fbk", solved, weights, preferred_element_type=jnp.float32)
     state = state.reshape(field_count, skel_total)
     for level in range(level_count):
-        padded = padded_2(state[None, None], (("gy", 0), ("gx", 1)), 1)
-        mixed = state - neighbour_mix(padded, up_rates[level])
+        mixed = state - neighbour_sum(state, up_rates[level])
         rounded = mixed.astype(jnp.bfloat16)
         partner = partner_2(rounded, "gx", level)
         state = jnp.dot(rounded, own[level], preferred_element_type=jnp.float32)
@@ -111,10 +129,7 @@
         sent = right_transpose(rounded, other[level])
         received = partner_2(sent.astype(jnp.bfloat16), "gx", level).astype(sent.dtype)
         mixed = right_transpose(rounded, own[level]) + received
-        padded = padded_2(mixed[None, None].astype(jnp.bfloat16), (("gy", 0), ("gx", 1)), 1).astype(
-            jnp.float32
-        )
-        state = mixed - neighbour_mix(padded, down_rates[level])
+        state = mixed - neighbour_sum(mixed.astype(jnp.bfloat16), down_rates[level])
     skeleton = state.reshape(field_count, box_count, skel_size)
     back = jnp.einsum(
         "fbk,bkq->fbq", skeleton.astype(jnp.bfloat16), weights, preferred_element_type=jnp.float32

time: 148 us -> 139 us (0.939)
  starting transfers between devices: 86.8 us -> 67.4 us
  waiting for transfers between devices: 25.6 us -> 41.2 us
  matrix products: 11.7 us -> 9.52 us
  blocking collectives: 17 us -> 15.4 us
    ppermute x24, starting transfers between devices: 80.3 us -> 61.3 us  [the longest x6 25.5 us: neighbours_of(): lax.ppermute(shard, 'gx', [(a, b) for a, b in pairs if 0 <= b < cols])]
    ppermute x24, waiting for transfers between devices: 8.39 us -> 20.3 us  [the longest x6 20.2 us: neighbours_of(): lax.ppermute(shard, 'gx', [(a, b) for a, b in pairs if 0 <= b < cols])]
    ppermute x6, waiting for transfers between devices: 12.9 us -> 16.7 us  [partner_2(): lax.ppermute(shard, axis, [(i, i ^ 1 << stride) for i in range(lax.axis_s...]
    dot_general x3, matrix products: 3.63 us -> 1.55 us  [body(): state = jnp.dot(rounded, own[level], preferred_element_type=jnp.float32)]
    all_to_all x1, blocking collectives: 17 us -> 15.4 us  [sent_to_all(): return lax.all_to_all(copies, axis, split_axis=0, concat_axis=0, tiled=True)]
  transfers between devices with their start and end apart: 31 -> 31, of which waited for: 12 -> 12; matrix products, arithmetic and copies ran while one was open for 5% -> 2% of each run, Pallas kernels for 0% -> 0%
where the time goes in v5:
time: 139 us; the launch traced here: 138 us
  starting transfers between devices  67.4 us (48%)
  waiting for transfers between devices  41.2 us (30%)
  blocking collectives  15.4 us (11%)
  matrix products  9.52 us (7%)
  local copies, waits for them, and re-layouts  3.77 us (3%)
    ppermute x6, starting transfers between devices, neighbours_of(): lax.ppermute(shard, 'gx', [(a, b) for a, b in pairs if 0 <= b < cols])  25.5 us
    ppermute x6, waiting for transfers between devices, neighbours_of(): lax.ppermute(shard, 'gx', [(a, b) for a, b in pairs if 0 <= b < cols])  20.2 us
    ppermute x6, starting transfers between devices, neighbours_of(): lax.ppermute(shard, 'gy', [(i + 1, i) for i in range(rows - 1)])  18.8 us
    ppermute x6, waiting for transfers between devices, partner_2(): lax.ppermute(shard, axis, [(i, i ^ 1 << stride) for i in range(lax.axis_s...  16.7 us
    ppermute x6, starting transfers between devices, neighbours_of(): lax.ppermute(shard, 'gy', [(i, i + 1) for i in range(rows - 1)])  16.4 us
    all_to_all x1, blocking collectives, sent_to_all(): return lax.all_to_all(copies, axis, split_axis=0, concat_axis=0, tiled=True)  15.4 us
    all_to_all x1, starting transfers between devices, sent_to_all(): return lax.all_to_all(copies, axis, split_axis=0, concat_axis=0, tiled=True)  4.92 us
    all_to_all x1, waiting for transfers between devices, sent_to_all(): return lax.all_to_all(copies, axis, split_axis=0, concat_axis=0, tiled=True)  4.27 us
  transfers between devices with their start and end apart: 31, of which 12 were waited for; matrix products, arithmetic and copies ran while one was open for 2% of the time, Pallas kernels for 0%

profile of v5, /device:TPU:10, one launch (start us, length us, event | category | flops | bytes accessed | tf_op | source)
XLA Modules:
  0.0 138.0 jit_solution(1011075485185480675)
XLA Ops:
  0.0 1.0 copy.29
  1.0 0.2 copy-done
  1.3 0.2 fusion.3
  1.5 1.1 convolution_bitcast_fusion.2
  2.6 0.3 fusion.4
  3.0 3.5 %collective-permute-start = (f32[16,512]{1,0:T(8,128)S(1)}, f32[16,512]{1,0:T(8,128)S(1)}, u32[]{:S(2)}, u32[]{:S(2)}) collective-permute-start(f32[16,512]{1,0:T(8,128)S(1)} %reshape.88), channel_id=1, source_target_pairs={{0,64},{64,128},{128,192},{1,65},{65,129},{129,193},{2,66},{66,130... | collective-permute-start | bytes 98312 | tf_op jit(solution)/shard_map/ppermute | solution.py:29
  6.5 2.4 %collective-permute-start.1 = (f32[16,512]{1,0:T(8,128)S(1)}, f32[16,512]{1,0:T(8,128)S(1)}, u32[]{:S(2)}, u32[]{:S(2)}) collective-permute-start(f32[16,512]{1,0:T(8,128)S(1)} %reshape.88), channel_id=1, source_target_pairs={{64,0},{128,64},{192,128},{65,1},{129,65},{193,129},{66,2},{130,66... | collective-permute-start | bytes 98312 | tf_op jit(solution)/shard_map/ppermute | solution.py:30
  8.9 0.1 collective-permute-start.2
  9.0 7.8 %collective-permute-start.3 = (f32[16,512]{1,0:T(8,128)S(1)}, f32[16,512]{1,0:T(8,128)S(1)}, u32[]{:S(2)}, u32[]{:S(2)}) collective-permute-start(f32[16,512]{1,0:T(8,128)S(1)} %reshape.88), channel_id=1, source_target_pairs={{1,2},{2,1},{3,4},{4,3},{5,6},{6,5},{7,8},{8,7},{9,10},{10,9},{11,... | collective-permute-start | bytes 98312 | tf_op jit(solution)/shard_map/ppermute | solution.py:32
  16.9 1.5 %collective-permute-done.3 = f32[16,512]{1,0:T(8,128)S(1)} collective-permute-done((f32[16,512]{1,0:T(8,128)S(1)}, f32[16,512]{1,0:T(8,128)S(1)}, u32[]{:S(2)}, u32[]{:S(2)}) %collective-permute-start.3) | collective-permute-done | bytes 32800 | tf_op jit(solution)/shard_map/ppermute | solution.py:32
  18.4 0.1 collective-permute-start.4
  18.5 1.2 fusion.25
  19.7 0.2 convolution_add_fusion.5
  19.9 3.5 %collective-permute-start.5 = (f32[16,512]{1,0:T(8,128)S(1)}, f32[16,512]{1,0:T(8,128)S(1)}, u32[]{:S(2)}, u32[]{:S(2)}) collective-permute-start(f32[16,512]{1,0:T(8,128)S(1)} %convolution_add_fusion.5), channel_id=1, source_target_pairs={{0,64},{64,128},{128,192},{1,65},{65,129},{129,193},{2,66},{66,130... | collective-permute-start | bytes 98312 | tf_op jit(solution)/shard_map/ppermute | solution.py:29
  23.4 2.4 %collective-permute-start.6 = (f32[16,512]{1,0:T(8,128)S(1)}, f32[16,512]{1,0:T(8,128)S(1)}, u32[]{:S(2)}, u32[]{:S(2)}) collective-permute-start(f32[16,512]{1,0:T(8,128)S(1)} %convolution_add_fusion.5), channel_id=1, source_target_pairs={{64,0},{128,64},{192,128},{65,1},{129,65},{193,129},{66,2},{130,66... | collective-permute-start | bytes 98312 | tf_op jit(solution)/shard_map/ppermute | solution.py:30
  25.9 6.2 %collective-permute-start.8 = (f32[16,512]{1,0:T(8,128)S(1)}, f32[16,512]{1,0:T(8,128)S(1)}, u32[]{:S(2)}, u32[]{:S(2)}) collective-permute-start(f32[16,512]{1,0:T(8,128)S(1)} %convolution_add_fusion.5), channel_id=1, source_target_pairs={{1,2},{2,1},{3,4},{4,3},{5,6},{6,5},{7,8},{8,7},{9,10},{10,9},{11,... | collective-permute-start | bytes 98312 | tf_op jit(solution)/shard_map/ppermute | solution.py:32
  32.1 1.6 %collective-permute-done.8 = f32[16,512]{1,0:T(8,128)S(1)} collective-permute-done((f32[16,512]{1,0:T(8,128)S(1)}, f32[16,512]{1,0:T(8,128)S(1)}, u32[]{:S(2)}, u32[]{:S(2)}) %collective-permute-start.8) | collective-permute-done | bytes 32800 | tf_op jit(solution)/shard_map/ppermute | solution.py:32
  33.7 0.1 collective-permute-start.9
  33.8 0.2 fusion.20
  34.0 3.5 %collective-permute-done.9 = bf16[16,512]{1,0:T(8,128)(2,1)S(1)} collective-permute-done((bf16[16,512]{1,0:T(8,128)(2,1)S(1)}, bf16[16,512]{1,0:T(8,128)(2,1)S(1)}, u32[]{:S(2)}, u32[]{:S(2)}) %collective-permute-start.9) | collective-permute-done | bytes 16416 | tf_op jit(solution)/shard_map/ppermute | solution.py:47
  37.5 0.2 convolution_add_fusion.4
  37.7 3.5 %collective-permute-start.10 = (f32[16,512]{1,0:T(8,128)S(1)}, f32[16,512]{1,0:T(8,128)S(1)}, u32[]{:S(2)}, u32[]{:S(2)}) collective-permute-start(f32[16,512]{1,0:T(8,128)S(1)} %convolution_add_fusion.4), channel_id=1, source_target_pairs={{0,64},{64,128},{128,192},{1,65},{65,129},{129,193},{2,66},{66,130... | collective-permute-start | bytes 98312 | tf_op jit(solution)/shard_map/ppermute | solution.py:29
  41.2 2.4 %collective-permute-start.11 = (f32[16,512]{1,0:T(8,128)S(1)}, f32[16,512]{1,0:T(8,128)S(1)}, u32[]{:S(2)}, u32[]{:S(2)}) collective-permute-start(f32[16,512]{1,0:T(8,128)S(1)} %convolution_add_fusion.4), channel_id=1, source_target_pairs={{64,0},{128,64},{192,128},{65,1},{129,65},{193,129},{66,2},{130,66... | collective-permute-start | bytes 98312 | tf_op jit(solution)/shard_map/ppermute | solution.py:30
  43.7 4.0 %collective-permute-start.13 = (f32[16,512]{1,0:T(8,128)S(1)}, f32[16,512]{1,0:T(8,128)S(1)}, u32[]{:S(2)}, u32[]{:S(2)}) collective-permute-start(f32[16,512]{1,0:T(8,128)S(1)} %convolution_add_fusion.4), channel_id=1, source_target_pairs={{1,2},{2,1},{3,4},{4,3},{5,6},{6,5},{7,8},{8,7},{9,10},{10,9},{11,... | collective-permute-start | bytes 98312 | tf_op jit(solution)/shard_map/ppermute | solution.py:32
  47.7 3.3 %collective-permute-done.13 = f32[16,512]{1,0:T(8,128)S(1)} collective-permute-done((f32[16,512]{1,0:T(8,128)S(1)}, f32[16,512]{1,0:T(8,128)S(1)}, u32[]{:S(2)}, u32[]{:S(2)}) %collective-permute-start.13) | collective-permute-done | bytes 32800 | tf_op jit(solution)/shard_map/ppermute | solution.py:32
  51.0 0.1 collective-permute-start.14
  51.1 0.2 fusion.15
  51.3 4.5 %collective-permute-done.14 = bf16[16,512]{1,0:T(8,128)(2,1)S(1)} collective-permute-done((bf16[16,512]{1,0:T(8,128)(2,1)S(1)}, bf16[16,512]{1,0:T(8,128)(2,1)S(1)}, u32[]{:S(2)}, u32[]{:S(2)}) %collective-permute-start.14) | collective-permute-done | bytes 16416 | tf_op jit(solution)/shard_map/ppermute | solution.py:47
  55.8 0.2 fusion.6
  55.9 0.1 convolution_convert_fusion.6
  56.1 0.2 reshape.93
  56.3 15.4 %all_to_all.10 = bf16[64,2,256]{2,1,0:T(2,128)(2,1)S(1)} all-to-all(bf16[64,2,256]{2,1,0:T(2,128)(2,1)S(1)} %reshape.93), channel_id=1, replica_groups=mesh['gy'=4,'gx'=64] {'gx'}, dimensions={0} | all-to-all | bytes 131072 | tf_op jit(solution)/shard_map/all_to_all | solution.py:52
  71.7 0.2 reshape.94
  71.9 0.3 reshape.89
  72.2 0.7 broadcast_in_dim.7
  72.9 4.9 %all-to-all-start.1 = ((bf16[4,16,2048]{2,1,0:T(8,128)(2,1)}), bf16[4,16,2048]{2,1,0:T(8,128)(2,1)S(1)}, u32[]{:S(2)}, u32[]{:S(2)}) async-start(bf16[4,16,2048]{2,1,0:T(8,128)(2,1)} %broadcast_in_dim.7), calls=%async_computation.1 | async-start | bytes 524288 | tf_op jit(solution)/shard_map/all_to_all | solution.py:52
  77.9 1.2 fusion.9
  79.1 4.3 %all-to-all-done.1 = bf16[4,16,2048]{2,1,0:T(8,128)(2,1)S(1)} async-done(((bf16[4,16,2048]{2,1,0:T(8,128)(2,1)}), bf16[4,16,2048]{2,1,0:T(8,128)(2,1)S(1)}, u32[]{:S(2)}, u32[]{:S(2)}) %all-to-all-start.1) | async-done | bytes 262176 | tf_op jit(solution)/shard_map/all_to_all | solution.py:52
  83.4 1.4 %fusion.5 = bf16[16,512]{1,0:T(8,128)(2,1)S(1)} fusion(f32[16,512]{1,0:T(8,128)S(1)} %fusion.9, bf16[16,8192]{1,0:T(8,128)(2,1)S(1)} %bitcast.126, bf16[8192,32]{0,1:T(8,128)(2,1)} %param.21, bf16[1,32,512]{2,1,0:T(8,128)(2,1)S(1)} %copy-done.5), kind=kOutput, calls=%fused_computation.17 | convolution fusion | flops 8929792 | bytes 868352 | tf_op jit(solution)/shard_map/dot_general | solution.py:126
  84.8 0.2 convolution_convert_fusion.4
  85.0 1.0 collective-permute-start.15
  86.0 3.7 %collective-permute-done.15 = bf16[16,512]{1,0:T(8,128)(2,1)S(1)} collective-permute-done((bf16[16,512]{1,0:T(8,128)(2,1)S(1)}, bf16[16,512]{1,0:T(8,128)(2,1)S(1)}, u32[]{:S(2)}, u32[]{:S(2)}) %collective-permute-start.15) | collective-permute-done | bytes 16416 | tf_op jit(solution)/shard_map/ppermute | solution.py:47
  89.7 1.3 fusion.49
  91.0 2.1 %collective-permute-start.16 = (bf16[16,512]{1,0:T(8,128)(2,1)S(1)}, bf16[16,512]{1,0:T(8,128)(2,1)S(1)}, u32[]{:S(2)}, u32[]{:S(2)}) collective-permute-start(bf16[16,512]{1,0:T(8,128)(2,1)S(1)} %get-tuple-element.29), channel_id=1, source_target_pairs={{0,64},{64,128},{128,192},{1,65},{65,129},{129,193},{2,66},{66,130... | collective-permute-start | bytes 49160 | tf_op jit(solution)/shard_map/ppermute | solution.py:29
  93.0 3.9 %collective-permute-start.17 = (bf16[16,512]{1,0:T(8,128)(2,1)S(1)}, bf16[16,512]{1,0:T(8,128)(2,1)S(1)}, u32[]{:S(2)}, u32[]{:S(2)}) collective-permute-start(bf16[16,512]{1,0:T(8,128)(2,1)S(1)} %get-tuple-element.29), channel_id=1, source_target_pairs={{64,0},{128,64},{192,128},{65,1},{129,65},{193,129},{66,2},{130,66... | collective-permute-start | bytes 49160 | tf_op jit(solution)/shard_map/ppermute | solution.py:30
  97.1 3.5 %collective-permute-start.19 = (bf16[16,512]{1,0:T(8,128)(2,1)S(1)}, bf16[16,512]{1,0:T(8,128)(2,1)S(1)}, u32[]{:S(2)}, u32[]{:S(2)}) collective-permute-start(bf16[16,512]{1,0:T(8,128)(2,1)S(1)} %get-tuple-element.29), channel_id=1, source_target_pairs={{1,2},{2,1},{3,4},{4,3},{5,6},{6,5},{7,8},{8,7},{9,10},{10,9},{11,... | collective-permute-start | bytes 49160 | tf_op jit(solution)/shard_map/ppermute | solution.py:32
  100.6 3.6 %collective-permute-done.19 = bf16[16,512]{1,0:T(8,128)(2,1)S(1)} collective-permute-done((bf16[16,512]{1,0:T(8,128)(2,1)S(1)}, bf16[16,512]{1,0:T(8,128)(2,1)S(1)}, u32[]{:S(2)}, u32[]{:S(2)}) %collective-permute-start.19) | collective-permute-done | bytes 16416 | tf_op jit(solution)/shard_map/ppermute | solution.py:32
  104.3 0.2 convolution_convert_fusion.3
  104.5 3.8 %collective-permute-done.20 = bf16[16,512]{1,0:T(8,128)(2,1)S(1)} collective-permute-done((bf16[16,512]{1,0:T(8,128)(2,1)S(1)}, bf16[16,512]{1,0:T(8,128)(2,1)S(1)}, u32[]{:S(2)}, u32[]{:S(2)}) %collective-permute-start.20) | collective-permute-done | bytes 16416 | tf_op jit(solution)/shard_map/ppermute | solution.py:47
  108.3 0.2 fusion.52
  108.5 1.9 %collective-permute-start.21 = (bf16[16,512]{1,0:T(8,128)(2,1)S(1)}, bf16[16,512]{1,0:T(8,128)(2,1)S(1)}, u32[]{:S(2)}, u32[]{:S(2)}) collective-permute-start(bf16[16,512]{1,0:T(8,128)(2,1)S(1)} %get-tuple-element.31), channel_id=1, source_target_pairs={{0,64},{64,128},{128,192},{1,65},{65,129},{129,193},{2,66},{66,130... | collective-permute-start | bytes 49160 | tf_op jit(solution)/shard_map/ppermute | solution.py:29
  110.4 3.9 %collective-permute-start.22 = (bf16[16,512]{1,0:T(8,128)(2,1)S(1)}, bf16[16,512]{1,0:T(8,128)(2,1)S(1)}, u32[]{:S(2)}, u32[]{:S(2)}) collective-permute-start(bf16[16,512]{1,0:T(8,128)(2,1)S(1)} %get-tuple-element.31), channel_id=1, source_target_pairs={{64,0},{128,64},{192,128},{65,1},{129,65},{193,129},{66,2},{130,66... | collective-permute-start | bytes 49160 | tf_op jit(solution)/shard_map/ppermute | solution.py:30
  114.5 1.9 %collective-permute-start.24 = (bf16[16,512]{1,0:T(8,128)(2,1)S(1)}, bf16[16,512]{1,0:T(8,128)(2,1)S(1)}, u32[]{:S(2)}, u32[]{:S(2)}) collective-permute-start(bf16[16,512]{1,0:T(8,128)(2,1)S(1)} %get-tuple-element.31), channel_id=1, source_target_pairs={{1,2},{2,1},{3,4},{4,3},{5,6},{6,5},{7,8},{8,7},{9,10},{10,9},{11,... | collective-permute-start | bytes 49160 | tf_op jit(solution)/shard_map/ppermute | solution.py:32
  116.4 5.2 %collective-permute-done.24 = bf16[16,512]{1,0:T(8,128)(2,1)S(1)} collective-permute-done((bf16[16,512]{1,0:T(8,128)(2,1)S(1)}, bf16[16,512]{1,0:T(8,128)(2,1)S(1)}, u32[]{:S(2)}, u32[]{:S(2)}) %collective-permute-start.24) | collective-permute-done | bytes 16416 | tf_op jit(solution)/shard_map/ppermute | solution.py:32
  121.7 0.2 convolution_convert_fusion.2
  121.9 1.2 collective-permute-done.25
  123.1 0.2 fusion.53
  123.3 1.9 %collective-permute-start.26 = (bf16[16,512]{1,0:T(8,128)(2,1)S(1)}, bf16[16,512]{1,0:T(8,128)(2,1)S(1)}, u32[]{:S(2)}, u32[]{:S(2)}) collective-permute-start(bf16[16,512]{1,0:T(8,128)(2,1)S(1)} %get-tuple-element.33), channel_id=1, source_target_pairs={{0,64},{64,128},{128,192},{1,65},{65,129},{129,193},{2,66},{66,130... | collective-permute-start | bytes 49160 | tf_op jit(solution)/shard_map/ppermute | solution.py:29
  125.3 3.9 %collective-permute-start.27 = (bf16[16,512]{1,0:T(8,128)(2,1)S(1)}, bf16[16,512]{1,0:T(8,128)(2,1)S(1)}, u32[]{:S(2)}, u32[]{:S(2)}) collective-permute-start(bf16[16,512]{1,0:T(8,128)(2,1)S(1)} %get-tuple-element.33), channel_id=1, source_target_pairs={{64,0},{128,64},{192,128},{65,1},{129,65},{193,129},{66,2},{130,66... | collective-permute-start | bytes 49160 | tf_op jit(solution)/shard_map/ppermute | solution.py:30
  129.3 2.1 %collective-permute-start.29 = (bf16[16,512]{1,0:T(8,128)(2,1)S(1)}, bf16[16,512]{1,0:T(8,128)(2,1)S(1)}, u32[]{:S(2)}, u32[]{:S(2)}) collective-permute-start(bf16[16,512]{1,0:T(8,128)(2,1)S(1)} %get-tuple-element.33), channel_id=1, source_target_pairs={{1,2},{2,1},{3,4},{4,3},{5,6},{6,5},{7,8},{8,7},{9,10},{10,9},{11,... | collective-permute-start | bytes 49160 | tf_op jit(solution)/shard_map/ppermute | solution.py:32
  131.4 5.1 %collective-permute-done.29 = bf16[16,512]{1,0:T(8,128)(2,1)S(1)} collective-permute-done((bf16[16,512]{1,0:T(8,128)(2,1)S(1)}, bf16[16,512]{1,0:T(8,128)(2,1)S(1)}, u32[]{:S(2)}, u32[]{:S(2)}) %collective-permute-start.29) | collective-permute-done | bytes 16416 | tf_op jit(solution)/shard_map/ppermute | solution.py:32
  136.6 0.3 fusion
  136.9 0.3 fusion.1
  137.3 0.7 reshape.92
  (58 shorter events, 1.1 us)
Async XLA Ops:
  0.0 1.3 copy-start
  0.0 2.6 %copy-start.8 = (s32[1,8,64]{2,1,0:T(8,128)S(1)}, s32[1,8,64]{2,1,0:T(8,128)}, u32[]{:S(2)}) copy-start(s32[1,8,64]{2,1,0:T(8,128)} %param.14) | copy-start | bytes 6148
  0.0 16.8 %copy-start.6 = (f32[1,3,4,512]{3,2,1,0:T(4,128)S(1)}, f32[1,3,4,512]{3,2,1,0:T(4,128)}, u32[]{:S(2)}) copy-start(f32[1,3,4,512]{3,2,1,0:T(4,128)} %param.15) | copy-start | bytes 73732
  0.0 19.7 %copy-start.1 = (bf16[1,3,512,512]{3,2,1,0:T(8,128)(2,1)S(1)}, bf16[1,3,512,512]{3,2,1,0:T(8,128)(2,1)}, u32[]{:S(2)}) copy-start(bf16[1,3,512,512]{3,2,1,0:T(8,128)(2,1)} %param.18) | copy-start | bytes 4718596
  3.0 13.8 %collective-permute-start = (f32[16,512]{1,0:T(8,128)S(1)}, f32[16,512]{1,0:T(8,128)S(1)}, u32[]{:S(2)}, u32[]{:S(2)}) collective-permute-start(f32[16,512]{1,0:T(8,128)S(1)} %reshape.88), channel_id=1, source_target_pairs={{0,64},{64,128},{128,192},{1,65},{65,129},{129,193},{2,66},{66,130... | collective-permute-start | bytes 98312 | tf_op jit(solution)/shard_map/ppermute | solution.py:29
  6.5 10.4 %collective-permute-start.1 = (f32[16,512]{1,0:T(8,128)S(1)}, f32[16,512]{1,0:T(8,128)S(1)}, u32[]{:S(2)}, u32[]{:S(2)}) collective-permute-start(f32[16,512]{1,0:T(8,128)S(1)} %reshape.88), channel_id=1, source_target_pairs={{64,0},{128,64},{192,128},{65,1},{129,65},{193,129},{66,2},{130,66... | collective-permute-start | bytes 98312 | tf_op jit(solution)/shard_map/ppermute | solution.py:30
  8.9 8.0 %collective-permute-start.2 = (f32[16,512]{1,0:T(8,128)S(1)}, f32[16,512]{1,0:T(8,128)S(1)}, u32[]{:S(2)}, u32[]{:S(2)}) collective-permute-start(f32[16,512]{1,0:T(8,128)S(1)} %reshape.88), channel_id=1, source_target_pairs={{0,1},{1,0},{2,3},{3,2},{4,5},{5,4},{6,7},{7,6},{8,9},{9,8},{10,11... | collective-permute-start | bytes 98312 | tf_op jit(solution)/shard_map/ppermute | solution.py:33
  9.0 9.4 %collective-permute-start.3 = (f32[16,512]{1,0:T(8,128)S(1)}, f32[16,512]{1,0:T(8,128)S(1)}, u32[]{:S(2)}, u32[]{:S(2)}) collective-permute-start(f32[16,512]{1,0:T(8,128)S(1)} %reshape.88), channel_id=1, source_target_pairs={{1,2},{2,1},{3,4},{4,3},{5,6},{6,5},{7,8},{8,7},{9,10},{10,9},{11,... | collective-permute-start | bytes 98312 | tf_op jit(solution)/shard_map/ppermute | solution.py:32
  16.9 17.0 %copy-start.2 = (bf16[1,3,512,512]{3,2,1,0:T(8,128)(2,1)S(1)}, bf16[1,3,512,512]{3,2,1,0:T(8,128)(2,1)}, u32[]{:S(2)}) copy-start(bf16[1,3,512,512]{3,2,1,0:T(8,128)(2,1)} %param.17) | copy-start | bytes 4718596
  18.4 1.3 collective-permute-start.4
  19.7 36.2 %copy-start.5 = (bf16[1,32,512]{2,1,0:T(8,128)(2,1)S(1)}, bf16[1,32,512]{2,1,0:T(8,128)(2,1)}, u32[]{:S(2)}) copy-start(bf16[1,32,512]{2,1,0:T(8,128)(2,1)} %param.20) | copy-start | bytes 98308
  19.9 12.2 %collective-permute-start.5 = (f32[16,512]{1,0:T(8,128)S(1)}, f32[16,512]{1,0:T(8,128)S(1)}, u32[]{:S(2)}, u32[]{:S(2)}) collective-permute-start(f32[16,512]{1,0:T(8,128)S(1)} %convolution_add_fusion.5), channel_id=1, source_target_pairs={{0,64},{64,128},{128,192},{1,65},{65,129},{129,193},{2,66},{66,130... | collective-permute-start | bytes 98312 | tf_op jit(solution)/shard_map/ppermute | solution.py:29
  23.4 8.7 %collective-permute-start.6 = (f32[16,512]{1,0:T(8,128)S(1)}, f32[16,512]{1,0:T(8,128)S(1)}, u32[]{:S(2)}, u32[]{:S(2)}) collective-permute-start(f32[16,512]{1,0:T(8,128)S(1)} %convolution_add_fusion.5), channel_id=1, source_target_pairs={{64,0},{128,64},{192,128},{65,1},{129,65},{193,129},{66,2},{130,66... | collective-permute-start | bytes 98312 | tf_op jit(solution)/shard_map/ppermute | solution.py:30
  25.8 6.4 %collective-permute-start.7 = (f32[16,512]{1,0:T(8,128)S(1)}, f32[16,512]{1,0:T(8,128)S(1)}, u32[]{:S(2)}, u32[]{:S(2)}) collective-permute-start(f32[16,512]{1,0:T(8,128)S(1)} %convolution_add_fusion.5), channel_id=1, source_target_pairs={{0,1},{1,0},{2,3},{3,2},{4,5},{5,4},{6,7},{7,6},{8,9},{9,8},{10,11... | collective-permute-start | bytes 98312 | tf_op jit(solution)/shard_map/ppermute | solution.py:33
  25.9 7.8 %collective-permute-start.8 = (f32[16,512]{1,0:T(8,128)S(1)}, f32[16,512]{1,0:T(8,128)S(1)}, u32[]{:S(2)}, u32[]{:S(2)}) collective-permute-start(f32[16,512]{1,0:T(8,128)S(1)} %convolution_add_fusion.5), channel_id=1, source_target_pairs={{1,2},{2,1},{3,4},{4,3},{5,6},{6,5},{7,8},{8,7},{9,10},{10,9},{11,... | collective-permute-start | bytes 98312 | tf_op jit(solution)/shard_map/ppermute | solution.py:32
  33.7 3.8 %collective-permute-start.9 = (bf16[16,512]{1,0:T(8,128)(2,1)S(1)}, bf16[16,512]{1,0:T(8,128)(2,1)S(1)}, u32[]{:S(2)}, u32[]{:S(2)}) collective-permute-start(bf16[16,512]{1,0:T(8,128)(2,1)S(1)} %subtract_convert_fusion.3), channel_id=1, source_target_pairs={{0,2},{1,3},{2,0},{3,1},{4,6},{5,7},{6,4},{7,5},{8,10},{9,11},{10,... | collective-permute-start | bytes 49160 | tf_op jit(solution)/shard_map/ppermute | solution.py:47
  37.7 10.0 %collective-permute-start.10 = (f32[16,512]{1,0:T(8,128)S(1)}, f32[16,512]{1,0:T(8,128)S(1)}, u32[]{:S(2)}, u32[]{:S(2)}) collective-permute-start(f32[16,512]{1,0:T(8,128)S(1)} %convolution_add_fusion.4), channel_id=1, source_target_pairs={{0,64},{64,128},{128,192},{1,65},{65,129},{129,193},{2,66},{66,130... | collective-permute-start | bytes 98312 | tf_op jit(solution)/shard_map/ppermute | solution.py:29
  41.2 6.5 %collective-permute-start.11 = (f32[16,512]{1,0:T(8,128)S(1)}, f32[16,512]{1,0:T(8,128)S(1)}, u32[]{:S(2)}, u32[]{:S(2)}) collective-permute-start(f32[16,512]{1,0:T(8,128)S(1)} %convolution_add_fusion.4), channel_id=1, source_target_pairs={{64,0},{128,64},{192,128},{65,1},{129,65},{193,129},{66,2},{130,66... | collective-permute-start | bytes 98312 | tf_op jit(solution)/shard_map/ppermute | solution.py:30
  43.6 4.2 %collective-permute-start.12 = (f32[16,512]{1,0:T(8,128)S(1)}, f32[16,512]{1,0:T(8,128)S(1)}, u32[]{:S(2)}, u32[]{:S(2)}) collective-permute-start(f32[16,512]{1,0:T(8,128)S(1)} %convolution_add_fusion.4), channel_id=1, source_target_pairs={{0,1},{1,0},{2,3},{3,2},{4,5},{5,4},{6,7},{7,6},{8,9},{9,8},{10,11... | collective-permute-start | bytes 98312 | tf_op jit(solution)/shard_map/ppermute | solution.py:33
  43.7 7.3 %collective-permute-start.13 = (f32[16,512]{1,0:T(8,128)S(1)}, f32[16,512]{1,0:T(8,128)S(1)}, u32[]{:S(2)}, u32[]{:S(2)}) collective-permute-start(f32[16,512]{1,0:T(8,128)S(1)} %convolution_add_fusion.4), channel_id=1, source_target_pairs={{1,2},{2,1},{3,4},{4,3},{5,6},{6,5},{7,8},{8,7},{9,10},{10,9},{11,... | collective-permute-start | bytes 98312 | tf_op jit(solution)/shard_map/ppermute | solution.py:32
  51.0 4.7 %collective-permute-start.14 = (bf16[16,512]{1,0:T(8,128)(2,1)S(1)}, bf16[16,512]{1,0:T(8,128)(2,1)S(1)}, u32[]{:S(2)}, u32[]{:S(2)}) collective-permute-start(bf16[16,512]{1,0:T(8,128)(2,1)S(1)} %subtract_convert_fusion.2), channel_id=1, source_target_pairs={{0,4},{1,5},{2,6},{3,7},{4,0},{5,1},{6,2},{7,3},{8,12},{9,13},{10,... | collective-permute-start | bytes 49160 | tf_op jit(solution)/shard_map/ppermute | solution.py:47
  72.9 10.4 %all-to-all-start.1 = ((bf16[4,16,2048]{2,1,0:T(8,128)(2,1)}), bf16[4,16,2048]{2,1,0:T(8,128)(2,1)S(1)}, u32[]{:S(2)}, u32[]{:S(2)}) async-start(bf16[4,16,2048]{2,1,0:T(8,128)(2,1)} %broadcast_in_dim.7), calls=%async_computation.1 | async-start | bytes 524288 | tf_op jit(solution)/shard_map/all_to_all | solution.py:52
  77.9 22.7 %copy-start.7 = (f32[1,3,4,512]{3,2,1,0:T(4,128)S(1)}, f32[1,3,4,512]{3,2,1,0:T(4,128)}, u32[]{:S(2)}) copy-start(f32[1,3,4,512]{3,2,1,0:T(4,128)} %param.16) | copy-start | bytes 73732
  84.8 23.5 %copy-start.3 = (bf16[1,3,512,512]{3,2,1,0:T(8,128)(2,1)S(1)}, bf16[1,3,512,512]{3,2,1,0:T(8,128)(2,1)}, u32[]{:S(2)}) copy-start(bf16[1,3,512,512]{3,2,1,0:T(8,128)(2,1)} %param.17) | copy-start | bytes 4718596
  85.0 4.7 %collective-permute-start.15 = (bf16[16,512]{1,0:T(8,128)(2,1)S(1)}, bf16[16,512]{1,0:T(8,128)(2,1)S(1)}, u32[]{:S(2)}, u32[]{:S(2)}) collective-permute-start(bf16[16,512]{1,0:T(8,128)(2,1)S(1)} %convolution_convert_fusion.4), channel_id=1, source_target_pairs={{0,4},{1,5},{2,6},{3,7},{4,0},{5,1},{6,2},{7,3},{8,12},{9,13},{10,... | collective-permute-start | bytes 49160 | tf_op jit(solution)/shard_map/ppermute | solution.py:47
  91.0 45.6 %copy-start.4 = (bf16[1,8,64,256]{3,2,1,0:T(8,128)(2,1)S(1)}, bf16[1,8,64,256]{3,2,1,0:T(8,128)(2,1)}, u32[]{:S(2)}) copy-start(bf16[1,8,64,256]{3,2,1,0:T(8,128)(2,1)} %param.13) | copy-start | bytes 786436
  91.0 9.6 %collective-permute-start.16 = (bf16[16,512]{1,0:T(8,128)(2,1)S(1)}, bf16[16,512]{1,0:T(8,128)(2,1)S(1)}, u32[]{:S(2)}, u32[]{:S(2)}) collective-permute-start(bf16[16,512]{1,0:T(8,128)(2,1)S(1)} %get-tuple-element.29), channel_id=1, source_target_pairs={{0,64},{64,128},{128,192},{1,65},{65,129},{129,193},{2,66},{66,130... | collective-permute-start | bytes 49160 | tf_op jit(solution)/shard_map/ppermute | solution.py:29
  93.0 7.5 %collective-permute-start.17 = (bf16[16,512]{1,0:T(8,128)(2,1)S(1)}, bf16[16,512]{1,0:T(8,128)(2,1)S(1)}, u32[]{:S(2)}, u32[]{:S(2)}) collective-permute-start(bf16[16,512]{1,0:T(8,128)(2,1)S(1)} %get-tuple-element.29), channel_id=1, source_target_pairs={{64,0},{128,64},{192,128},{65,1},{129,65},{193,129},{66,2},{130,66... | collective-permute-start | bytes 49160 | tf_op jit(solution)/shard_map/ppermute | solution.py:30
  97.0 3.6 %collective-permute-start.18 = (bf16[16,512]{1,0:T(8,128)(2,1)S(1)}, bf16[16,512]{1,0:T(8,128)(2,1)S(1)}, u32[]{:S(2)}, u32[]{:S(2)}) collective-permute-start(bf16[16,512]{1,0:T(8,128)(2,1)S(1)} %get-tuple-element.29), channel_id=1, source_target_pairs={{0,1},{1,0},{2,3},{3,2},{4,5},{5,4},{6,7},{7,6},{8,9},{9,8},{10,11... | collective-permute-start | bytes 49160 | tf_op jit(solution)/shard_map/ppermute | solution.py:33
  97.1 7.2 %collective-permute-start.19 = (bf16[16,512]{1,0:T(8,128)(2,1)S(1)}, bf16[16,512]{1,0:T(8,128)(2,1)S(1)}, u32[]{:S(2)}, u32[]{:S(2)}) collective-permute-start(bf16[16,512]{1,0:T(8,128)(2,1)S(1)} %get-tuple-element.29), channel_id=1, source_target_pairs={{1,2},{2,1},{3,4},{4,3},{5,6},{6,5},{7,8},{8,7},{9,10},{10,9},{11,... | collective-permute-start | bytes 49160 | tf_op jit(solution)/shard_map/ppermute | solution.py:32
  104.5 3.8 %collective-permute-start.20 = (bf16[16,512]{1,0:T(8,128)(2,1)S(1)}, bf16[16,512]{1,0:T(8,128)(2,1)S(1)}, u32[]{:S(2)}, u32[]{:S(2)}) collective-permute-start(bf16[16,512]{1,0:T(8,128)(2,1)S(1)} %convolution_convert_fusion.3), channel_id=1, source_target_pairs={{0,2},{1,3},{2,0},{3,1},{4,6},{5,7},{6,4},{7,5},{8,10},{9,11},{10,... | collective-permute-start | bytes 49160 | tf_op jit(solution)/shard_map/ppermute | solution.py:47
  108.5 7.9 %collective-permute-start.21 = (bf16[16,512]{1,0:T(8,128)(2,1)S(1)}, bf16[16,512]{1,0:T(8,128)(2,1)S(1)}, u32[]{:S(2)}, u32[]{:S(2)}) collective-permute-start(bf16[16,512]{1,0:T(8,128)(2,1)S(1)} %get-tuple-element.31), channel_id=1, source_target_pairs={{0,64},{64,128},{128,192},{1,65},{65,129},{129,193},{2,66},{66,130... | collective-permute-start | bytes 49160 | tf_op jit(solution)/shard_map/ppermute | solution.py:29
  110.4 6.0 %collective-permute-start.22 = (bf16[16,512]{1,0:T(8,128)(2,1)S(1)}, bf16[16,512]{1,0:T(8,128)(2,1)S(1)}, u32[]{:S(2)}, u32[]{:S(2)}) collective-permute-start(bf16[16,512]{1,0:T(8,128)(2,1)S(1)} %get-tuple-element.31), channel_id=1, source_target_pairs={{64,0},{128,64},{192,128},{65,1},{129,65},{193,129},{66,2},{130,66... | collective-permute-start | bytes 49160 | tf_op jit(solution)/shard_map/ppermute | solution.py:30
  114.4 2.1 %collective-permute-start.23 = (bf16[16,512]{1,0:T(8,128)(2,1)S(1)}, bf16[16,512]{1,0:T(8,128)(2,1)S(1)}, u32[]{:S(2)}, u32[]{:S(2)}) collective-permute-start(bf16[16,512]{1,0:T(8,128)(2,1)S(1)} %get-tuple-element.31), channel_id=1, source_target_pairs={{0,1},{1,0},{2,3},{3,2},{4,5},{5,4},{6,7},{7,6},{8,9},{9,8},{10,11... | collective-permute-start | bytes 49160 | tf_op jit(solution)/shard_map/ppermute | solution.py:33
  114.5 7.2 %collective-permute-start.24 = (bf16[16,512]{1,0:T(8,128)(2,1)S(1)}, bf16[16,512]{1,0:T(8,128)(2,1)S(1)}, u32[]{:S(2)}, u32[]{:S(2)}) collective-permute-start(bf16[16,512]{1,0:T(8,128)(2,1)S(1)} %get-tuple-element.31), channel_id=1, source_target_pairs={{1,2},{2,1},{3,4},{4,3},{5,6},{6,5},{7,8},{8,7},{9,10},{10,9},{11,... | collective-permute-start | bytes 49160 | tf_op jit(solution)/shard_map/ppermute | solution.py:32
  121.9 1.2 collective-permute-start.25
  123.3 8.0 %collective-permute-start.26 = (bf16[16,512]{1,0:T(8,128)(2,1)S(1)}, bf16[16,512]{1,0:T(8,128)(2,1)S(1)}, u32[]{:S(2)}, u32[]{:S(2)}) collective-permute-start(bf16[16,512]{1,0:T(8,128)(2,1)S(1)} %get-tuple-element.33), channel_id=1, source_target_pairs={{0,64},{64,128},{128,192},{1,65},{65,129},{129,193},{2,66},{66,130... | collective-permute-start | bytes 49160 | tf_op jit(solution)/shard_map/ppermute | solution.py:29
  125.3 6.1 %collective-permute-start.27 = (bf16[16,512]{1,0:T(8,128)(2,1)S(1)}, bf16[16,512]{1,0:T(8,128)(2,1)S(1)}, u32[]{:S(2)}, u32[]{:S(2)}) collective-permute-start(bf16[16,512]{1,0:T(8,128)(2,1)S(1)} %get-tuple-element.33), channel_id=1, source_target_pairs={{64,0},{128,64},{192,128},{65,1},{129,65},{193,129},{66,2},{130,66... | collective-permute-start | bytes 49160 | tf_op jit(solution)/shard_map/ppermute | solution.py:30
  129.2 2.2 %collective-permute-start.28 = (bf16[16,512]{1,0:T(8,128)(2,1)S(1)}, bf16[16,512]{1,0:T(8,128)(2,1)S(1)}, u32[]{:S(2)}, u32[]{:S(2)}) collective-permute-start(bf16[16,512]{1,0:T(8,128)(2,1)S(1)} %get-tuple-element.33), channel_id=1, source_target_pairs={{0,1},{1,0},{2,3},{3,2},{4,5},{5,4},{6,7},{7,6},{8,9},{9,8},{10,11... | collective-permute-start | bytes 49160 | tf_op jit(solution)/shard_map/ppermute | solution.py:33
  129.3 7.2 %collective-permute-start.29 = (bf16[16,512]{1,0:T(8,128)(2,1)S(1)}, bf16[16,512]{1,0:T(8,128)(2,1)S(1)}, u32[]{:S(2)}, u32[]{:S(2)}) collective-permute-start(bf16[16,512]{1,0:T(8,128)(2,1)S(1)} %get-tuple-element.33), channel_id=1, source_target_pairs={{1,2},{2,1},{3,4},{4,3},{5,6},{6,5},{7,8},{8,7},{9,10},{10,9},{11,... | collective-permute-start | bytes 49160 | tf_op jit(solution)/shard_map/ppermute | solution.py:32

commit v6 on v5

--- a/solution.py
+++ b/solution.py
@@ -24,16 +24,18 @@
     return shard
 
 
+def both_sides(shard, axis):
+    size = lax.axis_size(axis)
+    pairs = [(i, i + 1) if i % 2 else (i, i - 1) for i in range(size)]
+    across = lax.ppermute(shard, axis, [(a, b) for a, b in pairs if 0 <= b < size])
+    beside = lax.ppermute(shard, axis, [(i, i ^ 1) for i in range(size)])
+    odd = lax.axis_index(axis) % 2 == 1
+    return jnp.where(odd, beside, across), jnp.where(odd, across, beside)
+
+
 def neighbours_of(shard):
-    rows, cols = (lax.axis_size("gy"), lax.axis_size("gx"))
-    from_below = lax.ppermute(shard, "gy", [(i, i + 1) for i in range(rows - 1)])
-    from_above = lax.ppermute(shard, "gy", [(i + 1, i) for i in range(rows - 1)])
-    pairs = [(i, i + 1) if i % 2 else (i, i - 1) for i in range(cols)]
-    across = lax.ppermute(shard, "gx", [(a, b) for a, b in pairs if 0 <= b < cols])
-    beside = lax.ppermute(shard, "gx", [(i, i ^ 1) for i in range(cols)])
-    odd = lax.axis_index("gx") % 2 == 1
-    left = jnp.where(odd, beside, across)
-    right = jnp.where(odd, across, beside)
+    from_below, from_above = both_sides(shard, "gy")
+    left, right = both_sides(shard, "gx")
     return from_below, from_above, left, right
 
 

time: 139 us -> 124 us (0.89)
  starting transfers between devices: 67.4 us -> 52.9 us
    ppermute x24, starting transfers between devices: 61.3 us -> 47.4 us  [the longest x12 43.4 us: both_sides(): lax.ppermute(shard, axis, [(a, b) for a, b in pairs if 0 <= b < size])]
  transfers between devices with their start and end apart: 31 -> 31, of which waited for: 12 -> 13; matrix products, arithmetic and copies ran while one was open for 2% -> 2% of each run, Pallas kernels for 0% -> 0%
where the time goes in v6:
time: 124 us; the launch traced here: 123 us
  starting transfers between devices  52.9 us (43%)
  waiting for transfers between devices  40.7 us (33%)
  blocking collectives  15.6 us (13%)
  matrix products  9.52 us (8%)
  local copies, waits for them, and re-layouts  3.77 us (3%)
    ppermute x12, starting transfers between devices, both_sides(): lax.ppermute(shard, axis, [(a, b) for a, b in pairs if 0 <= b < size])  43.4 us
    ppermute x12, waiting for transfers between devices, both_sides(): lax.ppermute(shard, axis, [(a, b) for a, b in pairs if 0 <= b < size])  19.8 us
    ppermute x6, waiting for transfers between devices, partner_2(): lax.ppermute(shard, axis, [(i, i ^ 1 << stride) for i in range(lax.axis_s...  16.7 us
    all_to_all x1, blocking collectives, sent_to_all(): return lax.all_to_all(copies, axis, split_axis=0, concat_axis=0, tiled=True)  15.6 us
    all_to_all x1, starting transfers between devices, sent_to_all(): return lax.all_to_all(copies, axis, split_axis=0, concat_axis=0, tiled=True)  4.28 us
    all_to_all x1, waiting for transfers between devices, sent_to_all(): return lax.all_to_all(copies, axis, split_axis=0, concat_axis=0, tiled=True)  4.27 us
    ppermute x12, starting transfers between devices, both_sides(): beside = lax.ppermute(shard, axis, [(i, i ^ 1) for i in range(size)])  3.98 us
    dot_general x7, matrix products, right_transpose(): lax.dot_general(values, matrix, (((1,), (1,)), ((), ())), preferred_eleme...  2.58 us
  transfers between devices with their start and end apart: 31, of which 13 were waited for; matrix products, arithmetic and copies ran while one was open for 2% of the time, Pallas kernels for 0%

profile of v6, /device:TPU:10, one launch (start us, length us, event | category | flops | bytes accessed | tf_op | source)
XLA Modules:
  0.0 123.1 jit_solution(8351102786666538671)
XLA Ops:
  0.0 1.0 copy.29
  1.0 0.2 copy-done
  1.3 0.2 fusion.3
  1.5 1.1 convolution_bitcast_fusion.2
  2.6 0.3 fusion.4
  3.0 0.5 collective-permute-start
  3.5 4.3 %collective-permute-start.1 = (f32[16,512]{1,0:T(8,128)S(1)}, f32[16,512]{1,0:T(8,128)S(1)}, u32[]{:S(2)}, u32[]{:S(2)}) collective-permute-start(f32[16,512]{1,0:T(8,128)S(1)} %reshape.88), channel_id=1, source_target_pairs={{64,128},{128,64},{65,129},{129,65},{66,130},{130,66},{67,131},{13... | collective-permute-start | bytes 98312 | tf_op jit(solution)/shard_map/ppermute | solution.py:30
  7.8 0.1 collective-permute-start.2
  7.9 7.8 %collective-permute-start.3 = (f32[16,512]{1,0:T(8,128)S(1)}, f32[16,512]{1,0:T(8,128)S(1)}, u32[]{:S(2)}, u32[]{:S(2)}) collective-permute-start(f32[16,512]{1,0:T(8,128)S(1)} %reshape.88), channel_id=1, source_target_pairs={{1,2},{2,1},{3,4},{4,3},{5,6},{6,5},{7,8},{8,7},{9,10},{10,9},{11,... | collective-permute-start | bytes 98312 | tf_op jit(solution)/shard_map/ppermute | solution.py:30
  15.9 1.5 %collective-permute-done.3 = f32[16,512]{1,0:T(8,128)S(1)} collective-permute-done((f32[16,512]{1,0:T(8,128)S(1)}, f32[16,512]{1,0:T(8,128)S(1)}, u32[]{:S(2)}, u32[]{:S(2)}) %collective-permute-start.3) | collective-permute-done | bytes 32800 | tf_op jit(solution)/shard_map/ppermute | solution.py:30
  17.5 1.2 fusion.25
  18.7 0.2 convolution_add_fusion.5
  18.9 1.9 %collective-permute-start.6 = (f32[16,512]{1,0:T(8,128)S(1)}, f32[16,512]{1,0:T(8,128)S(1)}, u32[]{:S(2)}, u32[]{:S(2)}) collective-permute-start(f32[16,512]{1,0:T(8,128)S(1)} %convolution_add_fusion.5), channel_id=1, source_target_pairs={{64,128},{128,64},{65,129},{129,65},{66,130},{130,66},{67,131},{13... | collective-permute-start | bytes 98312 | tf_op jit(solution)/shard_map/ppermute | solution.py:30
  20.8 0.6 collective-permute-start.7
  21.4 5.7 %collective-permute-start.8 = (f32[16,512]{1,0:T(8,128)S(1)}, f32[16,512]{1,0:T(8,128)S(1)}, u32[]{:S(2)}, u32[]{:S(2)}) collective-permute-start(f32[16,512]{1,0:T(8,128)S(1)} %convolution_add_fusion.5), channel_id=1, source_target_pairs={{1,2},{2,1},{3,4},{4,3},{5,6},{6,5},{7,8},{8,7},{9,10},{10,9},{11,... | collective-permute-start | bytes 98312 | tf_op jit(solution)/shard_map/ppermute | solution.py:30
  27.2 1.6 %collective-permute-done.8 = f32[16,512]{1,0:T(8,128)S(1)} collective-permute-done((f32[16,512]{1,0:T(8,128)S(1)}, f32[16,512]{1,0:T(8,128)S(1)}, u32[]{:S(2)}, u32[]{:S(2)}) %collective-permute-start.8) | collective-permute-done | bytes 32800 | tf_op jit(solution)/shard_map/ppermute | solution.py:30
  28.7 0.1 collective-permute-start.9
  28.9 0.2 fusion.20
  29.0 3.5 %collective-permute-done.9 = bf16[16,512]{1,0:T(8,128)(2,1)S(1)} collective-permute-done((bf16[16,512]{1,0:T(8,128)(2,1)S(1)}, bf16[16,512]{1,0:T(8,128)(2,1)S(1)}, u32[]{:S(2)}, u32[]{:S(2)}) %collective-permute-start.9) | collective-permute-done | bytes 16416 | tf_op jit(solution)/shard_map/ppermute | solution.py:49
  32.6 0.2 convolution_add_fusion.4
  32.7 0.8 collective-permute-start.10
  33.5 3.1 %collective-permute-start.11 = (f32[16,512]{1,0:T(8,128)S(1)}, f32[16,512]{1,0:T(8,128)S(1)}, u32[]{:S(2)}, u32[]{:S(2)}) collective-permute-start(f32[16,512]{1,0:T(8,128)S(1)} %convolution_add_fusion.4), channel_id=1, source_target_pairs={{64,128},{128,64},{65,129},{129,65},{66,130},{130,66},{67,131},{13... | collective-permute-start | bytes 98312 | tf_op jit(solution)/shard_map/ppermute | solution.py:30
  36.7 0.1 collective-permute-start.12
  36.8 4.3 %collective-permute-start.13 = (f32[16,512]{1,0:T(8,128)S(1)}, f32[16,512]{1,0:T(8,128)S(1)}, u32[]{:S(2)}, u32[]{:S(2)}) collective-permute-start(f32[16,512]{1,0:T(8,128)S(1)} %convolution_add_fusion.4), channel_id=1, source_target_pairs={{1,2},{2,1},{3,4},{4,3},{5,6},{6,5},{7,8},{8,7},{9,10},{10,9},{11,... | collective-permute-start | bytes 98312 | tf_op jit(solution)/shard_map/ppermute | solution.py:30
  41.1 3.0 %collective-permute-done.13 = f32[16,512]{1,0:T(8,128)S(1)} collective-permute-done((f32[16,512]{1,0:T(8,128)S(1)}, f32[16,512]{1,0:T(8,128)S(1)}, u32[]{:S(2)}, u32[]{:S(2)}) %collective-permute-start.13) | collective-permute-done | bytes 32800 | tf_op jit(solution)/shard_map/ppermute | solution.py:30
  44.2 0.2 fusion.15
  44.4 4.5 %collective-permute-done.14 = bf16[16,512]{1,0:T(8,128)(2,1)S(1)} collective-permute-done((bf16[16,512]{1,0:T(8,128)(2,1)S(1)}, bf16[16,512]{1,0:T(8,128)(2,1)S(1)}, u32[]{:S(2)}, u32[]{:S(2)}) %collective-permute-start.14) | collective-permute-done | bytes 16416 | tf_op jit(solution)/shard_map/ppermute | solution.py:49
  48.9 0.2 fusion.6
  49.0 0.1 convolution_convert_fusion.6
  49.2 0.2 reshape.93
  49.4 15.6 %all_to_all.10 = bf16[64,2,256]{2,1,0:T(2,128)(2,1)S(1)} all-to-all(bf16[64,2,256]{2,1,0:T(2,128)(2,1)S(1)} %reshape.93), channel_id=1, replica_groups=mesh['gy'=4,'gx'=64] {'gx'}, dimensions={0} | all-to-all | bytes 131072 | tf_op jit(solution)/shard_map/all_to_all | solution.py:54
  65.0 0.2 reshape.94
  65.2 0.3 reshape.89
  65.5 0.7 broadcast_in_dim.7
  66.2 4.3 %all-to-all-start.1 = ((bf16[4,16,2048]{2,1,0:T(8,128)(2,1)}), bf16[4,16,2048]{2,1,0:T(8,128)(2,1)S(1)}, u32[]{:S(2)}, u32[]{:S(2)}) async-start(bf16[4,16,2048]{2,1,0:T(8,128)(2,1)} %broadcast_in_dim.7), calls=%async_computation.1 | async-start | bytes 524288 | tf_op jit(solution)/shard_map/all_to_all | solution.py:54
  70.5 1.2 fusion.9
  71.7 4.3 %all-to-all-done.1 = bf16[4,16,2048]{2,1,0:T(8,128)(2,1)S(1)} async-done(((bf16[4,16,2048]{2,1,0:T(8,128)(2,1)}), bf16[4,16,2048]{2,1,0:T(8,128)(2,1)S(1)}, u32[]{:S(2)}, u32[]{:S(2)}) %all-to-all-start.1) | async-done | bytes 262176 | tf_op jit(solution)/shard_map/all_to_all | solution.py:54
  76.0 1.4 %fusion.5 = bf16[16,512]{1,0:T(8,128)(2,1)S(1)} fusion(f32[16,512]{1,0:T(8,128)S(1)} %fusion.9, bf16[16,8192]{1,0:T(8,128)(2,1)S(1)} %bitcast.126, bf16[8192,32]{0,1:T(8,128)(2,1)} %param.21, bf16[1,32,512]{2,1,0:T(8,128)(2,1)S(1)} %copy-done.5), kind=kOutput, calls=%fused_computation.17 | convolution fusion | flops 8929792 | bytes 868352 | tf_op jit(solution)/shard_map/dot_general | solution.py:128
  77.5 0.2 convolution_convert_fusion.4
  77.7 1.0 collective-permute-start.15
  78.7 3.7 %collective-permute-done.15 = bf16[16,512]{1,0:T(8,128)(2,1)S(1)} collective-permute-done((bf16[16,512]{1,0:T(8,128)(2,1)S(1)}, bf16[16,512]{1,0:T(8,128)(2,1)S(1)}, u32[]{:S(2)}, u32[]{:S(2)}) %collective-permute-start.15) | collective-permute-done | bytes 16416 | tf_op jit(solution)/shard_map/ppermute | solution.py:49
  82.4 1.3 %fusion.49 = (bf16[16,512]{1,0:T(8,128)(2,1)S(1)}, f32[16,512]{1,0:T(8,128)S(1)}) fusion(bf16[16,512]{1,0:T(8,128)(2,1)S(1)} %collective-permute-done.15, bf16[16,512]{1,0:T(8,128)(2,1)S(1)} %fusion.5, bf16[1,3,512,512]{3,2,1,0:T(8,128)(2,1)} %param.17), kind=kOutput, calls=%fused_computation.74 | convolution fusion | flops 8413184 | bytes 606208 | tf_op jit(solution)/shard_map/dot_general | solution.py:74
  83.6 1.5 %collective-permute-start.16 = (bf16[16,512]{1,0:T(8,128)(2,1)S(1)}, bf16[16,512]{1,0:T(8,128)(2,1)S(1)}, u32[]{:S(2)}, u32[]{:S(2)}) collective-permute-start(bf16[16,512]{1,0:T(8,128)(2,1)S(1)} %get-tuple-element.29), channel_id=1, source_target_pairs={{0,64},{64,0},{128,192},{192,128},{1,65},{65,1},{129,193},{193,129... | collective-permute-start | bytes 49160 | tf_op jit(solution)/shard_map/ppermute | solution.py:31
  85.1 2.5 %collective-permute-start.17 = (bf16[16,512]{1,0:T(8,128)(2,1)S(1)}, bf16[16,512]{1,0:T(8,128)(2,1)S(1)}, u32[]{:S(2)}, u32[]{:S(2)}) collective-permute-start(bf16[16,512]{1,0:T(8,128)(2,1)S(1)} %get-tuple-element.29), channel_id=1, source_target_pairs={{64,128},{128,64},{65,129},{129,65},{66,130},{130,66},{67,131},{13... | collective-permute-start | bytes 49160 | tf_op jit(solution)/shard_map/ppermute | solution.py:30
  87.7 3.5 %collective-permute-start.19 = (bf16[16,512]{1,0:T(8,128)(2,1)S(1)}, bf16[16,512]{1,0:T(8,128)(2,1)S(1)}, u32[]{:S(2)}, u32[]{:S(2)}) collective-permute-start(bf16[16,512]{1,0:T(8,128)(2,1)S(1)} %get-tuple-element.29), channel_id=1, source_target_pairs={{1,2},{2,1},{3,4},{4,3},{5,6},{6,5},{7,8},{8,7},{9,10},{10,9},{11,... | collective-permute-start | bytes 49160 | tf_op jit(solution)/shard_map/ppermute | solution.py:30
  91.2 3.6 %collective-permute-done.19 = bf16[16,512]{1,0:T(8,128)(2,1)S(1)} collective-permute-done((bf16[16,512]{1,0:T(8,128)(2,1)S(1)}, bf16[16,512]{1,0:T(8,128)(2,1)S(1)}, u32[]{:S(2)}, u32[]{:S(2)}) %collective-permute-start.19) | collective-permute-done | bytes 16416 | tf_op jit(solution)/shard_map/ppermute | solution.py:30
  94.9 0.2 convolution_convert_fusion.3
  95.1 3.8 %collective-permute-done.20 = bf16[16,512]{1,0:T(8,128)(2,1)S(1)} collective-permute-done((bf16[16,512]{1,0:T(8,128)(2,1)S(1)}, bf16[16,512]{1,0:T(8,128)(2,1)S(1)}, u32[]{:S(2)}, u32[]{:S(2)}) %collective-permute-start.20) | collective-permute-done | bytes 16416 | tf_op jit(solution)/shard_map/ppermute | solution.py:49
  98.9 0.2 fusion.52
  99.1 3.4 %collective-permute-start.22 = (bf16[16,512]{1,0:T(8,128)(2,1)S(1)}, bf16[16,512]{1,0:T(8,128)(2,1)S(1)}, u32[]{:S(2)}, u32[]{:S(2)}) collective-permute-start(bf16[16,512]{1,0:T(8,128)(2,1)S(1)} %get-tuple-element.31), channel_id=1, source_target_pairs={{64,128},{128,64},{65,129},{129,65},{66,130},{130,66},{67,131},{13... | collective-permute-start | bytes 49160 | tf_op jit(solution)/shard_map/ppermute | solution.py:30
  102.5 0.3 collective-permute-start.23
  102.8 2.0 %collective-permute-start.24 = (bf16[16,512]{1,0:T(8,128)(2,1)S(1)}, bf16[16,512]{1,0:T(8,128)(2,1)S(1)}, u32[]{:S(2)}, u32[]{:S(2)}) collective-permute-start(bf16[16,512]{1,0:T(8,128)(2,1)S(1)} %get-tuple-element.31), channel_id=1, source_target_pairs={{1,2},{2,1},{3,4},{4,3},{5,6},{6,5},{7,8},{8,7},{9,10},{10,9},{11,... | collective-permute-start | bytes 49160 | tf_op jit(solution)/shard_map/ppermute | solution.py:30
  104.9 5.1 %collective-permute-done.24 = bf16[16,512]{1,0:T(8,128)(2,1)S(1)} collective-permute-done((bf16[16,512]{1,0:T(8,128)(2,1)S(1)}, bf16[16,512]{1,0:T(8,128)(2,1)S(1)}, u32[]{:S(2)}, u32[]{:S(2)}) %collective-permute-start.24) | collective-permute-done | bytes 16416 | tf_op jit(solution)/shard_map/ppermute | solution.py:30
  110.0 0.2 convolution_convert_fusion.2
  110.2 1.2 collective-permute-done.25
  111.4 0.2 fusion.53
  111.7 2.7 %collective-permute-start.27 = (bf16[16,512]{1,0:T(8,128)(2,1)S(1)}, bf16[16,512]{1,0:T(8,128)(2,1)S(1)}, u32[]{:S(2)}, u32[]{:S(2)}) collective-permute-start(bf16[16,512]{1,0:T(8,128)(2,1)S(1)} %get-tuple-element.33), channel_id=1, source_target_pairs={{64,128},{128,64},{65,129},{129,65},{66,130},{130,66},{67,131},{13... | collective-permute-start | bytes 49160 | tf_op jit(solution)/shard_map/ppermute | solution.py:30
  114.5 2.2 %collective-permute-start.29 = (bf16[16,512]{1,0:T(8,128)(2,1)S(1)}, bf16[16,512]{1,0:T(8,128)(2,1)S(1)}, u32[]{:S(2)}, u32[]{:S(2)}) collective-permute-start(bf16[16,512]{1,0:T(8,128)(2,1)S(1)} %get-tuple-element.33), channel_id=1, source_target_pairs={{1,2},{2,1},{3,4},{4,3},{5,6},{6,5},{7,8},{8,7},{9,10},{10,9},{11,... | collective-permute-start | bytes 49160 | tf_op jit(solution)/shard_map/ppermute | solution.py:30
  116.6 0.7 collective-permute-done.27
  117.3 4.3 %collective-permute-done.29 = bf16[16,512]{1,0:T(8,128)(2,1)S(1)} collective-permute-done((bf16[16,512]{1,0:T(8,128)(2,1)S(1)}, bf16[16,512]{1,0:T(8,128)(2,1)S(1)}, u32[]{:S(2)}, u32[]{:S(2)}) %collective-permute-start.29) | collective-permute-done | bytes 16416 | tf_op jit(solution)/shard_map/ppermute | solution.py:30
  121.7 0.1 reshape.91
  121.8 0.3 fusion
  122.1 0.3 fusion.1
  122.5 0.7 reshape.92
  (58 shorter events, 1.0 us)
Async XLA Ops:
  0.0 1.3 %copy-start = (bf16[1,8,256,256]{3,2,1,0:T(8,128)(2,1)S(1)}, bf16[1,8,256,256]{3,2,1,0:T(8,128)(2,1)}, u32[]{:S(2)}) copy-start(bf16[1,8,256,256]{3,2,1,0:T(8,128)(2,1)} %param.12) | copy-start | bytes 3145732
  0.0 2.6 %copy-start.8 = (s32[1,8,64]{2,1,0:T(8,128)S(1)}, s32[1,8,64]{2,1,0:T(8,128)}, u32[]{:S(2)}) copy-start(s32[1,8,64]{2,1,0:T(8,128)} %param.14) | copy-start | bytes 6148
  0.0 15.7 %copy-start.6 = (f32[1,3,4,512]{3,2,1,0:T(4,128)S(1)}, f32[1,3,4,512]{3,2,1,0:T(4,128)}, u32[]{:S(2)}) copy-start(f32[1,3,4,512]{3,2,1,0:T(4,128)} %param.15) | copy-start | bytes 73732
  0.0 18.7 %copy-start.1 = (bf16[1,3,512,512]{3,2,1,0:T(8,128)(2,1)S(1)}, bf16[1,3,512,512]{3,2,1,0:T(8,128)(2,1)}, u32[]{:S(2)}) copy-start(bf16[1,3,512,512]{3,2,1,0:T(8,128)(2,1)} %param.18) | copy-start | bytes 4718596
  3.0 12.8 %collective-permute-start = (f32[16,512]{1,0:T(8,128)S(1)}, f32[16,512]{1,0:T(8,128)S(1)}, u32[]{:S(2)}, u32[]{:S(2)}) collective-permute-start(f32[16,512]{1,0:T(8,128)S(1)} %reshape.88), channel_id=1, source_target_pairs={{0,64},{64,0},{128,192},{192,128},{1,65},{65,1},{129,193},{193,129... | collective-permute-start | bytes 98312 | tf_op jit(solution)/shard_map/ppermute | solution.py:31
  3.5 12.3 %collective-permute-start.1 = (f32[16,512]{1,0:T(8,128)S(1)}, f32[16,512]{1,0:T(8,128)S(1)}, u32[]{:S(2)}, u32[]{:S(2)}) collective-permute-start(f32[16,512]{1,0:T(8,128)S(1)} %reshape.88), channel_id=1, source_target_pairs={{64,128},{128,64},{65,129},{129,65},{66,130},{130,66},{67,131},{13... | collective-permute-start | bytes 98312 | tf_op jit(solution)/shard_map/ppermute | solution.py:30
  7.8 8.0 %collective-permute-start.2 = (f32[16,512]{1,0:T(8,128)S(1)}, f32[16,512]{1,0:T(8,128)S(1)}, u32[]{:S(2)}, u32[]{:S(2)}) collective-permute-start(f32[16,512]{1,0:T(8,128)S(1)} %reshape.88), channel_id=1, source_target_pairs={{0,1},{1,0},{2,3},{3,2},{4,5},{5,4},{6,7},{7,6},{8,9},{9,8},{10,11... | collective-permute-start | bytes 98312 | tf_op jit(solution)/shard_map/ppermute | solution.py:31
  7.9 9.4 %collective-permute-start.3 = (f32[16,512]{1,0:T(8,128)S(1)}, f32[16,512]{1,0:T(8,128)S(1)}, u32[]{:S(2)}, u32[]{:S(2)}) collective-permute-start(f32[16,512]{1,0:T(8,128)S(1)} %reshape.88), channel_id=1, source_target_pairs={{1,2},{2,1},{3,4},{4,3},{5,6},{6,5},{7,8},{8,7},{9,10},{10,9},{11,... | collective-permute-start | bytes 98312 | tf_op jit(solution)/shard_map/ppermute | solution.py:30
  15.8 13.0 %copy-start.2 = (bf16[1,3,512,512]{3,2,1,0:T(8,128)(2,1)S(1)}, bf16[1,3,512,512]{3,2,1,0:T(8,128)(2,1)}, u32[]{:S(2)}) copy-start(bf16[1,3,512,512]{3,2,1,0:T(8,128)(2,1)} %param.17) | copy-start | bytes 4718596
  17.4 1.3 %collective-permute-start.4 = (bf16[16,512]{1,0:T(8,128)(2,1)S(1)}, bf16[16,512]{1,0:T(8,128)(2,1)S(1)}, u32[]{:S(2)}, u32[]{:S(2)}) collective-permute-start(bf16[16,512]{1,0:T(8,128)(2,1)S(1)} %subtract_convert_fusion.4), channel_id=1, source_target_pairs={{0,1},{1,0},{2,3},{3,2},{4,5},{5,4},{6,7},{7,6},{8,9},{9,8},{10,11... | collective-permute-start | bytes 49160 | tf_op jit(solution)/shard_map/ppermute | solution.py:49
  18.7 30.4 %copy-start.5 = (bf16[1,32,512]{2,1,0:T(8,128)(2,1)S(1)}, bf16[1,32,512]{2,1,0:T(8,128)(2,1)}, u32[]{:S(2)}) copy-start(bf16[1,32,512]{2,1,0:T(8,128)(2,1)} %param.20) | copy-start | bytes 98308
  18.9 8.3 %collective-permute-start.5 = (f32[16,512]{1,0:T(8,128)S(1)}, f32[16,512]{1,0:T(8,128)S(1)}, u32[]{:S(2)}, u32[]{:S(2)}) collective-permute-start(f32[16,512]{1,0:T(8,128)S(1)} %convolution_add_fusion.5), channel_id=1, source_target_pairs={{0,64},{64,0},{128,192},{192,128},{1,65},{65,1},{129,193},{193,129... | collective-permute-start | bytes 98312 | tf_op jit(solution)/shard_map/ppermute | solution.py:31
  18.9 8.3 %collective-permute-start.6 = (f32[16,512]{1,0:T(8,128)S(1)}, f32[16,512]{1,0:T(8,128)S(1)}, u32[]{:S(2)}, u32[]{:S(2)}) collective-permute-start(f32[16,512]{1,0:T(8,128)S(1)} %convolution_add_fusion.5), channel_id=1, source_target_pairs={{64,128},{128,64},{65,129},{129,65},{66,130},{130,66},{67,131},{13... | collective-permute-start | bytes 98312 | tf_op jit(solution)/shard_map/ppermute | solution.py:30
  20.8 6.4 %collective-permute-start.7 = (f32[16,512]{1,0:T(8,128)S(1)}, f32[16,512]{1,0:T(8,128)S(1)}, u32[]{:S(2)}, u32[]{:S(2)}) collective-permute-start(f32[16,512]{1,0:T(8,128)S(1)} %convolution_add_fusion.5), channel_id=1, source_target_pairs={{0,1},{1,0},{2,3},{3,2},{4,5},{5,4},{6,7},{7,6},{8,9},{9,8},{10,11... | collective-permute-start | bytes 98312 | tf_op jit(solution)/shard_map/ppermute | solution.py:31
  21.4 7.3 %collective-permute-start.8 = (f32[16,512]{1,0:T(8,128)S(1)}, f32[16,512]{1,0:T(8,128)S(1)}, u32[]{:S(2)}, u32[]{:S(2)}) collective-permute-start(f32[16,512]{1,0:T(8,128)S(1)} %convolution_add_fusion.5), channel_id=1, source_target_pairs={{1,2},{2,1},{3,4},{4,3},{5,6},{6,5},{7,8},{8,7},{9,10},{10,9},{11,... | collective-permute-start | bytes 98312 | tf_op jit(solution)/shard_map/ppermute | solution.py:30
  28.7 3.8 %collective-permute-start.9 = (bf16[16,512]{1,0:T(8,128)(2,1)S(1)}, bf16[16,512]{1,0:T(8,128)(2,1)S(1)}, u32[]{:S(2)}, u32[]{:S(2)}) collective-permute-start(bf16[16,512]{1,0:T(8,128)(2,1)S(1)} %subtract_convert_fusion.3), channel_id=1, source_target_pairs={{0,2},{1,3},{2,0},{3,1},{4,6},{5,7},{6,4},{7,5},{8,10},{9,11},{10,... | collective-permute-start | bytes 49160 | tf_op jit(solution)/shard_map/ppermute | solution.py:49
  32.7 8.4 %collective-permute-start.10 = (f32[16,512]{1,0:T(8,128)S(1)}, f32[16,512]{1,0:T(8,128)S(1)}, u32[]{:S(2)}, u32[]{:S(2)}) collective-permute-start(f32[16,512]{1,0:T(8,128)S(1)} %convolution_add_fusion.4), channel_id=1, source_target_pairs={{0,64},{64,0},{128,192},{192,128},{1,65},{65,1},{129,193},{193,129... | collective-permute-start | bytes 98312 | tf_op jit(solution)/shard_map/ppermute | solution.py:31
  33.5 7.6 %collective-permute-start.11 = (f32[16,512]{1,0:T(8,128)S(1)}, f32[16,512]{1,0:T(8,128)S(1)}, u32[]{:S(2)}, u32[]{:S(2)}) collective-permute-start(f32[16,512]{1,0:T(8,128)S(1)} %convolution_add_fusion.4), channel_id=1, source_target_pairs={{64,128},{128,64},{65,129},{129,65},{66,130},{130,66},{67,131},{13... | collective-permute-start | bytes 98312 | tf_op jit(solution)/shard_map/ppermute | solution.py:30
  36.7 4.5 %collective-permute-start.12 = (f32[16,512]{1,0:T(8,128)S(1)}, f32[16,512]{1,0:T(8,128)S(1)}, u32[]{:S(2)}, u32[]{:S(2)}) collective-permute-start(f32[16,512]{1,0:T(8,128)S(1)} %convolution_add_fusion.4), channel_id=1, source_target_pairs={{0,1},{1,0},{2,3},{3,2},{4,5},{5,4},{6,7},{7,6},{8,9},{9,8},{10,11... | collective-permute-start | bytes 98312 | tf_op jit(solution)/shard_map/ppermute | solution.py:31
  36.8 7.3 %collective-permute-start.13 = (f32[16,512]{1,0:T(8,128)S(1)}, f32[16,512]{1,0:T(8,128)S(1)}, u32[]{:S(2)}, u32[]{:S(2)}) collective-permute-start(f32[16,512]{1,0:T(8,128)S(1)} %convolution_add_fusion.4), channel_id=1, source_target_pairs={{1,2},{2,1},{3,4},{4,3},{5,6},{6,5},{7,8},{8,7},{9,10},{10,9},{11,... | collective-permute-start | bytes 98312 | tf_op jit(solution)/shard_map/ppermute | solution.py:30
  44.1 4.7 %collective-permute-start.14 = (bf16[16,512]{1,0:T(8,128)(2,1)S(1)}, bf16[16,512]{1,0:T(8,128)(2,1)S(1)}, u32[]{:S(2)}, u32[]{:S(2)}) collective-permute-start(bf16[16,512]{1,0:T(8,128)(2,1)S(1)} %subtract_convert_fusion.2), channel_id=1, source_target_pairs={{0,4},{1,5},{2,6},{3,7},{4,0},{5,1},{6,2},{7,3},{8,12},{9,13},{10,... | collective-permute-start | bytes 49160 | tf_op jit(solution)/shard_map/ppermute | solution.py:49
  66.2 9.8 %all-to-all-start.1 = ((bf16[4,16,2048]{2,1,0:T(8,128)(2,1)}), bf16[4,16,2048]{2,1,0:T(8,128)(2,1)S(1)}, u32[]{:S(2)}, u32[]{:S(2)}) async-start(bf16[4,16,2048]{2,1,0:T(8,128)(2,1)} %broadcast_in_dim.7), calls=%async_computation.1 | async-start | bytes 524288 | tf_op jit(solution)/shard_map/all_to_all | solution.py:54
  70.5 20.6 %copy-start.7 = (f32[1,3,4,512]{3,2,1,0:T(4,128)S(1)}, f32[1,3,4,512]{3,2,1,0:T(4,128)}, u32[]{:S(2)}) copy-start(f32[1,3,4,512]{3,2,1,0:T(4,128)} %param.16) | copy-start | bytes 73732
  77.4 21.5 %copy-start.3 = (bf16[1,3,512,512]{3,2,1,0:T(8,128)(2,1)S(1)}, bf16[1,3,512,512]{3,2,1,0:T(8,128)(2,1)}, u32[]{:S(2)}) copy-start(bf16[1,3,512,512]{3,2,1,0:T(8,128)(2,1)} %param.17) | copy-start | bytes 4718596
  77.7 4.7 %collective-permute-start.15 = (bf16[16,512]{1,0:T(8,128)(2,1)S(1)}, bf16[16,512]{1,0:T(8,128)(2,1)S(1)}, u32[]{:S(2)}, u32[]{:S(2)}) collective-permute-start(bf16[16,512]{1,0:T(8,128)(2,1)S(1)} %convolution_convert_fusion.4), channel_id=1, source_target_pairs={{0,4},{1,5},{2,6},{3,7},{4,0},{5,1},{6,2},{7,3},{8,12},{9,13},{10,... | collective-permute-start | bytes 49160 | tf_op jit(solution)/shard_map/ppermute | solution.py:49
  83.6 38.1 %copy-start.4 = (bf16[1,8,64,256]{3,2,1,0:T(8,128)(2,1)S(1)}, bf16[1,8,64,256]{3,2,1,0:T(8,128)(2,1)}, u32[]{:S(2)}) copy-start(bf16[1,8,64,256]{3,2,1,0:T(8,128)(2,1)} %param.13) | copy-start | bytes 786436
  83.6 7.6 %collective-permute-start.16 = (bf16[16,512]{1,0:T(8,128)(2,1)S(1)}, bf16[16,512]{1,0:T(8,128)(2,1)S(1)}, u32[]{:S(2)}, u32[]{:S(2)}) collective-permute-start(bf16[16,512]{1,0:T(8,128)(2,1)S(1)} %get-tuple-element.29), channel_id=1, source_target_pairs={{0,64},{64,0},{128,192},{192,128},{1,65},{65,1},{129,193},{193,129... | collective-permute-start | bytes 49160 | tf_op jit(solution)/shard_map/ppermute | solution.py:31
  85.1 6.1 %collective-permute-start.17 = (bf16[16,512]{1,0:T(8,128)(2,1)S(1)}, bf16[16,512]{1,0:T(8,128)(2,1)S(1)}, u32[]{:S(2)}, u32[]{:S(2)}) collective-permute-start(bf16[16,512]{1,0:T(8,128)(2,1)S(1)} %get-tuple-element.29), channel_id=1, source_target_pairs={{64,128},{128,64},{65,129},{129,65},{66,130},{130,66},{67,131},{13... | collective-permute-start | bytes 49160 | tf_op jit(solution)/shard_map/ppermute | solution.py:30
  87.6 3.6 %collective-permute-start.18 = (bf16[16,512]{1,0:T(8,128)(2,1)S(1)}, bf16[16,512]{1,0:T(8,128)(2,1)S(1)}, u32[]{:S(2)}, u32[]{:S(2)}) collective-permute-start(bf16[16,512]{1,0:T(8,128)(2,1)S(1)} %get-tuple-element.29), channel_id=1, source_target_pairs={{0,1},{1,0},{2,3},{3,2},{4,5},{5,4},{6,7},{7,6},{8,9},{9,8},{10,11... | collective-permute-start | bytes 49160 | tf_op jit(solution)/shard_map/ppermute | solution.py:31
  87.7 7.2 %collective-permute-start.19 = (bf16[16,512]{1,0:T(8,128)(2,1)S(1)}, bf16[16,512]{1,0:T(8,128)(2,1)S(1)}, u32[]{:S(2)}, u32[]{:S(2)}) collective-permute-start(bf16[16,512]{1,0:T(8,128)(2,1)S(1)} %get-tuple-element.29), channel_id=1, source_target_pairs={{1,2},{2,1},{3,4},{4,3},{5,6},{6,5},{7,8},{8,7},{9,10},{10,9},{11,... | collective-permute-start | bytes 49160 | tf_op jit(solution)/shard_map/ppermute | solution.py:30
  95.1 3.8 %collective-permute-start.20 = (bf16[16,512]{1,0:T(8,128)(2,1)S(1)}, bf16[16,512]{1,0:T(8,128)(2,1)S(1)}, u32[]{:S(2)}, u32[]{:S(2)}) collective-permute-start(bf16[16,512]{1,0:T(8,128)(2,1)S(1)} %convolution_convert_fusion.3), channel_id=1, source_target_pairs={{0,2},{1,3},{2,0},{3,1},{4,6},{5,7},{6,4},{7,5},{8,10},{9,11},{10,... | collective-permute-start | bytes 49160 | tf_op jit(solution)/shard_map/ppermute | solution.py:49
  99.1 5.7 %collective-permute-start.21 = (bf16[16,512]{1,0:T(8,128)(2,1)S(1)}, bf16[16,512]{1,0:T(8,128)(2,1)S(1)}, u32[]{:S(2)}, u32[]{:S(2)}) collective-permute-start(bf16[16,512]{1,0:T(8,128)(2,1)S(1)} %get-tuple-element.31), channel_id=1, source_target_pairs={{0,64},{64,0},{128,192},{192,128},{1,65},{65,1},{129,193},{193,129... | collective-permute-start | bytes 49160 | tf_op jit(solution)/shard_map/ppermute | solution.py:31
  99.1 5.7 %collective-permute-start.22 = (bf16[16,512]{1,0:T(8,128)(2,1)S(1)}, bf16[16,512]{1,0:T(8,128)(2,1)S(1)}, u32[]{:S(2)}, u32[]{:S(2)}) collective-permute-start(bf16[16,512]{1,0:T(8,128)(2,1)S(1)} %get-tuple-element.31), channel_id=1, source_target_pairs={{64,128},{128,64},{65,129},{129,65},{66,130},{130,66},{67,131},{13... | collective-permute-start | bytes 49160 | tf_op jit(solution)/shard_map/ppermute | solution.py:30
  102.5 2.3 %collective-permute-start.23 = (bf16[16,512]{1,0:T(8,128)(2,1)S(1)}, bf16[16,512]{1,0:T(8,128)(2,1)S(1)}, u32[]{:S(2)}, u32[]{:S(2)}) collective-permute-start(bf16[16,512]{1,0:T(8,128)(2,1)S(1)} %get-tuple-element.31), channel_id=1, source_target_pairs={{0,1},{1,0},{2,3},{3,2},{4,5},{5,4},{6,7},{7,6},{8,9},{9,8},{10,11... | collective-permute-start | bytes 49160 | tf_op jit(solution)/shard_map/ppermute | solution.py:31
  102.8 7.2 %collective-permute-start.24 = (bf16[16,512]{1,0:T(8,128)(2,1)S(1)}, bf16[16,512]{1,0:T(8,128)(2,1)S(1)}, u32[]{:S(2)}, u32[]{:S(2)}) collective-permute-start(bf16[16,512]{1,0:T(8,128)(2,1)S(1)} %get-tuple-element.31), channel_id=1, source_target_pairs={{1,2},{2,1},{3,4},{4,3},{5,6},{6,5},{7,8},{8,7},{9,10},{10,9},{11,... | collective-permute-start | bytes 49160 | tf_op jit(solution)/shard_map/ppermute | solution.py:30
  110.2 1.2 collective-permute-start.25
  111.7 5.0 %collective-permute-start.26 = (bf16[16,512]{1,0:T(8,128)(2,1)S(1)}, bf16[16,512]{1,0:T(8,128)(2,1)S(1)}, u32[]{:S(2)}, u32[]{:S(2)}) collective-permute-start(bf16[16,512]{1,0:T(8,128)(2,1)S(1)} %get-tuple-element.33), channel_id=1, source_target_pairs={{0,64},{64,0},{128,192},{192,128},{1,65},{65,1},{129,193},{193,129... | collective-permute-start | bytes 49160 | tf_op jit(solution)/shard_map/ppermute | solution.py:31
  111.7 5.6 %collective-permute-start.27 = (bf16[16,512]{1,0:T(8,128)(2,1)S(1)}, bf16[16,512]{1,0:T(8,128)(2,1)S(1)}, u32[]{:S(2)}, u32[]{:S(2)}) collective-permute-start(bf16[16,512]{1,0:T(8,128)(2,1)S(1)} %get-tuple-element.33), channel_id=1, source_target_pairs={{64,128},{128,64},{65,129},{129,65},{66,130},{130,66},{67,131},{13... | collective-permute-start | bytes 49160 | tf_op jit(solution)/shard_map/ppermute | solution.py:30
  114.4 2.9 %collective-permute-start.28 = (bf16[16,512]{1,0:T(8,128)(2,1)S(1)}, bf16[16,512]{1,0:T(8,128)(2,1)S(1)}, u32[]{:S(2)}, u32[]{:S(2)}) collective-permute-start(bf16[16,512]{1,0:T(8,128)(2,1)S(1)} %get-tuple-element.33), channel_id=1, source_target_pairs={{0,1},{1,0},{2,3},{3,2},{4,5},{5,4},{6,7},{7,6},{8,9},{9,8},{10,11... | collective-permute-start | bytes 49160 | tf_op jit(solution)/shard_map/ppermute | solution.py:31
  114.5 7.2 %collective-permute-start.29 = (bf16[16,512]{1,0:T(8,128)(2,1)S(1)}, bf16[16,512]{1,0:T(8,128)(2,1)S(1)}, u32[]{:S(2)}, u32[]{:S(2)}) collective-permute-start(bf16[16,512]{1,0:T(8,128)(2,1)S(1)} %get-tuple-element.33), channel_id=1, source_target_pairs={{1,2},{2,1},{3,4},{4,3},{5,6},{6,5},{7,8},{8,7},{9,10},{10,9},{11,... | collective-permute-start | bytes 49160 | tf_op jit(solution)/shard_map/ppermute | solution.py:30

commit v7 on v6

--- a/solution.py
+++ b/solution.py
@@ -43,6 +43,20 @@
     below, above, left, right = neighbours_of(shard)
     total = coefs[0] * below + coefs[1] * above
     return total + coefs[2] * left + coefs[3] * right
+
+
+def doubled(shard, axis):
+    size = lax.axis_size(axis)
+    place = lax.axis_index(axis)
+    step = 1
+    while step < size:
+        other = lax.ppermute(shard, axis, [(i, i ^ step) for i in range(size)])
+        upper = (place // step) % 2 == 1
+        low = jnp.where(upper, other, shard)
+        high = jnp.where(upper, shard, other)
+        shard = jnp.concatenate([low, high], axis=1)
+        step *= 2
+    return shard
 
 
 def partner_2(shard, axis, stride):
@@ -122,8 +136,8 @@
     top_state = state.astype(jnp.bfloat16)
     comp = compress[0]
     small = right_transpose(top_state, comp).astype(jnp.bfloat16)
-    row_values = collect(small, "gx", 1)
-    coarse = jnp.dot(collect(row_values, "gy", 1), top_couple, preferred_element_type=jnp.float32)
+    gathered = doubled(doubled(small, "gx"), "gy")
+    coarse = jnp.dot(gathered, top_couple, preferred_element_type=jnp.float32)
     state = jnp.dot(top_state, top_inverse[0], preferred_element_type=jnp.float32)
     state = state + jnp.dot(coarse.astype(jnp.bfloat16), comp, preferred_element_type=jnp.float32)
     for level in reversed(range(level_count)):

time: 124 us -> 133 us (1.073)
  waiting for transfers between devices: 40.7 us -> 69.4 us
  blocking collectives: 15.6 us -> 0 us
  starting transfers between devices: 52.9 us -> 51.1 us
  local copies, waits for them, and re-layouts: 3.77 us -> 2.29 us
    ppermute x0 -> x8, waiting for transfers between devices: none -> 31.6 us  [doubled(): other = lax.ppermute(shard, axis, [(i, i ^ step) for i in range(size)])]
    all_to_all x1 -> x0, blocking collectives: 15.6 us -> none  [sent_to_all(): return lax.all_to_all(copies, axis, split_axis=0, concat_axis=0, tiled=True)]
    ppermute x0 -> x8, starting transfers between devices: none -> 5.24 us  [doubled(): other = lax.ppermute(shard, axis, [(i, i ^ step) for i in range(size)])]
    all_to_all x1 -> x0, starting transfers between devices: 4.28 us -> none  [sent_to_all(): return lax.all_to_all(copies, axis, split_axis=0, concat_axis=0, tiled=True)]
    all_to_all x1 -> x0, waiting for transfers between devices: 4.27 us -> none  [sent_to_all(): return lax.all_to_all(copies, axis, split_axis=0, concat_axis=0, tiled=True)]
    ppermute x12, starting transfers between devices: 3.98 us -> 2.52 us  [both_sides(): beside = lax.ppermute(shard, axis, [(i, i ^ 1) for i in range(size)])]
  transfers between devices with their start and end apart: 31 -> 38, of which waited for: 13 -> 21; matrix products, arithmetic and copies ran while one was open for 2% -> 1% of each run, Pallas kernels for 0% -> 0%
where the time goes in v7:
time: 133 us
  waiting for transfers between devices  69.4 us (52%)
  starting transfers between devices  51.1 us (38%)
  matrix products  8.47 us (6%)
  local copies, waits for them, and re-layouts  2.29 us (2%)
    ppermute x12, starting transfers between devices, both_sides(): lax.ppermute(shard, axis, [(a, b) for a, b in pairs if 0 <= b < size])  43.1 us
    ppermute x8, waiting for transfers between devices, doubled(): other = lax.ppermute(shard, axis, [(i, i ^ step) for i in range(size)])  31.6 us
    ppermute x12, waiting for transfers between devices, both_sides(): lax.ppermute(shard, axis, [(a, b) for a, b in pairs if 0 <= b < size])  20.2 us
    ppermute x6, waiting for transfers between devices, partner_2(): lax.ppermute(shard, axis, [(i, i ^ 1 << stride) for i in range(lax.axis_s...  17.6 us
    ppermute x8, starting transfers between devices, doubled(): other = lax.ppermute(shard, axis, [(i, i ^ step) for i in range(size)])  5.24 us
  transfers between devices with their start and end apart: 38, of which 21 were waited for; matrix products, arithmetic and copies ran while one was open for 1% of the time, Pallas kernels for 0%

profile of v7, /device:TPU:10, one launch (start us, length us, event | category | flops | bytes accessed | tf_op | source)
XLA Modules:
  0.0 132.6 jit_solution(14364255868411528426)
XLA Ops:
  0.0 1.0 copy.21
  1.0 0.2 copy-done
  1.3 0.2 fusion.3
  1.5 1.1 convolution_bitcast_fusion.2
  2.6 0.3 fusion.4
  3.0 0.5 collective-permute-start
  3.5 4.3 %collective-permute-start.1 = (f32[16,512]{1,0:T(8,128)S(1)}, f32[16,512]{1,0:T(8,128)S(1)}, u32[]{:S(2)}, u32[]{:S(2)}) collective-permute-start(f32[16,512]{1,0:T(8,128)S(1)} %reshape.82), channel_id=1, source_target_pairs={{64,128},{128,64},{65,129},{129,65},{66,130},{130,66},{67,131},{13... | collective-permute-start | bytes 98312 | tf_op jit(solution)/shard_map/ppermute | solution.py:30
  7.9 7.8 %collective-permute-start.3 = (f32[16,512]{1,0:T(8,128)S(1)}, f32[16,512]{1,0:T(8,128)S(1)}, u32[]{:S(2)}, u32[]{:S(2)}) collective-permute-start(f32[16,512]{1,0:T(8,128)S(1)} %reshape.82), channel_id=1, source_target_pairs={{1,2},{2,1},{3,4},{4,3},{5,6},{6,5},{7,8},{8,7},{9,10},{10,9},{11,... | collective-permute-start | bytes 98312 | tf_op jit(solution)/shard_map/ppermute | solution.py:30
  15.9 1.5 %collective-permute-done.3 = f32[16,512]{1,0:T(8,128)S(1)} collective-permute-done((f32[16,512]{1,0:T(8,128)S(1)}, f32[16,512]{1,0:T(8,128)S(1)}, u32[]{:S(2)}, u32[]{:S(2)}) %collective-permute-start.3) | collective-permute-done | bytes 32800 | tf_op jit(solution)/shard_map/ppermute | solution.py:30
  17.5 1.2 fusion.25
  18.7 0.2 convolution_add_fusion.5
  18.9 1.9 %collective-permute-start.6 = (f32[16,512]{1,0:T(8,128)S(1)}, f32[16,512]{1,0:T(8,128)S(1)}, u32[]{:S(2)}, u32[]{:S(2)}) collective-permute-start(f32[16,512]{1,0:T(8,128)S(1)} %convolution_add_fusion.5), channel_id=1, source_target_pairs={{64,128},{128,64},{65,129},{129,65},{66,130},{130,66},{67,131},{13... | collective-permute-start | bytes 98312 | tf_op jit(solution)/shard_map/ppermute | solution.py:30
  20.8 0.6 collective-permute-start.7
  21.4 5.7 %collective-permute-start.8 = (f32[16,512]{1,0:T(8,128)S(1)}, f32[16,512]{1,0:T(8,128)S(1)}, u32[]{:S(2)}, u32[]{:S(2)}) collective-permute-start(f32[16,512]{1,0:T(8,128)S(1)} %convolution_add_fusion.5), channel_id=1, source_target_pairs={{1,2},{2,1},{3,4},{4,3},{5,6},{6,5},{7,8},{8,7},{9,10},{10,9},{11,... | collective-permute-start | bytes 98312 | tf_op jit(solution)/shard_map/ppermute | solution.py:30
  27.2 1.6 %collective-permute-done.8 = f32[16,512]{1,0:T(8,128)S(1)} collective-permute-done((f32[16,512]{1,0:T(8,128)S(1)}, f32[16,512]{1,0:T(8,128)S(1)}, u32[]{:S(2)}, u32[]{:S(2)}) %collective-permute-start.8) | collective-permute-done | bytes 32800 | tf_op jit(solution)/shard_map/ppermute | solution.py:30
  28.9 0.2 fusion.20
  29.0 3.5 %collective-permute-done.9 = bf16[16,512]{1,0:T(8,128)(2,1)S(1)} collective-permute-done((bf16[16,512]{1,0:T(8,128)(2,1)S(1)}, bf16[16,512]{1,0:T(8,128)(2,1)S(1)}, u32[]{:S(2)}, u32[]{:S(2)}) %collective-permute-start.9) | collective-permute-done | bytes 16416 | tf_op jit(solution)/shard_map/ppermute | solution.py:63
  32.6 0.2 convolution_add_fusion.4
  32.7 0.8 collective-permute-start.10
  33.5 3.1 %collective-permute-start.11 = (f32[16,512]{1,0:T(8,128)S(1)}, f32[16,512]{1,0:T(8,128)S(1)}, u32[]{:S(2)}, u32[]{:S(2)}) collective-permute-start(f32[16,512]{1,0:T(8,128)S(1)} %convolution_add_fusion.4), channel_id=1, source_target_pairs={{64,128},{128,64},{65,129},{129,65},{66,130},{130,66},{67,131},{13... | collective-permute-start | bytes 98312 | tf_op jit(solution)/shard_map/ppermute | solution.py:30
  36.8 4.3 %collective-permute-start.13 = (f32[16,512]{1,0:T(8,128)S(1)}, f32[16,512]{1,0:T(8,128)S(1)}, u32[]{:S(2)}, u32[]{:S(2)}) collective-permute-start(f32[16,512]{1,0:T(8,128)S(1)} %convolution_add_fusion.4), channel_id=1, source_target_pairs={{1,2},{2,1},{3,4},{4,3},{5,6},{6,5},{7,8},{8,7},{9,10},{10,9},{11,... | collective-permute-start | bytes 98312 | tf_op jit(solution)/shard_map/ppermute | solution.py:30
  41.1 3.0 %collective-permute-done.13 = f32[16,512]{1,0:T(8,128)S(1)} collective-permute-done((f32[16,512]{1,0:T(8,128)S(1)}, f32[16,512]{1,0:T(8,128)S(1)}, u32[]{:S(2)}, u32[]{:S(2)}) %collective-permute-start.13) | collective-permute-done | bytes 32800 | tf_op jit(solution)/shard_map/ppermute | solution.py:30
  44.2 0.2 fusion.15
  44.4 4.5 %collective-permute-done.14 = bf16[16,512]{1,0:T(8,128)(2,1)S(1)} collective-permute-done((bf16[16,512]{1,0:T(8,128)(2,1)S(1)}, bf16[16,512]{1,0:T(8,128)(2,1)S(1)}, u32[]{:S(2)}, u32[]{:S(2)}) %collective-permute-start.14) | collective-permute-done | bytes 16416 | tf_op jit(solution)/shard_map/ppermute | solution.py:63
  48.9 0.2 fusion.6
  49.0 0.1 convolution_convert_fusion.6
  49.2 1.2 collective-permute-done.15
  50.5 3.6 %collective-permute-done.16 = bf16[16,64]{1,0:T(8,128)(2,1)S(1)} collective-permute-done((bf16[16,64]{1,0:T(8,128)(2,1)S(1)}, bf16[16,64]{1,0:T(8,128)(2,1)S(1)}, u32[]{:S(2)}, u32[]{:S(2)}) %collective-permute-start.16) | collective-permute-done | bytes 2080 | tf_op jit(solution)/shard_map/ppermute | solution.py:53
  54.3 4.5 %collective-permute-done.17 = bf16[16,128]{1,0:T(8,128)(2,1)S(1)} collective-permute-done((bf16[16,128]{1,0:T(8,128)(2,1)S(1)}, bf16[16,128]{1,0:T(8,128)(2,1)S(1)}, u32[]{:S(2)}, u32[]{:S(2)}) %collective-permute-start.17) | collective-permute-done | bytes 4128 | tf_op jit(solution)/shard_map/ppermute | solution.py:53
  58.8 2.2 %collective-permute-start.18 = (bf16[16,256]{1,0:T(8,128)(2,1)S(1)}, bf16[16,256]{1,0:T(8,128)(2,1)S(1)}, u32[]{:S(2)}, u32[]{:S(2)}) collective-permute-start(bf16[16,256]{1,0:T(8,128)(2,1)S(1)} %pad_maximum_fusion.4), channel_id=1, source_target_pairs={{0,8},{1,9},{2,10},{3,11},{4,12},{5,13},{6,14},{7,15},{8,0},{9,1},... | collective-permute-start | bytes 24584 | tf_op jit(solution)/shard_map/ppermute | solution.py:53
  61.0 5.4 %collective-permute-done.18 = bf16[16,256]{1,0:T(8,128)(2,1)S(1)} collective-permute-done((bf16[16,256]{1,0:T(8,128)(2,1)S(1)}, bf16[16,256]{1,0:T(8,128)(2,1)S(1)}, u32[]{:S(2)}, u32[]{:S(2)}) %collective-permute-start.18) | collective-permute-done | bytes 8224 | tf_op jit(solution)/shard_map/ppermute | solution.py:53
  66.6 3.7 %collective-permute-done.19 = bf16[16,512]{1,0:T(8,128)(2,1)S(1)} collective-permute-done((bf16[16,512]{1,0:T(8,128)(2,1)S(1)}, bf16[16,512]{1,0:T(8,128)(2,1)S(1)}, u32[]{:S(2)}, u32[]{:S(2)}) %collective-permute-start.19) | collective-permute-done | bytes 16416 | tf_op jit(solution)/shard_map/ppermute | solution.py:53
  70.3 2.5 %collective-permute-start.20 = (bf16[16,1024]{1,0:T(8,128)(2,1)S(1)}, bf16[16,1024]{1,0:T(8,128)(2,1)S(1)}, u32[]{:S(2)}, u32[]{:S(2)}) collective-permute-start(bf16[16,1024]{1,0:T(8,128)(2,1)S(1)} %pad_maximum_fusion.2), channel_id=1, source_target_pairs={{0,32},{1,33},{2,34},{3,35},{4,36},{5,37},{6,38},{7,39},{8,40},{9,... | collective-permute-start | bytes 98312 | tf_op jit(solution)/shard_map/ppermute | solution.py:53
  72.8 3.0 %collective-permute-done.20 = bf16[16,1024]{1,0:T(8,128)(2,1)S(1)} collective-permute-done((bf16[16,1024]{1,0:T(8,128)(2,1)S(1)}, bf16[16,1024]{1,0:T(8,128)(2,1)S(1)}, u32[]{:S(2)}, u32[]{:S(2)}) %collective-permute-start.20) | collective-permute-done | bytes 32800 | tf_op jit(solution)/shard_map/ppermute | solution.py:53
  76.0 4.2 %collective-permute-done.21 = bf16[16,2048]{1,0:T(8,128)(2,1)S(1)} collective-permute-done((bf16[16,2048]{1,0:T(8,128)(2,1)S(1)}, bf16[16,2048]{1,0:T(8,128)(2,1)S(1)}, u32[]{:S(2)}, u32[]{:S(2)}) %collective-permute-start.21) | collective-permute-done | bytes 65568 | tf_op jit(solution)/shard_map/ppermute | solution.py:53
  80.2 0.3 collective-permute-start.22
  80.6 0.2 fusion.9
  80.7 6.1 %collective-permute-done.22 = bf16[16,4096]{1,0:T(8,128)(2,1)S(1)} collective-permute-done((bf16[16,4096]{1,0:T(8,128)(2,1)S(1)}, bf16[16,4096]{1,0:T(8,128)(2,1)S(1)}, u32[]{:S(2)}, u32[]{:S(2)}) %collective-permute-start.22) | collective-permute-done | bytes 131104 | tf_op jit(solution)/shard_map/ppermute | solution.py:53
  86.8 1.4 %fusion.5 = bf16[16,512]{1,0:T(8,128)(2,1)S(1)} fusion(f32[16,512]{1,0:T(8,128)S(1)} %fusion.9, bf16[8192,32]{0,1:T(8,128)(2,1)} %param.21, bf16[16,4096]{1,0:T(8,128)(2,1)S(1)} %get-tuple-element.6, bf16[16,4096]{1,0:T(8,128)(2,1)S(1)} %get-tuple-element.5, bf16[1,32,512]{2,1,0:T(8,128)(2,1)S(1)} %copy-done.6), kind=kOutput, calls=%fused_computation.17 | convolution fusion | flops 9454080 | bytes 868352 | tf_op jit(solution)/shard_map/dot_general | solution.py:142
  88.3 0.2 convolution_convert_fusion.4
  88.5 4.6 %collective-permute-done.23 = bf16[16,512]{1,0:T(8,128)(2,1)S(1)} collective-permute-done((bf16[16,512]{1,0:T(8,128)(2,1)S(1)}, bf16[16,512]{1,0:T(8,128)(2,1)S(1)}, u32[]{:S(2)}, u32[]{:S(2)}) %collective-permute-start.23) | collective-permute-done | bytes 16416 | tf_op jit(solution)/shard_map/ppermute | solution.py:63
  93.2 1.3 fusion.57
  94.5 0.2 collective-permute-start.24
  94.7 2.7 %collective-permute-start.25 = (bf16[16,512]{1,0:T(8,128)(2,1)S(1)}, bf16[16,512]{1,0:T(8,128)(2,1)S(1)}, u32[]{:S(2)}, u32[]{:S(2)}) collective-permute-start(bf16[16,512]{1,0:T(8,128)(2,1)S(1)} %get-tuple-element.45), channel_id=1, source_target_pairs={{64,128},{128,64},{65,129},{129,65},{66,130},{130,66},{67,131},{13... | collective-permute-start | bytes 49160 | tf_op jit(solution)/shard_map/ppermute | solution.py:30
  97.5 3.3 %collective-permute-start.27 = (bf16[16,512]{1,0:T(8,128)(2,1)S(1)}, bf16[16,512]{1,0:T(8,128)(2,1)S(1)}, u32[]{:S(2)}, u32[]{:S(2)}) collective-permute-start(bf16[16,512]{1,0:T(8,128)(2,1)S(1)} %get-tuple-element.45), channel_id=1, source_target_pairs={{1,2},{2,1},{3,4},{4,3},{5,6},{6,5},{7,8},{8,7},{9,10},{10,9},{11,... | collective-permute-start | bytes 49160 | tf_op jit(solution)/shard_map/ppermute | solution.py:30
  100.8 3.8 %collective-permute-done.27 = bf16[16,512]{1,0:T(8,128)(2,1)S(1)} collective-permute-done((bf16[16,512]{1,0:T(8,128)(2,1)S(1)}, bf16[16,512]{1,0:T(8,128)(2,1)S(1)}, u32[]{:S(2)}, u32[]{:S(2)}) %collective-permute-start.27) | collective-permute-done | bytes 16416 | tf_op jit(solution)/shard_map/ppermute | solution.py:30
  104.7 0.2 convolution_convert_fusion.3
  104.9 3.8 %collective-permute-done.28 = bf16[16,512]{1,0:T(8,128)(2,1)S(1)} collective-permute-done((bf16[16,512]{1,0:T(8,128)(2,1)S(1)}, bf16[16,512]{1,0:T(8,128)(2,1)S(1)}, u32[]{:S(2)}, u32[]{:S(2)}) %collective-permute-start.28) | collective-permute-done | bytes 16416 | tf_op jit(solution)/shard_map/ppermute | solution.py:63
  108.7 0.2 fusion.62
  108.9 3.1 %collective-permute-start.30 = (bf16[16,512]{1,0:T(8,128)(2,1)S(1)}, bf16[16,512]{1,0:T(8,128)(2,1)S(1)}, u32[]{:S(2)}, u32[]{:S(2)}) collective-permute-start(bf16[16,512]{1,0:T(8,128)(2,1)S(1)} %get-tuple-element.47), channel_id=1, source_target_pairs={{64,128},{128,64},{65,129},{129,65},{66,130},{130,66},{67,131},{13... | collective-permute-start | bytes 49160 | tf_op jit(solution)/shard_map/ppermute | solution.py:30
  112.2 1.9 %collective-permute-start.32 = (bf16[16,512]{1,0:T(8,128)(2,1)S(1)}, bf16[16,512]{1,0:T(8,128)(2,1)S(1)}, u32[]{:S(2)}, u32[]{:S(2)}) collective-permute-start(bf16[16,512]{1,0:T(8,128)(2,1)S(1)} %get-tuple-element.47), channel_id=1, source_target_pairs={{1,2},{2,1},{3,4},{4,3},{5,6},{6,5},{7,8},{8,7},{9,10},{10,9},{11,... | collective-permute-start | bytes 49160 | tf_op jit(solution)/shard_map/ppermute | solution.py:30
  114.1 0.5 collective-permute-done.30
  114.6 4.8 %collective-permute-done.32 = bf16[16,512]{1,0:T(8,128)(2,1)S(1)} collective-permute-done((bf16[16,512]{1,0:T(8,128)(2,1)S(1)}, bf16[16,512]{1,0:T(8,128)(2,1)S(1)}, u32[]{:S(2)}, u32[]{:S(2)}) %collective-permute-start.32) | collective-permute-done | bytes 16416 | tf_op jit(solution)/shard_map/ppermute | solution.py:30
  119.4 0.2 convolution_convert_fusion.2
  119.6 1.2 collective-permute-done.33
  120.8 0.2 fusion.63
  121.0 2.7 %collective-permute-start.35 = (bf16[16,512]{1,0:T(8,128)(2,1)S(1)}, bf16[16,512]{1,0:T(8,128)(2,1)S(1)}, u32[]{:S(2)}, u32[]{:S(2)}) collective-permute-start(bf16[16,512]{1,0:T(8,128)(2,1)S(1)} %get-tuple-element.49), channel_id=1, source_target_pairs={{64,128},{128,64},{65,129},{129,65},{66,130},{130,66},{67,131},{13... | collective-permute-start | bytes 49160 | tf_op jit(solution)/shard_map/ppermute | solution.py:30
  123.9 2.1 %collective-permute-start.37 = (bf16[16,512]{1,0:T(8,128)(2,1)S(1)}, bf16[16,512]{1,0:T(8,128)(2,1)S(1)}, u32[]{:S(2)}, u32[]{:S(2)}) collective-permute-start(bf16[16,512]{1,0:T(8,128)(2,1)S(1)} %get-tuple-element.49), channel_id=1, source_target_pairs={{1,2},{2,1},{3,4},{4,3},{5,6},{6,5},{7,8},{8,7},{9,10},{10,9},{11,... | collective-permute-start | bytes 49160 | tf_op jit(solution)/shard_map/ppermute | solution.py:30
  125.9 0.7 collective-permute-done.35
  126.7 4.3 %collective-permute-done.37 = bf16[16,512]{1,0:T(8,128)(2,1)S(1)} collective-permute-done((bf16[16,512]{1,0:T(8,128)(2,1)S(1)}, bf16[16,512]{1,0:T(8,128)(2,1)S(1)}, u32[]{:S(2)}, u32[]{:S(2)}) %collective-permute-start.37) | collective-permute-done | bytes 16416 | tf_op jit(solution)/shard_map/ppermute | solution.py:30
  131.1 0.1 reshape.83
  131.2 0.3 fusion
  131.5 0.3 fusion.1
  131.9 0.7 reshape.84
  (81 shorter events, 1.9 us)
Async XLA Ops:
  0.0 1.3 copy-start
  0.0 2.6 %copy-start.9 = (s32[1,8,64]{2,1,0:T(8,128)S(1)}, s32[1,8,64]{2,1,0:T(8,128)}, u32[]{:S(2)}) copy-start(s32[1,8,64]{2,1,0:T(8,128)} %param.14) | copy-start | bytes 6148
  0.0 15.7 %copy-start.7 = (f32[1,3,4,512]{3,2,1,0:T(4,128)S(1)}, f32[1,3,4,512]{3,2,1,0:T(4,128)}, u32[]{:S(2)}) copy-start(f32[1,3,4,512]{3,2,1,0:T(4,128)} %param.15) | copy-start | bytes 73732
  0.0 18.7 %copy-start.1 = (bf16[1,3,512,512]{3,2,1,0:T(8,128)(2,1)S(1)}, bf16[1,3,512,512]{3,2,1,0:T(8,128)(2,1)}, u32[]{:S(2)}) copy-start(bf16[1,3,512,512]{3,2,1,0:T(8,128)(2,1)} %param.18) | copy-start | bytes 4718596
  3.0 12.8 %collective-permute-start = (f32[16,512]{1,0:T(8,128)S(1)}, f32[16,512]{1,0:T(8,128)S(1)}, u32[]{:S(2)}, u32[]{:S(2)}) collective-permute-start(f32[16,512]{1,0:T(8,128)S(1)} %reshape.82), channel_id=1, source_target_pairs={{0,64},{64,0},{128,192},{192,128},{1,65},{65,1},{129,193},{193,129... | collective-permute-start | bytes 98312 | tf_op jit(solution)/shard_map/ppermute | solution.py:31
  3.5 12.3 %collective-permute-start.1 = (f32[16,512]{1,0:T(8,128)S(1)}, f32[16,512]{1,0:T(8,128)S(1)}, u32[]{:S(2)}, u32[]{:S(2)}) collective-permute-start(f32[16,512]{1,0:T(8,128)S(1)} %reshape.82), channel_id=1, source_target_pairs={{64,128},{128,64},{65,129},{129,65},{66,130},{130,66},{67,131},{13... | collective-permute-start | bytes 98312 | tf_op jit(solution)/shard_map/ppermute | solution.py:30
  7.8 8.0 %collective-permute-start.2 = (f32[16,512]{1,0:T(8,128)S(1)}, f32[16,512]{1,0:T(8,128)S(1)}, u32[]{:S(2)}, u32[]{:S(2)}) collective-permute-start(f32[16,512]{1,0:T(8,128)S(1)} %reshape.82), channel_id=1, source_target_pairs={{0,1},{1,0},{2,3},{3,2},{4,5},{5,4},{6,7},{7,6},{8,9},{9,8},{10,11... | collective-permute-start | bytes 98312 | tf_op jit(solution)/shard_map/ppermute | solution.py:31
  7.9 9.4 %collective-permute-start.3 = (f32[16,512]{1,0:T(8,128)S(1)}, f32[16,512]{1,0:T(8,128)S(1)}, u32[]{:S(2)}, u32[]{:S(2)}) collective-permute-start(f32[16,512]{1,0:T(8,128)S(1)} %reshape.82), channel_id=1, source_target_pairs={{1,2},{2,1},{3,4},{4,3},{5,6},{6,5},{7,8},{8,7},{9,10},{10,9},{11,... | collective-permute-start | bytes 98312 | tf_op jit(solution)/shard_map/ppermute | solution.py:30
  15.8 13.0 %copy-start.2 = (bf16[1,3,512,512]{3,2,1,0:T(8,128)(2,1)S(1)}, bf16[1,3,512,512]{3,2,1,0:T(8,128)(2,1)}, u32[]{:S(2)}) copy-start(bf16[1,3,512,512]{3,2,1,0:T(8,128)(2,1)} %param.17) | copy-start | bytes 4718596
  17.4 1.3 collective-permute-start.4
  18.7 30.4 %copy-start.6 = (bf16[1,32,512]{2,1,0:T(8,128)(2,1)S(1)}, bf16[1,32,512]{2,1,0:T(8,128)(2,1)}, u32[]{:S(2)}) copy-start(bf16[1,32,512]{2,1,0:T(8,128)(2,1)} %param.20) | copy-start | bytes 98308
  18.9 8.3 %collective-permute-start.5 = (f32[16,512]{1,0:T(8,128)S(1)}, f32[16,512]{1,0:T(8,128)S(1)}, u32[]{:S(2)}, u32[]{:S(2)}) collective-permute-start(f32[16,512]{1,0:T(8,128)S(1)} %convolution_add_fusion.5), channel_id=1, source_target_pairs={{0,64},{64,0},{128,192},{192,128},{1,65},{65,1},{129,193},{193,129... | collective-permute-start | bytes 98312 | tf_op jit(solution)/shard_map/ppermute | solution.py:31
  18.9 8.3 %collective-permute-start.6 = (f32[16,512]{1,0:T(8,128)S(1)}, f32[16,512]{1,0:T(8,128)S(1)}, u32[]{:S(2)}, u32[]{:S(2)}) collective-permute-start(f32[16,512]{1,0:T(8,128)S(1)} %convolution_add_fusion.5), channel_id=1, source_target_pairs={{64,128},{128,64},{65,129},{129,65},{66,130},{130,66},{67,131},{13... | collective-permute-start | bytes 98312 | tf_op jit(solution)/shard_map/ppermute | solution.py:30
  20.8 6.4 %collective-permute-start.7 = (f32[16,512]{1,0:T(8,128)S(1)}, f32[16,512]{1,0:T(8,128)S(1)}, u32[]{:S(2)}, u32[]{:S(2)}) collective-permute-start(f32[16,512]{1,0:T(8,128)S(1)} %convolution_add_fusion.5), channel_id=1, source_target_pairs={{0,1},{1,0},{2,3},{3,2},{4,5},{5,4},{6,7},{7,6},{8,9},{9,8},{10,11... | collective-permute-start | bytes 98312 | tf_op jit(solution)/shard_map/ppermute | solution.py:31
  21.4 7.3 %collective-permute-start.8 = (f32[16,512]{1,0:T(8,128)S(1)}, f32[16,512]{1,0:T(8,128)S(1)}, u32[]{:S(2)}, u32[]{:S(2)}) collective-permute-start(f32[16,512]{1,0:T(8,128)S(1)} %convolution_add_fusion.5), channel_id=1, source_target_pairs={{1,2},{2,1},{3,4},{4,3},{5,6},{6,5},{7,8},{8,7},{9,10},{10,9},{11,... | collective-permute-start | bytes 98312 | tf_op jit(solution)/shard_map/ppermute | solution.py:30
  28.7 3.8 %collective-permute-start.9 = (bf16[16,512]{1,0:T(8,128)(2,1)S(1)}, bf16[16,512]{1,0:T(8,128)(2,1)S(1)}, u32[]{:S(2)}, u32[]{:S(2)}) collective-permute-start(bf16[16,512]{1,0:T(8,128)(2,1)S(1)} %subtract_convert_fusion.3), channel_id=1, source_target_pairs={{0,2},{1,3},{2,0},{3,1},{4,6},{5,7},{6,4},{7,5},{8,10},{9,11},{10,... | collective-permute-start | bytes 49160 | tf_op jit(solution)/shard_map/ppermute | solution.py:63
  29.0 51.5 %copy-start.5 = (bf16[1,512,512]{2,1,0:T(8,128)(2,1)S(1)}, bf16[1,512,512]{2,1,0:T(8,128)(2,1)}, u32[]{:S(2)}) copy-start(bf16[1,512,512]{2,1,0:T(8,128)(2,1)} %param.19) | copy-start | bytes 1572868
  32.7 8.4 %collective-permute-start.10 = (f32[16,512]{1,0:T(8,128)S(1)}, f32[16,512]{1,0:T(8,128)S(1)}, u32[]{:S(2)}, u32[]{:S(2)}) collective-permute-start(f32[16,512]{1,0:T(8,128)S(1)} %convolution_add_fusion.4), channel_id=1, source_target_pairs={{0,64},{64,0},{128,192},{192,128},{1,65},{65,1},{129,193},{193,129... | collective-permute-start | bytes 98312 | tf_op jit(solution)/shard_map/ppermute | solution.py:31
  33.5 7.6 %collective-permute-start.11 = (f32[16,512]{1,0:T(8,128)S(1)}, f32[16,512]{1,0:T(8,128)S(1)}, u32[]{:S(2)}, u32[]{:S(2)}) collective-permute-start(f32[16,512]{1,0:T(8,128)S(1)} %convolution_add_fusion.4), channel_id=1, source_target_pairs={{64,128},{128,64},{65,129},{129,65},{66,130},{130,66},{67,131},{13... | collective-permute-start | bytes 98312 | tf_op jit(solution)/shard_map/ppermute | solution.py:30
  36.7 4.5 %collective-permute-start.12 = (f32[16,512]{1,0:T(8,128)S(1)}, f32[16,512]{1,0:T(8,128)S(1)}, u32[]{:S(2)}, u32[]{:S(2)}) collective-permute-start(f32[16,512]{1,0:T(8,128)S(1)} %convolution_add_fusion.4), channel_id=1, source_target_pairs={{0,1},{1,0},{2,3},{3,2},{4,5},{5,4},{6,7},{7,6},{8,9},{9,8},{10,11... | collective-permute-start | bytes 98312 | tf_op jit(solution)/shard_map/ppermute | solution.py:31
  36.8 7.3 %collective-permute-start.13 = (f32[16,512]{1,0:T(8,128)S(1)}, f32[16,512]{1,0:T(8,128)S(1)}, u32[]{:S(2)}, u32[]{:S(2)}) collective-permute-start(f32[16,512]{1,0:T(8,128)S(1)} %convolution_add_fusion.4), channel_id=1, source_target_pairs={{1,2},{2,1},{3,4},{4,3},{5,6},{6,5},{7,8},{8,7},{9,10},{10,9},{11,... | collective-permute-start | bytes 98312 | tf_op jit(solution)/shard_map/ppermute | solution.py:30
  44.1 4.7 %collective-permute-start.14 = (bf16[16,512]{1,0:T(8,128)(2,1)S(1)}, bf16[16,512]{1,0:T(8,128)(2,1)S(1)}, u32[]{:S(2)}, u32[]{:S(2)}) collective-permute-start(bf16[16,512]{1,0:T(8,128)(2,1)S(1)} %subtract_convert_fusion.2), channel_id=1, source_target_pairs={{0,4},{1,5},{2,6},{3,7},{4,0},{5,1},{6,2},{7,3},{8,12},{9,13},{10,... | collective-permute-start | bytes 49160 | tf_op jit(solution)/shard_map/ppermute | solution.py:63
  49.2 1.2 collective-permute-start.15
  50.4 3.6 %collective-permute-start.16 = (bf16[16,64]{1,0:T(8,128)(2,1)S(1)}, bf16[16,64]{1,0:T(8,128)(2,1)S(1)}, u32[]{:S(2)}, u32[]{:S(2)}) collective-permute-start(bf16[16,64]{1,0:T(8,128)(2,1)S(1)} %pad_maximum_fusion.5), channel_id=1, source_target_pairs={{0,2},{1,3},{2,0},{3,1},{4,6},{5,7},{6,4},{7,5},{8,10},{9,11},{10,... | collective-permute-start | bytes 6152 | tf_op jit(solution)/shard_map/ppermute | solution.py:53
  54.2 4.5 %collective-permute-start.17 = (bf16[16,128]{1,0:T(8,128)(2,1)S(1)}, bf16[16,128]{1,0:T(8,128)(2,1)S(1)}, u32[]{:S(2)}, u32[]{:S(2)}) collective-permute-start(bf16[16,128]{1,0:T(8,128)(2,1)S(1)} %pad_maximum_fusion.6), channel_id=1, source_target_pairs={{0,4},{1,5},{2,6},{3,7},{4,0},{5,1},{6,2},{7,3},{8,12},{9,13},{10,... | collective-permute-start | bytes 12296 | tf_op jit(solution)/shard_map/ppermute | solution.py:53
  58.8 7.6 %collective-permute-start.18 = (bf16[16,256]{1,0:T(8,128)(2,1)S(1)}, bf16[16,256]{1,0:T(8,128)(2,1)S(1)}, u32[]{:S(2)}, u32[]{:S(2)}) collective-permute-start(bf16[16,256]{1,0:T(8,128)(2,1)S(1)} %pad_maximum_fusion.4), channel_id=1, source_target_pairs={{0,8},{1,9},{2,10},{3,11},{4,12},{5,13},{6,14},{7,15},{8,0},{9,1},... | collective-permute-start | bytes 24584 | tf_op jit(solution)/shard_map/ppermute | solution.py:53
  66.4 3.8 %collective-permute-start.19 = (bf16[16,512]{1,0:T(8,128)(2,1)S(1)}, bf16[16,512]{1,0:T(8,128)(2,1)S(1)}, u32[]{:S(2)}, u32[]{:S(2)}) collective-permute-start(bf16[16,512]{1,0:T(8,128)(2,1)S(1)} %pad_maximum_fusion.3), channel_id=1, source_target_pairs={{0,16},{1,17},{2,18},{3,19},{4,20},{5,21},{6,22},{7,23},{8,24},{9,... | collective-permute-start | bytes 49160 | tf_op jit(solution)/shard_map/ppermute | solution.py:53
  70.3 5.5 %collective-permute-start.20 = (bf16[16,1024]{1,0:T(8,128)(2,1)S(1)}, bf16[16,1024]{1,0:T(8,128)(2,1)S(1)}, u32[]{:S(2)}, u32[]{:S(2)}) collective-permute-start(bf16[16,1024]{1,0:T(8,128)(2,1)S(1)} %pad_maximum_fusion.2), channel_id=1, source_target_pairs={{0,32},{1,33},{2,34},{3,35},{4,36},{5,37},{6,38},{7,39},{8,40},{9,... | collective-permute-start | bytes 98312 | tf_op jit(solution)/shard_map/ppermute | solution.py:53
  75.8 4.4 %collective-permute-start.21 = (bf16[16,2048]{1,0:T(8,128)(2,1)S(1)}, bf16[16,2048]{1,0:T(8,128)(2,1)S(1)}, u32[]{:S(2)}, u32[]{:S(2)}) collective-permute-start(bf16[16,2048]{1,0:T(8,128)(2,1)S(1)} %pad_maximum_fusion.1), channel_id=1, source_target_pairs={{0,64},{64,0},{128,192},{192,128},{1,65},{65,1},{129,193},{193,129... | collective-permute-start | bytes 196616 | tf_op jit(solution)/shard_map/ppermute | solution.py:53
  80.2 20.5 %copy-start.8 = (f32[1,3,4,512]{3,2,1,0:T(4,128)S(1)}, f32[1,3,4,512]{3,2,1,0:T(4,128)}, u32[]{:S(2)}) copy-start(f32[1,3,4,512]{3,2,1,0:T(4,128)} %param.16) | copy-start | bytes 73732
  80.2 6.6 %collective-permute-start.22 = (bf16[16,4096]{1,0:T(8,128)(2,1)S(1)}, bf16[16,4096]{1,0:T(8,128)(2,1)S(1)}, u32[]{:S(2)}, u32[]{:S(2)}) collective-permute-start(bf16[16,4096]{1,0:T(8,128)(2,1)S(1)} %pad_maximum_fusion), channel_id=1, source_target_pairs={{0,128},{64,192},{128,0},{192,64},{1,129},{65,193},{129,1},{193,65... | collective-permute-start | bytes 393224 | tf_op jit(solution)/shard_map/ppermute | solution.py:53
  88.2 20.4 %copy-start.3 = (bf16[1,3,512,512]{3,2,1,0:T(8,128)(2,1)S(1)}, bf16[1,3,512,512]{3,2,1,0:T(8,128)(2,1)}, u32[]{:S(2)}) copy-start(bf16[1,3,512,512]{3,2,1,0:T(8,128)(2,1)} %param.17) | copy-start | bytes 4718596
  88.5 4.7 %collective-permute-start.23 = (bf16[16,512]{1,0:T(8,128)(2,1)S(1)}, bf16[16,512]{1,0:T(8,128)(2,1)S(1)}, u32[]{:S(2)}, u32[]{:S(2)}) collective-permute-start(bf16[16,512]{1,0:T(8,128)(2,1)S(1)} %convolution_convert_fusion.4), channel_id=1, source_target_pairs={{0,4},{1,5},{2,6},{3,7},{4,0},{5,1},{6,2},{7,3},{8,12},{9,13},{10,... | collective-permute-start | bytes 49160 | tf_op jit(solution)/shard_map/ppermute | solution.py:63
  94.5 36.7 %copy-start.4 = (bf16[1,8,64,256]{3,2,1,0:T(8,128)(2,1)S(1)}, bf16[1,8,64,256]{3,2,1,0:T(8,128)(2,1)}, u32[]{:S(2)}) copy-start(bf16[1,8,64,256]{3,2,1,0:T(8,128)(2,1)} %param.13) | copy-start | bytes 786436
  94.5 6.3 %collective-permute-start.24 = (bf16[16,512]{1,0:T(8,128)(2,1)S(1)}, bf16[16,512]{1,0:T(8,128)(2,1)S(1)}, u32[]{:S(2)}, u32[]{:S(2)}) collective-permute-start(bf16[16,512]{1,0:T(8,128)(2,1)S(1)} %get-tuple-element.45), channel_id=1, source_target_pairs={{0,64},{64,0},{128,192},{192,128},{1,65},{65,1},{129,193},{193,129... | collective-permute-start | bytes 49160 | tf_op jit(solution)/shard_map/ppermute | solution.py:31
  94.7 6.1 %collective-permute-start.25 = (bf16[16,512]{1,0:T(8,128)(2,1)S(1)}, bf16[16,512]{1,0:T(8,128)(2,1)S(1)}, u32[]{:S(2)}, u32[]{:S(2)}) collective-permute-start(bf16[16,512]{1,0:T(8,128)(2,1)S(1)} %get-tuple-element.45), channel_id=1, source_target_pairs={{64,128},{128,64},{65,129},{129,65},{66,130},{130,66},{67,131},{13... | collective-permute-start | bytes 49160 | tf_op jit(solution)/shard_map/ppermute | solution.py:30
  97.4 3.4 %collective-permute-start.26 = (bf16[16,512]{1,0:T(8,128)(2,1)S(1)}, bf16[16,512]{1,0:T(8,128)(2,1)S(1)}, u32[]{:S(2)}, u32[]{:S(2)}) collective-permute-start(bf16[16,512]{1,0:T(8,128)(2,1)S(1)} %get-tuple-element.45), channel_id=1, source_target_pairs={{0,1},{1,0},{2,3},{3,2},{4,5},{5,4},{6,7},{7,6},{8,9},{9,8},{10,11... | collective-permute-start | bytes 49160 | tf_op jit(solution)/shard_map/ppermute | solution.py:31
  97.5 7.2 %collective-permute-start.27 = (bf16[16,512]{1,0:T(8,128)(2,1)S(1)}, bf16[16,512]{1,0:T(8,128)(2,1)S(1)}, u32[]{:S(2)}, u32[]{:S(2)}) collective-permute-start(bf16[16,512]{1,0:T(8,128)(2,1)S(1)} %get-tuple-element.45), channel_id=1, source_target_pairs={{1,2},{2,1},{3,4},{4,3},{5,6},{6,5},{7,8},{8,7},{9,10},{10,9},{11,... | collective-permute-start | bytes 49160 | tf_op jit(solution)/shard_map/ppermute | solution.py:30
  104.9 3.8 %collective-permute-start.28 = (bf16[16,512]{1,0:T(8,128)(2,1)S(1)}, bf16[16,512]{1,0:T(8,128)(2,1)S(1)}, u32[]{:S(2)}, u32[]{:S(2)}) collective-permute-start(bf16[16,512]{1,0:T(8,128)(2,1)S(1)} %convolution_convert_fusion.3), channel_id=1, source_target_pairs={{0,2},{1,3},{2,0},{3,1},{4,6},{5,7},{6,4},{7,5},{8,10},{9,11},{10,... | collective-permute-start | bytes 49160 | tf_op jit(solution)/shard_map/ppermute | solution.py:63
  108.9 5.2 %collective-permute-start.29 = (bf16[16,512]{1,0:T(8,128)(2,1)S(1)}, bf16[16,512]{1,0:T(8,128)(2,1)S(1)}, u32[]{:S(2)}, u32[]{:S(2)}) collective-permute-start(bf16[16,512]{1,0:T(8,128)(2,1)S(1)} %get-tuple-element.47), channel_id=1, source_target_pairs={{0,64},{64,0},{128,192},{192,128},{1,65},{65,1},{129,193},{193,129... | collective-permute-start | bytes 49160 | tf_op jit(solution)/shard_map/ppermute | solution.py:31
  108.9 5.6 %collective-permute-start.30 = (bf16[16,512]{1,0:T(8,128)(2,1)S(1)}, bf16[16,512]{1,0:T(8,128)(2,1)S(1)}, u32[]{:S(2)}, u32[]{:S(2)}) collective-permute-start(bf16[16,512]{1,0:T(8,128)(2,1)S(1)} %get-tuple-element.47), channel_id=1, source_target_pairs={{64,128},{128,64},{65,129},{129,65},{66,130},{130,66},{67,131},{13... | collective-permute-start | bytes 49160 | tf_op jit(solution)/shard_map/ppermute | solution.py:30
  112.1 2.5 %collective-permute-start.31 = (bf16[16,512]{1,0:T(8,128)(2,1)S(1)}, bf16[16,512]{1,0:T(8,128)(2,1)S(1)}, u32[]{:S(2)}, u32[]{:S(2)}) collective-permute-start(bf16[16,512]{1,0:T(8,128)(2,1)S(1)} %get-tuple-element.47), channel_id=1, source_target_pairs={{0,1},{1,0},{2,3},{3,2},{4,5},{5,4},{6,7},{7,6},{8,9},{9,8},{10,11... | collective-permute-start | bytes 49160 | tf_op jit(solution)/shard_map/ppermute | solution.py:31
  112.2 7.2 %collective-permute-start.32 = (bf16[16,512]{1,0:T(8,128)(2,1)S(1)}, bf16[16,512]{1,0:T(8,128)(2,1)S(1)}, u32[]{:S(2)}, u32[]{:S(2)}) collective-permute-start(bf16[16,512]{1,0:T(8,128)(2,1)S(1)} %get-tuple-element.47), channel_id=1, source_target_pairs={{1,2},{2,1},{3,4},{4,3},{5,6},{6,5},{7,8},{8,7},{9,10},{10,9},{11,... | collective-permute-start | bytes 49160 | tf_op jit(solution)/shard_map/ppermute | solution.py:30
  119.6 1.2 collective-permute-start.33
  121.0 4.9 %collective-permute-start.34 = (bf16[16,512]{1,0:T(8,128)(2,1)S(1)}, bf16[16,512]{1,0:T(8,128)(2,1)S(1)}, u32[]{:S(2)}, u32[]{:S(2)}) collective-permute-start(bf16[16,512]{1,0:T(8,128)(2,1)S(1)} %get-tuple-element.49), channel_id=1, source_target_pairs={{0,64},{64,0},{128,192},{192,128},{1,65},{65,1},{129,193},{193,129... | collective-permute-start | bytes 49160 | tf_op jit(solution)/shard_map/ppermute | solution.py:31
  121.0 5.6 %collective-permute-start.35 = (bf16[16,512]{1,0:T(8,128)(2,1)S(1)}, bf16[16,512]{1,0:T(8,128)(2,1)S(1)}, u32[]{:S(2)}, u32[]{:S(2)}) collective-permute-start(bf16[16,512]{1,0:T(8,128)(2,1)S(1)} %get-tuple-element.49), channel_id=1, source_target_pairs={{64,128},{128,64},{65,129},{129,65},{66,130},{130,66},{67,131},{13... | collective-permute-start | bytes 49160 | tf_op jit(solution)/shard_map/ppermute | solution.py:30
  123.8 2.9 %collective-permute-start.36 = (bf16[16,512]{1,0:T(8,128)(2,1)S(1)}, bf16[16,512]{1,0:T(8,128)(2,1)S(1)}, u32[]{:S(2)}, u32[]{:S(2)}) collective-permute-start(bf16[16,512]{1,0:T(8,128)(2,1)S(1)} %get-tuple-element.49), channel_id=1, source_target_pairs={{0,1},{1,0},{2,3},{3,2},{4,5},{5,4},{6,7},{7,6},{8,9},{9,8},{10,11... | collective-permute-start | bytes 49160 | tf_op jit(solution)/shard_map/ppermute | solution.py:31
  123.9 7.2 %collective-permute-start.37 = (bf16[16,512]{1,0:T(8,128)(2,1)S(1)}, bf16[16,512]{1,0:T(8,128)(2,1)S(1)}, u32[]{:S(2)}, u32[]{:S(2)}) collective-permute-start(bf16[16,512]{1,0:T(8,128)(2,1)S(1)} %get-tuple-element.49), channel_id=1, source_target_pairs={{1,2},{2,1},{3,4},{4,3},{5,6},{6,5},{7,8},{8,7},{9,10},{10,9},{11,... | collective-permute-start | bytes 49160 | tf_op jit(solution)/shard_map/ppermute | solution.py:30

commit v8 on v6

--- a/solution.py
+++ b/solution.py
@@ -4,43 +4,24 @@
 from jax.sharding import PartitionSpec as P
 
 
-def padded_2(shard, sides, width):
-    edges = {}
-    for axis, dim in sides:
-        size, length = (lax.axis_size(axis), shard.shape[dim])
-        up = [(i, (i + 1) % size) for i in range(size - 1)]
-        last = lax.slice_in_dim(shard, length - width, length, axis=dim)
-        leading = lax.slice_in_dim(shard, 0, width, axis=dim)
-        edges[dim] = (
-            lax.ppermute(last, axis, up),
-            lax.ppermute(leading, axis, [(b, a) for a, b in up]),
-        )
-    done = []
-    for _, dim in sides:
-        low, high = edges[dim]
-        around = [(width, width) if d in done else (0, 0) for d in range(shard.ndim)]
-        shard = jnp.concatenate([jnp.pad(low, around), shard, jnp.pad(high, around)], axis=dim)
-        done.append(dim)
-    return shard
-
-
-def both_sides(shard, axis):
+def both_sides(shard, axis, beside=None):
     size = lax.axis_size(axis)
     pairs = [(i, i + 1) if i % 2 else (i, i - 1) for i in range(size)]
     across = lax.ppermute(shard, axis, [(a, b) for a, b in pairs if 0 <= b < size])
-    beside = lax.ppermute(shard, axis, [(i, i ^ 1) for i in range(size)])
+    if beside is None:
+        beside = lax.ppermute(shard, axis, [(i, i ^ 1) for i in range(size)])
     odd = lax.axis_index(axis) % 2 == 1
     return jnp.where(odd, beside, across), jnp.where(odd, across, beside)
 
 
-def neighbours_of(shard):
+def neighbours_of(shard, beside=None):
+    left, right = both_sides(shard, "gx", beside)
     from_below, from_above = both_sides(shard, "gy")
-    left, right = both_sides(shard, "gx")
     return from_below, from_above, left, right
 
 
-def neighbour_sum(shard, coefs):
-    below, above, left, right = neighbours_of(shard)
+def neighbour_sum(shard, coefs, beside=None):
+    below, above, left, right = neighbours_of(shard, beside)
     total = coefs[0] * below + coefs[1] * above
     return total + coefs[2] * left + coefs[3] * right
 
@@ -63,11 +44,6 @@
 def collect(shard, axis, dim):
     parts = sent_to_all(shard, axis)
     return joined_along(parts, dim)
-
-
-def neighbour_mix(padded, coefs):
-    total = coefs[0] * padded[0, 1] + coefs[1] * padded[2, 1]
-    return total + coefs[2] * padded[1, 0] + coefs[3] * padded[1, 2]
 
 
 def right_transpose(values, matrix):
@@ -128,10 +104,17 @@
     state = state + jnp.dot(coarse.astype(jnp.bfloat16), comp, preferred_element_type=jnp.float32)
     for level in reversed(range(level_count)):
         rounded = state.astype(jnp.bfloat16)
-        sent = right_transpose(rounded, other[level])
-        received = partner_2(sent.astype(jnp.bfloat16), "gx", level).astype(sent.dtype)
-        mixed = right_transpose(rounded, own[level]) + received
-        state = mixed - neighbour_sum(mixed.astype(jnp.bfloat16), down_rates[level])
+        sent = right_transpose(rounded, other[level]).astype(jnp.bfloat16).astype(jnp.float32)
+        local = lax.optimization_barrier(right_transpose(rounded, own[level]))
+        if level == 0:
+            both = partner_2(jnp.stack([sent, local]), "gx", level)
+            mixed = local + both[0]
+            beside = (both[1] + sent).astype(jnp.bfloat16)
+        else:
+            mixed = local + partner_2(sent.astype(jnp.bfloat16), "gx", level).astype(jnp.float32)
+            beside = None
+        rates = down_rates[level]
+        state = mixed - neighbour_sum(mixed.astype(jnp.bfloat16), rates, beside)
     skeleton = state.reshape(field_count, box_count, skel_size)
     back = jnp.einsum(
         "fbk,bkq->fbq", skeleton.astype(jnp.bfloat16), weights, preferred_element_type=jnp.float32

time: 124 us -> 122 us (0.984)
    ppermute x6, waiting for transfers between devices: 16.7 us -> 15.2 us  [partner_2(): lax.ppermute(shard, axis, [(i, i ^ 1 << stride) for i in range(lax.axis_s...]
    ppermute x12 -> x11, starting transfers between devices: 3.98 us -> 3.68 us  [both_sides(): beside = lax.ppermute(shard, axis, [(i, i ^ 1) for i in range(size)])]
  transfers between devices with their start and end apart: 31 -> 30, of which waited for: 13 -> 14; matrix products, arithmetic and copies ran while one was open for 2% -> 4% of each run, Pallas kernels for 0% -> 0%
where the time goes in v8:
time: 122 us; the launch traced here: 121 us
  starting transfers between devices  52.4 us (43%)
  waiting for transfers between devices  39.5 us (32%)
  blocking collectives  15.6 us (13%)
  matrix products  9.53 us (8%)
  local copies, waits for them, and re-layouts  3.79 us (3%)
    ppermute x12, starting transfers between devices, both_sides(): lax.ppermute(shard, axis, [(a, b) for a, b in pairs if 0 <= b < size])  43.1 us
    ppermute x12, waiting for transfers between devices, both_sides(): lax.ppermute(shard, axis, [(a, b) for a, b in pairs if 0 <= b < size])  20 us
    all_to_all x1, blocking collectives, sent_to_all(): return lax.all_to_all(copies, axis, split_axis=0, concat_axis=0, tiled=True)  15.6 us
    ppermute x6, waiting for transfers between devices, partner_2(): lax.ppermute(shard, axis, [(i, i ^ 1 << stride) for i in range(lax.axis_s...  15.2 us
    all_to_all x1, starting transfers between devices, sent_to_all(): return lax.all_to_all(copies, axis, split_axis=0, concat_axis=0, tiled=True)  4.28 us
    all_to_all x1, waiting for transfers between devices, sent_to_all(): return lax.all_to_all(copies, axis, split_axis=0, concat_axis=0, tiled=True)  4.27 us
    ppermute x11, starting transfers between devices, both_sides(): beside = lax.ppermute(shard, axis, [(i, i ^ 1) for i in range(size)])  3.68 us
    dot_general x7, matrix products, right_transpose(): lax.dot_general(values, matrix, (((1,), (1,)), ((), ())), preferred_eleme...  2.59 us
  transfers between devices with their start and end apart: 30, of which 14 were waited for; matrix products, arithmetic and copies ran while one was open for 4% of the time, Pallas kernels for 0%

profile of v8, /device:TPU:10, one launch (start us, length us, event | category | flops | bytes accessed | tf_op | source)
XLA Modules:
  0.0 121.5 jit_solution(11363780894281996910)
XLA Ops:
  0.0 1.0 copy.29
  1.0 0.2 copy-done
  1.3 0.2 fusion.3
  1.5 1.1 convolution_bitcast_fusion.2
  2.6 0.3 fusion.4
  3.0 0.5 collective-permute-start
  3.5 4.3 %collective-permute-start.1 = (f32[16,512]{1,0:T(8,128)S(1)}, f32[16,512]{1,0:T(8,128)S(1)}, u32[]{:S(2)}, u32[]{:S(2)}) collective-permute-start(f32[16,512]{1,0:T(8,128)S(1)} %reshape.88), channel_id=1, source_target_pairs={{64,128},{128,64},{65,129},{129,65},{66,130},{130,66},{67,131},{13... | collective-permute-start | bytes 98312 | tf_op jit(solution)/shard_map/ppermute | solution.py:10
  7.8 0.1 collective-permute-start.2
  7.9 7.8 %collective-permute-start.3 = (f32[16,512]{1,0:T(8,128)S(1)}, f32[16,512]{1,0:T(8,128)S(1)}, u32[]{:S(2)}, u32[]{:S(2)}) collective-permute-start(f32[16,512]{1,0:T(8,128)S(1)} %reshape.88), channel_id=1, source_target_pairs={{1,2},{2,1},{3,4},{4,3},{5,6},{6,5},{7,8},{8,7},{9,10},{10,9},{11,... | collective-permute-start | bytes 98312 | tf_op jit(solution)/shard_map/ppermute | solution.py:10
  15.9 1.5 %collective-permute-done.3 = f32[16,512]{1,0:T(8,128)S(1)} collective-permute-done((f32[16,512]{1,0:T(8,128)S(1)}, f32[16,512]{1,0:T(8,128)S(1)}, u32[]{:S(2)}, u32[]{:S(2)}) %collective-permute-start.3) | collective-permute-done | bytes 32800 | tf_op jit(solution)/shard_map/ppermute | solution.py:10
  17.5 1.2 fusion.28
  18.7 0.2 convolution_add_fusion.3
  18.9 1.9 %collective-permute-start.6 = (f32[16,512]{1,0:T(8,128)S(1)}, f32[16,512]{1,0:T(8,128)S(1)}, u32[]{:S(2)}, u32[]{:S(2)}) collective-permute-start(f32[16,512]{1,0:T(8,128)S(1)} %convolution_add_fusion.3), channel_id=1, source_target_pairs={{64,128},{128,64},{65,129},{129,65},{66,130},{130,66},{67,131},{13... | collective-permute-start | bytes 98312 | tf_op jit(solution)/shard_map/ppermute | solution.py:10
  20.8 0.6 collective-permute-start.7
  21.4 5.7 %collective-permute-start.8 = (f32[16,512]{1,0:T(8,128)S(1)}, f32[16,512]{1,0:T(8,128)S(1)}, u32[]{:S(2)}, u32[]{:S(2)}) collective-permute-start(f32[16,512]{1,0:T(8,128)S(1)} %convolution_add_fusion.3), channel_id=1, source_target_pairs={{1,2},{2,1},{3,4},{4,3},{5,6},{6,5},{7,8},{8,7},{9,10},{10,9},{11,... | collective-permute-start | bytes 98312 | tf_op jit(solution)/shard_map/ppermute | solution.py:10
  27.2 1.6 %collective-permute-done.8 = f32[16,512]{1,0:T(8,128)S(1)} collective-permute-done((f32[16,512]{1,0:T(8,128)S(1)}, f32[16,512]{1,0:T(8,128)S(1)}, u32[]{:S(2)}, u32[]{:S(2)}) %collective-permute-start.8) | collective-permute-done | bytes 32800 | tf_op jit(solution)/shard_map/ppermute | solution.py:10
  28.7 0.1 collective-permute-start.9
  28.9 0.2 fusion.22
  29.0 3.5 %collective-permute-done.9 = bf16[16,512]{1,0:T(8,128)(2,1)S(1)} collective-permute-done((bf16[16,512]{1,0:T(8,128)(2,1)S(1)}, bf16[16,512]{1,0:T(8,128)(2,1)S(1)}, u32[]{:S(2)}, u32[]{:S(2)}) %collective-permute-start.9) | collective-permute-done | bytes 16416 | tf_op jit(solution)/shard_map/ppermute | solution.py:30
  32.6 0.2 convolution_add_fusion.2
  32.7 0.8 collective-permute-start.10
  33.5 3.1 %collective-permute-start.11 = (f32[16,512]{1,0:T(8,128)S(1)}, f32[16,512]{1,0:T(8,128)S(1)}, u32[]{:S(2)}, u32[]{:S(2)}) collective-permute-start(f32[16,512]{1,0:T(8,128)S(1)} %convolution_add_fusion.2), channel_id=1, source_target_pairs={{64,128},{128,64},{65,129},{129,65},{66,130},{130,66},{67,131},{13... | collective-permute-start | bytes 98312 | tf_op jit(solution)/shard_map/ppermute | solution.py:10
  36.7 0.1 collective-permute-start.12
  36.8 4.3 %collective-permute-start.13 = (f32[16,512]{1,0:T(8,128)S(1)}, f32[16,512]{1,0:T(8,128)S(1)}, u32[]{:S(2)}, u32[]{:S(2)}) collective-permute-start(f32[16,512]{1,0:T(8,128)S(1)} %convolution_add_fusion.2), channel_id=1, source_target_pairs={{1,2},{2,1},{3,4},{4,3},{5,6},{6,5},{7,8},{8,7},{9,10},{10,9},{11,... | collective-permute-start | bytes 98312 | tf_op jit(solution)/shard_map/ppermute | solution.py:10
  41.1 3.0 %collective-permute-done.13 = f32[16,512]{1,0:T(8,128)S(1)} collective-permute-done((f32[16,512]{1,0:T(8,128)S(1)}, f32[16,512]{1,0:T(8,128)S(1)}, u32[]{:S(2)}, u32[]{:S(2)}) %collective-permute-start.13) | collective-permute-done | bytes 32800 | tf_op jit(solution)/shard_map/ppermute | solution.py:10
  44.1 0.1 collective-permute-start.14
  44.2 0.2 fusion.16
  44.4 4.5 %collective-permute-done.14 = bf16[16,512]{1,0:T(8,128)(2,1)S(1)} collective-permute-done((bf16[16,512]{1,0:T(8,128)(2,1)S(1)}, bf16[16,512]{1,0:T(8,128)(2,1)S(1)}, u32[]{:S(2)}, u32[]{:S(2)}) %collective-permute-start.14) | collective-permute-done | bytes 16416 | tf_op jit(solution)/shard_map/ppermute | solution.py:30
  48.9 0.2 fusion.6
  49.0 0.1 convolution_convert_fusion.6
  49.2 0.2 reshape.93
  49.4 15.6 %all_to_all.10 = bf16[64,2,256]{2,1,0:T(2,128)(2,1)S(1)} all-to-all(bf16[64,2,256]{2,1,0:T(2,128)(2,1)S(1)} %reshape.93), channel_id=1, replica_groups=mesh['gy'=4,'gx'=64] {'gx'}, dimensions={0} | all-to-all | bytes 131072 | tf_op jit(solution)/shard_map/all_to_all | solution.py:35
  65.0 0.2 reshape.94
  65.2 0.3 reshape.89
  65.5 0.7 broadcast_in_dim.7
  66.2 4.3 %all-to-all-start.1 = ((bf16[4,16,2048]{2,1,0:T(8,128)(2,1)}), bf16[4,16,2048]{2,1,0:T(8,128)(2,1)S(1)}, u32[]{:S(2)}, u32[]{:S(2)}) async-start(bf16[4,16,2048]{2,1,0:T(8,128)(2,1)} %broadcast_in_dim.7), calls=%async_computation.1 | async-start | bytes 524288 | tf_op jit(solution)/shard_map/all_to_all | solution.py:35
  70.5 1.2 %fusion.10 = f32[16,512]{1,0:T(8,128)S(1)} fusion(bf16[16,512]{1,0:T(8,128)(2,1)S(1)} %fusion.6, bf16[1,512,512]{2,1,0:T(8,128)(2,1)} %param.19), kind=kOutput, calls=%fused_computation.25 | convolution fusion | flops 8388608 | bytes 573440 | tf_op jit(solution)/shard_map/dot_general | solution.py:103
  71.7 4.3 %all-to-all-done.1 = bf16[4,16,2048]{2,1,0:T(8,128)(2,1)S(1)} async-done(((bf16[4,16,2048]{2,1,0:T(8,128)(2,1)}), bf16[4,16,2048]{2,1,0:T(8,128)(2,1)S(1)}, u32[]{:S(2)}, u32[]{:S(2)}) %all-to-all-start.1) | async-done | bytes 262176 | tf_op jit(solution)/shard_map/all_to_all | solution.py:35
  76.0 1.4 %fusion.5 = bf16[16,512]{1,0:T(8,128)(2,1)S(1)} fusion(f32[16,512]{1,0:T(8,128)S(1)} %fusion.10, bf16[16,8192]{1,0:T(8,128)(2,1)S(1)} %bitcast.138, bf16[8192,32]{0,1:T(8,128)(2,1)} %param.21, bf16[1,32,512]{2,1,0:T(8,128)(2,1)S(1)} %copy-done.5), kind=kOutput, calls=%fused_computation.15 | convolution fusion | flops 8929792 | bytes 868352 | tf_op jit(solution)/shard_map/dot_general | solution.py:104
  77.5 0.2 convolution_convert_fusion.4
  77.7 1.0 collective-permute-start.15
  78.7 1.3 %fusion.14 = f32[16,512]{1,0:T(8,128)S(1)} fusion(bf16[16,512]{1,0:T(8,128)(2,1)S(1)} %fusion.5, bf16[1,3,512,512]{3,2,1,0:T(8,128)(2,1)} %param.17), kind=kOutput, calls=%fused_computation.29 | convolution fusion | flops 8388608 | bytes 573440 | tf_op jit(solution)/shard_map/dot_general | solution.py:50
  79.9 2.4 %collective-permute-done.15 = bf16[16,512]{1,0:T(8,128)(2,1)S(1)} collective-permute-done((bf16[16,512]{1,0:T(8,128)(2,1)S(1)}, bf16[16,512]{1,0:T(8,128)(2,1)S(1)}, u32[]{:S(2)}, u32[]{:S(2)}) %collective-permute-start.15) | collective-permute-done | bytes 16416 | tf_op jit(solution)/shard_map/ppermute | solution.py:30
  82.4 1.5 %collective-permute-start.16 = (bf16[16,512]{1,0:T(8,128)(2,1)S(1)}, bf16[16,512]{1,0:T(8,128)(2,1)S(1)}, u32[]{:S(2)}, u32[]{:S(2)}) collective-permute-start(bf16[16,512]{1,0:T(8,128)(2,1)S(1)} %fusion.55), channel_id=1, source_target_pairs={{0,64},{64,0},{128,192},{192,128},{1,65},{65,1},{129,193},{193,129... | collective-permute-start | bytes 49160 | tf_op jit(solution)/shard_map/ppermute | solution.py:12
  83.8 2.5 %collective-permute-start.17 = (bf16[16,512]{1,0:T(8,128)(2,1)S(1)}, bf16[16,512]{1,0:T(8,128)(2,1)S(1)}, u32[]{:S(2)}, u32[]{:S(2)}) collective-permute-start(bf16[16,512]{1,0:T(8,128)(2,1)S(1)} %fusion.55), channel_id=1, source_target_pairs={{64,128},{128,64},{65,129},{129,65},{66,130},{130,66},{67,131},{13... | collective-permute-start | bytes 49160 | tf_op jit(solution)/shard_map/ppermute | solution.py:10
  86.4 3.5 %collective-permute-start.19 = (bf16[16,512]{1,0:T(8,128)(2,1)S(1)}, bf16[16,512]{1,0:T(8,128)(2,1)S(1)}, u32[]{:S(2)}, u32[]{:S(2)}) collective-permute-start(bf16[16,512]{1,0:T(8,128)(2,1)S(1)} %fusion.55), channel_id=1, source_target_pairs={{1,2},{2,1},{3,4},{4,3},{5,6},{6,5},{7,8},{8,7},{9,10},{10,9},{11,... | collective-permute-start | bytes 49160 | tf_op jit(solution)/shard_map/ppermute | solution.py:10
  89.9 3.6 %collective-permute-done.19 = bf16[16,512]{1,0:T(8,128)(2,1)S(1)} collective-permute-done((bf16[16,512]{1,0:T(8,128)(2,1)S(1)}, bf16[16,512]{1,0:T(8,128)(2,1)S(1)}, u32[]{:S(2)}, u32[]{:S(2)}) %collective-permute-start.19) | collective-permute-done | bytes 16416 | tf_op jit(solution)/shard_map/ppermute | solution.py:10
  93.6 0.2 convolution_convert_fusion.3
  93.9 0.2 fusion.20
  94.1 3.5 %collective-permute-done.20 = bf16[16,512]{1,0:T(8,128)(2,1)S(1)} collective-permute-done((bf16[16,512]{1,0:T(8,128)(2,1)S(1)}, bf16[16,512]{1,0:T(8,128)(2,1)S(1)}, u32[]{:S(2)}, u32[]{:S(2)}) %collective-permute-start.20) | collective-permute-done | bytes 16416 | tf_op jit(solution)/shard_map/ppermute | solution.py:30
  97.6 3.4 %collective-permute-start.22 = (bf16[16,512]{1,0:T(8,128)(2,1)S(1)}, bf16[16,512]{1,0:T(8,128)(2,1)S(1)}, u32[]{:S(2)}, u32[]{:S(2)}) collective-permute-start(bf16[16,512]{1,0:T(8,128)(2,1)S(1)} %fusion.56), channel_id=1, source_target_pairs={{64,128},{128,64},{65,129},{129,65},{66,130},{130,66},{67,131},{13... | collective-permute-start | bytes 49160 | tf_op jit(solution)/shard_map/ppermute | solution.py:10
  101.1 2.0 %collective-permute-start.24 = (bf16[16,512]{1,0:T(8,128)(2,1)S(1)}, bf16[16,512]{1,0:T(8,128)(2,1)S(1)}, u32[]{:S(2)}, u32[]{:S(2)}) collective-permute-start(bf16[16,512]{1,0:T(8,128)(2,1)S(1)} %fusion.56), channel_id=1, source_target_pairs={{1,2},{2,1},{3,4},{4,3},{5,6},{6,5},{7,8},{8,7},{9,10},{10,9},{11,... | collective-permute-start | bytes 49160 | tf_op jit(solution)/shard_map/ppermute | solution.py:10
  103.1 0.1 collective-permute-done.22
  103.2 5.0 %collective-permute-done.24 = bf16[16,512]{1,0:T(8,128)(2,1)S(1)} collective-permute-done((bf16[16,512]{1,0:T(8,128)(2,1)S(1)}, bf16[16,512]{1,0:T(8,128)(2,1)S(1)}, u32[]{:S(2)}, u32[]{:S(2)}) %collective-permute-start.24) | collective-permute-done | bytes 16416 | tf_op jit(solution)/shard_map/ppermute | solution.py:10
  108.3 0.2 fusion.7
  108.5 0.3 fusion.26
  108.9 1.2 %collective-permute-done.25 = f32[2,16,512]{2,1,0:T(8,128)S(1)} collective-permute-done((f32[2,16,512]{2,1,0:T(8,128)S(1)}, f32[2,16,512]{2,1,0:T(8,128)S(1)}, u32[]{:S(2)}, u32[]{:S(2)}) %collective-permute-start.25) | collective-permute-done | bytes 65568 | tf_op jit(solution)/shard_map/ppermute | solution.py:30
  110.1 2.6 %collective-permute-start.27 = (bf16[16,512]{1,0:T(8,128)(2,1)S(1)}, bf16[16,512]{1,0:T(8,128)(2,1)S(1)}, u32[]{:S(2)}, u32[]{:S(2)}) collective-permute-start(bf16[16,512]{1,0:T(8,128)(2,1)S(1)} %fusion.57), channel_id=1, source_target_pairs={{64,128},{128,64},{65,129},{129,65},{66,130},{130,66},{67,131},{13... | collective-permute-start | bytes 49160 | tf_op jit(solution)/shard_map/ppermute | solution.py:10
  112.8 1.9 %collective-permute-start.28 = (bf16[16,512]{1,0:T(8,128)(2,1)S(1)}, bf16[16,512]{1,0:T(8,128)(2,1)S(1)}, u32[]{:S(2)}, u32[]{:S(2)}) collective-permute-start(bf16[16,512]{1,0:T(8,128)(2,1)S(1)} %fusion.57), channel_id=1, source_target_pairs={{1,2},{2,1},{3,4},{4,3},{5,6},{6,5},{7,8},{8,7},{9,10},{10,9},{11,... | collective-permute-start | bytes 49160 | tf_op jit(solution)/shard_map/ppermute | solution.py:10
  114.7 1.0 collective-permute-done.27
  115.8 4.2 %collective-permute-done.28 = bf16[16,512]{1,0:T(8,128)(2,1)S(1)} collective-permute-done((bf16[16,512]{1,0:T(8,128)(2,1)S(1)}, bf16[16,512]{1,0:T(8,128)(2,1)S(1)}, u32[]{:S(2)}, u32[]{:S(2)}) %collective-permute-start.28) | collective-permute-done | bytes 16416 | tf_op jit(solution)/shard_map/ppermute | solution.py:10
  120.1 0.3 fusion
  120.4 0.3 fusion.1
  120.8 0.7 reshape.92
  (60 shorter events, 1.1 us)
Async XLA Ops:
  0.0 1.3 %copy-start = (bf16[1,8,256,256]{3,2,1,0:T(8,128)(2,1)S(1)}, bf16[1,8,256,256]{3,2,1,0:T(8,128)(2,1)}, u32[]{:S(2)}) copy-start(bf16[1,8,256,256]{3,2,1,0:T(8,128)(2,1)} %param.12) | copy-start | bytes 3145732
  0.0 2.6 %copy-start.8 = (s32[1,8,64]{2,1,0:T(8,128)S(1)}, s32[1,8,64]{2,1,0:T(8,128)}, u32[]{:S(2)}) copy-start(s32[1,8,64]{2,1,0:T(8,128)} %param.14) | copy-start | bytes 6148
  0.0 15.7 %copy-start.6 = (f32[1,3,4,512]{3,2,1,0:T(4,128)S(1)}, f32[1,3,4,512]{3,2,1,0:T(4,128)}, u32[]{:S(2)}) copy-start(f32[1,3,4,512]{3,2,1,0:T(4,128)} %param.15) | copy-start | bytes 73732
  0.0 18.7 %copy-start.1 = (bf16[1,3,512,512]{3,2,1,0:T(8,128)(2,1)S(1)}, bf16[1,3,512,512]{3,2,1,0:T(8,128)(2,1)}, u32[]{:S(2)}) copy-start(bf16[1,3,512,512]{3,2,1,0:T(8,128)(2,1)} %param.18) | copy-start | bytes 4718596
  3.0 12.8 %collective-permute-start = (f32[16,512]{1,0:T(8,128)S(1)}, f32[16,512]{1,0:T(8,128)S(1)}, u32[]{:S(2)}, u32[]{:S(2)}) collective-permute-start(f32[16,512]{1,0:T(8,128)S(1)} %reshape.88), channel_id=1, source_target_pairs={{0,64},{64,0},{128,192},{192,128},{1,65},{65,1},{129,193},{193,129... | collective-permute-start | bytes 98312 | tf_op jit(solution)/shard_map/ppermute | solution.py:12
  3.5 12.3 %collective-permute-start.1 = (f32[16,512]{1,0:T(8,128)S(1)}, f32[16,512]{1,0:T(8,128)S(1)}, u32[]{:S(2)}, u32[]{:S(2)}) collective-permute-start(f32[16,512]{1,0:T(8,128)S(1)} %reshape.88), channel_id=1, source_target_pairs={{64,128},{128,64},{65,129},{129,65},{66,130},{130,66},{67,131},{13... | collective-permute-start | bytes 98312 | tf_op jit(solution)/shard_map/ppermute | solution.py:10
  7.8 8.0 %collective-permute-start.2 = (f32[16,512]{1,0:T(8,128)S(1)}, f32[16,512]{1,0:T(8,128)S(1)}, u32[]{:S(2)}, u32[]{:S(2)}) collective-permute-start(f32[16,512]{1,0:T(8,128)S(1)} %reshape.88), channel_id=1, source_target_pairs={{0,1},{1,0},{2,3},{3,2},{4,5},{5,4},{6,7},{7,6},{8,9},{9,8},{10,11... | collective-permute-start | bytes 98312 | tf_op jit(solution)/shard_map/ppermute | solution.py:12
  7.9 9.4 %collective-permute-start.3 = (f32[16,512]{1,0:T(8,128)S(1)}, f32[16,512]{1,0:T(8,128)S(1)}, u32[]{:S(2)}, u32[]{:S(2)}) collective-permute-start(f32[16,512]{1,0:T(8,128)S(1)} %reshape.88), channel_id=1, source_target_pairs={{1,2},{2,1},{3,4},{4,3},{5,6},{6,5},{7,8},{8,7},{9,10},{10,9},{11,... | collective-permute-start | bytes 98312 | tf_op jit(solution)/shard_map/ppermute | solution.py:10
  15.8 13.0 %copy-start.2 = (bf16[1,3,512,512]{3,2,1,0:T(8,128)(2,1)S(1)}, bf16[1,3,512,512]{3,2,1,0:T(8,128)(2,1)}, u32[]{:S(2)}) copy-start(bf16[1,3,512,512]{3,2,1,0:T(8,128)(2,1)} %param.17) | copy-start | bytes 4718596
  17.4 1.3 %collective-permute-start.4 = (bf16[16,512]{1,0:T(8,128)(2,1)S(1)}, bf16[16,512]{1,0:T(8,128)(2,1)S(1)}, u32[]{:S(2)}, u32[]{:S(2)}) collective-permute-start(bf16[16,512]{1,0:T(8,128)(2,1)S(1)} %subtract_convert_fusion.4), channel_id=1, source_target_pairs={{0,1},{1,0},{2,3},{3,2},{4,5},{5,4},{6,7},{7,6},{8,9},{9,8},{10,11... | collective-permute-start | bytes 49160 | tf_op jit(solution)/shard_map/ppermute | solution.py:30
  18.7 30.4 %copy-start.5 = (bf16[1,32,512]{2,1,0:T(8,128)(2,1)S(1)}, bf16[1,32,512]{2,1,0:T(8,128)(2,1)}, u32[]{:S(2)}) copy-start(bf16[1,32,512]{2,1,0:T(8,128)(2,1)} %param.20) | copy-start | bytes 98308
  18.9 8.3 %collective-permute-start.5 = (f32[16,512]{1,0:T(8,128)S(1)}, f32[16,512]{1,0:T(8,128)S(1)}, u32[]{:S(2)}, u32[]{:S(2)}) collective-permute-start(f32[16,512]{1,0:T(8,128)S(1)} %convolution_add_fusion.3), channel_id=1, source_target_pairs={{0,64},{64,0},{128,192},{192,128},{1,65},{65,1},{129,193},{193,129... | collective-permute-start | bytes 98312 | tf_op jit(solution)/shard_map/ppermute | solution.py:12
  18.9 8.3 %collective-permute-start.6 = (f32[16,512]{1,0:T(8,128)S(1)}, f32[16,512]{1,0:T(8,128)S(1)}, u32[]{:S(2)}, u32[]{:S(2)}) collective-permute-start(f32[16,512]{1,0:T(8,128)S(1)} %convolution_add_fusion.3), channel_id=1, source_target_pairs={{64,128},{128,64},{65,129},{129,65},{66,130},{130,66},{67,131},{13... | collective-permute-start | bytes 98312 | tf_op jit(solution)/shard_map/ppermute | solution.py:10
  20.8 6.4 %collective-permute-start.7 = (f32[16,512]{1,0:T(8,128)S(1)}, f32[16,512]{1,0:T(8,128)S(1)}, u32[]{:S(2)}, u32[]{:S(2)}) collective-permute-start(f32[16,512]{1,0:T(8,128)S(1)} %convolution_add_fusion.3), channel_id=1, source_target_pairs={{0,1},{1,0},{2,3},{3,2},{4,5},{5,4},{6,7},{7,6},{8,9},{9,8},{10,11... | collective-permute-start | bytes 98312 | tf_op jit(solution)/shard_map/ppermute | solution.py:12
  21.4 7.3 %collective-permute-start.8 = (f32[16,512]{1,0:T(8,128)S(1)}, f32[16,512]{1,0:T(8,128)S(1)}, u32[]{:S(2)}, u32[]{:S(2)}) collective-permute-start(f32[16,512]{1,0:T(8,128)S(1)} %convolution_add_fusion.3), channel_id=1, source_target_pairs={{1,2},{2,1},{3,4},{4,3},{5,6},{6,5},{7,8},{8,7},{9,10},{10,9},{11,... | collective-permute-start | bytes 98312 | tf_op jit(solution)/shard_map/ppermute | solution.py:10
  28.7 3.8 %collective-permute-start.9 = (bf16[16,512]{1,0:T(8,128)(2,1)S(1)}, bf16[16,512]{1,0:T(8,128)(2,1)S(1)}, u32[]{:S(2)}, u32[]{:S(2)}) collective-permute-start(bf16[16,512]{1,0:T(8,128)(2,1)S(1)} %subtract_convert_fusion.3), channel_id=1, source_target_pairs={{0,2},{1,3},{2,0},{3,1},{4,6},{5,7},{6,4},{7,5},{8,10},{9,11},{10,... | collective-permute-start | bytes 49160 | tf_op jit(solution)/shard_map/ppermute | solution.py:30
  32.7 8.4 %collective-permute-start.10 = (f32[16,512]{1,0:T(8,128)S(1)}, f32[16,512]{1,0:T(8,128)S(1)}, u32[]{:S(2)}, u32[]{:S(2)}) collective-permute-start(f32[16,512]{1,0:T(8,128)S(1)} %convolution_add_fusion.2), channel_id=1, source_target_pairs={{0,64},{64,0},{128,192},{192,128},{1,65},{65,1},{129,193},{193,129... | collective-permute-start | bytes 98312 | tf_op jit(solution)/shard_map/ppermute | solution.py:12
  33.5 7.6 %collective-permute-start.11 = (f32[16,512]{1,0:T(8,128)S(1)}, f32[16,512]{1,0:T(8,128)S(1)}, u32[]{:S(2)}, u32[]{:S(2)}) collective-permute-start(f32[16,512]{1,0:T(8,128)S(1)} %convolution_add_fusion.2), channel_id=1, source_target_pairs={{64,128},{128,64},{65,129},{129,65},{66,130},{130,66},{67,131},{13... | collective-permute-start | bytes 98312 | tf_op jit(solution)/shard_map/ppermute | solution.py:10
  36.7 4.5 %collective-permute-start.12 = (f32[16,512]{1,0:T(8,128)S(1)}, f32[16,512]{1,0:T(8,128)S(1)}, u32[]{:S(2)}, u32[]{:S(2)}) collective-permute-start(f32[16,512]{1,0:T(8,128)S(1)} %convolution_add_fusion.2), channel_id=1, source_target_pairs={{0,1},{1,0},{2,3},{3,2},{4,5},{5,4},{6,7},{7,6},{8,9},{9,8},{10,11... | collective-permute-start | bytes 98312 | tf_op jit(solution)/shard_map/ppermute | solution.py:12
  36.8 7.3 %collective-permute-start.13 = (f32[16,512]{1,0:T(8,128)S(1)}, f32[16,512]{1,0:T(8,128)S(1)}, u32[]{:S(2)}, u32[]{:S(2)}) collective-permute-start(f32[16,512]{1,0:T(8,128)S(1)} %convolution_add_fusion.2), channel_id=1, source_target_pairs={{1,2},{2,1},{3,4},{4,3},{5,6},{6,5},{7,8},{8,7},{9,10},{10,9},{11,... | collective-permute-start | bytes 98312 | tf_op jit(solution)/shard_map/ppermute | solution.py:10
  44.1 4.7 %collective-permute-start.14 = (bf16[16,512]{1,0:T(8,128)(2,1)S(1)}, bf16[16,512]{1,0:T(8,128)(2,1)S(1)}, u32[]{:S(2)}, u32[]{:S(2)}) collective-permute-start(bf16[16,512]{1,0:T(8,128)(2,1)S(1)} %subtract_convert_fusion.2), channel_id=1, source_target_pairs={{0,4},{1,5},{2,6},{3,7},{4,0},{5,1},{6,2},{7,3},{8,12},{9,13},{10,... | collective-permute-start | bytes 49160 | tf_op jit(solution)/shard_map/ppermute | solution.py:30
  66.2 9.8 %all-to-all-start.1 = ((bf16[4,16,2048]{2,1,0:T(8,128)(2,1)}), bf16[4,16,2048]{2,1,0:T(8,128)(2,1)S(1)}, u32[]{:S(2)}, u32[]{:S(2)}) async-start(bf16[4,16,2048]{2,1,0:T(8,128)(2,1)} %broadcast_in_dim.7), calls=%async_computation.1 | async-start | bytes 524288 | tf_op jit(solution)/shard_map/all_to_all | solution.py:35
  70.5 19.3 %copy-start.7 = (f32[1,3,4,512]{3,2,1,0:T(4,128)S(1)}, f32[1,3,4,512]{3,2,1,0:T(4,128)}, u32[]{:S(2)}) copy-start(f32[1,3,4,512]{3,2,1,0:T(4,128)} %param.16) | copy-start | bytes 73732
  77.4 16.4 %copy-start.3 = (bf16[1,3,512,512]{3,2,1,0:T(8,128)(2,1)S(1)}, bf16[1,3,512,512]{3,2,1,0:T(8,128)(2,1)}, u32[]{:S(2)}) copy-start(bf16[1,3,512,512]{3,2,1,0:T(8,128)(2,1)} %param.17) | copy-start | bytes 4718596
  77.7 4.7 %collective-permute-start.15 = (bf16[16,512]{1,0:T(8,128)(2,1)S(1)}, bf16[16,512]{1,0:T(8,128)(2,1)S(1)}, u32[]{:S(2)}, u32[]{:S(2)}) collective-permute-start(bf16[16,512]{1,0:T(8,128)(2,1)S(1)} %convolution_convert_fusion.4), channel_id=1, source_target_pairs={{0,4},{1,5},{2,6},{3,7},{4,0},{5,1},{6,2},{7,3},{8,12},{9,13},{10,... | collective-permute-start | bytes 49160 | tf_op jit(solution)/shard_map/ppermute | solution.py:30
  82.4 7.5 %collective-permute-start.16 = (bf16[16,512]{1,0:T(8,128)(2,1)S(1)}, bf16[16,512]{1,0:T(8,128)(2,1)S(1)}, u32[]{:S(2)}, u32[]{:S(2)}) collective-permute-start(bf16[16,512]{1,0:T(8,128)(2,1)S(1)} %fusion.55), channel_id=1, source_target_pairs={{0,64},{64,0},{128,192},{192,128},{1,65},{65,1},{129,193},{193,129... | collective-permute-start | bytes 49160 | tf_op jit(solution)/shard_map/ppermute | solution.py:12
  83.8 6.1 %collective-permute-start.17 = (bf16[16,512]{1,0:T(8,128)(2,1)S(1)}, bf16[16,512]{1,0:T(8,128)(2,1)S(1)}, u32[]{:S(2)}, u32[]{:S(2)}) collective-permute-start(bf16[16,512]{1,0:T(8,128)(2,1)S(1)} %fusion.55), channel_id=1, source_target_pairs={{64,128},{128,64},{65,129},{129,65},{66,130},{130,66},{67,131},{13... | collective-permute-start | bytes 49160 | tf_op jit(solution)/shard_map/ppermute | solution.py:10
  86.3 3.6 %collective-permute-start.18 = (bf16[16,512]{1,0:T(8,128)(2,1)S(1)}, bf16[16,512]{1,0:T(8,128)(2,1)S(1)}, u32[]{:S(2)}, u32[]{:S(2)}) collective-permute-start(bf16[16,512]{1,0:T(8,128)(2,1)S(1)} %fusion.55), channel_id=1, source_target_pairs={{0,1},{1,0},{2,3},{3,2},{4,5},{5,4},{6,7},{7,6},{8,9},{9,8},{10,11... | collective-permute-start | bytes 49160 | tf_op jit(solution)/shard_map/ppermute | solution.py:12
  86.4 7.2 %collective-permute-start.19 = (bf16[16,512]{1,0:T(8,128)(2,1)S(1)}, bf16[16,512]{1,0:T(8,128)(2,1)S(1)}, u32[]{:S(2)}, u32[]{:S(2)}) collective-permute-start(bf16[16,512]{1,0:T(8,128)(2,1)S(1)} %fusion.55), channel_id=1, source_target_pairs={{1,2},{2,1},{3,4},{4,3},{5,6},{6,5},{7,8},{8,7},{9,10},{10,9},{11,... | collective-permute-start | bytes 49160 | tf_op jit(solution)/shard_map/ppermute | solution.py:10
  89.9 30.2 %copy-start.4 = (bf16[1,8,64,256]{3,2,1,0:T(8,128)(2,1)S(1)}, bf16[1,8,64,256]{3,2,1,0:T(8,128)(2,1)}, u32[]{:S(2)}) copy-start(bf16[1,8,64,256]{3,2,1,0:T(8,128)(2,1)} %param.13) | copy-start | bytes 786436
  93.8 3.8 %collective-permute-start.20 = (bf16[16,512]{1,0:T(8,128)(2,1)S(1)}, bf16[16,512]{1,0:T(8,128)(2,1)S(1)}, u32[]{:S(2)}, u32[]{:S(2)}) collective-permute-start(bf16[16,512]{1,0:T(8,128)(2,1)S(1)} %convolution_convert_fusion.3), channel_id=1, source_target_pairs={{0,2},{1,3},{2,0},{3,1},{4,6},{5,7},{6,4},{7,5},{8,10},{9,11},{10,... | collective-permute-start | bytes 49160 | tf_op jit(solution)/shard_map/ppermute | solution.py:30
  97.6 5.5 %collective-permute-start.21 = (bf16[16,512]{1,0:T(8,128)(2,1)S(1)}, bf16[16,512]{1,0:T(8,128)(2,1)S(1)}, u32[]{:S(2)}, u32[]{:S(2)}) collective-permute-start(bf16[16,512]{1,0:T(8,128)(2,1)S(1)} %fusion.56), channel_id=1, source_target_pairs={{0,64},{64,0},{128,192},{192,128},{1,65},{65,1},{129,193},{193,129... | collective-permute-start | bytes 49160 | tf_op jit(solution)/shard_map/ppermute | solution.py:12
  97.6 5.6 %collective-permute-start.22 = (bf16[16,512]{1,0:T(8,128)(2,1)S(1)}, bf16[16,512]{1,0:T(8,128)(2,1)S(1)}, u32[]{:S(2)}, u32[]{:S(2)}) collective-permute-start(bf16[16,512]{1,0:T(8,128)(2,1)S(1)} %fusion.56), channel_id=1, source_target_pairs={{64,128},{128,64},{65,129},{129,65},{66,130},{130,66},{67,131},{13... | collective-permute-start | bytes 49160 | tf_op jit(solution)/shard_map/ppermute | solution.py:10
  101.0 2.3 %collective-permute-start.23 = (bf16[16,512]{1,0:T(8,128)(2,1)S(1)}, bf16[16,512]{1,0:T(8,128)(2,1)S(1)}, u32[]{:S(2)}, u32[]{:S(2)}) collective-permute-start(bf16[16,512]{1,0:T(8,128)(2,1)S(1)} %fusion.56), channel_id=1, source_target_pairs={{0,1},{1,0},{2,3},{3,2},{4,5},{5,4},{6,7},{7,6},{8,9},{9,8},{10,11... | collective-permute-start | bytes 49160 | tf_op jit(solution)/shard_map/ppermute | solution.py:12
  101.1 7.2 %collective-permute-start.24 = (bf16[16,512]{1,0:T(8,128)(2,1)S(1)}, bf16[16,512]{1,0:T(8,128)(2,1)S(1)}, u32[]{:S(2)}, u32[]{:S(2)}) collective-permute-start(bf16[16,512]{1,0:T(8,128)(2,1)S(1)} %fusion.56), channel_id=1, source_target_pairs={{1,2},{2,1},{3,4},{4,3},{5,6},{6,5},{7,8},{8,7},{9,10},{10,9},{11,... | collective-permute-start | bytes 49160 | tf_op jit(solution)/shard_map/ppermute | solution.py:10
  108.8 1.3 %collective-permute-start.25 = (f32[2,16,512]{2,1,0:T(8,128)S(1)}, f32[2,16,512]{2,1,0:T(8,128)S(1)}, u32[]{:S(2)}, u32[]{:S(2)}) collective-permute-start(f32[2,16,512]{2,1,0:T(8,128)S(1)} %pad_maximum_fusion), channel_id=1, source_target_pairs={{0,1},{1,0},{2,3},{3,2},{4,5},{5,4},{6,7},{7,6},{8,9},{9,8},{10,11... | collective-permute-start | bytes 196616 | tf_op jit(solution)/shard_map/ppermute | solution.py:30
  110.1 4.6 %collective-permute-start.26 = (bf16[16,512]{1,0:T(8,128)(2,1)S(1)}, bf16[16,512]{1,0:T(8,128)(2,1)S(1)}, u32[]{:S(2)}, u32[]{:S(2)}) collective-permute-start(bf16[16,512]{1,0:T(8,128)(2,1)S(1)} %fusion.57), channel_id=1, source_target_pairs={{0,64},{64,0},{128,192},{192,128},{1,65},{65,1},{129,193},{193,129... | collective-permute-start | bytes 49160 | tf_op jit(solution)/shard_map/ppermute | solution.py:12
  110.1 5.6 %collective-permute-start.27 = (bf16[16,512]{1,0:T(8,128)(2,1)S(1)}, bf16[16,512]{1,0:T(8,128)(2,1)S(1)}, u32[]{:S(2)}, u32[]{:S(2)}) collective-permute-start(bf16[16,512]{1,0:T(8,128)(2,1)S(1)} %fusion.57), channel_id=1, source_target_pairs={{64,128},{128,64},{65,129},{129,65},{66,130},{130,66},{67,131},{13... | collective-permute-start | bytes 49160 | tf_op jit(solution)/shard_map/ppermute | solution.py:10
  112.8 7.2 %collective-permute-start.28 = (bf16[16,512]{1,0:T(8,128)(2,1)S(1)}, bf16[16,512]{1,0:T(8,128)(2,1)S(1)}, u32[]{:S(2)}, u32[]{:S(2)}) collective-permute-start(bf16[16,512]{1,0:T(8,128)(2,1)S(1)} %fusion.57), channel_id=1, source_target_pairs={{1,2},{2,1},{3,4},{4,3},{5,6},{6,5},{7,8},{8,7},{9,10},{10,9},{11,... | collective-permute-start | bytes 49160 | tf_op jit(solution)/shard_map/ppermute | solution.py:10

commit v9 on v6

--- a/solution.py
+++ b/solution.py
@@ -2,26 +2,6 @@
 import jax.numpy as jnp
 from jax import lax
 from jax.sharding import PartitionSpec as P
-
-
-def padded_2(shard, sides, width):
-    edges = {}
-    for axis, dim in sides:
-        size, length = (lax.axis_size(axis), shard.shape[dim])
-        up = [(i, (i + 1) % size) for i in range(size - 1)]
-        last = lax.slice_in_dim(shard, length - width, length, axis=dim)
-        leading = lax.slice_in_dim(shard, 0, width, axis=dim)
-        edges[dim] = (
-            lax.ppermute(last, axis, up),
-            lax.ppermute(leading, axis, [(b, a) for a, b in up]),
-        )
-    done = []
-    for _, dim in sides:
-        low, high = edges[dim]
-        around = [(width, width) if d in done else (0, 0) for d in range(shard.ndim)]
-        shard = jnp.concatenate([jnp.pad(low, around), shard, jnp.pad(high, around)], axis=dim)
-        done.append(dim)
-    return shard
 
 
 def both_sides(shard, axis):
@@ -34,8 +14,8 @@
 
 
 def neighbours_of(shard):
+    left, right = both_sides(shard, "gx")
     from_below, from_above = both_sides(shard, "gy")
-    left, right = both_sides(shard, "gx")
     return from_below, from_above, left, right
 
 
@@ -63,11 +43,6 @@
 def collect(shard, axis, dim):
     parts = sent_to_all(shard, axis)
     return joined_along(parts, dim)
-
-
-def neighbour_mix(padded, coefs):
-    total = coefs[0] * padded[0, 1] + coefs[1] * padded[2, 1]
-    return total + coefs[2] * padded[1, 0] + coefs[3] * padded[1, 2]
 
 
 def right_transpose(values, matrix):
@@ -114,7 +89,7 @@
     state = picked - jnp.einsum("fbq,bkq->fbk", solved, weights, preferred_element_type=jnp.float32)
     state = state.reshape(field_count, skel_total)
     for level in range(level_count):
-        mixed = state - neighbour_sum(state, up_rates[level])
+        mixed = state - neighbour_sum(state.astype(jnp.bfloat16), up_rates[level])
         rounded = mixed.astype(jnp.bfloat16)
         partner = partner_2(rounded, "gx", level)
         state = jnp.dot(rounded, own[level], preferred_element_type=jnp.float32)
@@ -130,7 +105,7 @@
         rounded = state.astype(jnp.bfloat16)
         sent = right_transpose(rounded, other[level])
         received = partner_2(sent.astype(jnp.bfloat16), "gx", level).astype(sent.dtype)
-        mixed = right_transpose(rounded, own[level]) + received
+        mixed = lax.optimization_barrier(right_transpose(rounded, own[level])) + received
         state = mixed - neighbour_sum(mixed.astype(jnp.bfloat16), down_rates[level])
     skeleton = state.reshape(field_count, box_count, skel_size)
     back = jnp.einsum(

time: 124 us -> 122 us (0.984)
  waiting for transfers between devices: 40.7 us -> 36.4 us
  matrix products: 9.52 us -> 11.6 us
    ppermute x6, waiting for transfers between devices: 16.7 us -> 12.8 us  [partner_2(): lax.ppermute(shard, axis, [(i, i ^ 1 << stride) for i in range(lax.axis_s...]
    dot_general x3, matrix products: 1.55 us -> 3.64 us  [body(): state = jnp.dot(rounded, own[level], preferred_element_type=jnp.float32)]
  transfers between devices with their start and end apart: 31 -> 31, of which waited for: 13 -> 13; matrix products, arithmetic and copies ran while one was open for 2% -> 6% of each run, Pallas kernels for 0% -> 0%
where the time goes in v9:
time: 122 us; the launch traced here: 121 us
  starting transfers between devices  52.9 us (43%)
  waiting for transfers between devices  36.4 us (30%)
  blocking collectives  15.5 us (13%)
  matrix products  11.6 us (10%)
  local copies, waits for them, and re-layouts  3.78 us (3%)
    ppermute x12, starting transfers between devices, both_sides(): lax.ppermute(shard, axis, [(a, b) for a, b in pairs if 0 <= b < size])  43.4 us
    ppermute x12, waiting for transfers between devices, both_sides(): lax.ppermute(shard, axis, [(a, b) for a, b in pairs if 0 <= b < size])  19.3 us
    all_to_all x1, blocking collectives, sent_to_all(): return lax.all_to_all(copies, axis, split_axis=0, concat_axis=0, tiled=True)  15.5 us
    ppermute x6, waiting for transfers between devices, partner_2(): lax.ppermute(shard, axis, [(i, i ^ 1 << stride) for i in range(lax.axis_s...  12.8 us
    all_to_all x1, starting transfers between devices, sent_to_all(): return lax.all_to_all(copies, axis, split_axis=0, concat_axis=0, tiled=True)  4.28 us
    all_to_all x1, waiting for transfers between devices, sent_to_all(): return lax.all_to_all(copies, axis, split_axis=0, concat_axis=0, tiled=True)  4.27 us
    ppermute x12, starting transfers between devices, both_sides(): beside = lax.ppermute(shard, axis, [(i, i ^ 1) for i in range(size)])  3.99 us
    dot_general x3, matrix products, body(): state = jnp.dot(rounded, own[level], preferred_element_type=jnp.float32)  3.64 us
  transfers between devices with their start and end apart: 31, of which 13 were waited for; matrix products, arithmetic and copies ran while one was open for 6% of the time, Pallas kernels for 0%

profile of v9, /device:TPU:10, one launch (start us, length us, event | category | flops | bytes accessed | tf_op | source)
XLA Modules:
  0.0 120.9 jit_solution(17016210728064270522)
XLA Ops:
  0.0 1.0 copy.29
  1.0 0.2 copy-done
  1.3 0.2 fusion.3
  1.5 1.1 convolution_bitcast_fusion.2
  2.6 0.3 fusion.4
  3.0 0.5 collective-permute-start
  3.5 4.3 %collective-permute-start.1 = (bf16[16,512]{1,0:T(8,128)(2,1)S(1)}, bf16[16,512]{1,0:T(8,128)(2,1)S(1)}, u32[]{:S(2)}, u32[]{:S(2)}) collective-permute-start(bf16[16,512]{1,0:T(8,128)(2,1)S(1)} %convert_element_type.158), channel_id=1, source_target_pairs={{64,128},{128,64},{65,129},{129,65},{66,130},{130,66},{67,131},{13... | collective-permute-start | bytes 49160 | tf_op jit(solution)/shard_map/ppermute | solution.py:10
  8.0 7.8 %collective-permute-start.3 = (bf16[16,512]{1,0:T(8,128)(2,1)S(1)}, bf16[16,512]{1,0:T(8,128)(2,1)S(1)}, u32[]{:S(2)}, u32[]{:S(2)}) collective-permute-start(bf16[16,512]{1,0:T(8,128)(2,1)S(1)} %convert_element_type.158), channel_id=1, source_target_pairs={{1,2},{2,1},{3,4},{4,3},{5,6},{6,5},{7,8},{8,7},{9,10},{10,9},{11,... | collective-permute-start | bytes 49160 | tf_op jit(solution)/shard_map/ppermute | solution.py:10
  15.9 1.3 %collective-permute-done.3 = bf16[16,512]{1,0:T(8,128)(2,1)S(1)} collective-permute-done((bf16[16,512]{1,0:T(8,128)(2,1)S(1)}, bf16[16,512]{1,0:T(8,128)(2,1)S(1)}, u32[]{:S(2)}, u32[]{:S(2)}) %collective-permute-start.3) | collective-permute-done | bytes 16416 | tf_op jit(solution)/shard_map/ppermute | solution.py:10
  17.2 0.1 collective-permute-start.4
  17.3 1.2 %fusion.27 = f32[16,512]{1,0:T(8,128)S(1)} fusion(bf16[16,512]{1,0:T(8,128)(2,1)S(1)} %subtract_convert_fusion.4, bf16[1,3,512,512]{3,2,1,0:T(8,128)(2,1)} %param.17), kind=kOutput, calls=%fused_computation.42 | convolution fusion | flops 8388608 | bytes 573440 | tf_op jit(solution)/shard_map/dot_general | solution.py:95
  18.6 0.2 fusion.56
  18.8 1.9 %collective-permute-start.6 = (bf16[16,512]{1,0:T(8,128)(2,1)S(1)}, bf16[16,512]{1,0:T(8,128)(2,1)S(1)}, u32[]{:S(2)}, u32[]{:S(2)}) collective-permute-start(bf16[16,512]{1,0:T(8,128)(2,1)S(1)} %get-tuple-element.29), channel_id=1, source_target_pairs={{64,128},{128,64},{65,129},{129,65},{66,130},{130,66},{67,131},{13... | collective-permute-start | bytes 49160 | tf_op jit(solution)/shard_map/ppermute | solution.py:10
  20.7 0.6 collective-permute-start.7
  21.3 5.7 %collective-permute-start.8 = (bf16[16,512]{1,0:T(8,128)(2,1)S(1)}, bf16[16,512]{1,0:T(8,128)(2,1)S(1)}, u32[]{:S(2)}, u32[]{:S(2)}) collective-permute-start(bf16[16,512]{1,0:T(8,128)(2,1)S(1)} %get-tuple-element.29), channel_id=1, source_target_pairs={{1,2},{2,1},{3,4},{4,3},{5,6},{6,5},{7,8},{8,7},{9,10},{10,9},{11,... | collective-permute-start | bytes 49160 | tf_op jit(solution)/shard_map/ppermute | solution.py:10
  27.0 1.4 %collective-permute-done.8 = bf16[16,512]{1,0:T(8,128)(2,1)S(1)} collective-permute-done((bf16[16,512]{1,0:T(8,128)(2,1)S(1)}, bf16[16,512]{1,0:T(8,128)(2,1)S(1)}, u32[]{:S(2)}, u32[]{:S(2)}) %collective-permute-start.8) | collective-permute-done | bytes 16416 | tf_op jit(solution)/shard_map/ppermute | solution.py:10
  28.4 0.1 collective-permute-start.9
  28.5 1.2 %fusion.21 = f32[16,512]{1,0:T(8,128)S(1)} fusion(bf16[16,512]{1,0:T(8,128)(2,1)S(1)} %subtract_convert_fusion.3, bf16[1,3,512,512]{3,2,1,0:T(8,128)(2,1)} %param.17), kind=kOutput, calls=%fused_computation.36 | convolution fusion | flops 8388608 | bytes 573440 | tf_op jit(solution)/shard_map/dot_general | solution.py:95
  29.8 2.5 %collective-permute-done.9 = bf16[16,512]{1,0:T(8,128)(2,1)S(1)} collective-permute-done((bf16[16,512]{1,0:T(8,128)(2,1)S(1)}, bf16[16,512]{1,0:T(8,128)(2,1)S(1)}, u32[]{:S(2)}, u32[]{:S(2)}) %collective-permute-start.9) | collective-permute-done | bytes 16416 | tf_op jit(solution)/shard_map/ppermute | solution.py:29
  32.3 0.2 fusion.57
  32.4 0.8 collective-permute-start.10
  33.2 3.1 %collective-permute-start.11 = (bf16[16,512]{1,0:T(8,128)(2,1)S(1)}, bf16[16,512]{1,0:T(8,128)(2,1)S(1)}, u32[]{:S(2)}, u32[]{:S(2)}) collective-permute-start(bf16[16,512]{1,0:T(8,128)(2,1)S(1)} %get-tuple-element.31), channel_id=1, source_target_pairs={{64,128},{128,64},{65,129},{129,65},{66,130},{130,66},{67,131},{13... | collective-permute-start | bytes 49160 | tf_op jit(solution)/shard_map/ppermute | solution.py:10
  36.5 4.3 %collective-permute-start.13 = (bf16[16,512]{1,0:T(8,128)(2,1)S(1)}, bf16[16,512]{1,0:T(8,128)(2,1)S(1)}, u32[]{:S(2)}, u32[]{:S(2)}) collective-permute-start(bf16[16,512]{1,0:T(8,128)(2,1)S(1)} %get-tuple-element.31), channel_id=1, source_target_pairs={{1,2},{2,1},{3,4},{4,3},{5,6},{6,5},{7,8},{8,7},{9,10},{10,9},{11,... | collective-permute-start | bytes 49160 | tf_op jit(solution)/shard_map/ppermute | solution.py:10
  40.8 2.8 %collective-permute-done.13 = bf16[16,512]{1,0:T(8,128)(2,1)S(1)} collective-permute-done((bf16[16,512]{1,0:T(8,128)(2,1)S(1)}, bf16[16,512]{1,0:T(8,128)(2,1)S(1)}, u32[]{:S(2)}, u32[]{:S(2)}) %collective-permute-start.13) | collective-permute-done | bytes 16416 | tf_op jit(solution)/shard_map/ppermute | solution.py:10
  43.7 0.1 collective-permute-start.14
  43.8 1.2 %fusion.15 = f32[16,512]{1,0:T(8,128)S(1)} fusion(bf16[16,512]{1,0:T(8,128)(2,1)S(1)} %subtract_convert_fusion.2, bf16[1,3,512,512]{3,2,1,0:T(8,128)(2,1)} %param.17), kind=kOutput, calls=%fused_computation.30 | convolution fusion | flops 8388608 | bytes 573440 | tf_op jit(solution)/shard_map/dot_general | solution.py:95
  45.0 3.4 %collective-permute-done.14 = bf16[16,512]{1,0:T(8,128)(2,1)S(1)} collective-permute-done((bf16[16,512]{1,0:T(8,128)(2,1)S(1)}, bf16[16,512]{1,0:T(8,128)(2,1)S(1)}, u32[]{:S(2)}, u32[]{:S(2)}) %collective-permute-start.14) | collective-permute-done | bytes 16416 | tf_op jit(solution)/shard_map/ppermute | solution.py:29
  48.4 0.2 fusion.6
  48.6 0.1 convolution_convert_fusion.6
  48.8 0.2 reshape.93
  48.9 15.5 %all_to_all.10 = bf16[64,2,256]{2,1,0:T(2,128)(2,1)S(1)} all-to-all(bf16[64,2,256]{2,1,0:T(2,128)(2,1)S(1)} %reshape.93), channel_id=1, replica_groups=mesh['gy'=4,'gx'=64] {'gx'}, dimensions={0} | all-to-all | bytes 131072 | tf_op jit(solution)/shard_map/all_to_all | solution.py:34
  64.5 0.2 reshape.94
  64.8 0.3 reshape.89
  65.0 0.7 broadcast_in_dim.7
  65.8 4.3 %all-to-all-start.1 = ((bf16[4,16,2048]{2,1,0:T(8,128)(2,1)}), bf16[4,16,2048]{2,1,0:T(8,128)(2,1)S(1)}, u32[]{:S(2)}, u32[]{:S(2)}) async-start(bf16[4,16,2048]{2,1,0:T(8,128)(2,1)} %broadcast_in_dim.7), calls=%async_computation.1 | async-start | bytes 524288 | tf_op jit(solution)/shard_map/all_to_all | solution.py:34
  70.0 1.2 %fusion.9 = f32[16,512]{1,0:T(8,128)S(1)} fusion(bf16[16,512]{1,0:T(8,128)(2,1)S(1)} %fusion.6, bf16[1,512,512]{2,1,0:T(8,128)(2,1)} %param.19), kind=kOutput, calls=%fused_computation.24 | convolution fusion | flops 8388608 | bytes 573440 | tf_op jit(solution)/shard_map/dot_general | solution.py:102
  71.3 4.3 %all-to-all-done.1 = bf16[4,16,2048]{2,1,0:T(8,128)(2,1)S(1)} async-done(((bf16[4,16,2048]{2,1,0:T(8,128)(2,1)}), bf16[4,16,2048]{2,1,0:T(8,128)(2,1)S(1)}, u32[]{:S(2)}, u32[]{:S(2)}) %all-to-all-start.1) | async-done | bytes 262176 | tf_op jit(solution)/shard_map/all_to_all | solution.py:34
  75.5 1.4 %fusion.5 = bf16[16,512]{1,0:T(8,128)(2,1)S(1)} fusion(f32[16,512]{1,0:T(8,128)S(1)} %fusion.9, bf16[16,8192]{1,0:T(8,128)(2,1)S(1)} %bitcast.124, bf16[8192,32]{0,1:T(8,128)(2,1)} %param.21, bf16[1,32,512]{2,1,0:T(8,128)(2,1)S(1)} %copy-done.4), kind=kOutput, calls=%fused_computation.15 | convolution fusion | flops 8929792 | bytes 868352 | tf_op jit(solution)/shard_map/dot_general | solution.py:103
  77.0 0.2 convolution_convert_fusion.4
  77.2 1.0 collective-permute-start.15
  78.2 1.3 %fusion.13 = f32[16,512]{1,0:T(8,128)S(1)} fusion(bf16[16,512]{1,0:T(8,128)(2,1)S(1)} %fusion.5, bf16[1,3,512,512]{3,2,1,0:T(8,128)(2,1)} %param.17), kind=kOutput, calls=%fused_computation.28 | convolution fusion | flops 8388608 | bytes 573440 | tf_op jit(solution)/shard_map/dot_general | solution.py:49
  79.4 2.4 %collective-permute-done.15 = bf16[16,512]{1,0:T(8,128)(2,1)S(1)} collective-permute-done((bf16[16,512]{1,0:T(8,128)(2,1)S(1)}, bf16[16,512]{1,0:T(8,128)(2,1)S(1)}, u32[]{:S(2)}, u32[]{:S(2)}) %collective-permute-start.15) | collective-permute-done | bytes 16416 | tf_op jit(solution)/shard_map/ppermute | solution.py:29
  81.9 1.5 %collective-permute-start.16 = (bf16[16,512]{1,0:T(8,128)(2,1)S(1)}, bf16[16,512]{1,0:T(8,128)(2,1)S(1)}, u32[]{:S(2)}, u32[]{:S(2)}) collective-permute-start(bf16[16,512]{1,0:T(8,128)(2,1)S(1)} %fusion.51), channel_id=1, source_target_pairs={{0,64},{64,0},{128,192},{192,128},{1,65},{65,1},{129,193},{193,129... | collective-permute-start | bytes 49160 | tf_op jit(solution)/shard_map/ppermute | solution.py:11
  83.3 2.5 %collective-permute-start.17 = (bf16[16,512]{1,0:T(8,128)(2,1)S(1)}, bf16[16,512]{1,0:T(8,128)(2,1)S(1)}, u32[]{:S(2)}, u32[]{:S(2)}) collective-permute-start(bf16[16,512]{1,0:T(8,128)(2,1)S(1)} %fusion.51), channel_id=1, source_target_pairs={{64,128},{128,64},{65,129},{129,65},{66,130},{130,66},{67,131},{13... | collective-permute-start | bytes 49160 | tf_op jit(solution)/shard_map/ppermute | solution.py:10
  85.9 3.5 %collective-permute-start.19 = (bf16[16,512]{1,0:T(8,128)(2,1)S(1)}, bf16[16,512]{1,0:T(8,128)(2,1)S(1)}, u32[]{:S(2)}, u32[]{:S(2)}) collective-permute-start(bf16[16,512]{1,0:T(8,128)(2,1)S(1)} %fusion.51), channel_id=1, source_target_pairs={{1,2},{2,1},{3,4},{4,3},{5,6},{6,5},{7,8},{8,7},{9,10},{10,9},{11,... | collective-permute-start | bytes 49160 | tf_op jit(solution)/shard_map/ppermute | solution.py:10
  89.4 3.6 %collective-permute-done.19 = bf16[16,512]{1,0:T(8,128)(2,1)S(1)} collective-permute-done((bf16[16,512]{1,0:T(8,128)(2,1)S(1)}, bf16[16,512]{1,0:T(8,128)(2,1)S(1)}, u32[]{:S(2)}, u32[]{:S(2)}) %collective-permute-start.19) | collective-permute-done | bytes 16416 | tf_op jit(solution)/shard_map/ppermute | solution.py:10
  93.1 0.2 convolution_convert_fusion.3
  93.4 0.2 fusion.19
  93.6 3.5 %collective-permute-done.20 = bf16[16,512]{1,0:T(8,128)(2,1)S(1)} collective-permute-done((bf16[16,512]{1,0:T(8,128)(2,1)S(1)}, bf16[16,512]{1,0:T(8,128)(2,1)S(1)}, u32[]{:S(2)}, u32[]{:S(2)}) %collective-permute-start.20) | collective-permute-done | bytes 16416 | tf_op jit(solution)/shard_map/ppermute | solution.py:29
  97.1 3.4 %collective-permute-start.22 = (bf16[16,512]{1,0:T(8,128)(2,1)S(1)}, bf16[16,512]{1,0:T(8,128)(2,1)S(1)}, u32[]{:S(2)}, u32[]{:S(2)}) collective-permute-start(bf16[16,512]{1,0:T(8,128)(2,1)S(1)} %fusion.52), channel_id=1, source_target_pairs={{64,128},{128,64},{65,129},{129,65},{66,130},{130,66},{67,131},{13... | collective-permute-start | bytes 49160 | tf_op jit(solution)/shard_map/ppermute | solution.py:10
  100.5 0.3 collective-permute-start.23
  100.8 2.0 %collective-permute-start.24 = (bf16[16,512]{1,0:T(8,128)(2,1)S(1)}, bf16[16,512]{1,0:T(8,128)(2,1)S(1)}, u32[]{:S(2)}, u32[]{:S(2)}) collective-permute-start(bf16[16,512]{1,0:T(8,128)(2,1)S(1)} %fusion.52), channel_id=1, source_target_pairs={{1,2},{2,1},{3,4},{4,3},{5,6},{6,5},{7,8},{8,7},{9,10},{10,9},{11,... | collective-permute-start | bytes 49160 | tf_op jit(solution)/shard_map/ppermute | solution.py:10
  102.8 5.1 %collective-permute-done.24 = bf16[16,512]{1,0:T(8,128)(2,1)S(1)} collective-permute-done((bf16[16,512]{1,0:T(8,128)(2,1)S(1)}, bf16[16,512]{1,0:T(8,128)(2,1)S(1)}, u32[]{:S(2)}, u32[]{:S(2)}) %collective-permute-start.24) | collective-permute-done | bytes 16416 | tf_op jit(solution)/shard_map/ppermute | solution.py:10
  108.0 0.2 convolution_convert_fusion.2
  108.2 0.3 fusion.25
  108.5 0.9 collective-permute-done.25
  109.4 2.6 %collective-permute-start.27 = (bf16[16,512]{1,0:T(8,128)(2,1)S(1)}, bf16[16,512]{1,0:T(8,128)(2,1)S(1)}, u32[]{:S(2)}, u32[]{:S(2)}) collective-permute-start(bf16[16,512]{1,0:T(8,128)(2,1)S(1)} %fusion.53), channel_id=1, source_target_pairs={{64,128},{128,64},{65,129},{129,65},{66,130},{130,66},{67,131},{13... | collective-permute-start | bytes 49160 | tf_op jit(solution)/shard_map/ppermute | solution.py:10
  112.2 2.2 %collective-permute-start.29 = (bf16[16,512]{1,0:T(8,128)(2,1)S(1)}, bf16[16,512]{1,0:T(8,128)(2,1)S(1)}, u32[]{:S(2)}, u32[]{:S(2)}) collective-permute-start(bf16[16,512]{1,0:T(8,128)(2,1)S(1)} %fusion.53), channel_id=1, source_target_pairs={{1,2},{2,1},{3,4},{4,3},{5,6},{6,5},{7,8},{8,7},{9,10},{10,9},{11,... | collective-permute-start | bytes 49160 | tf_op jit(solution)/shard_map/ppermute | solution.py:10
  114.4 0.7 collective-permute-done.27
  115.1 4.3 %collective-permute-done.29 = bf16[16,512]{1,0:T(8,128)(2,1)S(1)} collective-permute-done((bf16[16,512]{1,0:T(8,128)(2,1)S(1)}, bf16[16,512]{1,0:T(8,128)(2,1)S(1)}, u32[]{:S(2)}, u32[]{:S(2)}) %collective-permute-start.29) | collective-permute-done | bytes 16416 | tf_op jit(solution)/shard_map/ppermute | solution.py:10
  119.4 0.1 reshape.91
  119.5 0.3 fusion
  119.8 0.3 fusion.1
  120.2 0.7 reshape.92
  (60 shorter events, 1.0 us)
Async XLA Ops:
  0.0 1.3 %copy-start = (bf16[1,8,256,256]{3,2,1,0:T(8,128)(2,1)S(1)}, bf16[1,8,256,256]{3,2,1,0:T(8,128)(2,1)}, u32[]{:S(2)}) copy-start(bf16[1,8,256,256]{3,2,1,0:T(8,128)(2,1)} %param.12) | copy-start | bytes 3145732
  0.0 2.6 %copy-start.7 = (s32[1,8,64]{2,1,0:T(8,128)S(1)}, s32[1,8,64]{2,1,0:T(8,128)}, u32[]{:S(2)}) copy-start(s32[1,8,64]{2,1,0:T(8,128)} %param.14) | copy-start | bytes 6148
  0.0 15.8 %copy-start.5 = (f32[1,3,4,512]{3,2,1,0:T(4,128)S(1)}, f32[1,3,4,512]{3,2,1,0:T(4,128)}, u32[]{:S(2)}) copy-start(f32[1,3,4,512]{3,2,1,0:T(4,128)} %param.15) | copy-start | bytes 73732
  0.0 18.6 %copy-start.1 = (bf16[1,3,512,512]{3,2,1,0:T(8,128)(2,1)S(1)}, bf16[1,3,512,512]{3,2,1,0:T(8,128)(2,1)}, u32[]{:S(2)}) copy-start(bf16[1,3,512,512]{3,2,1,0:T(8,128)(2,1)} %param.18) | copy-start | bytes 4718596
  3.0 12.8 %collective-permute-start = (bf16[16,512]{1,0:T(8,128)(2,1)S(1)}, bf16[16,512]{1,0:T(8,128)(2,1)S(1)}, u32[]{:S(2)}, u32[]{:S(2)}) collective-permute-start(bf16[16,512]{1,0:T(8,128)(2,1)S(1)} %convert_element_type.158), channel_id=1, source_target_pairs={{0,64},{64,0},{128,192},{192,128},{1,65},{65,1},{129,193},{193,129... | collective-permute-start | bytes 49160 | tf_op jit(solution)/shard_map/ppermute | solution.py:11
  3.5 12.3 %collective-permute-start.1 = (bf16[16,512]{1,0:T(8,128)(2,1)S(1)}, bf16[16,512]{1,0:T(8,128)(2,1)S(1)}, u32[]{:S(2)}, u32[]{:S(2)}) collective-permute-start(bf16[16,512]{1,0:T(8,128)(2,1)S(1)} %convert_element_type.158), channel_id=1, source_target_pairs={{64,128},{128,64},{65,129},{129,65},{66,130},{130,66},{67,131},{13... | collective-permute-start | bytes 49160 | tf_op jit(solution)/shard_map/ppermute | solution.py:10
  7.9 8.0 %collective-permute-start.2 = (bf16[16,512]{1,0:T(8,128)(2,1)S(1)}, bf16[16,512]{1,0:T(8,128)(2,1)S(1)}, u32[]{:S(2)}, u32[]{:S(2)}) collective-permute-start(bf16[16,512]{1,0:T(8,128)(2,1)S(1)} %convert_element_type.158), channel_id=1, source_target_pairs={{0,1},{1,0},{2,3},{3,2},{4,5},{5,4},{6,7},{7,6},{8,9},{9,8},{10,11... | collective-permute-start | bytes 49160 | tf_op jit(solution)/shard_map/ppermute | solution.py:11
  8.0 9.3 %collective-permute-start.3 = (bf16[16,512]{1,0:T(8,128)(2,1)S(1)}, bf16[16,512]{1,0:T(8,128)(2,1)S(1)}, u32[]{:S(2)}, u32[]{:S(2)}) collective-permute-start(bf16[16,512]{1,0:T(8,128)(2,1)S(1)} %convert_element_type.158), channel_id=1, source_target_pairs={{1,2},{2,1},{3,4},{4,3},{5,6},{6,5},{7,8},{8,7},{9,10},{10,9},{11,... | collective-permute-start | bytes 49160 | tf_op jit(solution)/shard_map/ppermute | solution.py:10
  17.2 1.3 %collective-permute-start.4 = (bf16[16,512]{1,0:T(8,128)(2,1)S(1)}, bf16[16,512]{1,0:T(8,128)(2,1)S(1)}, u32[]{:S(2)}, u32[]{:S(2)}) collective-permute-start(bf16[16,512]{1,0:T(8,128)(2,1)S(1)} %subtract_convert_fusion.4), channel_id=1, source_target_pairs={{0,1},{1,0},{2,3},{3,2},{4,5},{5,4},{6,7},{7,6},{8,9},{9,8},{10,11... | collective-permute-start | bytes 49160 | tf_op jit(solution)/shard_map/ppermute | solution.py:29
  18.6 30.0 %copy-start.4 = (bf16[1,32,512]{2,1,0:T(8,128)(2,1)S(1)}, bf16[1,32,512]{2,1,0:T(8,128)(2,1)}, u32[]{:S(2)}) copy-start(bf16[1,32,512]{2,1,0:T(8,128)(2,1)} %param.20) | copy-start | bytes 98308
  18.8 8.3 %collective-permute-start.5 = (bf16[16,512]{1,0:T(8,128)(2,1)S(1)}, bf16[16,512]{1,0:T(8,128)(2,1)S(1)}, u32[]{:S(2)}, u32[]{:S(2)}) collective-permute-start(bf16[16,512]{1,0:T(8,128)(2,1)S(1)} %get-tuple-element.29), channel_id=1, source_target_pairs={{0,64},{64,0},{128,192},{192,128},{1,65},{65,1},{129,193},{193,129... | collective-permute-start | bytes 49160 | tf_op jit(solution)/shard_map/ppermute | solution.py:11
  18.8 8.3 %collective-permute-start.6 = (bf16[16,512]{1,0:T(8,128)(2,1)S(1)}, bf16[16,512]{1,0:T(8,128)(2,1)S(1)}, u32[]{:S(2)}, u32[]{:S(2)}) collective-permute-start(bf16[16,512]{1,0:T(8,128)(2,1)S(1)} %get-tuple-element.29), channel_id=1, source_target_pairs={{64,128},{128,64},{65,129},{129,65},{66,130},{130,66},{67,131},{13... | collective-permute-start | bytes 49160 | tf_op jit(solution)/shard_map/ppermute | solution.py:10
  20.7 6.3 %collective-permute-start.7 = (bf16[16,512]{1,0:T(8,128)(2,1)S(1)}, bf16[16,512]{1,0:T(8,128)(2,1)S(1)}, u32[]{:S(2)}, u32[]{:S(2)}) collective-permute-start(bf16[16,512]{1,0:T(8,128)(2,1)S(1)} %get-tuple-element.29), channel_id=1, source_target_pairs={{0,1},{1,0},{2,3},{3,2},{4,5},{5,4},{6,7},{7,6},{8,9},{9,8},{10,11... | collective-permute-start | bytes 49160 | tf_op jit(solution)/shard_map/ppermute | solution.py:11
  21.3 7.2 %collective-permute-start.8 = (bf16[16,512]{1,0:T(8,128)(2,1)S(1)}, bf16[16,512]{1,0:T(8,128)(2,1)S(1)}, u32[]{:S(2)}, u32[]{:S(2)}) collective-permute-start(bf16[16,512]{1,0:T(8,128)(2,1)S(1)} %get-tuple-element.29), channel_id=1, source_target_pairs={{1,2},{2,1},{3,4},{4,3},{5,6},{6,5},{7,8},{8,7},{9,10},{10,9},{11,... | collective-permute-start | bytes 49160 | tf_op jit(solution)/shard_map/ppermute | solution.py:10
  28.4 3.8 %collective-permute-start.9 = (bf16[16,512]{1,0:T(8,128)(2,1)S(1)}, bf16[16,512]{1,0:T(8,128)(2,1)S(1)}, u32[]{:S(2)}, u32[]{:S(2)}) collective-permute-start(bf16[16,512]{1,0:T(8,128)(2,1)S(1)} %subtract_convert_fusion.3), channel_id=1, source_target_pairs={{0,2},{1,3},{2,0},{3,1},{4,6},{5,7},{6,4},{7,5},{8,10},{9,11},{10,... | collective-permute-start | bytes 49160 | tf_op jit(solution)/shard_map/ppermute | solution.py:29
  32.4 8.4 %collective-permute-start.10 = (bf16[16,512]{1,0:T(8,128)(2,1)S(1)}, bf16[16,512]{1,0:T(8,128)(2,1)S(1)}, u32[]{:S(2)}, u32[]{:S(2)}) collective-permute-start(bf16[16,512]{1,0:T(8,128)(2,1)S(1)} %get-tuple-element.31), channel_id=1, source_target_pairs={{0,64},{64,0},{128,192},{192,128},{1,65},{65,1},{129,193},{193,129... | collective-permute-start | bytes 49160 | tf_op jit(solution)/shard_map/ppermute | solution.py:11
  33.2 7.6 %collective-permute-start.11 = (bf16[16,512]{1,0:T(8,128)(2,1)S(1)}, bf16[16,512]{1,0:T(8,128)(2,1)S(1)}, u32[]{:S(2)}, u32[]{:S(2)}) collective-permute-start(bf16[16,512]{1,0:T(8,128)(2,1)S(1)} %get-tuple-element.31), channel_id=1, source_target_pairs={{64,128},{128,64},{65,129},{129,65},{66,130},{130,66},{67,131},{13... | collective-permute-start | bytes 49160 | tf_op jit(solution)/shard_map/ppermute | solution.py:10
  36.4 4.4 %collective-permute-start.12 = (bf16[16,512]{1,0:T(8,128)(2,1)S(1)}, bf16[16,512]{1,0:T(8,128)(2,1)S(1)}, u32[]{:S(2)}, u32[]{:S(2)}) collective-permute-start(bf16[16,512]{1,0:T(8,128)(2,1)S(1)} %get-tuple-element.31), channel_id=1, source_target_pairs={{0,1},{1,0},{2,3},{3,2},{4,5},{5,4},{6,7},{7,6},{8,9},{9,8},{10,11... | collective-permute-start | bytes 49160 | tf_op jit(solution)/shard_map/ppermute | solution.py:11
  36.5 7.2 %collective-permute-start.13 = (bf16[16,512]{1,0:T(8,128)(2,1)S(1)}, bf16[16,512]{1,0:T(8,128)(2,1)S(1)}, u32[]{:S(2)}, u32[]{:S(2)}) collective-permute-start(bf16[16,512]{1,0:T(8,128)(2,1)S(1)} %get-tuple-element.31), channel_id=1, source_target_pairs={{1,2},{2,1},{3,4},{4,3},{5,6},{6,5},{7,8},{8,7},{9,10},{10,9},{11,... | collective-permute-start | bytes 49160 | tf_op jit(solution)/shard_map/ppermute | solution.py:10
  43.7 4.7 %collective-permute-start.14 = (bf16[16,512]{1,0:T(8,128)(2,1)S(1)}, bf16[16,512]{1,0:T(8,128)(2,1)S(1)}, u32[]{:S(2)}, u32[]{:S(2)}) collective-permute-start(bf16[16,512]{1,0:T(8,128)(2,1)S(1)} %subtract_convert_fusion.2), channel_id=1, source_target_pairs={{0,4},{1,5},{2,6},{3,7},{4,0},{5,1},{6,2},{7,3},{8,12},{9,13},{10,... | collective-permute-start | bytes 49160 | tf_op jit(solution)/shard_map/ppermute | solution.py:29
  65.8 9.8 %all-to-all-start.1 = ((bf16[4,16,2048]{2,1,0:T(8,128)(2,1)}), bf16[4,16,2048]{2,1,0:T(8,128)(2,1)S(1)}, u32[]{:S(2)}, u32[]{:S(2)}) async-start(bf16[4,16,2048]{2,1,0:T(8,128)(2,1)} %broadcast_in_dim.7), calls=%async_computation.1 | async-start | bytes 524288 | tf_op jit(solution)/shard_map/all_to_all | solution.py:34
  70.0 19.3 %copy-start.6 = (f32[1,3,4,512]{3,2,1,0:T(4,128)S(1)}, f32[1,3,4,512]{3,2,1,0:T(4,128)}, u32[]{:S(2)}) copy-start(f32[1,3,4,512]{3,2,1,0:T(4,128)} %param.16) | copy-start | bytes 73732
  76.9 16.4 %copy-start.2 = (bf16[1,3,512,512]{3,2,1,0:T(8,128)(2,1)S(1)}, bf16[1,3,512,512]{3,2,1,0:T(8,128)(2,1)}, u32[]{:S(2)}) copy-start(bf16[1,3,512,512]{3,2,1,0:T(8,128)(2,1)} %param.17) | copy-start | bytes 4718596
  77.2 4.7 %collective-permute-start.15 = (bf16[16,512]{1,0:T(8,128)(2,1)S(1)}, bf16[16,512]{1,0:T(8,128)(2,1)S(1)}, u32[]{:S(2)}, u32[]{:S(2)}) collective-permute-start(bf16[16,512]{1,0:T(8,128)(2,1)S(1)} %convolution_convert_fusion.4), channel_id=1, source_target_pairs={{0,4},{1,5},{2,6},{3,7},{4,0},{5,1},{6,2},{7,3},{8,12},{9,13},{10,... | collective-permute-start | bytes 49160 | tf_op jit(solution)/shard_map/ppermute | solution.py:29
  79.4 40.0 %copy-start.3 = (bf16[1,8,64,256]{3,2,1,0:T(8,128)(2,1)S(1)}, bf16[1,8,64,256]{3,2,1,0:T(8,128)(2,1)}, u32[]{:S(2)}) copy-start(bf16[1,8,64,256]{3,2,1,0:T(8,128)(2,1)} %param.13) | copy-start | bytes 786436
  81.9 7.5 %collective-permute-start.16 = (bf16[16,512]{1,0:T(8,128)(2,1)S(1)}, bf16[16,512]{1,0:T(8,128)(2,1)S(1)}, u32[]{:S(2)}, u32[]{:S(2)}) collective-permute-start(bf16[16,512]{1,0:T(8,128)(2,1)S(1)} %fusion.51), channel_id=1, source_target_pairs={{0,64},{64,0},{128,192},{192,128},{1,65},{65,1},{129,193},{193,129... | collective-permute-start | bytes 49160 | tf_op jit(solution)/shard_map/ppermute | solution.py:11
  83.3 6.1 %collective-permute-start.17 = (bf16[16,512]{1,0:T(8,128)(2,1)S(1)}, bf16[16,512]{1,0:T(8,128)(2,1)S(1)}, u32[]{:S(2)}, u32[]{:S(2)}) collective-permute-start(bf16[16,512]{1,0:T(8,128)(2,1)S(1)} %fusion.51), channel_id=1, source_target_pairs={{64,128},{128,64},{65,129},{129,65},{66,130},{130,66},{67,131},{13... | collective-permute-start | bytes 49160 | tf_op jit(solution)/shard_map/ppermute | solution.py:10
  85.8 3.6 %collective-permute-start.18 = (bf16[16,512]{1,0:T(8,128)(2,1)S(1)}, bf16[16,512]{1,0:T(8,128)(2,1)S(1)}, u32[]{:S(2)}, u32[]{:S(2)}) collective-permute-start(bf16[16,512]{1,0:T(8,128)(2,1)S(1)} %fusion.51), channel_id=1, source_target_pairs={{0,1},{1,0},{2,3},{3,2},{4,5},{5,4},{6,7},{7,6},{8,9},{9,8},{10,11... | collective-permute-start | bytes 49160 | tf_op jit(solution)/shard_map/ppermute | solution.py:11
  85.9 7.2 %collective-permute-start.19 = (bf16[16,512]{1,0:T(8,128)(2,1)S(1)}, bf16[16,512]{1,0:T(8,128)(2,1)S(1)}, u32[]{:S(2)}, u32[]{:S(2)}) collective-permute-start(bf16[16,512]{1,0:T(8,128)(2,1)S(1)} %fusion.51), channel_id=1, source_target_pairs={{1,2},{2,1},{3,4},{4,3},{5,6},{6,5},{7,8},{8,7},{9,10},{10,9},{11,... | collective-permute-start | bytes 49160 | tf_op jit(solution)/shard_map/ppermute | solution.py:10
  93.3 3.8 %collective-permute-start.20 = (bf16[16,512]{1,0:T(8,128)(2,1)S(1)}, bf16[16,512]{1,0:T(8,128)(2,1)S(1)}, u32[]{:S(2)}, u32[]{:S(2)}) collective-permute-start(bf16[16,512]{1,0:T(8,128)(2,1)S(1)} %convolution_convert_fusion.3), channel_id=1, source_target_pairs={{0,2},{1,3},{2,0},{3,1},{4,6},{5,7},{6,4},{7,5},{8,10},{9,11},{10,... | collective-permute-start | bytes 49160 | tf_op jit(solution)/shard_map/ppermute | solution.py:29
  97.1 5.7 %collective-permute-start.21 = (bf16[16,512]{1,0:T(8,128)(2,1)S(1)}, bf16[16,512]{1,0:T(8,128)(2,1)S(1)}, u32[]{:S(2)}, u32[]{:S(2)}) collective-permute-start(bf16[16,512]{1,0:T(8,128)(2,1)S(1)} %fusion.52), channel_id=1, source_target_pairs={{0,64},{64,0},{128,192},{192,128},{1,65},{65,1},{129,193},{193,129... | collective-permute-start | bytes 49160 | tf_op jit(solution)/shard_map/ppermute | solution.py:11
  97.1 5.7 %collective-permute-start.22 = (bf16[16,512]{1,0:T(8,128)(2,1)S(1)}, bf16[16,512]{1,0:T(8,128)(2,1)S(1)}, u32[]{:S(2)}, u32[]{:S(2)}) collective-permute-start(bf16[16,512]{1,0:T(8,128)(2,1)S(1)} %fusion.52), channel_id=1, source_target_pairs={{64,128},{128,64},{65,129},{129,65},{66,130},{130,66},{67,131},{13... | collective-permute-start | bytes 49160 | tf_op jit(solution)/shard_map/ppermute | solution.py:10
  100.5 2.3 %collective-permute-start.23 = (bf16[16,512]{1,0:T(8,128)(2,1)S(1)}, bf16[16,512]{1,0:T(8,128)(2,1)S(1)}, u32[]{:S(2)}, u32[]{:S(2)}) collective-permute-start(bf16[16,512]{1,0:T(8,128)(2,1)S(1)} %fusion.52), channel_id=1, source_target_pairs={{0,1},{1,0},{2,3},{3,2},{4,5},{5,4},{6,7},{7,6},{8,9},{9,8},{10,11... | collective-permute-start | bytes 49160 | tf_op jit(solution)/shard_map/ppermute | solution.py:11
  100.8 7.2 %collective-permute-start.24 = (bf16[16,512]{1,0:T(8,128)(2,1)S(1)}, bf16[16,512]{1,0:T(8,128)(2,1)S(1)}, u32[]{:S(2)}, u32[]{:S(2)}) collective-permute-start(bf16[16,512]{1,0:T(8,128)(2,1)S(1)} %fusion.52), channel_id=1, source_target_pairs={{1,2},{2,1},{3,4},{4,3},{5,6},{6,5},{7,8},{8,7},{9,10},{10,9},{11,... | collective-permute-start | bytes 49160 | tf_op jit(solution)/shard_map/ppermute | solution.py:10
  108.2 1.2 collective-permute-start.25
  109.4 4.9 %collective-permute-start.26 = (bf16[16,512]{1,0:T(8,128)(2,1)S(1)}, bf16[16,512]{1,0:T(8,128)(2,1)S(1)}, u32[]{:S(2)}, u32[]{:S(2)}) collective-permute-start(bf16[16,512]{1,0:T(8,128)(2,1)S(1)} %fusion.53), channel_id=1, source_target_pairs={{0,64},{64,0},{128,192},{192,128},{1,65},{65,1},{129,193},{193,129... | collective-permute-start | bytes 49160 | tf_op jit(solution)/shard_map/ppermute | solution.py:11
  109.4 5.6 %collective-permute-start.27 = (bf16[16,512]{1,0:T(8,128)(2,1)S(1)}, bf16[16,512]{1,0:T(8,128)(2,1)S(1)}, u32[]{:S(2)}, u32[]{:S(2)}) collective-permute-start(bf16[16,512]{1,0:T(8,128)(2,1)S(1)} %fusion.53), channel_id=1, source_target_pairs={{64,128},{128,64},{65,129},{129,65},{66,130},{130,66},{67,131},{13... | collective-permute-start | bytes 49160 | tf_op jit(solution)/shard_map/ppermute | solution.py:10
  112.1 3.0 %collective-permute-start.28 = (bf16[16,512]{1,0:T(8,128)(2,1)S(1)}, bf16[16,512]{1,0:T(8,128)(2,1)S(1)}, u32[]{:S(2)}, u32[]{:S(2)}) collective-permute-start(bf16[16,512]{1,0:T(8,128)(2,1)S(1)} %fusion.53), channel_id=1, source_target_pairs={{0,1},{1,0},{2,3},{3,2},{4,5},{5,4},{6,7},{7,6},{8,9},{9,8},{10,11... | collective-permute-start | bytes 49160 | tf_op jit(solution)/shard_map/ppermute | solution.py:11
  112.2 7.2 %collective-permute-start.29 = (bf16[16,512]{1,0:T(8,128)(2,1)S(1)}, bf16[16,512]{1,0:T(8,128)(2,1)S(1)}, u32[]{:S(2)}, u32[]{:S(2)}) collective-permute-start(bf16[16,512]{1,0:T(8,128)(2,1)S(1)} %fusion.53), channel_id=1, source_target_pairs={{1,2},{2,1},{3,4},{4,3},{5,6},{6,5},{7,8},{8,7},{9,10},{10,9},{11,... | collective-permute-start | bytes 49160 | tf_op jit(solution)/shard_map/ppermute | solution.py:10

commit v10 on v9

--- a/solution.py
+++ b/solution.py
@@ -1,7 +1,10 @@
 import jax
 import jax.numpy as jnp
 from jax import lax
-from jax.sharding import PartitionSpec as P
+from jax.sharding import Mesh, PartitionSpec as P
+
+
+GX = ("gxa", "gxb")
 
 
 def both_sides(shard, axis):
@@ -14,7 +17,7 @@
 
 
 def neighbours_of(shard):
-    left, right = both_sides(shard, "gx")
+    left, right = both_sides(shard, GX)
     from_below, from_above = both_sides(shard, "gy")
     return from_below, from_above, left, right
 
@@ -91,20 +94,21 @@
     for level in range(level_count):
         mixed = state - neighbour_sum(state.astype(jnp.bfloat16), up_rates[level])
         rounded = mixed.astype(jnp.bfloat16)
-        partner = partner_2(rounded, "gx", level)
+        partner = partner_2(rounded, GX, level)
         state = jnp.dot(rounded, own[level], preferred_element_type=jnp.float32)
         state = state + jnp.dot(partner, other[level], preferred_element_type=jnp.float32)
     top_state = state.astype(jnp.bfloat16)
     comp = compress[0]
     small = right_transpose(top_state, comp).astype(jnp.bfloat16)
-    row_values = collect(small, "gx", 1)
-    coarse = jnp.dot(collect(row_values, "gy", 1), top_couple, preferred_element_type=jnp.float32)
+    row_values = collect(small, "gxb", 1)
+    gathered = collect(row_values, ("gy", "gxa"), 1)
+    coarse = jnp.dot(gathered, top_couple, preferred_element_type=jnp.float32)
     state = jnp.dot(top_state, top_inverse[0], preferred_element_type=jnp.float32)
     state = state + jnp.dot(coarse.astype(jnp.bfloat16), comp, preferred_element_type=jnp.float32)
     for level in reversed(range(level_count)):
         rounded = state.astype(jnp.bfloat16)
         sent = right_transpose(rounded, other[level])
-        received = partner_2(sent.astype(jnp.bfloat16), "gx", level).astype(sent.dtype)
+        received = partner_2(sent.astype(jnp.bfloat16), GX, level).astype(sent.dtype)
         mixed = lax.optimization_barrier(right_transpose(rounded, own[level])) + received
         state = mixed - neighbour_sum(mixed.astype(jnp.bfloat16), down_rates[level])
     skeleton = state.reshape(field_count, box_count, skel_size)
@@ -119,18 +123,20 @@
 
 def solution(mesh):
     placed = (
-        P("gy", None, "gx"),
-        P("gy", "gx", None, None),
-        P("gy", "gx", None, None),
-        P("gy", "gx", None),
-        P("gy", "gx", None, None),
-        P("gy", "gx", None, None),
-        P("gy", "gx", None, None),
-        P("gy", "gx", None, None),
-        P("gy", "gx", None),
-        P("gy", "gx", None),
-        P(None, ("gy", "gx")),
+        P("gy", None, GX),
+        P("gy", GX, None, None),
+        P("gy", GX, None, None),
+        P("gy", GX, None),
+        P("gy", GX, None, None),
+        P("gy", GX, None, None),
+        P("gy", GX, None, None),
+        P("gy", GX, None, None),
+        P("gy", GX, None),
+        P("gy", GX, None),
+        P(None, ("gy",) + GX),
     )
+    rows, cols = mesh.devices.shape
+    split = Mesh(mesh.devices.reshape(rows, 4, cols // 4), ("gy",) + GX)
     return jax.shard_map(
-        body, mesh=mesh, in_specs=placed, out_specs=P("gy", None, "gx"), check_vma=False
+        body, mesh=split, in_specs=placed, out_specs=P("gy", None, GX), check_vma=False
     )

time: 122 us -> 120 us (0.984)
  blocking collectives: 15.5 us -> 10.9 us
  starting transfers between devices: 52.9 us -> 55.6 us
  waiting for transfers between devices: 36.4 us -> 38.3 us
    all_to_all x1, blocking collectives: 15.5 us -> 10.9 us  [sent_to_all(): return lax.all_to_all(copies, axis, split_axis=0, concat_axis=0, tiled=True)]
    all_to_all x1, starting transfers between devices: 4.28 us -> 6.74 us  [sent_to_all(): return lax.all_to_all(copies, axis, split_axis=0, concat_axis=0, tiled=True)]
    all_to_all x1, waiting for transfers between devices: 4.27 us -> 5.66 us  [sent_to_all(): return lax.all_to_all(copies, axis, split_axis=0, concat_axis=0, tiled=True)]
  transfers between devices with their start and end apart: 31 -> 31, of which waited for: 13 -> 13; matrix products, arithmetic and copies ran while one was open for 6% -> 5% of each run, Pallas kernels for 0% -> 0%
where the time goes in v10:
time: 120 us
  starting transfers between devices  55.6 us (46%)
  waiting for transfers between devices  38.3 us (32%)
  blocking collectives  10.9 us (9%)
  matrix products  10.6 us (9%)
  local copies, waits for them, and re-layouts  3.41 us (3%)
    ppermute x12, starting transfers between devices, both_sides(): lax.ppermute(shard, axis, [(a, b) for a, b in pairs if 0 <= b < size])  43.3 us
    ppermute x12, waiting for transfers between devices, both_sides(): lax.ppermute(shard, axis, [(a, b) for a, b in pairs if 0 <= b < size])  19.3 us
    ppermute x6, waiting for transfers between devices, partner_2(): lax.ppermute(shard, axis, [(i, i ^ 1 << stride) for i in range(lax.axis_s...  13.3 us
    all_to_all x1, blocking collectives, sent_to_all(): return lax.all_to_all(copies, axis, split_axis=0, concat_axis=0, tiled=True)  10.9 us
    all_to_all x1, starting transfers between devices, sent_to_all(): return lax.all_to_all(copies, axis, split_axis=0, concat_axis=0, tiled=True)  6.74 us
    all_to_all x1, waiting for transfers between devices, sent_to_all(): return lax.all_to_all(copies, axis, split_axis=0, concat_axis=0, tiled=True)  5.66 us
    ppermute x12, starting transfers between devices, both_sides(): beside = lax.ppermute(shard, axis, [(i, i ^ 1) for i in range(size)])  4.67 us
    dot_general x3, matrix products, body(): state = jnp.dot(rounded, own[level], preferred_element_type=jnp.float32)  3.64 us
  transfers between devices with their start and end apart: 31, of which 13 were waited for; matrix products, arithmetic and copies ran while one was open for 5% of the time, Pallas kernels for 0%

profile of v10, /device:TPU:10, one launch (start us, length us, event | category | flops | bytes accessed | tf_op | source)
XLA Modules:
  0.0 119.5 jit_solution(3498200517078828080)
XLA Ops:
  0.0 1.0 copy.29
  1.0 0.2 copy-done
  1.3 0.2 fusion.3
  1.5 1.1 convolution_bitcast_fusion.2
  2.6 0.3 fusion.4
  3.0 0.5 collective-permute-start
  3.5 4.3 %collective-permute-start.1 = (bf16[16,512]{1,0:T(8,128)(2,1)S(1)}, bf16[16,512]{1,0:T(8,128)(2,1)S(1)}, u32[]{:S(2)}, u32[]{:S(2)}) collective-permute-start(bf16[16,512]{1,0:T(8,128)(2,1)S(1)} %convert_element_type.158), channel_id=1, source_target_pairs={{64,128},{128,64},{65,129},{129,65},{66,130},{130,66},{67,131},{13... | collective-permute-start | bytes 49160 | tf_op jit(solution)/shard_map/ppermute | solution.py:13
  8.0 7.8 %collective-permute-start.3 = (bf16[16,512]{1,0:T(8,128)(2,1)S(1)}, bf16[16,512]{1,0:T(8,128)(2,1)S(1)}, u32[]{:S(2)}, u32[]{:S(2)}) collective-permute-start(bf16[16,512]{1,0:T(8,128)(2,1)S(1)} %convert_element_type.158), channel_id=1, source_target_pairs={{1,2},{2,1},{3,4},{4,3},{5,6},{6,5},{7,8},{8,7},{9,10},{10,9},{11,... | collective-permute-start | bytes 49160 | tf_op jit(solution)/shard_map/ppermute | solution.py:13
  15.9 1.3 %collective-permute-done.3 = bf16[16,512]{1,0:T(8,128)(2,1)S(1)} collective-permute-done((bf16[16,512]{1,0:T(8,128)(2,1)S(1)}, bf16[16,512]{1,0:T(8,128)(2,1)S(1)}, u32[]{:S(2)}, u32[]{:S(2)}) %collective-permute-start.3) | collective-permute-done | bytes 16416 | tf_op jit(solution)/shard_map/ppermute | solution.py:13
  17.2 0.1 collective-permute-start.4
  17.3 1.2 %fusion.27 = f32[16,512]{1,0:T(8,128)S(1)} fusion(bf16[16,512]{1,0:T(8,128)(2,1)S(1)} %subtract_convert_fusion.4, bf16[1,3,512,512]{3,2,1,0:T(8,128)(2,1)} %param.17), kind=kOutput, calls=%fused_computation.42 | convolution fusion | flops 8388608 | bytes 573440 | tf_op jit(solution)/shard_map/dot_general | solution.py:98
  18.6 0.2 fusion.56
  18.8 1.9 %collective-permute-start.6 = (bf16[16,512]{1,0:T(8,128)(2,1)S(1)}, bf16[16,512]{1,0:T(8,128)(2,1)S(1)}, u32[]{:S(2)}, u32[]{:S(2)}) collective-permute-start(bf16[16,512]{1,0:T(8,128)(2,1)S(1)} %get-tuple-element.29), channel_id=1, source_target_pairs={{64,128},{128,64},{65,129},{129,65},{66,130},{130,66},{67,131},{13... | collective-permute-start | bytes 49160 | tf_op jit(solution)/shard_map/ppermute | solution.py:13
  20.7 0.6 collective-permute-start.7
  21.3 5.7 %collective-permute-start.8 = (bf16[16,512]{1,0:T(8,128)(2,1)S(1)}, bf16[16,512]{1,0:T(8,128)(2,1)S(1)}, u32[]{:S(2)}, u32[]{:S(2)}) collective-permute-start(bf16[16,512]{1,0:T(8,128)(2,1)S(1)} %get-tuple-element.29), channel_id=1, source_target_pairs={{1,2},{2,1},{3,4},{4,3},{5,6},{6,5},{7,8},{8,7},{9,10},{10,9},{11,... | collective-permute-start | bytes 49160 | tf_op jit(solution)/shard_map/ppermute | solution.py:13
  27.0 1.4 %collective-permute-done.8 = bf16[16,512]{1,0:T(8,128)(2,1)S(1)} collective-permute-done((bf16[16,512]{1,0:T(8,128)(2,1)S(1)}, bf16[16,512]{1,0:T(8,128)(2,1)S(1)}, u32[]{:S(2)}, u32[]{:S(2)}) %collective-permute-start.8) | collective-permute-done | bytes 16416 | tf_op jit(solution)/shard_map/ppermute | solution.py:13
  28.5 0.1 collective-permute-start.9
  28.6 1.2 %fusion.21 = f32[16,512]{1,0:T(8,128)S(1)} fusion(bf16[16,512]{1,0:T(8,128)(2,1)S(1)} %subtract_convert_fusion.3, bf16[1,3,512,512]{3,2,1,0:T(8,128)(2,1)} %param.17), kind=kOutput, calls=%fused_computation.36 | convolution fusion | flops 8388608 | bytes 573440 | tf_op jit(solution)/shard_map/dot_general | solution.py:98
  29.8 2.5 %collective-permute-done.9 = bf16[16,512]{1,0:T(8,128)(2,1)S(1)} collective-permute-done((bf16[16,512]{1,0:T(8,128)(2,1)S(1)}, bf16[16,512]{1,0:T(8,128)(2,1)S(1)}, u32[]{:S(2)}, u32[]{:S(2)}) %collective-permute-start.9) | collective-permute-done | bytes 16416 | tf_op jit(solution)/shard_map/ppermute | solution.py:32
  32.3 0.2 fusion.57
  32.5 0.8 collective-permute-start.10
  33.2 3.1 %collective-permute-start.11 = (bf16[16,512]{1,0:T(8,128)(2,1)S(1)}, bf16[16,512]{1,0:T(8,128)(2,1)S(1)}, u32[]{:S(2)}, u32[]{:S(2)}) collective-permute-start(bf16[16,512]{1,0:T(8,128)(2,1)S(1)} %get-tuple-element.31), channel_id=1, source_target_pairs={{64,128},{128,64},{65,129},{129,65},{66,130},{130,66},{67,131},{13... | collective-permute-start | bytes 49160 | tf_op jit(solution)/shard_map/ppermute | solution.py:13
  36.4 0.1 collective-permute-start.12
  36.5 4.3 %collective-permute-start.13 = (bf16[16,512]{1,0:T(8,128)(2,1)S(1)}, bf16[16,512]{1,0:T(8,128)(2,1)S(1)}, u32[]{:S(2)}, u32[]{:S(2)}) collective-permute-start(bf16[16,512]{1,0:T(8,128)(2,1)S(1)} %get-tuple-element.31), channel_id=1, source_target_pairs={{1,2},{2,1},{3,4},{4,3},{5,6},{6,5},{7,8},{8,7},{9,10},{10,9},{11,... | collective-permute-start | bytes 49160 | tf_op jit(solution)/shard_map/ppermute | solution.py:13
  40.8 2.8 %collective-permute-done.13 = bf16[16,512]{1,0:T(8,128)(2,1)S(1)} collective-permute-done((bf16[16,512]{1,0:T(8,128)(2,1)S(1)}, bf16[16,512]{1,0:T(8,128)(2,1)S(1)}, u32[]{:S(2)}, u32[]{:S(2)}) %collective-permute-start.13) | collective-permute-done | bytes 16416 | tf_op jit(solution)/shard_map/ppermute | solution.py:13
  43.7 0.1 collective-permute-start.14
  43.8 1.2 %fusion.15 = f32[16,512]{1,0:T(8,128)S(1)} fusion(bf16[16,512]{1,0:T(8,128)(2,1)S(1)} %subtract_convert_fusion.2, bf16[1,3,512,512]{3,2,1,0:T(8,128)(2,1)} %param.17), kind=kOutput, calls=%fused_computation.30 | convolution fusion | flops 8388608 | bytes 573440 | tf_op jit(solution)/shard_map/dot_general | solution.py:98
  45.0 3.4 %collective-permute-done.14 = bf16[16,512]{1,0:T(8,128)(2,1)S(1)} collective-permute-done((bf16[16,512]{1,0:T(8,128)(2,1)S(1)}, bf16[16,512]{1,0:T(8,128)(2,1)S(1)}, u32[]{:S(2)}, u32[]{:S(2)}) %collective-permute-start.14) | collective-permute-done | bytes 16416 | tf_op jit(solution)/shard_map/ppermute | solution.py:32
  48.4 0.2 fusion.6
  48.6 0.1 convolution_convert_fusion.6
  48.7 0.1 reshape.93
  48.8 10.9 %all_to_all.10 = bf16[16,2,256]{2,1,0:T(2,128)(2,1)S(1)} all-to-all(bf16[16,2,256]{2,1,0:T(2,128)(2,1)S(1)} %reshape.93), channel_id=1, replica_groups=mesh['gy'=4,'gxa'=4,'gxb'=16] {'gxb'}, dimensions={0} | all-to-all | bytes 32768 | tf_op jit(solution)/shard_map/all_to_all | solution.py:37
  59.8 0.1 reshape.94
  59.9 0.1 reshape.89
  60.0 0.7 broadcast_in_dim.7
  60.8 6.7 %all-to-all-start.1 = ((bf16[16,16,512]{2,1,0:T(8,128)(2,1)}), bf16[16,16,512]{2,1,0:T(8,128)(2,1)S(1)}, u32[]{:S(2)}, u32[]{:S(2)}) async-start(bf16[16,16,512]{2,1,0:T(8,128)(2,1)} %broadcast_in_dim.7), calls=%async_computation.1 | async-start | bytes 524288 | tf_op jit(solution)/shard_map/all_to_all | solution.py:37
  67.5 0.2 fusion.9
  67.7 5.7 %all-to-all-done.1 = bf16[16,16,512]{2,1,0:T(8,128)(2,1)S(1)} async-done(((bf16[16,16,512]{2,1,0:T(8,128)(2,1)}), bf16[16,16,512]{2,1,0:T(8,128)(2,1)S(1)}, u32[]{:S(2)}, u32[]{:S(2)}) %all-to-all-start.1) | async-done | bytes 262176 | tf_op jit(solution)/shard_map/all_to_all | solution.py:37
  73.4 1.4 %fusion.5 = bf16[16,512]{1,0:T(8,128)(2,1)S(1)} fusion(f32[16,512]{1,0:T(8,128)S(1)} %fusion.9, bf16[16,8192]{1,0:T(8,128)(2,1)S(1)} %bitcast.123, bf16[8192,32]{0,1:T(8,128)(2,1)} %param.21, bf16[1,32,512]{2,1,0:T(8,128)(2,1)S(1)} %copy-done.5), kind=kOutput, calls=%fused_computation.15 | convolution fusion | flops 8929792 | bytes 868352 | tf_op jit(solution)/shard_map/dot_general | solution.py:107
  74.8 0.2 convolution_convert_fusion.4
  75.0 0.6 collective-permute-start.15
  75.7 1.3 %fusion.13 = f32[16,512]{1,0:T(8,128)S(1)} fusion(bf16[16,512]{1,0:T(8,128)(2,1)S(1)} %fusion.5, bf16[1,3,512,512]{3,2,1,0:T(8,128)(2,1)} %param.17), kind=kOutput, calls=%fused_computation.28 | convolution fusion | flops 8388608 | bytes 573440 | tf_op jit(solution)/shard_map/dot_general | solution.py:52
  76.9 2.9 %collective-permute-done.15 = bf16[16,512]{1,0:T(8,128)(2,1)S(1)} collective-permute-done((bf16[16,512]{1,0:T(8,128)(2,1)S(1)}, bf16[16,512]{1,0:T(8,128)(2,1)S(1)}, u32[]{:S(2)}, u32[]{:S(2)}) %collective-permute-start.15) | collective-permute-done | bytes 16416 | tf_op jit(solution)/shard_map/ppermute | solution.py:32
  79.9 2.3 %collective-permute-start.16 = (bf16[16,512]{1,0:T(8,128)(2,1)S(1)}, bf16[16,512]{1,0:T(8,128)(2,1)S(1)}, u32[]{:S(2)}, u32[]{:S(2)}) collective-permute-start(bf16[16,512]{1,0:T(8,128)(2,1)S(1)} %fusion.51), channel_id=1, source_target_pairs={{0,64},{64,0},{128,192},{192,128},{1,65},{65,1},{129,193},{193,129... | collective-permute-start | bytes 49160 | tf_op jit(solution)/shard_map/ppermute | solution.py:14
  82.2 2.1 %collective-permute-start.17 = (bf16[16,512]{1,0:T(8,128)(2,1)S(1)}, bf16[16,512]{1,0:T(8,128)(2,1)S(1)}, u32[]{:S(2)}, u32[]{:S(2)}) collective-permute-start(bf16[16,512]{1,0:T(8,128)(2,1)S(1)} %fusion.51), channel_id=1, source_target_pairs={{64,128},{128,64},{65,129},{129,65},{66,130},{130,66},{67,131},{13... | collective-permute-start | bytes 49160 | tf_op jit(solution)/shard_map/ppermute | solution.py:13
  84.4 3.5 %collective-permute-start.19 = (bf16[16,512]{1,0:T(8,128)(2,1)S(1)}, bf16[16,512]{1,0:T(8,128)(2,1)S(1)}, u32[]{:S(2)}, u32[]{:S(2)}) collective-permute-start(bf16[16,512]{1,0:T(8,128)(2,1)S(1)} %fusion.51), channel_id=1, source_target_pairs={{1,2},{2,1},{3,4},{4,3},{5,6},{6,5},{7,8},{8,7},{9,10},{10,9},{11,... | collective-permute-start | bytes 49160 | tf_op jit(solution)/shard_map/ppermute | solution.py:13
  88.0 3.6 %collective-permute-done.19 = bf16[16,512]{1,0:T(8,128)(2,1)S(1)} collective-permute-done((bf16[16,512]{1,0:T(8,128)(2,1)S(1)}, bf16[16,512]{1,0:T(8,128)(2,1)S(1)}, u32[]{:S(2)}, u32[]{:S(2)}) %collective-permute-start.19) | collective-permute-done | bytes 16416 | tf_op jit(solution)/shard_map/ppermute | solution.py:13
  91.6 0.2 convolution_convert_fusion.3
  91.9 0.2 fusion.19
  92.1 3.5 %collective-permute-done.20 = bf16[16,512]{1,0:T(8,128)(2,1)S(1)} collective-permute-done((bf16[16,512]{1,0:T(8,128)(2,1)S(1)}, bf16[16,512]{1,0:T(8,128)(2,1)S(1)}, u32[]{:S(2)}, u32[]{:S(2)}) %collective-permute-start.20) | collective-permute-done | bytes 16416 | tf_op jit(solution)/shard_map/ppermute | solution.py:32
  95.7 3.7 %collective-permute-start.22 = (bf16[16,512]{1,0:T(8,128)(2,1)S(1)}, bf16[16,512]{1,0:T(8,128)(2,1)S(1)}, u32[]{:S(2)}, u32[]{:S(2)}) collective-permute-start(bf16[16,512]{1,0:T(8,128)(2,1)S(1)} %fusion.52), channel_id=1, source_target_pairs={{64,128},{128,64},{65,129},{129,65},{66,130},{130,66},{67,131},{13... | collective-permute-start | bytes 49160 | tf_op jit(solution)/shard_map/ppermute | solution.py:13
  99.4 2.0 %collective-permute-start.24 = (bf16[16,512]{1,0:T(8,128)(2,1)S(1)}, bf16[16,512]{1,0:T(8,128)(2,1)S(1)}, u32[]{:S(2)}, u32[]{:S(2)}) collective-permute-start(bf16[16,512]{1,0:T(8,128)(2,1)S(1)} %fusion.52), channel_id=1, source_target_pairs={{1,2},{2,1},{3,4},{4,3},{5,6},{6,5},{7,8},{8,7},{9,10},{10,9},{11,... | collective-permute-start | bytes 49160 | tf_op jit(solution)/shard_map/ppermute | solution.py:13
  101.5 5.1 %collective-permute-done.24 = bf16[16,512]{1,0:T(8,128)(2,1)S(1)} collective-permute-done((bf16[16,512]{1,0:T(8,128)(2,1)S(1)}, bf16[16,512]{1,0:T(8,128)(2,1)S(1)}, u32[]{:S(2)}, u32[]{:S(2)}) %collective-permute-start.24) | collective-permute-done | bytes 16416 | tf_op jit(solution)/shard_map/ppermute | solution.py:13
  106.6 0.2 convolution_convert_fusion.2
  106.9 0.3 fusion.25
  107.1 0.9 collective-permute-done.25
  108.1 2.6 %collective-permute-start.27 = (bf16[16,512]{1,0:T(8,128)(2,1)S(1)}, bf16[16,512]{1,0:T(8,128)(2,1)S(1)}, u32[]{:S(2)}, u32[]{:S(2)}) collective-permute-start(bf16[16,512]{1,0:T(8,128)(2,1)S(1)} %fusion.53), channel_id=1, source_target_pairs={{64,128},{128,64},{65,129},{129,65},{66,130},{130,66},{67,131},{13... | collective-permute-start | bytes 49160 | tf_op jit(solution)/shard_map/ppermute | solution.py:13
  110.9 2.2 %collective-permute-start.29 = (bf16[16,512]{1,0:T(8,128)(2,1)S(1)}, bf16[16,512]{1,0:T(8,128)(2,1)S(1)}, u32[]{:S(2)}, u32[]{:S(2)}) collective-permute-start(bf16[16,512]{1,0:T(8,128)(2,1)S(1)} %fusion.53), channel_id=1, source_target_pairs={{1,2},{2,1},{3,4},{4,3},{5,6},{6,5},{7,8},{8,7},{9,10},{10,9},{11,... | collective-permute-start | bytes 49160 | tf_op jit(solution)/shard_map/ppermute | solution.py:13
  113.0 0.7 collective-permute-done.27
  113.7 4.3 %collective-permute-done.29 = bf16[16,512]{1,0:T(8,128)(2,1)S(1)} collective-permute-done((bf16[16,512]{1,0:T(8,128)(2,1)S(1)}, bf16[16,512]{1,0:T(8,128)(2,1)S(1)}, u32[]{:S(2)}, u32[]{:S(2)}) %collective-permute-start.29) | collective-permute-done | bytes 16416 | tf_op jit(solution)/shard_map/ppermute | solution.py:13
  118.1 0.1 reshape.91
  118.2 0.3 fusion
  118.5 0.3 fusion.1
  118.9 0.7 reshape.92
  (64 shorter events, 1.0 us)
Async XLA Ops:
  0.0 1.3 %copy-start = (bf16[1,8,256,256]{3,2,1,0:T(8,128)(2,1)S(1)}, bf16[1,8,256,256]{3,2,1,0:T(8,128)(2,1)}, u32[]{:S(2)}) copy-start(bf16[1,8,256,256]{3,2,1,0:T(8,128)(2,1)} %param.12) | copy-start | bytes 3145732
  0.0 2.6 %copy-start.8 = (s32[1,8,64]{2,1,0:T(8,128)S(1)}, s32[1,8,64]{2,1,0:T(8,128)}, u32[]{:S(2)}) copy-start(s32[1,8,64]{2,1,0:T(8,128)} %param.14) | copy-start | bytes 6148
  0.0 15.8 %copy-start.6 = (f32[1,3,4,512]{3,2,1,0:T(4,128)S(1)}, f32[1,3,4,512]{3,2,1,0:T(4,128)}, u32[]{:S(2)}) copy-start(f32[1,3,4,512]{3,2,1,0:T(4,128)} %param.15) | copy-start | bytes 73732
  0.0 18.6 %copy-start.1 = (bf16[1,3,512,512]{3,2,1,0:T(8,128)(2,1)S(1)}, bf16[1,3,512,512]{3,2,1,0:T(8,128)(2,1)}, u32[]{:S(2)}) copy-start(bf16[1,3,512,512]{3,2,1,0:T(8,128)(2,1)} %param.18) | copy-start | bytes 4718596
  3.0 12.8 %collective-permute-start = (bf16[16,512]{1,0:T(8,128)(2,1)S(1)}, bf16[16,512]{1,0:T(8,128)(2,1)S(1)}, u32[]{:S(2)}, u32[]{:S(2)}) collective-permute-start(bf16[16,512]{1,0:T(8,128)(2,1)S(1)} %convert_element_type.158), channel_id=1, source_target_pairs={{0,64},{64,0},{128,192},{192,128},{1,65},{65,1},{129,193},{193,129... | collective-permute-start | bytes 49160 | tf_op jit(solution)/shard_map/ppermute | solution.py:14
  3.5 12.3 %collective-permute-start.1 = (bf16[16,512]{1,0:T(8,128)(2,1)S(1)}, bf16[16,512]{1,0:T(8,128)(2,1)S(1)}, u32[]{:S(2)}, u32[]{:S(2)}) collective-permute-start(bf16[16,512]{1,0:T(8,128)(2,1)S(1)} %convert_element_type.158), channel_id=1, source_target_pairs={{64,128},{128,64},{65,129},{129,65},{66,130},{130,66},{67,131},{13... | collective-permute-start | bytes 49160 | tf_op jit(solution)/shard_map/ppermute | solution.py:13
  7.9 8.0 %collective-permute-start.2 = (bf16[16,512]{1,0:T(8,128)(2,1)S(1)}, bf16[16,512]{1,0:T(8,128)(2,1)S(1)}, u32[]{:S(2)}, u32[]{:S(2)}) collective-permute-start(bf16[16,512]{1,0:T(8,128)(2,1)S(1)} %convert_element_type.158), channel_id=1, source_target_pairs={{0,1},{1,0},{2,3},{3,2},{4,5},{5,4},{6,7},{7,6},{8,9},{9,8},{10,11... | collective-permute-start | bytes 49160 | tf_op jit(solution)/shard_map/ppermute | solution.py:14
  8.0 9.3 %collective-permute-start.3 = (bf16[16,512]{1,0:T(8,128)(2,1)S(1)}, bf16[16,512]{1,0:T(8,128)(2,1)S(1)}, u32[]{:S(2)}, u32[]{:S(2)}) collective-permute-start(bf16[16,512]{1,0:T(8,128)(2,1)S(1)} %convert_element_type.158), channel_id=1, source_target_pairs={{1,2},{2,1},{3,4},{4,3},{5,6},{6,5},{7,8},{8,7},{9,10},{10,9},{11,... | collective-permute-start | bytes 49160 | tf_op jit(solution)/shard_map/ppermute | solution.py:13
  17.2 1.3 %collective-permute-start.4 = (bf16[16,512]{1,0:T(8,128)(2,1)S(1)}, bf16[16,512]{1,0:T(8,128)(2,1)S(1)}, u32[]{:S(2)}, u32[]{:S(2)}) collective-permute-start(bf16[16,512]{1,0:T(8,128)(2,1)S(1)} %subtract_convert_fusion.4), channel_id=1, source_target_pairs={{0,1},{1,0},{2,3},{3,2},{4,5},{5,4},{6,7},{7,6},{8,9},{9,8},{10,11... | collective-permute-start | bytes 49160 | tf_op jit(solution)/shard_map/ppermute | solution.py:32
  18.6 30.0 %copy-start.5 = (bf16[1,32,512]{2,1,0:T(8,128)(2,1)S(1)}, bf16[1,32,512]{2,1,0:T(8,128)(2,1)}, u32[]{:S(2)}) copy-start(bf16[1,32,512]{2,1,0:T(8,128)(2,1)} %param.20) | copy-start | bytes 98308
  18.8 8.3 %collective-permute-start.5 = (bf16[16,512]{1,0:T(8,128)(2,1)S(1)}, bf16[16,512]{1,0:T(8,128)(2,1)S(1)}, u32[]{:S(2)}, u32[]{:S(2)}) collective-permute-start(bf16[16,512]{1,0:T(8,128)(2,1)S(1)} %get-tuple-element.29), channel_id=1, source_target_pairs={{0,64},{64,0},{128,192},{192,128},{1,65},{65,1},{129,193},{193,129... | collective-permute-start | bytes 49160 | tf_op jit(solution)/shard_map/ppermute | solution.py:14
  18.8 8.3 %collective-permute-start.6 = (bf16[16,512]{1,0:T(8,128)(2,1)S(1)}, bf16[16,512]{1,0:T(8,128)(2,1)S(1)}, u32[]{:S(2)}, u32[]{:S(2)}) collective-permute-start(bf16[16,512]{1,0:T(8,128)(2,1)S(1)} %get-tuple-element.29), channel_id=1, source_target_pairs={{64,128},{128,64},{65,129},{129,65},{66,130},{130,66},{67,131},{13... | collective-permute-start | bytes 49160 | tf_op jit(solution)/shard_map/ppermute | solution.py:13
  20.7 6.3 %collective-permute-start.7 = (bf16[16,512]{1,0:T(8,128)(2,1)S(1)}, bf16[16,512]{1,0:T(8,128)(2,1)S(1)}, u32[]{:S(2)}, u32[]{:S(2)}) collective-permute-start(bf16[16,512]{1,0:T(8,128)(2,1)S(1)} %get-tuple-element.29), channel_id=1, source_target_pairs={{0,1},{1,0},{2,3},{3,2},{4,5},{5,4},{6,7},{7,6},{8,9},{9,8},{10,11... | collective-permute-start | bytes 49160 | tf_op jit(solution)/shard_map/ppermute | solution.py:14
  21.3 7.2 %collective-permute-start.8 = (bf16[16,512]{1,0:T(8,128)(2,1)S(1)}, bf16[16,512]{1,0:T(8,128)(2,1)S(1)}, u32[]{:S(2)}, u32[]{:S(2)}) collective-permute-start(bf16[16,512]{1,0:T(8,128)(2,1)S(1)} %get-tuple-element.29), channel_id=1, source_target_pairs={{1,2},{2,1},{3,4},{4,3},{5,6},{6,5},{7,8},{8,7},{9,10},{10,9},{11,... | collective-permute-start | bytes 49160 | tf_op jit(solution)/shard_map/ppermute | solution.py:13
  28.5 3.8 %collective-permute-start.9 = (bf16[16,512]{1,0:T(8,128)(2,1)S(1)}, bf16[16,512]{1,0:T(8,128)(2,1)S(1)}, u32[]{:S(2)}, u32[]{:S(2)}) collective-permute-start(bf16[16,512]{1,0:T(8,128)(2,1)S(1)} %subtract_convert_fusion.3), channel_id=1, source_target_pairs={{0,2},{1,3},{2,0},{3,1},{4,6},{5,7},{6,4},{7,5},{8,10},{9,11},{10,... | collective-permute-start | bytes 49160 | tf_op jit(solution)/shard_map/ppermute | solution.py:32
  29.8 37.7 %copy-start.4 = (bf16[1,512,512]{2,1,0:T(8,128)(2,1)S(1)}, bf16[1,512,512]{2,1,0:T(8,128)(2,1)}, u32[]{:S(2)}) copy-start(bf16[1,512,512]{2,1,0:T(8,128)(2,1)} %param.19) | copy-start | bytes 1572868
  32.5 8.4 %collective-permute-start.10 = (bf16[16,512]{1,0:T(8,128)(2,1)S(1)}, bf16[16,512]{1,0:T(8,128)(2,1)S(1)}, u32[]{:S(2)}, u32[]{:S(2)}) collective-permute-start(bf16[16,512]{1,0:T(8,128)(2,1)S(1)} %get-tuple-element.31), channel_id=1, source_target_pairs={{0,64},{64,0},{128,192},{192,128},{1,65},{65,1},{129,193},{193,129... | collective-permute-start | bytes 49160 | tf_op jit(solution)/shard_map/ppermute | solution.py:14
  33.2 7.6 %collective-permute-start.11 = (bf16[16,512]{1,0:T(8,128)(2,1)S(1)}, bf16[16,512]{1,0:T(8,128)(2,1)S(1)}, u32[]{:S(2)}, u32[]{:S(2)}) collective-permute-start(bf16[16,512]{1,0:T(8,128)(2,1)S(1)} %get-tuple-element.31), channel_id=1, source_target_pairs={{64,128},{128,64},{65,129},{129,65},{66,130},{130,66},{67,131},{13... | collective-permute-start | bytes 49160 | tf_op jit(solution)/shard_map/ppermute | solution.py:13
  36.4 4.4 %collective-permute-start.12 = (bf16[16,512]{1,0:T(8,128)(2,1)S(1)}, bf16[16,512]{1,0:T(8,128)(2,1)S(1)}, u32[]{:S(2)}, u32[]{:S(2)}) collective-permute-start(bf16[16,512]{1,0:T(8,128)(2,1)S(1)} %get-tuple-element.31), channel_id=1, source_target_pairs={{0,1},{1,0},{2,3},{3,2},{4,5},{5,4},{6,7},{7,6},{8,9},{9,8},{10,11... | collective-permute-start | bytes 49160 | tf_op jit(solution)/shard_map/ppermute | solution.py:14
  36.5 7.2 %collective-permute-start.13 = (bf16[16,512]{1,0:T(8,128)(2,1)S(1)}, bf16[16,512]{1,0:T(8,128)(2,1)S(1)}, u32[]{:S(2)}, u32[]{:S(2)}) collective-permute-start(bf16[16,512]{1,0:T(8,128)(2,1)S(1)} %get-tuple-element.31), channel_id=1, source_target_pairs={{1,2},{2,1},{3,4},{4,3},{5,6},{6,5},{7,8},{8,7},{9,10},{10,9},{11,... | collective-permute-start | bytes 49160 | tf_op jit(solution)/shard_map/ppermute | solution.py:13
  43.7 4.7 %collective-permute-start.14 = (bf16[16,512]{1,0:T(8,128)(2,1)S(1)}, bf16[16,512]{1,0:T(8,128)(2,1)S(1)}, u32[]{:S(2)}, u32[]{:S(2)}) collective-permute-start(bf16[16,512]{1,0:T(8,128)(2,1)S(1)} %subtract_convert_fusion.2), channel_id=1, source_target_pairs={{0,4},{1,5},{2,6},{3,7},{4,0},{5,1},{6,2},{7,3},{8,12},{9,13},{10,... | collective-permute-start | bytes 49160 | tf_op jit(solution)/shard_map/ppermute | solution.py:32
  60.8 12.6 %all-to-all-start.1 = ((bf16[16,16,512]{2,1,0:T(8,128)(2,1)}), bf16[16,16,512]{2,1,0:T(8,128)(2,1)S(1)}, u32[]{:S(2)}, u32[]{:S(2)}) async-start(bf16[16,16,512]{2,1,0:T(8,128)(2,1)} %broadcast_in_dim.7), calls=%async_computation.1 | async-start | bytes 524288 | tf_op jit(solution)/shard_map/all_to_all | solution.py:37
  67.7 20.2 %copy-start.7 = (f32[1,3,4,512]{3,2,1,0:T(4,128)S(1)}, f32[1,3,4,512]{3,2,1,0:T(4,128)}, u32[]{:S(2)}) copy-start(f32[1,3,4,512]{3,2,1,0:T(4,128)} %param.16) | copy-start | bytes 73732
  74.8 17.1 %copy-start.2 = (bf16[1,3,512,512]{3,2,1,0:T(8,128)(2,1)S(1)}, bf16[1,3,512,512]{3,2,1,0:T(8,128)(2,1)}, u32[]{:S(2)}) copy-start(bf16[1,3,512,512]{3,2,1,0:T(8,128)(2,1)} %param.17) | copy-start | bytes 4718596
  75.0 4.8 %collective-permute-start.15 = (bf16[16,512]{1,0:T(8,128)(2,1)S(1)}, bf16[16,512]{1,0:T(8,128)(2,1)S(1)}, u32[]{:S(2)}, u32[]{:S(2)}) collective-permute-start(bf16[16,512]{1,0:T(8,128)(2,1)S(1)} %convolution_convert_fusion.4), channel_id=1, source_target_pairs={{0,4},{1,5},{2,6},{3,7},{4,0},{5,1},{6,2},{7,3},{8,12},{9,13},{10,... | collective-permute-start | bytes 49160 | tf_op jit(solution)/shard_map/ppermute | solution.py:32
  76.9 41.2 %copy-start.3 = (bf16[1,8,64,256]{3,2,1,0:T(8,128)(2,1)S(1)}, bf16[1,8,64,256]{3,2,1,0:T(8,128)(2,1)}, u32[]{:S(2)}) copy-start(bf16[1,8,64,256]{3,2,1,0:T(8,128)(2,1)} %param.13) | copy-start | bytes 786436
  79.9 8.1 %collective-permute-start.16 = (bf16[16,512]{1,0:T(8,128)(2,1)S(1)}, bf16[16,512]{1,0:T(8,128)(2,1)S(1)}, u32[]{:S(2)}, u32[]{:S(2)}) collective-permute-start(bf16[16,512]{1,0:T(8,128)(2,1)S(1)} %fusion.51), channel_id=1, source_target_pairs={{0,64},{64,0},{128,192},{192,128},{1,65},{65,1},{129,193},{193,129... | collective-permute-start | bytes 49160 | tf_op jit(solution)/shard_map/ppermute | solution.py:14
  82.2 5.8 %collective-permute-start.17 = (bf16[16,512]{1,0:T(8,128)(2,1)S(1)}, bf16[16,512]{1,0:T(8,128)(2,1)S(1)}, u32[]{:S(2)}, u32[]{:S(2)}) collective-permute-start(bf16[16,512]{1,0:T(8,128)(2,1)S(1)} %fusion.51), channel_id=1, source_target_pairs={{64,128},{128,64},{65,129},{129,65},{66,130},{130,66},{67,131},{13... | collective-permute-start | bytes 49160 | tf_op jit(solution)/shard_map/ppermute | solution.py:13
  84.3 3.6 %collective-permute-start.18 = (bf16[16,512]{1,0:T(8,128)(2,1)S(1)}, bf16[16,512]{1,0:T(8,128)(2,1)S(1)}, u32[]{:S(2)}, u32[]{:S(2)}) collective-permute-start(bf16[16,512]{1,0:T(8,128)(2,1)S(1)} %fusion.51), channel_id=1, source_target_pairs={{0,1},{1,0},{2,3},{3,2},{4,5},{5,4},{6,7},{7,6},{8,9},{9,8},{10,11... | collective-permute-start | bytes 49160 | tf_op jit(solution)/shard_map/ppermute | solution.py:14
  84.4 7.2 %collective-permute-start.19 = (bf16[16,512]{1,0:T(8,128)(2,1)S(1)}, bf16[16,512]{1,0:T(8,128)(2,1)S(1)}, u32[]{:S(2)}, u32[]{:S(2)}) collective-permute-start(bf16[16,512]{1,0:T(8,128)(2,1)S(1)} %fusion.51), channel_id=1, source_target_pairs={{1,2},{2,1},{3,4},{4,3},{5,6},{6,5},{7,8},{8,7},{9,10},{10,9},{11,... | collective-permute-start | bytes 49160 | tf_op jit(solution)/shard_map/ppermute | solution.py:13
  91.9 3.8 %collective-permute-start.20 = (bf16[16,512]{1,0:T(8,128)(2,1)S(1)}, bf16[16,512]{1,0:T(8,128)(2,1)S(1)}, u32[]{:S(2)}, u32[]{:S(2)}) collective-permute-start(bf16[16,512]{1,0:T(8,128)(2,1)S(1)} %convolution_convert_fusion.3), channel_id=1, source_target_pairs={{0,2},{1,3},{2,0},{3,1},{4,6},{5,7},{6,4},{7,5},{8,10},{9,11},{10,... | collective-permute-start | bytes 49160 | tf_op jit(solution)/shard_map/ppermute | solution.py:32
  92.1 26.4 %copy-start.9 = (s32[1,8,64]{2,1,0:T(8,128)S(1)}, s32[1,8,64]{2,1,0:T(8,128)}, u32[]{:S(2)}) copy-start(s32[1,8,64]{2,1,0:T(8,128)} %param.14) | copy-start | bytes 6148
  95.6 5.8 %collective-permute-start.21 = (bf16[16,512]{1,0:T(8,128)(2,1)S(1)}, bf16[16,512]{1,0:T(8,128)(2,1)S(1)}, u32[]{:S(2)}, u32[]{:S(2)}) collective-permute-start(bf16[16,512]{1,0:T(8,128)(2,1)S(1)} %fusion.52), channel_id=1, source_target_pairs={{0,64},{64,0},{128,192},{192,128},{1,65},{65,1},{129,193},{193,129... | collective-permute-start | bytes 49160 | tf_op jit(solution)/shard_map/ppermute | solution.py:14
  95.7 5.8 %collective-permute-start.22 = (bf16[16,512]{1,0:T(8,128)(2,1)S(1)}, bf16[16,512]{1,0:T(8,128)(2,1)S(1)}, u32[]{:S(2)}, u32[]{:S(2)}) collective-permute-start(bf16[16,512]{1,0:T(8,128)(2,1)S(1)} %fusion.52), channel_id=1, source_target_pairs={{64,128},{128,64},{65,129},{129,65},{66,130},{130,66},{67,131},{13... | collective-permute-start | bytes 49160 | tf_op jit(solution)/shard_map/ppermute | solution.py:13
  99.3 2.2 %collective-permute-start.23 = (bf16[16,512]{1,0:T(8,128)(2,1)S(1)}, bf16[16,512]{1,0:T(8,128)(2,1)S(1)}, u32[]{:S(2)}, u32[]{:S(2)}) collective-permute-start(bf16[16,512]{1,0:T(8,128)(2,1)S(1)} %fusion.52), channel_id=1, source_target_pairs={{0,1},{1,0},{2,3},{3,2},{4,5},{5,4},{6,7},{7,6},{8,9},{9,8},{10,11... | collective-permute-start | bytes 49160 | tf_op jit(solution)/shard_map/ppermute | solution.py:14
  99.4 7.2 %collective-permute-start.24 = (bf16[16,512]{1,0:T(8,128)(2,1)S(1)}, bf16[16,512]{1,0:T(8,128)(2,1)S(1)}, u32[]{:S(2)}, u32[]{:S(2)}) collective-permute-start(bf16[16,512]{1,0:T(8,128)(2,1)S(1)} %fusion.52), channel_id=1, source_target_pairs={{1,2},{2,1},{3,4},{4,3},{5,6},{6,5},{7,8},{8,7},{9,10},{10,9},{11,... | collective-permute-start | bytes 49160 | tf_op jit(solution)/shard_map/ppermute | solution.py:13
  106.9 1.2 %collective-permute-start.25 = (bf16[16,512]{1,0:T(8,128)(2,1)S(1)}, bf16[16,512]{1,0:T(8,128)(2,1)S(1)}, u32[]{:S(2)}, u32[]{:S(2)}) collective-permute-start(bf16[16,512]{1,0:T(8,128)(2,1)S(1)} %convolution_convert_fusion.2), channel_id=1, source_target_pairs={{0,1},{1,0},{2,3},{3,2},{4,5},{5,4},{6,7},{7,6},{8,9},{9,8},{10,11... | collective-permute-start | bytes 49160 | tf_op jit(solution)/shard_map/ppermute | solution.py:32
  108.1 4.9 %collective-permute-start.26 = (bf16[16,512]{1,0:T(8,128)(2,1)S(1)}, bf16[16,512]{1,0:T(8,128)(2,1)S(1)}, u32[]{:S(2)}, u32[]{:S(2)}) collective-permute-start(bf16[16,512]{1,0:T(8,128)(2,1)S(1)} %fusion.53), channel_id=1, source_target_pairs={{0,64},{64,0},{128,192},{192,128},{1,65},{65,1},{129,193},{193,129... | collective-permute-start | bytes 49160 | tf_op jit(solution)/shard_map/ppermute | solution.py:14
  108.1 5.6 %collective-permute-start.27 = (bf16[16,512]{1,0:T(8,128)(2,1)S(1)}, bf16[16,512]{1,0:T(8,128)(2,1)S(1)}, u32[]{:S(2)}, u32[]{:S(2)}) collective-permute-start(bf16[16,512]{1,0:T(8,128)(2,1)S(1)} %fusion.53), channel_id=1, source_target_pairs={{64,128},{128,64},{65,129},{129,65},{66,130},{130,66},{67,131},{13... | collective-permute-start | bytes 49160 | tf_op jit(solution)/shard_map/ppermute | solution.py:13
  110.8 3.0 %collective-permute-start.28 = (bf16[16,512]{1,0:T(8,128)(2,1)S(1)}, bf16[16,512]{1,0:T(8,128)(2,1)S(1)}, u32[]{:S(2)}, u32[]{:S(2)}) collective-permute-start(bf16[16,512]{1,0:T(8,128)(2,1)S(1)} %fusion.53), channel_id=1, source_target_pairs={{0,1},{1,0},{2,3},{3,2},{4,5},{5,4},{6,7},{7,6},{8,9},{9,8},{10,11... | collective-permute-start | bytes 49160 | tf_op jit(solution)/shard_map/ppermute | solution.py:14
  110.9 7.2 %collective-permute-start.29 = (bf16[16,512]{1,0:T(8,128)(2,1)S(1)}, bf16[16,512]{1,0:T(8,128)(2,1)S(1)}, u32[]{:S(2)}, u32[]{:S(2)}) collective-permute-start(bf16[16,512]{1,0:T(8,128)(2,1)S(1)} %fusion.53), channel_id=1, source_target_pairs={{1,2},{2,1},{3,4},{4,3},{5,6},{6,5},{7,8},{8,7},{9,10},{10,9},{11,... | collective-permute-start | bytes 49160 | tf_op jit(solution)/shard_map/ppermute | solution.py:13
